TPU v7x, 512 devices: a whole 4x4x16 slice. The times are simulated.
512 devices in a mesh: pipe: 16 (over z), seq: 8 (over y, core), dp: 4 (over x).
Axes of the slice: x: 4, y: 4, z: 16, core: 2. Of those that a mesh axis runs over, the one named last changes fastest.
Arguments:
- acts: bfloat16 [16, 4, 1024, 8192], P('pipe', 'dp', 'seq'), may hold values from -6 to 6
- top_grad: bfloat16 [4, 1024, 8192], P('dp', 'seq'), may hold values from -6 to 6
- a_rows: bfloat16 [16, 32, 8192], P('pipe', None, ('seq', 'dp')), may hold values from -1 to 1
- b_rows: bfloat16 [16, 32, 8192], P('pipe', None, ('seq', 'dp')), may hold values from -0.375 to 0.375
- gain: bfloat16 [16, 8192], P('pipe', ('seq', 'dp')), may hold values from 0.5 to 1.5
Outputs:
- grad_a: float32 [16, 32, 8192], P('pipe', None, ('seq', 'dp'))
- grad_b: float32 [16, 32, 8192], P('pipe', None, ('seq', 'dp'))
- grad_gain: float32 [16, 8192], P('pipe', ('seq', 'dp'))
- clip_factors: float32 [4], P('dp')
All inputs are finite; a program needn't handle non-finite values.
Results may differ from a plain program's by a relative error of at most 0.019.
Values may be sent and summed in bfloat16 or wider, within the bound.
No kernel may reach another device: no remote copies, remote signals or barrier semaphores. Data moves between devices by JAX's collectives and lax.ppermute only.
A program may use at most 64 MiB of HBM per device.

v0:
```python
import math

import jax
import jax.numpy as jnp
from jax import lax
from jax.sharding import PartitionSpec as P

rows_per_block = 32


def from_behind(value, axis, steps):
    count = lax.axis_size(axis)
    initial, last = (max(0, -steps), min(count, count - steps))
    return lax.ppermute(value, axis, [(source, source + steps) for source in range(initial, last)])


def on_device(acts, top_grad, a_rows, b_rows, gain):
    sections = lax.axis_size("pipe")
    section = lax.axis_index("pipe")
    hidden = acts[0, 0]
    top = top_grad[0]
    a_whole, b_whole, gain_whole = (
        lax.all_gather(a_rows, ("seq", "dp"), axis=2, tiled=True),
        lax.all_gather(b_rows, ("seq", "dp"), axis=2, tiled=True),
        lax.all_gather(gain[:, None, :], ("seq", "dp"), axis=2, tiled=True),
    )
    a_full = a_whole[0]
    b_full = b_whole[0]
    gain_float = gain_whole[0, 0].astype(jnp.float32)
    rows, width = hidden.shape
    rank = a_full.shape[0]
    block_total = rows // rows_per_block
    hidden_float = hidden.astype(jnp.float32)
    inverse_root_mean = jnp.sqrt(
        jnp.mean(hidden_float * hidden_float, axis=-1, keepdims=True) + 1e-05
    )
    input_normalized = hidden_float / inverse_root_mean
    normalized_rows = (input_normalized * gain_float).astype(jnp.bfloat16)
    low = jnp.dot(normalized_rows, a_full.T, preferred_element_type=jnp.float32).astype(
        jnp.bfloat16
    )
    contract_last = (((1,), (1,)), ((), ()))
    contract_first = (((0,), (0,)), ((), ()))

    def back_block(upstream_gradient, block_offset):
        input_portion = lax.dynamic_slice_in_dim(input_normalized, block_offset, rows_per_block, 0)
        r_part = lax.dynamic_slice_in_dim(inverse_root_mean, block_offset, rows_per_block, 0)
        d_low = lax.dot_general(
            upstream_gradient, b_full, contract_last, preferred_element_type=jnp.float32
        ).astype(jnp.bfloat16)
        normalized_gradient = jnp.dot(d_low, a_full, preferred_element_type=jnp.float32)
        input_gradient = normalized_gradient * gain_float
        hidden_gradient = (
            upstream_gradient.astype(jnp.float32)
            + (
                input_gradient
                - input_portion * jnp.mean(input_gradient * input_portion, axis=-1, keepdims=True)
            )
            / r_part
        )
        return hidden_gradient.astype(jnp.bfloat16)

    def turn(turn_index, carry):
        incoming, mine = carry
        block_index = turn_index - (sections - 1 - section)
        inside = jnp.logical_and(block_index >= 0, block_index < block_total)
        block_offset = jnp.clip(block_index, 0, block_total - 1) * rows_per_block
        top_block = lax.dynamic_slice_in_dim(top, block_offset, rows_per_block, 0)
        source = jnp.where(section == sections - 1, top_block, incoming)
        kept = lax.dynamic_slice_in_dim(mine, block_offset, rows_per_block, 0)
        mine = lax.dynamic_update_slice_in_dim(
            mine, jnp.where(inside, source, kept), block_offset, 0
        )
        result = back_block(source, block_offset)
        incoming = from_behind(result, "pipe", -1)
        return (incoming, mine)

    begin = (
        jnp.zeros((rows_per_block, width), jnp.bfloat16),
        jnp.zeros((rows, width), jnp.bfloat16),
    )
    mine = lax.fori_loop(0, sections + block_total - 1, turn, begin)[1]
    d_low = lax.dot_general(mine, b_full, contract_last, preferred_element_type=jnp.float32).astype(
        jnp.bfloat16
    )
    normalized_gradient = jnp.dot(d_low, a_full, preferred_element_type=jnp.float32)
    grad_a = lax.dot_general(
        d_low, normalized_rows, contract_first, preferred_element_type=jnp.float32
    )
    grad_b = lax.dot_general(low, mine, contract_first, preferred_element_type=jnp.float32)
    gain_gradient = jnp.sum(normalized_gradient * input_normalized, axis=0)[None, :]
    grad_a, grad_b, gain_gradient = (grad_a, grad_b, gain_gradient)
    sum_a, sum_b, sum_g = lax.psum((grad_a, grad_b, gain_gradient), "seq")
    square = jnp.sum(sum_a * sum_a) + jnp.sum(sum_b * sum_b) + jnp.sum(sum_g * sum_g)
    total = lax.psum(square, "pipe")
    share = width // lax.axis_size("seq")
    offset = lax.axis_index("seq") * share
    part_a = lax.dynamic_slice_in_dim(sum_a, offset, share, 1)
    part_b = lax.dynamic_slice_in_dim(sum_b, offset, share, 1)
    part_g = lax.dynamic_slice_in_dim(sum_g, offset, share, 1)
    bound = math.sqrt(sections * (2 * rank + 1) * width)
    factor = bound / (jnp.sqrt(total) + 0.01 * bound)
    out_a, out_b, out_g = (
        lax.psum_scatter(factor * part_a, "dp", scatter_dimension=1, tiled=True),
        lax.psum_scatter(factor * part_b, "dp", scatter_dimension=1, tiled=True),
        lax.psum_scatter(factor * part_g, "dp", scatter_dimension=1, tiled=True),
    )
    return (out_a[None], out_b[None], out_g, jnp.reshape(factor, (1,)))


def solution(mesh):
    in_specs = (
        P("pipe", "dp", "seq", None),
        P("dp", "seq", None),
        P("pipe", None, ("seq", "dp")),
        P("pipe", None, ("seq", "dp")),
        P("pipe", ("seq", "dp")),
    )
    out_specs = (
        P("pipe", None, ("seq", "dp")),
        P("pipe", None, ("seq", "dp")),
        P("pipe", ("seq", "dp")),
        P("dp"),
    )
    return jax.shard_map(
        on_device, mesh=mesh, in_specs=in_specs, out_specs=out_specs, check_vma=False
    )
```

profile of v0, /device:TPU:6, one launch (start us, length us, event | category | flops | bytes accessed | tf_op | source)
XLA Modules:
  0.0 736.8 jit_solution(11694105464308485738)
XLA Ops:
  7.2 2.2 fusion.3
  9.5 2.4 fusion.1
  11.9 37.6 %all_gather.10 = bf16[1,32,8192]{2,1,0:T(8,128)(2,1)S(1)} all-gather(bf16[1,32,256]{2,1,0:T(8,128)(2,1)S(1)} %copy-done.2), channel_id=1, replica_groups=mesh['pipe'=16,'seq'=8,'dp'=4] {'seq','dp'}, dimensions={2}, use_global_device_ids=true | all-gather | bytes 540672 | tf_op jit(solution)/shard_map/all_gather | solution.py:23
  49.5 33.8 %all-gather = bf16[1,8192]{1,0:T(2,128)(2,1)S(1)} all-gather(bf16[1,256]{1,0:T(2,128)(2,1)S(1)} %copy-done.4), channel_id=2, replica_groups=mesh['pipe'=16,'seq'=8,'dp'=4] {'seq','dp'}, dimensions={1}, use_global_device_ids=true | all-gather | bytes 16896 | tf_op jit(solution)/shard_map/all_gather | solution.py:25
  83.4 33.1 %all_gather.9 = bf16[1,32,8192]{2,1,0:T(8,128)(2,1)S(1)} all-gather(bf16[1,32,256]{2,1,0:T(8,128)(2,1)S(1)} %copy-done.3), channel_id=1, replica_groups=mesh['pipe'=16,'seq'=8,'dp'=4] {'seq','dp'}, dimensions={2}, use_global_device_ids=true | all-gather | bytes 540672 | tf_op jit(solution)/shard_map/all_gather | solution.py:24
  118.1 392.1 %while.17 = (s32[]{:T(128)}, bf16[32,8192]{1,0:T(8,128)(2,1)S(1)}, bf16[128,8192]{1,0:T(8,128)(2,1)}, pred[]{:T(512)}, s32[]{:T(128)}, /*index=5*/bf16[128,8192]...) while((s32[]{:T(128)}, bf16[32,8192]{1,0:T(8,128)(2,1)S(1)}, ...), condition=%wide.region_3.4_spmd, body=%wide.region_1.3_spmd.sunk | while | flops 36439052 | bytes 11568829 | solution.py:82
  118.1 2.2 select_dynamic-update-slice_fusion.2
  122.5 2.3 add_convert_fusion.2
  126.1 14.6 %collective-permute-done = bf16[32,8192]{1,0:T(8,128)(2,1)S(1)} collective-permute-done((bf16[32,8192]{1,0:T(8,128)(2,1)}, bf16[32,8192]{1,0:T(8,128)(2,1)S(1)}, u32[]{:S(2)}, u32[]{:S(2)}) %collective-permute-start) | collective-permute-done | bytes 524320 | tf_op jit(solution)/shard_map/while/body/eval_jaxpr/ppermute | solution.py:14
  140.7 2.2 select_dynamic-update-slice_fusion.2
  145.1 2.3 add_convert_fusion.2
  148.7 13.8 %collective-permute-done = bf16[32,8192]{1,0:T(8,128)(2,1)S(1)} collective-permute-done((bf16[32,8192]{1,0:T(8,128)(2,1)}, bf16[32,8192]{1,0:T(8,128)(2,1)S(1)}, u32[]{:S(2)}, u32[]{:S(2)}) %collective-permute-start) | collective-permute-done | bytes 524320 | tf_op jit(solution)/shard_map/while/body/eval_jaxpr/ppermute | solution.py:14
  166.9 2.3 add_convert_fusion.2
  170.5 12.9 %collective-permute-done = bf16[32,8192]{1,0:T(8,128)(2,1)S(1)} collective-permute-done((bf16[32,8192]{1,0:T(8,128)(2,1)}, bf16[32,8192]{1,0:T(8,128)(2,1)S(1)}, u32[]{:S(2)}, u32[]{:S(2)}) %collective-permute-start) | collective-permute-done | bytes 524320 | tf_op jit(solution)/shard_map/while/body/eval_jaxpr/ppermute | solution.py:14
  183.4 2.2 select_dynamic-update-slice_fusion.2
  187.8 2.3 add_convert_fusion.2
  191.3 12.0 %collective-permute-done = bf16[32,8192]{1,0:T(8,128)(2,1)S(1)} collective-permute-done((bf16[32,8192]{1,0:T(8,128)(2,1)}, bf16[32,8192]{1,0:T(8,128)(2,1)S(1)}, u32[]{:S(2)}, u32[]{:S(2)}) %collective-permute-start) | collective-permute-done | bytes 524320 | tf_op jit(solution)/shard_map/while/body/eval_jaxpr/ppermute | solution.py:14
  203.4 2.2 select_dynamic-update-slice_fusion.2
  207.8 2.3 add_convert_fusion.2
  211.4 12.6 %collective-permute-done = bf16[32,8192]{1,0:T(8,128)(2,1)S(1)} collective-permute-done((bf16[32,8192]{1,0:T(8,128)(2,1)}, bf16[32,8192]{1,0:T(8,128)(2,1)S(1)}, u32[]{:S(2)}, u32[]{:S(2)}) %collective-permute-start) | collective-permute-done | bytes 524320 | tf_op jit(solution)/shard_map/while/body/eval_jaxpr/ppermute | solution.py:14
  224.0 2.2 select_dynamic-update-slice_fusion.2
  228.4 2.3 add_convert_fusion.2
  232.0 11.7 %collective-permute-done = bf16[32,8192]{1,0:T(8,128)(2,1)S(1)} collective-permute-done((bf16[32,8192]{1,0:T(8,128)(2,1)}, bf16[32,8192]{1,0:T(8,128)(2,1)S(1)}, u32[]{:S(2)}, u32[]{:S(2)}) %collective-permute-start) | collective-permute-done | bytes 524320 | tf_op jit(solution)/shard_map/while/body/eval_jaxpr/ppermute | solution.py:14
  243.7 2.2 select_dynamic-update-slice_fusion.2
  248.1 2.3 add_convert_fusion.2
  251.7 10.9 %collective-permute-done = bf16[32,8192]{1,0:T(8,128)(2,1)S(1)} collective-permute-done((bf16[32,8192]{1,0:T(8,128)(2,1)}, bf16[32,8192]{1,0:T(8,128)(2,1)S(1)}, u32[]{:S(2)}, u32[]{:S(2)}) %collective-permute-start) | collective-permute-done | bytes 524320 | tf_op jit(solution)/shard_map/while/body/eval_jaxpr/ppermute | solution.py:14
  262.5 2.2 select_dynamic-update-slice_fusion.2
  267.0 2.3 add_convert_fusion.2
  270.5 10.4 %collective-permute-done = bf16[32,8192]{1,0:T(8,128)(2,1)S(1)} collective-permute-done((bf16[32,8192]{1,0:T(8,128)(2,1)}, bf16[32,8192]{1,0:T(8,128)(2,1)S(1)}, u32[]{:S(2)}, u32[]{:S(2)}) %collective-permute-start) | collective-permute-done | bytes 524320 | tf_op jit(solution)/shard_map/while/body/eval_jaxpr/ppermute | solution.py:14
  285.3 2.3 add_convert_fusion.2
  288.9 10.7 %collective-permute-done = bf16[32,8192]{1,0:T(8,128)(2,1)S(1)} collective-permute-done((bf16[32,8192]{1,0:T(8,128)(2,1)}, bf16[32,8192]{1,0:T(8,128)(2,1)S(1)}, u32[]{:S(2)}, u32[]{:S(2)}) %collective-permute-start) | collective-permute-done | bytes 524320 | tf_op jit(solution)/shard_map/while/body/eval_jaxpr/ppermute | solution.py:14
  304.0 2.3 add_convert_fusion.2
  307.5 11.2 %collective-permute-done = bf16[32,8192]{1,0:T(8,128)(2,1)S(1)} collective-permute-done((bf16[32,8192]{1,0:T(8,128)(2,1)}, bf16[32,8192]{1,0:T(8,128)(2,1)S(1)}, u32[]{:S(2)}, u32[]{:S(2)}) %collective-permute-start) | collective-permute-done | bytes 524320 | tf_op jit(solution)/shard_map/while/body/eval_jaxpr/ppermute | solution.py:14
  323.1 2.3 add_convert_fusion.2
  326.7 11.2 %collective-permute-done = bf16[32,8192]{1,0:T(8,128)(2,1)S(1)} collective-permute-done((bf16[32,8192]{1,0:T(8,128)(2,1)}, bf16[32,8192]{1,0:T(8,128)(2,1)S(1)}, u32[]{:S(2)}, u32[]{:S(2)}) %collective-permute-start) | collective-permute-done | bytes 524320 | tf_op jit(solution)/shard_map/while/body/eval_jaxpr/ppermute | solution.py:14
  342.3 2.3 add_convert_fusion.2
  345.9 11.2 %collective-permute-done = bf16[32,8192]{1,0:T(8,128)(2,1)S(1)} collective-permute-done((bf16[32,8192]{1,0:T(8,128)(2,1)}, bf16[32,8192]{1,0:T(8,128)(2,1)S(1)}, u32[]{:S(2)}, u32[]{:S(2)}) %collective-permute-start) | collective-permute-done | bytes 524320 | tf_op jit(solution)/shard_map/while/body/eval_jaxpr/ppermute | solution.py:14
  361.5 2.3 add_convert_fusion.2
  365.1 11.2 %collective-permute-done = bf16[32,8192]{1,0:T(8,128)(2,1)S(1)} collective-permute-done((bf16[32,8192]{1,0:T(8,128)(2,1)}, bf16[32,8192]{1,0:T(8,128)(2,1)S(1)}, u32[]{:S(2)}, u32[]{:S(2)}) %collective-permute-start) | collective-permute-done | bytes 524320 | tf_op jit(solution)/shard_map/while/body/eval_jaxpr/ppermute | solution.py:14
  380.7 2.3 add_convert_fusion.2
  384.3 11.9 %collective-permute-done = bf16[32,8192]{1,0:T(8,128)(2,1)S(1)} collective-permute-done((bf16[32,8192]{1,0:T(8,128)(2,1)}, bf16[32,8192]{1,0:T(8,128)(2,1)S(1)}, u32[]{:S(2)}, u32[]{:S(2)}) %collective-permute-start) | collective-permute-done | bytes 524320 | tf_op jit(solution)/shard_map/while/body/eval_jaxpr/ppermute | solution.py:14
  400.6 2.3 add_convert_fusion.2
  404.2 13.3 %collective-permute-done = bf16[32,8192]{1,0:T(8,128)(2,1)S(1)} collective-permute-done((bf16[32,8192]{1,0:T(8,128)(2,1)}, bf16[32,8192]{1,0:T(8,128)(2,1)S(1)}, u32[]{:S(2)}, u32[]{:S(2)}) %collective-permute-start) | collective-permute-done | bytes 524320 | tf_op jit(solution)/shard_map/while/body/eval_jaxpr/ppermute | solution.py:14
  421.9 2.3 add_convert_fusion.2
  425.5 15.2 %collective-permute-done = bf16[32,8192]{1,0:T(8,128)(2,1)S(1)} collective-permute-done((bf16[32,8192]{1,0:T(8,128)(2,1)}, bf16[32,8192]{1,0:T(8,128)(2,1)S(1)}, u32[]{:S(2)}, u32[]{:S(2)}) %collective-permute-start) | collective-permute-done | bytes 524320 | tf_op jit(solution)/shard_map/while/body/eval_jaxpr/ppermute | solution.py:14
  440.7 2.2 select_dynamic-update-slice_fusion.2
  445.2 2.3 add_convert_fusion.2
  448.7 16.1 %collective-permute-done = bf16[32,8192]{1,0:T(8,128)(2,1)S(1)} collective-permute-done((bf16[32,8192]{1,0:T(8,128)(2,1)}, bf16[32,8192]{1,0:T(8,128)(2,1)S(1)}, u32[]{:S(2)}, u32[]{:S(2)}) %collective-permute-start) | collective-permute-done | bytes 524320 | tf_op jit(solution)/shard_map/while/body/eval_jaxpr/ppermute | solution.py:14
  464.8 2.2 select_dynamic-update-slice_fusion.2
  469.2 2.3 add_convert_fusion.2
  472.8 17.3 %collective-permute-done = bf16[32,8192]{1,0:T(8,128)(2,1)S(1)} collective-permute-done((bf16[32,8192]{1,0:T(8,128)(2,1)}, bf16[32,8192]{1,0:T(8,128)(2,1)S(1)}, u32[]{:S(2)}, u32[]{:S(2)}) %collective-permute-start) | collective-permute-done | bytes 524320 | tf_op jit(solution)/shard_map/while/body/eval_jaxpr/ppermute | solution.py:14
  490.2 2.2 select_dynamic-update-slice_fusion.2
  494.6 2.3 add_convert_fusion.2
  498.2 12.0 %collective-permute-done = bf16[32,8192]{1,0:T(8,128)(2,1)S(1)} collective-permute-done((bf16[32,8192]{1,0:T(8,128)(2,1)}, bf16[32,8192]{1,0:T(8,128)(2,1)S(1)}, u32[]{:S(2)}, u32[]{:S(2)}) %collective-permute-start) | collective-permute-done | bytes 524320 | tf_op jit(solution)/shard_map/while/body/eval_jaxpr/ppermute | solution.py:14
  510.2 4.9 fusion.16
  515.1 2.5 convolution_convert_fusion.1
  519.6 2.4 fusion.11
  522.0 23.6 %psum.30 = f32[1,8192]{1,0:T(1,128)S(1)} all-reduce(f32[1,8192]{1,0:T(1,128)S(1)} %bitcast.65), channel_id=1, replica_groups=mesh['pipe'=16,'seq'=8,'dp'=4] {'seq'}, use_global_device_ids=true, to_apply=%region_9.10 | all-reduce | flops 8192 | bytes 65536 | tf_op jit(solution)/shard_map/psum | solution.py:93
  546.2 58.5 %all-reduce.3.cloned.1.call-done = (f32[32,8192]{1,0:T(8,128)}, f32[32,8192]{1,0:T(8,128)}) async-done(((f32[32,8192]{1,0:T(8,128)}, f32[32,8192]{1,0:T(8,128)}), (f32[32,8192]{1,0:T(8,128)}, f32[32,8192]{1,0:T(8,128)})) %all-reduce.3.cloned.1.call-update) | async-done | bytes 2097168 | tf_op jit(solution)/shard_map/psum | solution.py:93
  604.7 2.4 multiply_reduce_fusion.1
  609.1 31.8 %psum.31 = f32[]{:T(128)} all-reduce(f32[]{:T(128)S(6)} %add.88), channel_id=1, replica_groups=mesh['pipe'=16,'seq'=8,'dp'=4] {'pipe'}, use_global_device_ids=true, to_apply=%region_11.12 | all-reduce | flops 1 | bytes 8 | tf_op jit(solution)/shard_map/psum | solution.py:95
  646.0 19.9 %reduce-scatter.10.cloned.1.call-done = f32[256,1]{1,0:T(8,128)} async-done(((f32[1024,1]{1,0:T(8,128)}), f32[256,1]{1,0:T(8,128)}) %reduce-scatter.10.cloned.1.call-update) | async-done | bytes 1040
  667.4 30.3 %reduce-scatter.8.cloned.1.call-done = f32[32,256]{1,0:T(8,128)} async-done(((f32[32,1024]{1,0:T(8,128)}), f32[32,256]{1,0:T(8,128)}) %reduce-scatter.8.cloned.1.call-update) | async-done | bytes 32784 | tf_op jit(solution)/shard_map/reduce_scatter | solution.py:105
  697.8 31.4 %reduce-scatter.6.cloned.1.call-done = f32[32,256]{1,0:T(8,128)} async-done(((f32[32,1024]{1,0:T(8,128)}), f32[32,256]{1,0:T(8,128)}) %reduce-scatter.6.cloned.1.call-update) | async-done | bytes 32784 | tf_op jit(solution)/shard_map/reduce_scatter | solution.py:104
  (114 shorter events, 95.9 us)
Async XLA Ops:
  7.2 597.5 %all-reduce.3.cloned.1.call-start = ((), (), s32[]{:S(2)}) async-start(), calls=%async_computation.6 | async-start | bytes 4194304 | tf_op jit(solution)/shard_map/psum | solution.py:93
  7.2 2.3 copy-start
  9.5 2.4 copy-start.2
  9.5 40.0 %copy-start.4 = (bf16[1,256]{1,0:T(2,128)(2,1)S(1)}, bf16[1,256]{1,0:T(2,128)(2,1)}, u32[]{:S(2)}) copy-start(bf16[1,256]{1,0:T(2,128)(2,1)} %param.11) | copy-start | bytes 1540
  9.5 73.9 %copy-start.3 = (bf16[1,32,256]{2,1,0:T(8,128)(2,1)S(1)}, bf16[1,32,256]{2,1,0:T(8,128)(2,1)}, u32[]{:S(2)}) copy-start(bf16[1,32,256]{2,1,0:T(8,128)(2,1)} %param.10) | copy-start | bytes 49156
  124.8 15.9 %collective-permute-start = (bf16[32,8192]{1,0:T(8,128)(2,1)}, bf16[32,8192]{1,0:T(8,128)(2,1)S(1)}, u32[]{:S(2)}, u32[]{:S(2)}) collective-permute-start(bf16[32,8192]{1,0:T(8,128)(2,1)} %add_convert_fusion.2), channel_id=1, source_target_pairs={{32,0},{64,32},{96,64},{128,96},{160,128},{192,160},{224,192},{256... | collective-permute-start | bytes 1572872 | tf_op jit(solution)/shard_map/while/body/eval_jaxpr/ppermute | solution.py:14
  147.4 15.0 %collective-permute-start = (bf16[32,8192]{1,0:T(8,128)(2,1)}, bf16[32,8192]{1,0:T(8,128)(2,1)S(1)}, u32[]{:S(2)}, u32[]{:S(2)}) collective-permute-start(bf16[32,8192]{1,0:T(8,128)(2,1)} %add_convert_fusion.2), channel_id=1, source_target_pairs={{32,0},{64,32},{96,64},{128,96},{160,128},{192,160},{224,192},{256... | collective-permute-start | bytes 1572872 | tf_op jit(solution)/shard_map/while/body/eval_jaxpr/ppermute | solution.py:14
  169.2 14.2 %collective-permute-start = (bf16[32,8192]{1,0:T(8,128)(2,1)}, bf16[32,8192]{1,0:T(8,128)(2,1)S(1)}, u32[]{:S(2)}, u32[]{:S(2)}) collective-permute-start(bf16[32,8192]{1,0:T(8,128)(2,1)} %add_convert_fusion.2), channel_id=1, source_target_pairs={{32,0},{64,32},{96,64},{128,96},{160,128},{192,160},{224,192},{256... | collective-permute-start | bytes 1572872 | tf_op jit(solution)/shard_map/while/body/eval_jaxpr/ppermute | solution.py:14
  190.1 13.3 %collective-permute-start = (bf16[32,8192]{1,0:T(8,128)(2,1)}, bf16[32,8192]{1,0:T(8,128)(2,1)S(1)}, u32[]{:S(2)}, u32[]{:S(2)}) collective-permute-start(bf16[32,8192]{1,0:T(8,128)(2,1)} %add_convert_fusion.2), channel_id=1, source_target_pairs={{32,0},{64,32},{96,64},{128,96},{160,128},{192,160},{224,192},{256... | collective-permute-start | bytes 1572872 | tf_op jit(solution)/shard_map/while/body/eval_jaxpr/ppermute | solution.py:14
  210.1 13.9 %collective-permute-start = (bf16[32,8192]{1,0:T(8,128)(2,1)}, bf16[32,8192]{1,0:T(8,128)(2,1)S(1)}, u32[]{:S(2)}, u32[]{:S(2)}) collective-permute-start(bf16[32,8192]{1,0:T(8,128)(2,1)} %add_convert_fusion.2), channel_id=1, source_target_pairs={{32,0},{64,32},{96,64},{128,96},{160,128},{192,160},{224,192},{256... | collective-permute-start | bytes 1572872 | tf_op jit(solution)/shard_map/while/body/eval_jaxpr/ppermute | solution.py:14
  230.7 13.0 %collective-permute-start = (bf16[32,8192]{1,0:T(8,128)(2,1)}, bf16[32,8192]{1,0:T(8,128)(2,1)S(1)}, u32[]{:S(2)}, u32[]{:S(2)}) collective-permute-start(bf16[32,8192]{1,0:T(8,128)(2,1)} %add_convert_fusion.2), channel_id=1, source_target_pairs={{32,0},{64,32},{96,64},{128,96},{160,128},{192,160},{224,192},{256... | collective-permute-start | bytes 1572872 | tf_op jit(solution)/shard_map/while/body/eval_jaxpr/ppermute | solution.py:14
  250.4 12.2 %collective-permute-start = (bf16[32,8192]{1,0:T(8,128)(2,1)}, bf16[32,8192]{1,0:T(8,128)(2,1)S(1)}, u32[]{:S(2)}, u32[]{:S(2)}) collective-permute-start(bf16[32,8192]{1,0:T(8,128)(2,1)} %add_convert_fusion.2), channel_id=1, source_target_pairs={{32,0},{64,32},{96,64},{128,96},{160,128},{192,160},{224,192},{256... | collective-permute-start | bytes 1572872 | tf_op jit(solution)/shard_map/while/body/eval_jaxpr/ppermute | solution.py:14
  269.2 11.6 %collective-permute-start = (bf16[32,8192]{1,0:T(8,128)(2,1)}, bf16[32,8192]{1,0:T(8,128)(2,1)S(1)}, u32[]{:S(2)}, u32[]{:S(2)}) collective-permute-start(bf16[32,8192]{1,0:T(8,128)(2,1)} %add_convert_fusion.2), channel_id=1, source_target_pairs={{32,0},{64,32},{96,64},{128,96},{160,128},{192,160},{224,192},{256... | collective-permute-start | bytes 1572872 | tf_op jit(solution)/shard_map/while/body/eval_jaxpr/ppermute | solution.py:14
  287.6 12.0 %collective-permute-start = (bf16[32,8192]{1,0:T(8,128)(2,1)}, bf16[32,8192]{1,0:T(8,128)(2,1)S(1)}, u32[]{:S(2)}, u32[]{:S(2)}) collective-permute-start(bf16[32,8192]{1,0:T(8,128)(2,1)} %add_convert_fusion.2), channel_id=1, source_target_pairs={{32,0},{64,32},{96,64},{128,96},{160,128},{192,160},{224,192},{256... | collective-permute-start | bytes 1572872 | tf_op jit(solution)/shard_map/while/body/eval_jaxpr/ppermute | solution.py:14
  306.2 12.5 %collective-permute-start = (bf16[32,8192]{1,0:T(8,128)(2,1)}, bf16[32,8192]{1,0:T(8,128)(2,1)S(1)}, u32[]{:S(2)}, u32[]{:S(2)}) collective-permute-start(bf16[32,8192]{1,0:T(8,128)(2,1)} %add_convert_fusion.2), channel_id=1, source_target_pairs={{32,0},{64,32},{96,64},{128,96},{160,128},{192,160},{224,192},{256... | collective-permute-start | bytes 1572872 | tf_op jit(solution)/shard_map/while/body/eval_jaxpr/ppermute | solution.py:14
  325.4 12.5 %collective-permute-start = (bf16[32,8192]{1,0:T(8,128)(2,1)}, bf16[32,8192]{1,0:T(8,128)(2,1)S(1)}, u32[]{:S(2)}, u32[]{:S(2)}) collective-permute-start(bf16[32,8192]{1,0:T(8,128)(2,1)} %add_convert_fusion.2), channel_id=1, source_target_pairs={{32,0},{64,32},{96,64},{128,96},{160,128},{192,160},{224,192},{256... | collective-permute-start | bytes 1572872 | tf_op jit(solution)/shard_map/while/body/eval_jaxpr/ppermute | solution.py:14
  344.6 12.5 %collective-permute-start = (bf16[32,8192]{1,0:T(8,128)(2,1)}, bf16[32,8192]{1,0:T(8,128)(2,1)S(1)}, u32[]{:S(2)}, u32[]{:S(2)}) collective-permute-start(bf16[32,8192]{1,0:T(8,128)(2,1)} %add_convert_fusion.2), channel_id=1, source_target_pairs={{32,0},{64,32},{96,64},{128,96},{160,128},{192,160},{224,192},{256... | collective-permute-start | bytes 1572872 | tf_op jit(solution)/shard_map/while/body/eval_jaxpr/ppermute | solution.py:14
  363.8 12.5 %collective-permute-start = (bf16[32,8192]{1,0:T(8,128)(2,1)}, bf16[32,8192]{1,0:T(8,128)(2,1)S(1)}, u32[]{:S(2)}, u32[]{:S(2)}) collective-permute-start(bf16[32,8192]{1,0:T(8,128)(2,1)} %add_convert_fusion.2), channel_id=1, source_target_pairs={{32,0},{64,32},{96,64},{128,96},{160,128},{192,160},{224,192},{256... | collective-permute-start | bytes 1572872 | tf_op jit(solution)/shard_map/while/body/eval_jaxpr/ppermute | solution.py:14
  383.0 13.2 %collective-permute-start = (bf16[32,8192]{1,0:T(8,128)(2,1)}, bf16[32,8192]{1,0:T(8,128)(2,1)S(1)}, u32[]{:S(2)}, u32[]{:S(2)}) collective-permute-start(bf16[32,8192]{1,0:T(8,128)(2,1)} %add_convert_fusion.2), channel_id=1, source_target_pairs={{32,0},{64,32},{96,64},{128,96},{160,128},{192,160},{224,192},{256... | collective-permute-start | bytes 1572872 | tf_op jit(solution)/shard_map/while/body/eval_jaxpr/ppermute | solution.py:14
  402.9 14.6 %collective-permute-start = (bf16[32,8192]{1,0:T(8,128)(2,1)}, bf16[32,8192]{1,0:T(8,128)(2,1)S(1)}, u32[]{:S(2)}, u32[]{:S(2)}) collective-permute-start(bf16[32,8192]{1,0:T(8,128)(2,1)} %add_convert_fusion.2), channel_id=1, source_target_pairs={{32,0},{64,32},{96,64},{128,96},{160,128},{192,160},{224,192},{256... | collective-permute-start | bytes 1572872 | tf_op jit(solution)/shard_map/while/body/eval_jaxpr/ppermute | solution.py:14
  424.2 16.5 %collective-permute-start = (bf16[32,8192]{1,0:T(8,128)(2,1)}, bf16[32,8192]{1,0:T(8,128)(2,1)S(1)}, u32[]{:S(2)}, u32[]{:S(2)}) collective-permute-start(bf16[32,8192]{1,0:T(8,128)(2,1)} %add_convert_fusion.2), channel_id=1, source_target_pairs={{32,0},{64,32},{96,64},{128,96},{160,128},{192,160},{224,192},{256... | collective-permute-start | bytes 1572872 | tf_op jit(solution)/shard_map/while/body/eval_jaxpr/ppermute | solution.py:14
  447.4 17.4 %collective-permute-start = (bf16[32,8192]{1,0:T(8,128)(2,1)}, bf16[32,8192]{1,0:T(8,128)(2,1)S(1)}, u32[]{:S(2)}, u32[]{:S(2)}) collective-permute-start(bf16[32,8192]{1,0:T(8,128)(2,1)} %add_convert_fusion.2), channel_id=1, source_target_pairs={{32,0},{64,32},{96,64},{128,96},{160,128},{192,160},{224,192},{256... | collective-permute-start | bytes 1572872 | tf_op jit(solution)/shard_map/while/body/eval_jaxpr/ppermute | solution.py:14
  471.5 18.6 %collective-permute-start = (bf16[32,8192]{1,0:T(8,128)(2,1)}, bf16[32,8192]{1,0:T(8,128)(2,1)S(1)}, u32[]{:S(2)}, u32[]{:S(2)}) collective-permute-start(bf16[32,8192]{1,0:T(8,128)(2,1)} %add_convert_fusion.2), channel_id=1, source_target_pairs={{32,0},{64,32},{96,64},{128,96},{160,128},{192,160},{224,192},{256... | collective-permute-start | bytes 1572872 | tf_op jit(solution)/shard_map/while/body/eval_jaxpr/ppermute | solution.py:14
  496.9 13.3 %collective-permute-start = (bf16[32,8192]{1,0:T(8,128)(2,1)}, bf16[32,8192]{1,0:T(8,128)(2,1)S(1)}, u32[]{:S(2)}, u32[]{:S(2)}) collective-permute-start(bf16[32,8192]{1,0:T(8,128)(2,1)} %add_convert_fusion.2), channel_id=1, source_target_pairs={{32,0},{64,32},{96,64},{128,96},{160,128},{192,160},{224,192},{256... | collective-permute-start | bytes 1572872 | tf_op jit(solution)/shard_map/while/body/eval_jaxpr/ppermute | solution.py:14
  515.1 2.6 copy-start.1
  519.6 146.3 %reduce-scatter.10.cloned.1.call-start = ((), (), s32[]{:S(2)}) async-start(), calls=%async_computation.5 | async-start | bytes 655360
  642.7 55.1 %reduce-scatter.8.cloned.1.call-start = ((), (), s32[]{:S(2)}) async-start(), calls=%async_computation.4 | async-start | bytes 163840 | tf_op jit(solution)/shard_map/reduce_scatter | solution.py:105
  644.3 84.8 %reduce-scatter.6.cloned.1.call-start = ((), (), s32[]{:S(2)}) async-start(), calls=%async_computation.3 | async-start | bytes 163840 | tf_op jit(solution)/shard_map/reduce_scatter | solution.py:104
Sparse Core Ops, SparseCore 0:
  519.7 84.9 all-reduce.2
  642.8 23.0 reduce-scatter.9
  669.2 28.4 reduce-scatter.7
  701.0 28.1 reduce-scatter.5
where the time goes:
time: 741 us; the launch traced here: 737 us
  waiting for transfers between devices  380 us (51%)
  blocking collectives  160 us (22%)
  other arithmetic  96.6 us (13%)
  matrix products  51.7 us (7%)
  starting transfers between devices  24.5 us (3%)
  between operations  17.7 us (2%)
    ppermute x19, waiting for transfers between devices, from_behind(): lax.ppermute(value, axis, [(source, source + steps) for source in range(i...  240 us
    psum x1, waiting for transfers between devices, on_device(): sum_a, sum_b, sum_g = lax.psum((grad_a, grad_b, gain_gradient), 'seq')  58.5 us
    convert_element_type x19, other arithmetic, back_block(): return hidden_gradient.astype(jnp.bfloat16)  43.6 us
    dynamic_update_slice x19, other arithmetic, turn(): lax.dynamic_update_slice_in_dim(mine, jnp.where(inside, source, kept), bl...  42 us
    dot_general x19, matrix products, back_block(): jnp.dot(d_low, a_full, preferred_element_type=jnp.float32)  40.1 us
    all_gather x1, blocking collectives, on_device(): lax.all_gather(a_rows, ('seq', 'dp'), axis=2, tiled=True)  37.6 us
    all_gather x1, blocking collectives, on_device(): lax.all_gather(gain[:, None, :], ('seq', 'dp'), axis=2, tiled=True)  33.8 us
    all_gather x1, blocking collectives, on_device(): lax.all_gather(b_rows, ('seq', 'dp'), axis=2, tiled=True)  33.1 us
  transfers between devices with their start and end apart: 23, of which 23 were waited for; matrix products, arithmetic and copies ran while one was open for 1% of the time, Pallas kernels for 0%

commit v1 on v0

v1 whole, which is shorter than its diff:
```python
import math

import jax
import jax.numpy as jnp
from jax import lax
from jax.sharding import PartitionSpec as P

rows_per_block = 16


def from_behind(value, axis, steps):
    count = lax.axis_size(axis)
    initial, last = (max(0, -steps), min(count, count - steps))
    return lax.ppermute(value, axis, [(source, source + steps) for source in range(initial, last)])


def on_device(acts, top_grad, a_rows, b_rows, gain):
    sections = lax.axis_size("pipe")
    section = lax.axis_index("pipe")
    hidden = acts[0, 0]
    top = top_grad[0]
    rank = a_rows.shape[1]
    params = jnp.concatenate([a_rows[0], b_rows[0], gain], axis=0)
    whole = lax.all_gather(params, ("seq", "dp"), axis=1, tiled=True)
    a_full = whole[:rank]
    b_full = whole[rank : 2 * rank]
    gain_float = whole[2 * rank].astype(jnp.float32)
    rows, width = hidden.shape
    block_total = rows // rows_per_block
    hidden_float = hidden.astype(jnp.float32)
    inverse_root_mean = jnp.sqrt(
        jnp.mean(hidden_float * hidden_float, axis=-1, keepdims=True) + 1e-05
    )
    input_normalized = hidden_float / inverse_root_mean
    normalized_rows = (input_normalized * gain_float).astype(jnp.bfloat16)
    low = jnp.dot(normalized_rows, a_full.T, preferred_element_type=jnp.float32).astype(
        jnp.bfloat16
    )
    contract_last = (((1,), (1,)), ((), ()))
    contract_first = (((0,), (0,)), ((), ()))

    def back_block(upstream_gradient, block_offset):
        hidden_part = lax.dynamic_slice_in_dim(hidden, block_offset, rows_per_block, 0)
        r_part = lax.dynamic_slice_in_dim(inverse_root_mean, block_offset, rows_per_block, 0)
        input_portion = hidden_part.astype(jnp.float32) / r_part
        d_low = lax.dot_general(
            upstream_gradient, b_full, contract_last, preferred_element_type=jnp.float32
        ).astype(jnp.bfloat16)
        normalized_gradient = jnp.dot(d_low, a_full, preferred_element_type=jnp.float32)
        input_gradient = normalized_gradient * gain_float
        hidden_gradient = (
            upstream_gradient.astype(jnp.float32)
            + (
                input_gradient
                - input_portion * jnp.mean(input_gradient * input_portion, axis=-1, keepdims=True)
            )
            / r_part
        )
        return hidden_gradient.astype(jnp.bfloat16)

    def turn(turn_index, carry):
        incoming, store = carry
        block_index = turn_index - (sections - 1 - section)
        inside = jnp.logical_and(block_index >= 0, block_index < block_total)
        block_offset = jnp.clip(block_index, 0, block_total - 1) * rows_per_block
        top_block = lax.dynamic_slice_in_dim(top, block_offset, rows_per_block, 0)
        source = jnp.where(section == sections - 1, top_block, incoming)
        slot = jnp.where(inside, block_index, block_total)
        store = lax.dynamic_update_slice_in_dim(store, source[None], slot, 0)
        result = back_block(source, block_offset)
        incoming = from_behind(result, "pipe", -1)
        return (incoming, store)

    begin = (
        jnp.zeros((rows_per_block, width), jnp.bfloat16),
        jnp.zeros((block_total + 1, rows_per_block, width), jnp.bfloat16),
    )
    store = lax.fori_loop(0, sections + block_total - 1, turn, begin)[1]
    mine = store[:block_total].reshape(rows, width)
    d_low = lax.dot_general(mine, b_full, contract_last, preferred_element_type=jnp.float32).astype(
        jnp.bfloat16
    )
    normalized_gradient = jnp.dot(d_low, a_full, preferred_element_type=jnp.float32)
    grad_a = lax.dot_general(
        d_low, normalized_rows, contract_first, preferred_element_type=jnp.float32
    )
    grad_b = lax.dot_general(low, mine, contract_first, preferred_element_type=jnp.float32)
    gain_gradient = jnp.sum(normalized_gradient * input_normalized, axis=0)[None, :]
    grads = jnp.concatenate([grad_a, grad_b, gain_gradient], axis=0)
    part = lax.psum_scatter(grads, "seq", scatter_dimension=1, tiled=True)
    examples = lax.axis_size("dp")
    example = lax.axis_index("dp")
    square = jnp.sum(part * part)
    squares = jnp.where(jnp.arange(examples) == example, square, 0.0).astype(jnp.float32)
    totals = lax.psum(squares, ("pipe", "seq", "dp"))
    bound = math.sqrt(sections * (2 * rank + 1) * width)
    factors = bound / (jnp.sqrt(totals) + 0.01 * bound)
    gathered = lax.all_gather(part, "dp", axis=0, tiled=False)
    share = part.shape[1] // examples
    pieces = lax.dynamic_slice_in_dim(gathered, example * share, share, 2)
    combined = jnp.sum(factors[:, None, None] * pieces, axis=0)
    out_a = combined[:rank]
    out_b = combined[rank : 2 * rank]
    out_g = combined[2 * rank :]
    factor = lax.dynamic_slice_in_dim(factors, example, 1, 0)
    return (out_a[None], out_b[None], out_g, factor)


def solution(mesh):
    in_specs = (
        P("pipe", "dp", "seq", None),
        P("dp", "seq", None),
        P("pipe", None, ("seq", "dp")),
        P("pipe", None, ("seq", "dp")),
        P("pipe", ("seq", "dp")),
    )
    out_specs = (
        P("pipe", None, ("seq", "dp")),
        P("pipe", None, ("seq", "dp")),
        P("pipe", ("seq", "dp")),
        P("dp"),
    )
    return jax.shard_map(
        on_device, mesh=mesh, in_specs=in_specs, out_specs=out_specs, check_vma=False
    )
```

time: 741 us -> 597 us (0.81)
  waiting for transfers between devices: 380 us -> 307 us
  blocking collectives: 160 us -> 102 us
  other arithmetic: 96.6 us -> 75.5 us
    all_gather x3 -> x0, blocking collectives: 105 us -> none  [the longest x1 37.6 us: on_device(): lax.all_gather(a_rows, ('seq', 'dp'), axis=2, tiled=True)]
    all_gather x0 -> x2, waiting for transfers between devices: none -> 62.7 us  [the longest x1 62.7 us: on_device(): whole = lax.all_gather(params, ('seq', 'dp'), axis=1, tiled=True)]
    psum x1 -> x0, waiting for transfers between devices: 58.5 us -> none  [on_device(): sum_a, sum_b, sum_g = lax.psum((grad_a, grad_b, gain_gradient), 'seq')]
    psum x2 -> x1, blocking collectives: 55.4 us -> 102 us  [on_device(): totals = lax.psum(squares, ('pipe', 'seq', 'dp'))]
    ppermute x19 -> x23, waiting for transfers between devices: 240 us -> 199 us  [from_behind(): lax.ppermute(value, axis, [(source, source + steps) for source in range(i...]
    unnamed x5 -> x3, waiting for transfers between devices: 20 us -> 0.05 us
    dynamic_update_slice x19 -> x23, other arithmetic: 42 us -> 23.3 us  [turn(): store = lax.dynamic_update_slice_in_dim(store, source[None], slot, 0)]
    reduce_scatter x2 -> x1, waiting for transfers between devices: 61.7 us -> 44.9 us  [on_device(): part = lax.psum_scatter(grads, 'seq', scatter_dimension=1, tiled=True)]
  transfers between devices with their start and end apart: 23 -> 26, of which waited for: 23 -> 25; matrix products, arithmetic and copies ran while one was open for 1% -> 1% of each run, Pallas kernels for 0% -> 0%
where the time goes in v1:
time: 597 us; the launch traced here: 592 us
  waiting for transfers between devices  307 us (51%)
  blocking collectives  102 us (17%)
  other arithmetic  75.5 us (13%)
  matrix products  54.4 us (9%)
  starting transfers between devices  29.6 us (5%)
  between operations  13.9 us (2%)
  local copies, waits for them, and re-layouts  8.42 us (1%)
    ppermute x23, waiting for transfers between devices, from_behind(): lax.ppermute(value, axis, [(source, source + steps) for source in range(i...  199 us
    psum x1, blocking collectives, on_device(): totals = lax.psum(squares, ('pipe', 'seq', 'dp'))  102 us
    all_gather x1, waiting for transfers between devices, on_device(): whole = lax.all_gather(params, ('seq', 'dp'), axis=1, tiled=True)  62.7 us
    dot_general x23, matrix products, back_block(): jnp.dot(d_low, a_full, preferred_element_type=jnp.float32)  44.9 us
    reduce_scatter x1, waiting for transfers between devices, on_device(): part = lax.psum_scatter(grads, 'seq', scatter_dimension=1, tiled=True)  44.9 us
    convert_element_type x23, other arithmetic, back_block(): return hidden_gradient.astype(jnp.bfloat16)  42.7 us
    ppermute x23, starting transfers between devices, from_behind(): lax.ppermute(value, axis, [(source, source + steps) for source in range(i...  29.4 us
    dynamic_update_slice x23, other arithmetic, turn(): store = lax.dynamic_update_slice_in_dim(store, source[None], slot, 0)  23.3 us
  transfers between devices with their start and end apart: 26, of which 25 were waited for; matrix products, arithmetic and copies ran while one was open for 1% of the time, Pallas kernels for 0%

profile of v1, /device:TPU:6, one launch (start us, length us, event | category | flops | bytes accessed | tf_op | source)
XLA Modules:
  0.0 591.6 jit_solution(15978239011922078406)
XLA Ops:
  8.7 2.1 fusion.1
  10.8 62.7 %all-gather.5.cloned.1.call-done = bf16[65,8192]{1,0:T(8,128)(2,1)} async-done(((bf16[65,256]{1,0:T(8,128)(2,1)}), bf16[65,8192]{1,0:T(8,128)(2,1)}) %all-gather.5.cloned.1.call-update) | async-done | bytes 1064976 | tf_op jit(solution)/shard_map/all_gather | solution.py:24
  74.3 2.2 fusion.11
  76.9 342.0 %while.17 = (s32[]{:T(128)}, bf16[16,8192]{1,0:T(8,128)(2,1)S(1)}, bf16[9,16,8192]{2,1,0:T(8,128)(2,1)S(1)}, pred[]{:T(512)}, s32[]{:T(128)}, /*index=5*/bf16[12...) while((s32[]{:T(128)}, bf16[16,8192]{1,0:T(8,128)(2,1)S(1)}, ...), condition=%wide.region_3.4_spmd, body=%wide.region_1.3_spmd.sunk | while | flops 18612752 | bytes 5538680 | solution.py:78
  78.0 2.0 multiply_reduce_fusion.3
  79.9 1.9 add_convert_fusion.2
  83.1 9.2 %collective-permute-done = bf16[16,8192]{1,0:T(8,128)(2,1)S(1)} collective-permute-done((bf16[16,8192]{1,0:T(8,128)(2,1)}, bf16[16,8192]{1,0:T(8,128)(2,1)S(1)}, u32[]{:S(2)}, u32[]{:S(2)}) %collective-permute-start) | collective-permute-done | bytes 262176 | tf_op jit(solution)/shard_map/while/body/eval_jaxpr/ppermute | solution.py:14
  93.4 2.0 multiply_reduce_fusion.3
  95.4 1.9 add_convert_fusion.2
  98.5 8.4 %collective-permute-done = bf16[16,8192]{1,0:T(8,128)(2,1)S(1)} collective-permute-done((bf16[16,8192]{1,0:T(8,128)(2,1)}, bf16[16,8192]{1,0:T(8,128)(2,1)S(1)}, u32[]{:S(2)}, u32[]{:S(2)}) %collective-permute-start) | collective-permute-done | bytes 262176 | tf_op jit(solution)/shard_map/while/body/eval_jaxpr/ppermute | solution.py:14
  108.0 2.0 multiply_reduce_fusion.3
  110.0 1.9 add_convert_fusion.2
  113.1 7.5 %collective-permute-done = bf16[16,8192]{1,0:T(8,128)(2,1)S(1)} collective-permute-done((bf16[16,8192]{1,0:T(8,128)(2,1)}, bf16[16,8192]{1,0:T(8,128)(2,1)S(1)}, u32[]{:S(2)}, u32[]{:S(2)}) %collective-permute-start) | collective-permute-done | bytes 262176 | tf_op jit(solution)/shard_map/while/body/eval_jaxpr/ppermute | solution.py:14
  121.7 2.0 multiply_reduce_fusion.3
  123.7 1.9 add_convert_fusion.2
  126.8 8.2 %collective-permute-done = bf16[16,8192]{1,0:T(8,128)(2,1)S(1)} collective-permute-done((bf16[16,8192]{1,0:T(8,128)(2,1)}, bf16[16,8192]{1,0:T(8,128)(2,1)S(1)}, u32[]{:S(2)}, u32[]{:S(2)}) %collective-permute-start) | collective-permute-done | bytes 262176 | tf_op jit(solution)/shard_map/while/body/eval_jaxpr/ppermute | solution.py:14
  136.1 2.0 multiply_reduce_fusion.3
  138.1 1.9 add_convert_fusion.2
  141.2 7.5 %collective-permute-done = bf16[16,8192]{1,0:T(8,128)(2,1)S(1)} collective-permute-done((bf16[16,8192]{1,0:T(8,128)(2,1)}, bf16[16,8192]{1,0:T(8,128)(2,1)S(1)}, u32[]{:S(2)}, u32[]{:S(2)}) %collective-permute-start) | collective-permute-done | bytes 262176 | tf_op jit(solution)/shard_map/while/body/eval_jaxpr/ppermute | solution.py:14
  149.9 2.0 multiply_reduce_fusion.3
  151.8 1.9 add_convert_fusion.2
  155.0 8.0 %collective-permute-done = bf16[16,8192]{1,0:T(8,128)(2,1)S(1)} collective-permute-done((bf16[16,8192]{1,0:T(8,128)(2,1)}, bf16[16,8192]{1,0:T(8,128)(2,1)S(1)}, u32[]{:S(2)}, u32[]{:S(2)}) %collective-permute-start) | collective-permute-done | bytes 262176 | tf_op jit(solution)/shard_map/while/body/eval_jaxpr/ppermute | solution.py:14
  164.1 2.0 multiply_reduce_fusion.3
  166.1 1.9 add_convert_fusion.2
  169.2 8.4 %collective-permute-done = bf16[16,8192]{1,0:T(8,128)(2,1)S(1)} collective-permute-done((bf16[16,8192]{1,0:T(8,128)(2,1)}, bf16[16,8192]{1,0:T(8,128)(2,1)S(1)}, u32[]{:S(2)}, u32[]{:S(2)}) %collective-permute-start) | collective-permute-done | bytes 262176 | tf_op jit(solution)/shard_map/while/body/eval_jaxpr/ppermute | solution.py:14
  178.7 2.0 multiply_reduce_fusion.3
  180.7 1.9 add_convert_fusion.2
  183.8 8.4 %collective-permute-done = bf16[16,8192]{1,0:T(8,128)(2,1)S(1)} collective-permute-done((bf16[16,8192]{1,0:T(8,128)(2,1)}, bf16[16,8192]{1,0:T(8,128)(2,1)S(1)}, u32[]{:S(2)}, u32[]{:S(2)}) %collective-permute-start) | collective-permute-done | bytes 262176 | tf_op jit(solution)/shard_map/while/body/eval_jaxpr/ppermute | solution.py:14
  193.3 2.0 multiply_reduce_fusion.3
  195.2 1.9 add_convert_fusion.2
  198.4 8.4 %collective-permute-done = bf16[16,8192]{1,0:T(8,128)(2,1)S(1)} collective-permute-done((bf16[16,8192]{1,0:T(8,128)(2,1)}, bf16[16,8192]{1,0:T(8,128)(2,1)S(1)}, u32[]{:S(2)}, u32[]{:S(2)}) %collective-permute-start) | collective-permute-done | bytes 262176 | tf_op jit(solution)/shard_map/while/body/eval_jaxpr/ppermute | solution.py:14
  207.9 2.0 multiply_reduce_fusion.3
  209.8 1.9 add_convert_fusion.2
  213.0 8.4 %collective-permute-done = bf16[16,8192]{1,0:T(8,128)(2,1)S(1)} collective-permute-done((bf16[16,8192]{1,0:T(8,128)(2,1)}, bf16[16,8192]{1,0:T(8,128)(2,1)S(1)}, u32[]{:S(2)}, u32[]{:S(2)}) %collective-permute-start) | collective-permute-done | bytes 262176 | tf_op jit(solution)/shard_map/while/body/eval_jaxpr/ppermute | solution.py:14
  222.4 2.0 multiply_reduce_fusion.3
  227.6 8.4 %collective-permute-done = bf16[16,8192]{1,0:T(8,128)(2,1)S(1)} collective-permute-done((bf16[16,8192]{1,0:T(8,128)(2,1)}, bf16[16,8192]{1,0:T(8,128)(2,1)S(1)}, u32[]{:S(2)}, u32[]{:S(2)}) %collective-permute-start) | collective-permute-done | bytes 262176 | tf_op jit(solution)/shard_map/while/body/eval_jaxpr/ppermute | solution.py:14
  237.0 2.0 multiply_reduce_fusion.3
  242.1 9.6 %collective-permute-done = bf16[16,8192]{1,0:T(8,128)(2,1)S(1)} collective-permute-done((bf16[16,8192]{1,0:T(8,128)(2,1)}, bf16[16,8192]{1,0:T(8,128)(2,1)S(1)}, u32[]{:S(2)}, u32[]{:S(2)}) %collective-permute-start) | collective-permute-done | bytes 262176 | tf_op jit(solution)/shard_map/while/body/eval_jaxpr/ppermute | solution.py:14
  252.8 2.0 multiply_reduce_fusion.3
  257.9 11.1 %collective-permute-done = bf16[16,8192]{1,0:T(8,128)(2,1)S(1)} collective-permute-done((bf16[16,8192]{1,0:T(8,128)(2,1)}, bf16[16,8192]{1,0:T(8,128)(2,1)S(1)}, u32[]{:S(2)}, u32[]{:S(2)}) %collective-permute-start) | collective-permute-done | bytes 262176 | tf_op jit(solution)/shard_map/while/body/eval_jaxpr/ppermute | solution.py:14
  270.2 2.0 multiply_reduce_fusion.3
  275.3 11.5 %collective-permute-done = bf16[16,8192]{1,0:T(8,128)(2,1)S(1)} collective-permute-done((bf16[16,8192]{1,0:T(8,128)(2,1)}, bf16[16,8192]{1,0:T(8,128)(2,1)S(1)}, u32[]{:S(2)}, u32[]{:S(2)}) %collective-permute-start) | collective-permute-done | bytes 262176 | tf_op jit(solution)/shard_map/while/body/eval_jaxpr/ppermute | solution.py:14
  287.9 2.0 multiply_reduce_fusion.3
  293.0 10.5 %collective-permute-done = bf16[16,8192]{1,0:T(8,128)(2,1)S(1)} collective-permute-done((bf16[16,8192]{1,0:T(8,128)(2,1)}, bf16[16,8192]{1,0:T(8,128)(2,1)S(1)}, u32[]{:S(2)}, u32[]{:S(2)}) %collective-permute-start) | collective-permute-done | bytes 262176 | tf_op jit(solution)/shard_map/while/body/eval_jaxpr/ppermute | solution.py:14
  304.6 2.0 multiply_reduce_fusion.3
  309.7 8.7 %collective-permute-done = bf16[16,8192]{1,0:T(8,128)(2,1)S(1)} collective-permute-done((bf16[16,8192]{1,0:T(8,128)(2,1)}, bf16[16,8192]{1,0:T(8,128)(2,1)S(1)}, u32[]{:S(2)}, u32[]{:S(2)}) %collective-permute-start) | collective-permute-done | bytes 262176 | tf_op jit(solution)/shard_map/while/body/eval_jaxpr/ppermute | solution.py:14
  319.5 2.0 multiply_reduce_fusion.3
  324.6 7.6 %collective-permute-done = bf16[16,8192]{1,0:T(8,128)(2,1)S(1)} collective-permute-done((bf16[16,8192]{1,0:T(8,128)(2,1)}, bf16[16,8192]{1,0:T(8,128)(2,1)S(1)}, u32[]{:S(2)}, u32[]{:S(2)}) %collective-permute-start) | collective-permute-done | bytes 262176 | tf_op jit(solution)/shard_map/while/body/eval_jaxpr/ppermute | solution.py:14
  333.2 2.0 multiply_reduce_fusion.3
  338.3 7.8 %collective-permute-done = bf16[16,8192]{1,0:T(8,128)(2,1)S(1)} collective-permute-done((bf16[16,8192]{1,0:T(8,128)(2,1)}, bf16[16,8192]{1,0:T(8,128)(2,1)S(1)}, u32[]{:S(2)}, u32[]{:S(2)}) %collective-permute-start) | collective-permute-done | bytes 262176 | tf_op jit(solution)/shard_map/while/body/eval_jaxpr/ppermute | solution.py:14
  347.2 2.0 multiply_reduce_fusion.3
  352.4 8.1 %collective-permute-done = bf16[16,8192]{1,0:T(8,128)(2,1)S(1)} collective-permute-done((bf16[16,8192]{1,0:T(8,128)(2,1)}, bf16[16,8192]{1,0:T(8,128)(2,1)S(1)}, u32[]{:S(2)}, u32[]{:S(2)}) %collective-permute-start) | collective-permute-done | bytes 262176 | tf_op jit(solution)/shard_map/while/body/eval_jaxpr/ppermute | solution.py:14
  361.6 2.0 multiply_reduce_fusion.3
  366.7 8.4 %collective-permute-done = bf16[16,8192]{1,0:T(8,128)(2,1)S(1)} collective-permute-done((bf16[16,8192]{1,0:T(8,128)(2,1)}, bf16[16,8192]{1,0:T(8,128)(2,1)S(1)}, u32[]{:S(2)}, u32[]{:S(2)}) %collective-permute-start) | collective-permute-done | bytes 262176 | tf_op jit(solution)/shard_map/while/body/eval_jaxpr/ppermute | solution.py:14
  376.1 2.0 multiply_reduce_fusion.3
  381.3 8.4 %collective-permute-done = bf16[16,8192]{1,0:T(8,128)(2,1)S(1)} collective-permute-done((bf16[16,8192]{1,0:T(8,128)(2,1)}, bf16[16,8192]{1,0:T(8,128)(2,1)S(1)}, u32[]{:S(2)}, u32[]{:S(2)}) %collective-permute-start) | collective-permute-done | bytes 262176 | tf_op jit(solution)/shard_map/while/body/eval_jaxpr/ppermute | solution.py:14
  390.7 2.0 multiply_reduce_fusion.3
  395.8 8.4 %collective-permute-done = bf16[16,8192]{1,0:T(8,128)(2,1)S(1)} collective-permute-done((bf16[16,8192]{1,0:T(8,128)(2,1)}, bf16[16,8192]{1,0:T(8,128)(2,1)S(1)}, u32[]{:S(2)}, u32[]{:S(2)}) %collective-permute-start) | collective-permute-done | bytes 262176 | tf_op jit(solution)/shard_map/while/body/eval_jaxpr/ppermute | solution.py:14
  405.3 2.0 multiply_reduce_fusion.3
  410.4 8.4 %collective-permute-done = bf16[16,8192]{1,0:T(8,128)(2,1)S(1)} collective-permute-done((bf16[16,8192]{1,0:T(8,128)(2,1)}, bf16[16,8192]{1,0:T(8,128)(2,1)S(1)}, u32[]{:S(2)}, u32[]{:S(2)}) %collective-permute-start) | collective-permute-done | bytes 262176 | tf_op jit(solution)/shard_map/while/body/eval_jaxpr/ppermute | solution.py:14
  424.0 4.3 fusion.3
  428.3 2.5 fusion.2
  432.5 44.9 %reduce-scatter.2.cloned.1.call-done = f32[65,1024]{1,0:T(8,128)} async-done(((f32[65,8192]{1,0:T(8,128)}), f32[65,1024]{1,0:T(8,128)}) %reduce-scatter.2.cloned.1.call-update) | async-done | bytes 266256 | tf_op jit(solution)/shard_map/reduce_scatter | solution.py:90
  479.7 102.5 %psum.7 = f32[4]{0:T(128)S(1)} all-reduce(f32[4]{0:T(128)S(1)} %compare_select_fusion), channel_id=1, replica_groups=mesh['pipe'=16,'seq'=8,'dp'=4] {'pipe','seq','dp'}, use_global_device_ids=true, to_apply=%region_7.8 | all-reduce | flops 4 | bytes 32 | tf_op jit(solution)/shard_map/psum | solution.py:95
  (144 shorter events, 93.3 us)
Async XLA Ops:
  7.2 66.3 %all-gather.5.cloned.1.call-start = ((), (), s32[]{:S(2)}) async-start(), calls=%async_computation.1 | async-start | bytes 1216512 | tf_op jit(solution)/shard_map/all_gather | solution.py:24
  8.6 468.8 %reduce-scatter.2.cloned.1.call-start = ((), (), s32[]{:S(2)}) async-start(), calls=%async_computation.2 | async-start | bytes 2654208 | tf_op jit(solution)/shard_map/reduce_scatter | solution.py:90
  81.8 10.5 %collective-permute-start = (bf16[16,8192]{1,0:T(8,128)(2,1)}, bf16[16,8192]{1,0:T(8,128)(2,1)S(1)}, u32[]{:S(2)}, u32[]{:S(2)}) collective-permute-start(bf16[16,8192]{1,0:T(8,128)(2,1)} %add_convert_fusion.2), channel_id=1, source_target_pairs={{32,0},{64,32},{96,64},{128,96},{160,128},{192,160},{224,192},{256... | collective-permute-start | bytes 786440 | tf_op jit(solution)/shard_map/while/body/eval_jaxpr/ppermute | solution.py:14
  97.2 9.7 %collective-permute-start = (bf16[16,8192]{1,0:T(8,128)(2,1)}, bf16[16,8192]{1,0:T(8,128)(2,1)S(1)}, u32[]{:S(2)}, u32[]{:S(2)}) collective-permute-start(bf16[16,8192]{1,0:T(8,128)(2,1)} %add_convert_fusion.2), channel_id=1, source_target_pairs={{32,0},{64,32},{96,64},{128,96},{160,128},{192,160},{224,192},{256... | collective-permute-start | bytes 786440 | tf_op jit(solution)/shard_map/while/body/eval_jaxpr/ppermute | solution.py:14
  111.8 8.8 %collective-permute-start = (bf16[16,8192]{1,0:T(8,128)(2,1)}, bf16[16,8192]{1,0:T(8,128)(2,1)S(1)}, u32[]{:S(2)}, u32[]{:S(2)}) collective-permute-start(bf16[16,8192]{1,0:T(8,128)(2,1)} %add_convert_fusion.2), channel_id=1, source_target_pairs={{32,0},{64,32},{96,64},{128,96},{160,128},{192,160},{224,192},{256... | collective-permute-start | bytes 786440 | tf_op jit(solution)/shard_map/while/body/eval_jaxpr/ppermute | solution.py:14
  125.6 9.5 %collective-permute-start = (bf16[16,8192]{1,0:T(8,128)(2,1)}, bf16[16,8192]{1,0:T(8,128)(2,1)S(1)}, u32[]{:S(2)}, u32[]{:S(2)}) collective-permute-start(bf16[16,8192]{1,0:T(8,128)(2,1)} %add_convert_fusion.2), channel_id=1, source_target_pairs={{32,0},{64,32},{96,64},{128,96},{160,128},{192,160},{224,192},{256... | collective-permute-start | bytes 786440 | tf_op jit(solution)/shard_map/while/body/eval_jaxpr/ppermute | solution.py:14
  139.9 8.8 %collective-permute-start = (bf16[16,8192]{1,0:T(8,128)(2,1)}, bf16[16,8192]{1,0:T(8,128)(2,1)S(1)}, u32[]{:S(2)}, u32[]{:S(2)}) collective-permute-start(bf16[16,8192]{1,0:T(8,128)(2,1)} %add_convert_fusion.2), channel_id=1, source_target_pairs={{32,0},{64,32},{96,64},{128,96},{160,128},{192,160},{224,192},{256... | collective-permute-start | bytes 786440 | tf_op jit(solution)/shard_map/while/body/eval_jaxpr/ppermute | solution.py:14
  153.7 9.3 %collective-permute-start = (bf16[16,8192]{1,0:T(8,128)(2,1)}, bf16[16,8192]{1,0:T(8,128)(2,1)S(1)}, u32[]{:S(2)}, u32[]{:S(2)}) collective-permute-start(bf16[16,8192]{1,0:T(8,128)(2,1)} %add_convert_fusion.2), channel_id=1, source_target_pairs={{32,0},{64,32},{96,64},{128,96},{160,128},{192,160},{224,192},{256... | collective-permute-start | bytes 786440 | tf_op jit(solution)/shard_map/while/body/eval_jaxpr/ppermute | solution.py:14
  167.9 9.7 %collective-permute-start = (bf16[16,8192]{1,0:T(8,128)(2,1)}, bf16[16,8192]{1,0:T(8,128)(2,1)S(1)}, u32[]{:S(2)}, u32[]{:S(2)}) collective-permute-start(bf16[16,8192]{1,0:T(8,128)(2,1)} %add_convert_fusion.2), channel_id=1, source_target_pairs={{32,0},{64,32},{96,64},{128,96},{160,128},{192,160},{224,192},{256... | collective-permute-start | bytes 786440 | tf_op jit(solution)/shard_map/while/body/eval_jaxpr/ppermute | solution.py:14
  182.5 9.7 %collective-permute-start = (bf16[16,8192]{1,0:T(8,128)(2,1)}, bf16[16,8192]{1,0:T(8,128)(2,1)S(1)}, u32[]{:S(2)}, u32[]{:S(2)}) collective-permute-start(bf16[16,8192]{1,0:T(8,128)(2,1)} %add_convert_fusion.2), channel_id=1, source_target_pairs={{32,0},{64,32},{96,64},{128,96},{160,128},{192,160},{224,192},{256... | collective-permute-start | bytes 786440 | tf_op jit(solution)/shard_map/while/body/eval_jaxpr/ppermute | solution.py:14
  197.1 9.7 %collective-permute-start = (bf16[16,8192]{1,0:T(8,128)(2,1)}, bf16[16,8192]{1,0:T(8,128)(2,1)S(1)}, u32[]{:S(2)}, u32[]{:S(2)}) collective-permute-start(bf16[16,8192]{1,0:T(8,128)(2,1)} %add_convert_fusion.2), channel_id=1, source_target_pairs={{32,0},{64,32},{96,64},{128,96},{160,128},{192,160},{224,192},{256... | collective-permute-start | bytes 786440 | tf_op jit(solution)/shard_map/while/body/eval_jaxpr/ppermute | solution.py:14
  211.7 9.7 %collective-permute-start = (bf16[16,8192]{1,0:T(8,128)(2,1)}, bf16[16,8192]{1,0:T(8,128)(2,1)S(1)}, u32[]{:S(2)}, u32[]{:S(2)}) collective-permute-start(bf16[16,8192]{1,0:T(8,128)(2,1)} %add_convert_fusion.2), channel_id=1, source_target_pairs={{32,0},{64,32},{96,64},{128,96},{160,128},{192,160},{224,192},{256... | collective-permute-start | bytes 786440 | tf_op jit(solution)/shard_map/while/body/eval_jaxpr/ppermute | solution.py:14
  226.3 9.7 %collective-permute-start = (bf16[16,8192]{1,0:T(8,128)(2,1)}, bf16[16,8192]{1,0:T(8,128)(2,1)S(1)}, u32[]{:S(2)}, u32[]{:S(2)}) collective-permute-start(bf16[16,8192]{1,0:T(8,128)(2,1)} %add_convert_fusion.2), channel_id=1, source_target_pairs={{32,0},{64,32},{96,64},{128,96},{160,128},{192,160},{224,192},{256... | collective-permute-start | bytes 786440 | tf_op jit(solution)/shard_map/while/body/eval_jaxpr/ppermute | solution.py:14
  240.9 10.9 %collective-permute-start = (bf16[16,8192]{1,0:T(8,128)(2,1)}, bf16[16,8192]{1,0:T(8,128)(2,1)S(1)}, u32[]{:S(2)}, u32[]{:S(2)}) collective-permute-start(bf16[16,8192]{1,0:T(8,128)(2,1)} %add_convert_fusion.2), channel_id=1, source_target_pairs={{32,0},{64,32},{96,64},{128,96},{160,128},{192,160},{224,192},{256... | collective-permute-start | bytes 786440 | tf_op jit(solution)/shard_map/while/body/eval_jaxpr/ppermute | solution.py:14
  256.6 12.4 %collective-permute-start = (bf16[16,8192]{1,0:T(8,128)(2,1)}, bf16[16,8192]{1,0:T(8,128)(2,1)S(1)}, u32[]{:S(2)}, u32[]{:S(2)}) collective-permute-start(bf16[16,8192]{1,0:T(8,128)(2,1)} %add_convert_fusion.2), channel_id=1, source_target_pairs={{32,0},{64,32},{96,64},{128,96},{160,128},{192,160},{224,192},{256... | collective-permute-start | bytes 786440 | tf_op jit(solution)/shard_map/while/body/eval_jaxpr/ppermute | solution.py:14
  274.0 12.8 %collective-permute-start = (bf16[16,8192]{1,0:T(8,128)(2,1)}, bf16[16,8192]{1,0:T(8,128)(2,1)S(1)}, u32[]{:S(2)}, u32[]{:S(2)}) collective-permute-start(bf16[16,8192]{1,0:T(8,128)(2,1)} %add_convert_fusion.2), channel_id=1, source_target_pairs={{32,0},{64,32},{96,64},{128,96},{160,128},{192,160},{224,192},{256... | collective-permute-start | bytes 786440 | tf_op jit(solution)/shard_map/while/body/eval_jaxpr/ppermute | solution.py:14
  291.7 11.8 %collective-permute-start = (bf16[16,8192]{1,0:T(8,128)(2,1)}, bf16[16,8192]{1,0:T(8,128)(2,1)S(1)}, u32[]{:S(2)}, u32[]{:S(2)}) collective-permute-start(bf16[16,8192]{1,0:T(8,128)(2,1)} %add_convert_fusion.2), channel_id=1, source_target_pairs={{32,0},{64,32},{96,64},{128,96},{160,128},{192,160},{224,192},{256... | collective-permute-start | bytes 786440 | tf_op jit(solution)/shard_map/while/body/eval_jaxpr/ppermute | solution.py:14
  308.4 9.9 %collective-permute-start = (bf16[16,8192]{1,0:T(8,128)(2,1)}, bf16[16,8192]{1,0:T(8,128)(2,1)S(1)}, u32[]{:S(2)}, u32[]{:S(2)}) collective-permute-start(bf16[16,8192]{1,0:T(8,128)(2,1)} %add_convert_fusion.2), channel_id=1, source_target_pairs={{32,0},{64,32},{96,64},{128,96},{160,128},{192,160},{224,192},{256... | collective-permute-start | bytes 786440 | tf_op jit(solution)/shard_map/while/body/eval_jaxpr/ppermute | solution.py:14
  323.3 8.8 %collective-permute-start = (bf16[16,8192]{1,0:T(8,128)(2,1)}, bf16[16,8192]{1,0:T(8,128)(2,1)S(1)}, u32[]{:S(2)}, u32[]{:S(2)}) collective-permute-start(bf16[16,8192]{1,0:T(8,128)(2,1)} %add_convert_fusion.2), channel_id=1, source_target_pairs={{32,0},{64,32},{96,64},{128,96},{160,128},{192,160},{224,192},{256... | collective-permute-start | bytes 786440 | tf_op jit(solution)/shard_map/while/body/eval_jaxpr/ppermute | solution.py:14
  337.1 9.1 %collective-permute-start = (bf16[16,8192]{1,0:T(8,128)(2,1)}, bf16[16,8192]{1,0:T(8,128)(2,1)S(1)}, u32[]{:S(2)}, u32[]{:S(2)}) collective-permute-start(bf16[16,8192]{1,0:T(8,128)(2,1)} %add_convert_fusion.2), channel_id=1, source_target_pairs={{32,0},{64,32},{96,64},{128,96},{160,128},{192,160},{224,192},{256... | collective-permute-start | bytes 786440 | tf_op jit(solution)/shard_map/while/body/eval_jaxpr/ppermute | solution.py:14
  351.1 9.4 %collective-permute-start = (bf16[16,8192]{1,0:T(8,128)(2,1)}, bf16[16,8192]{1,0:T(8,128)(2,1)S(1)}, u32[]{:S(2)}, u32[]{:S(2)}) collective-permute-start(bf16[16,8192]{1,0:T(8,128)(2,1)} %add_convert_fusion.2), channel_id=1, source_target_pairs={{32,0},{64,32},{96,64},{128,96},{160,128},{192,160},{224,192},{256... | collective-permute-start | bytes 786440 | tf_op jit(solution)/shard_map/while/body/eval_jaxpr/ppermute | solution.py:14
  365.4 9.7 %collective-permute-start = (bf16[16,8192]{1,0:T(8,128)(2,1)}, bf16[16,8192]{1,0:T(8,128)(2,1)S(1)}, u32[]{:S(2)}, u32[]{:S(2)}) collective-permute-start(bf16[16,8192]{1,0:T(8,128)(2,1)} %add_convert_fusion.2), channel_id=1, source_target_pairs={{32,0},{64,32},{96,64},{128,96},{160,128},{192,160},{224,192},{256... | collective-permute-start | bytes 786440 | tf_op jit(solution)/shard_map/while/body/eval_jaxpr/ppermute | solution.py:14
  380.0 9.7 %collective-permute-start = (bf16[16,8192]{1,0:T(8,128)(2,1)}, bf16[16,8192]{1,0:T(8,128)(2,1)S(1)}, u32[]{:S(2)}, u32[]{:S(2)}) collective-permute-start(bf16[16,8192]{1,0:T(8,128)(2,1)} %add_convert_fusion.2), channel_id=1, source_target_pairs={{32,0},{64,32},{96,64},{128,96},{160,128},{192,160},{224,192},{256... | collective-permute-start | bytes 786440 | tf_op jit(solution)/shard_map/while/body/eval_jaxpr/ppermute | solution.py:14
  394.5 9.7 %collective-permute-start = (bf16[16,8192]{1,0:T(8,128)(2,1)}, bf16[16,8192]{1,0:T(8,128)(2,1)S(1)}, u32[]{:S(2)}, u32[]{:S(2)}) collective-permute-start(bf16[16,8192]{1,0:T(8,128)(2,1)} %add_convert_fusion.2), channel_id=1, source_target_pairs={{32,0},{64,32},{96,64},{128,96},{160,128},{192,160},{224,192},{256... | collective-permute-start | bytes 786440 | tf_op jit(solution)/shard_map/while/body/eval_jaxpr/ppermute | solution.py:14
  409.1 9.7 %collective-permute-start = (bf16[16,8192]{1,0:T(8,128)(2,1)}, bf16[16,8192]{1,0:T(8,128)(2,1)S(1)}, u32[]{:S(2)}, u32[]{:S(2)}) collective-permute-start(bf16[16,8192]{1,0:T(8,128)(2,1)} %add_convert_fusion.2), channel_id=1, source_target_pairs={{32,0},{64,32},{96,64},{128,96},{160,128},{192,160},{224,192},{256... | collective-permute-start | bytes 786440 | tf_op jit(solution)/shard_map/while/body/eval_jaxpr/ppermute | solution.py:14
  418.8 0.6 copy-start.6
  419.4 1.7 copy-start.3
  419.6 1.3 copy-start
  419.6 2.5 copy-start.2
  419.6 2.5 copy-start.7
  422.1 1.8 copy-start.1
  428.3 2.5 copy-start.4
  428.3 2.5 copy-start.5
  432.4 150.4 %all-gather.7.cloned.1.call-start = ((), (), s32[]{:S(2)}) async-start(), calls=%async_computation.3 | async-start | bytes 1474560 | tf_op jit(solution)/shard_map/all_gather | solution.py:98
Sparse Core Ops, SparseCore 0:
  11.0 62.3 all-gather.4
  432.6 44.8 reduce-scatter.1
  479.5 30.0 all-gather.6

commit v2 on v1

--- a/solution.py
+++ b/solution.py
@@ -21,7 +21,7 @@
     top = top_grad[0]
     rank = a_rows.shape[1]
     params = jnp.concatenate([a_rows[0], b_rows[0], gain], axis=0)
-    whole = lax.all_gather(params, ("seq", "dp"), axis=1, tiled=True)
+    whole = lax.all_gather(lax.all_gather(params, "dp", axis=1, tiled=True), "seq", axis=1, tiled=True)
     a_full = whole[:rank]
     b_full = whole[rank : 2 * rank]
     gain_float = whole[2 * rank].astype(jnp.float32)
@@ -75,7 +75,7 @@
         jnp.zeros((rows_per_block, width), jnp.bfloat16),
         jnp.zeros((block_total + 1, rows_per_block, width), jnp.bfloat16),
     )
-    store = lax.fori_loop(0, sections + block_total - 1, turn, begin)[1]
+    store = lax.fori_loop(0, sections + block_total - 1, turn, begin, unroll=True)[1]
     mine = store[:block_total].reshape(rows, width)
     d_low = lax.dot_general(mine, b_full, contract_last, preferred_element_type=jnp.float32).astype(
         jnp.bfloat16
@@ -91,18 +91,29 @@
     examples = lax.axis_size("dp")
     example = lax.axis_index("dp")
     square = jnp.sum(part * part)
-    squares = jnp.where(jnp.arange(examples) == example, square, 0.0).astype(jnp.float32)
-    totals = lax.psum(squares, ("pipe", "seq", "dp"))
+    total = lax.psum(square, "pipe")
+    count = lax.axis_size("seq")
+    step = 1
+    while step < count:
+        total = total + lax.ppermute(
+            total, "seq", [(source, (source + step) % count) for source in range(count)]
+        )
+        step *= 2
     bound = math.sqrt(sections * (2 * rank + 1) * width)
-    factors = bound / (jnp.sqrt(totals) + 0.01 * bound)
-    gathered = lax.all_gather(part, "dp", axis=0, tiled=False)
+    factor = bound / (jnp.sqrt(total) + 0.01 * bound)
+    scaled = factor * part
     share = part.shape[1] // examples
-    pieces = lax.dynamic_slice_in_dim(gathered, example * share, share, 2)
-    combined = jnp.sum(factors[:, None, None] * pieces, axis=0)
+    combined = lax.dynamic_slice_in_dim(scaled, example * share, share, 1)
+    for step in range(1, examples):
+        target = lax.rem(example + step, examples)
+        piece = lax.dynamic_slice_in_dim(scaled, target * share, share, 1)
+        combined = combined + lax.ppermute(
+            piece, "dp", [(source, (source + step) % examples) for source in range(examples)]
+        )
     out_a = combined[:rank]
     out_b = combined[rank : 2 * rank]
     out_g = combined[2 * rank :]
-    factor = lax.dynamic_slice_in_dim(factors, example, 1, 0)
+    factor = jnp.reshape(factor, (1,))
     return (out_a[None], out_b[None], out_g, factor)
 
 

time: 597 us -> 579 us (0.970)
  blocking collectives: 102 us -> 47.2 us
  waiting for transfers between devices: 307 us -> 274 us
  other arithmetic: 75.5 us -> 104 us
  starting transfers between devices: 29.6 us -> 44.8 us
  local copies, waits for them, and re-layouts: 8.42 us -> 19.7 us
  matrix products: 54.4 us -> 65.5 us
    psum x1, blocking collectives: 102 us -> 31.8 us  [on_device(): total = lax.psum(square, 'pipe')]
    all_gather x2 -> x1, waiting for transfers between devices: 62.7 us -> 30.6 us  [on_device(): lax.all_gather(lax.all_gather(params, 'dp', axis=1, tiled=True), 'seq', a...]
    dynamic_update_slice x23, other arithmetic: 23.3 us -> 41 us  [turn(): store = lax.dynamic_update_slice_in_dim(store, source[None], slot, 0)]
    ppermute x0 -> x6, starting transfers between devices: none -> 16.2 us  [the longest x3 9.81 us: on_device(): lax.ppermute(piece, 'dp', [(source, (source + step) % examples) for sourc...]
    all_gather x0 -> x1, blocking collectives: none -> 15.4 us  [on_device(): lax.all_gather(params, 'dp', axis=1, tiled=True)]
    ppermute x23 -> x22, waiting for transfers between devices: 199 us -> 184 us  [from_behind(): lax.ppermute(value, axis, [(source, source + steps) for source in range(i...]
    ppermute x0 -> x6, waiting for transfers between devices: none -> 13.7 us  [the longest x3 11.4 us: on_device(): lax.ppermute(total, 'seq', [(source, (source + step) % count) for source...]
    dot_general x23 -> x22, matrix products: 44.9 us -> 58.5 us  [back_block(): jnp.dot(d_low, a_full, preferred_element_type=jnp.float32)]
  transfers between devices with their start and end apart: 26 -> 30, of which waited for: 25 -> 29; matrix products, arithmetic and copies ran while one was open for 1% -> 1% of each run, Pallas kernels for 0% -> 0%
where the time goes in v2:
time: 579 us; the launch traced here: 574 us
  waiting for transfers between devices  274 us (47%)
  other arithmetic  104 us (18%)
  matrix products  65.5 us (11%)
  blocking collectives  47.2 us (8%)
  starting transfers between devices  44.8 us (8%)
  local copies, waits for them, and re-layouts  19.7 us (3%)
  between operations  18.8 us (3%)
    ppermute x22, waiting for transfers between devices, from_behind(): lax.ppermute(value, axis, [(source, source + steps) for source in range(i...  184 us
    dot_general x22, matrix products, back_block(): jnp.dot(d_low, a_full, preferred_element_type=jnp.float32)  58.5 us
    reduce_scatter x1, waiting for transfers between devices, on_device(): part = lax.psum_scatter(grads, 'seq', scatter_dimension=1, tiled=True)  45.2 us
    convert_element_type x22, other arithmetic, back_block(): return hidden_gradient.astype(jnp.bfloat16)  42.1 us
    dynamic_update_slice x23, other arithmetic, turn(): store = lax.dynamic_update_slice_in_dim(store, source[None], slot, 0)  41 us
    psum x1, blocking collectives, on_device(): total = lax.psum(square, 'pipe')  31.8 us
    all_gather x1, waiting for transfers between devices, on_device(): lax.all_gather(lax.all_gather(params, 'dp', axis=1, tiled=True), 'seq', a...  30.6 us
    ppermute x22, starting transfers between devices, from_behind(): lax.ppermute(value, axis, [(source, source + steps) for source in range(i...  28.5 us
  transfers between devices with their start and end apart: 30, of which 29 were waited for; matrix products, arithmetic and copies ran while one was open for 1% of the time, Pallas kernels for 0%

profile of v2, /device:TPU:6, one launch (start us, length us, event | category | flops | bytes accessed | tf_op | source)
XLA Modules:
  0.0 573.9 jit_solution(13669943799900050849)
XLA Ops:
  8.1 15.4 %all_gather.6 = bf16[65,1024]{1,0:T(8,128)(2,1)} all-gather(bf16[65,256]{1,0:T(8,128)(2,1)S(1)} %pad_maximum_fusion.1), channel_id=1, replica_groups=mesh['pipe'=16,'seq'=8,'dp'=4] {'dp'}, dimensions={1}, use_global_device_ids=true | all-gather | bytes 166400 | tf_op jit(solution)/shard_map/all_gather | solution.py:24
  23.6 2.1 fusion
  25.8 30.6 %all-gather.2.cloned.1.call-done = bf16[65,8192]{1,0:T(8,128)(2,1)} async-done(((bf16[65,1024]{1,0:T(8,128)(2,1)}), bf16[65,8192]{1,0:T(8,128)(2,1)}) %all-gather.2.cloned.1.call-update) | async-done | bytes 1064976 | tf_op jit(solution)/shard_map/all_gather | solution.py:24
  57.4 2.0 multiply_reduce_fusion.21
  66.0 6.0 %collective-permute-done = bf16[16,8192]{1,0:T(8,128)(2,1)} collective-permute-done((bf16[16,8192]{1,0:T(8,128)(2,1)}, bf16[16,8192]{1,0:T(8,128)(2,1)}, u32[]{:S(2)}, u32[]{:S(2)}) %collective-permute-start) | collective-permute-done | bytes 262176 | tf_op jit(solution)/shard_map/eval_jaxpr/ppermute | solution.py:14
  73.8 2.8 multiply_reduce_fusion.20
  80.4 8.4 %collective-permute-done.1 = bf16[16,8192]{1,0:T(8,128)(2,1)S(1)} collective-permute-done((bf16[16,8192]{1,0:T(8,128)(2,1)}, bf16[16,8192]{1,0:T(8,128)(2,1)S(1)}, u32[]{:S(2)}, u32[]{:S(2)}) %collective-permute-start.1) | collective-permute-done | bytes 262176 | tf_op jit(solution)/shard_map/eval_jaxpr/ppermute | solution.py:14
  91.3 2.2 multiply_reduce_fusion.19
  93.6 2.0 add_convert_fusion.19
  96.8 7.5 %collective-permute-done.2 = bf16[16,8192]{1,0:T(8,128)(2,1)S(1)} collective-permute-done((bf16[16,8192]{1,0:T(8,128)(2,1)}, bf16[16,8192]{1,0:T(8,128)(2,1)S(1)}, u32[]{:S(2)}, u32[]{:S(2)}) %collective-permute-start.2) | collective-permute-done | bytes 262176 | tf_op jit(solution)/shard_map/eval_jaxpr/ppermute | solution.py:14
  106.8 2.2 multiply_reduce_fusion.18
  109.1 2.0 add_convert_fusion.18
  113.2 7.3 %collective-permute-done.3 = bf16[16,8192]{1,0:T(8,128)(2,1)S(1)} collective-permute-done((bf16[16,8192]{1,0:T(8,128)(2,1)}, bf16[16,8192]{1,0:T(8,128)(2,1)S(1)}, u32[]{:S(2)}, u32[]{:S(2)}) %collective-permute-start.3) | collective-permute-done | bytes 262176 | tf_op jit(solution)/shard_map/eval_jaxpr/ppermute | solution.py:14
  123.0 2.8 multiply_reduce_fusion.17
  129.7 7.5 %collective-permute-done.4 = bf16[16,8192]{1,0:T(8,128)(2,1)S(1)} collective-permute-done((bf16[16,8192]{1,0:T(8,128)(2,1)}, bf16[16,8192]{1,0:T(8,128)(2,1)S(1)}, u32[]{:S(2)}, u32[]{:S(2)}) %collective-permute-start.4) | collective-permute-done | bytes 262176 | tf_op jit(solution)/shard_map/eval_jaxpr/ppermute | solution.py:14
  139.7 2.8 multiply_reduce_fusion.16
  143.2 1.9 add_convert_fusion.16
  146.4 8.0 %collective-permute-done.5 = bf16[16,8192]{1,0:T(8,128)(2,1)S(1)} collective-permute-done((bf16[16,8192]{1,0:T(8,128)(2,1)}, bf16[16,8192]{1,0:T(8,128)(2,1)S(1)}, u32[]{:S(2)}, u32[]{:S(2)}) %collective-permute-start.5) | collective-permute-done | bytes 262176 | tf_op jit(solution)/shard_map/eval_jaxpr/ppermute | solution.py:14
  157.0 2.8 multiply_reduce_fusion.15
  163.7 8.4 %collective-permute-done.6 = bf16[16,8192]{1,0:T(8,128)(2,1)S(1)} collective-permute-done((bf16[16,8192]{1,0:T(8,128)(2,1)}, bf16[16,8192]{1,0:T(8,128)(2,1)S(1)}, u32[]{:S(2)}, u32[]{:S(2)}) %collective-permute-start.6) | collective-permute-done | bytes 262176 | tf_op jit(solution)/shard_map/eval_jaxpr/ppermute | solution.py:14
  174.6 2.8 multiply_reduce_fusion.14
  181.3 8.4 %collective-permute-done.7 = bf16[16,8192]{1,0:T(8,128)(2,1)S(1)} collective-permute-done((bf16[16,8192]{1,0:T(8,128)(2,1)}, bf16[16,8192]{1,0:T(8,128)(2,1)S(1)}, u32[]{:S(2)}, u32[]{:S(2)}) %collective-permute-start.7) | collective-permute-done | bytes 262176 | tf_op jit(solution)/shard_map/eval_jaxpr/ppermute | solution.py:14
  192.2 2.8 multiply_reduce_fusion.13
  195.6 1.9 add_convert_fusion.13
  198.9 8.4 %collective-permute-done.8 = bf16[16,8192]{1,0:T(8,128)(2,1)S(1)} collective-permute-done((bf16[16,8192]{1,0:T(8,128)(2,1)}, bf16[16,8192]{1,0:T(8,128)(2,1)S(1)}, u32[]{:S(2)}, u32[]{:S(2)}) %collective-permute-start.8) | collective-permute-done | bytes 262176 | tf_op jit(solution)/shard_map/eval_jaxpr/ppermute | solution.py:14
  209.7 2.8 multiply_reduce_fusion.12
  213.2 1.9 add_convert_fusion.12
  216.5 8.4 %collective-permute-done.9 = bf16[16,8192]{1,0:T(8,128)(2,1)S(1)} collective-permute-done((bf16[16,8192]{1,0:T(8,128)(2,1)}, bf16[16,8192]{1,0:T(8,128)(2,1)S(1)}, u32[]{:S(2)}, u32[]{:S(2)}) %collective-permute-start.9) | collective-permute-done | bytes 262176 | tf_op jit(solution)/shard_map/eval_jaxpr/ppermute | solution.py:14
  227.3 2.8 multiply_reduce_fusion.11
  234.1 8.4 %collective-permute-done.10 = bf16[16,8192]{1,0:T(8,128)(2,1)S(1)} collective-permute-done((bf16[16,8192]{1,0:T(8,128)(2,1)}, bf16[16,8192]{1,0:T(8,128)(2,1)S(1)}, u32[]{:S(2)}, u32[]{:S(2)}) %collective-permute-start.10) | collective-permute-done | bytes 262176 | tf_op jit(solution)/shard_map/eval_jaxpr/ppermute | solution.py:14
  244.9 2.8 multiply_reduce_fusion.10
  251.6 8.4 %collective-permute-done.11 = bf16[16,8192]{1,0:T(8,128)(2,1)S(1)} collective-permute-done((bf16[16,8192]{1,0:T(8,128)(2,1)}, bf16[16,8192]{1,0:T(8,128)(2,1)S(1)}, u32[]{:S(2)}, u32[]{:S(2)}) %collective-permute-start.11) | collective-permute-done | bytes 262176 | tf_op jit(solution)/shard_map/eval_jaxpr/ppermute | solution.py:14
  262.5 2.8 multiply_reduce_fusion.9
  269.4 8.4 %collective-permute-done.12 = bf16[16,8192]{1,0:T(8,128)(2,1)S(1)} collective-permute-done((bf16[16,8192]{1,0:T(8,128)(2,1)}, bf16[16,8192]{1,0:T(8,128)(2,1)S(1)}, u32[]{:S(2)}, u32[]{:S(2)}) %collective-permute-start.12) | collective-permute-done | bytes 262176 | tf_op jit(solution)/shard_map/eval_jaxpr/ppermute | solution.py:14
  280.3 2.8 multiply_reduce_fusion.8
  287.0 8.7 %collective-permute-done.13 = bf16[16,8192]{1,0:T(8,128)(2,1)S(1)} collective-permute-done((bf16[16,8192]{1,0:T(8,128)(2,1)}, bf16[16,8192]{1,0:T(8,128)(2,1)S(1)}, u32[]{:S(2)}, u32[]{:S(2)}) %collective-permute-start.13) | collective-permute-done | bytes 262176 | tf_op jit(solution)/shard_map/eval_jaxpr/ppermute | solution.py:14
  298.2 2.8 multiply_reduce_fusion.7
  304.9 10.1 %collective-permute-done.14 = bf16[16,8192]{1,0:T(8,128)(2,1)S(1)} collective-permute-done((bf16[16,8192]{1,0:T(8,128)(2,1)}, bf16[16,8192]{1,0:T(8,128)(2,1)S(1)}, u32[]{:S(2)}, u32[]{:S(2)}) %collective-permute-start.14) | collective-permute-done | bytes 262176 | tf_op jit(solution)/shard_map/eval_jaxpr/ppermute | solution.py:14
  317.5 2.8 multiply_reduce_fusion.6
  324.3 11.7 %collective-permute-done.15 = bf16[16,8192]{1,0:T(8,128)(2,1)S(1)} collective-permute-done((bf16[16,8192]{1,0:T(8,128)(2,1)}, bf16[16,8192]{1,0:T(8,128)(2,1)S(1)}, u32[]{:S(2)}, u32[]{:S(2)}) %collective-permute-start.15) | collective-permute-done | bytes 262176 | tf_op jit(solution)/shard_map/eval_jaxpr/ppermute | solution.py:14
  338.4 2.8 multiply_reduce_fusion.5
  345.1 11.1 %collective-permute-done.16 = bf16[16,8192]{1,0:T(8,128)(2,1)S(1)} collective-permute-done((bf16[16,8192]{1,0:T(8,128)(2,1)}, bf16[16,8192]{1,0:T(8,128)(2,1)S(1)}, u32[]{:S(2)}, u32[]{:S(2)}) %collective-permute-start.16) | collective-permute-done | bytes 262176 | tf_op jit(solution)/shard_map/eval_jaxpr/ppermute | solution.py:14
  358.7 2.8 multiply_reduce_fusion.4
  365.4 9.2 %collective-permute-done.17 = bf16[16,8192]{1,0:T(8,128)(2,1)S(1)} collective-permute-done((bf16[16,8192]{1,0:T(8,128)(2,1)}, bf16[16,8192]{1,0:T(8,128)(2,1)S(1)}, u32[]{:S(2)}, u32[]{:S(2)}) %collective-permute-start.17) | collective-permute-done | bytes 262176 | tf_op jit(solution)/shard_map/eval_jaxpr/ppermute | solution.py:14
  377.2 2.8 multiply_reduce_fusion.3
  383.8 7.9 %collective-permute-done.18 = bf16[16,8192]{1,0:T(8,128)(2,1)S(1)} collective-permute-done((bf16[16,8192]{1,0:T(8,128)(2,1)}, bf16[16,8192]{1,0:T(8,128)(2,1)S(1)}, u32[]{:S(2)}, u32[]{:S(2)}) %collective-permute-start.18) | collective-permute-done | bytes 262176 | tf_op jit(solution)/shard_map/eval_jaxpr/ppermute | solution.py:14
  394.2 2.8 multiply_reduce_fusion.2
  400.9 7.6 %collective-permute-done.19 = bf16[16,8192]{1,0:T(8,128)(2,1)S(1)} collective-permute-done((bf16[16,8192]{1,0:T(8,128)(2,1)}, bf16[16,8192]{1,0:T(8,128)(2,1)S(1)}, u32[]{:S(2)}, u32[]{:S(2)}) %collective-permute-start.19) | collective-permute-done | bytes 262176 | tf_op jit(solution)/shard_map/eval_jaxpr/ppermute | solution.py:14
  410.9 2.2 multiply_reduce_fusion.1
  413.2 2.0 add_convert_fusion.1
  416.4 8.0 %collective-permute-done.20 = bf16[16,8192]{1,0:T(8,128)(2,1)S(1)} collective-permute-done((bf16[16,8192]{1,0:T(8,128)(2,1)}, bf16[16,8192]{1,0:T(8,128)(2,1)S(1)}, u32[]{:S(2)}, u32[]{:S(2)}) %collective-permute-start.20) | collective-permute-done | bytes 262176 | tf_op jit(solution)/shard_map/eval_jaxpr/ppermute | solution.py:14
  427.0 2.2 multiply_reduce_fusion
  433.1 6.8 %collective-permute-done.21 = bf16[16,8192]{1,0:T(8,128)(2,1)S(1)} collective-permute-done((bf16[16,8192]{1,0:T(8,128)(2,1)S(1)}, bf16[16,8192]{1,0:T(8,128)(2,1)S(1)}, u32[]{:S(2)}, u32[]{:S(2)}) %collective-permute-start.21) | collective-permute-done | bytes 262176 | tf_op jit(solution)/shard_map/eval_jaxpr/ppermute | solution.py:14
  446.5 4.0 fusion.2
  452.2 45.2 %reduce-scatter.2.cloned.1.call-done = f32[65,1024]{1,0:T(8,128)} async-done(((f32[65,8192]{1,0:T(8,128)}), f32[65,1024]{1,0:T(8,128)}) %reduce-scatter.2.cloned.1.call-update) | async-done | bytes 266256 | tf_op jit(solution)/shard_map/reduce_scatter | solution.py:90
  499.1 31.8 %psum.7 = f32[]{:T(128)} all-reduce(f32[]{:T(128)} %multiply_reduce_fusion.22), channel_id=1, replica_groups=mesh['pipe'=16,'seq'=8,'dp'=4] {'pipe'}, use_global_device_ids=true, to_apply=%region_26.27 | all-reduce | flops 1 | bytes 8 | tf_op jit(solution)/shard_map/psum | solution.py:94
  530.9 4.3 collective-permute-done.22
  536.5 3.2 collective-permute-start.23
  539.7 3.4 collective-permute-done.23
  543.8 3.2 collective-permute-start.24
  547.0 3.7 collective-permute-done.24
  552.6 2.8 collective-permute-start.27
  555.4 3.1 collective-permute-start.26
  558.5 3.9 collective-permute-start.25
  (159 shorter events, 143.7 us)
Async XLA Ops:
  7.2 50.2 %copy-start = (bf16[1,1,128,8192]{3,2,1,0:T(8,128)(2,1)S(1)}, bf16[1,1,128,8192]{3,2,1,0:T(8,128)(2,1)}, u32[]{:S(2)}) copy-start(bf16[1,1,128,8192]{3,2,1,0:T(8,128)(2,1)} %param.5) | copy-start | bytes 6291460
  7.2 49.2 %all-gather.2.cloned.1.call-start = ((), (), s32[]{:S(2)}) async-start(), calls=%async_computation.1 | async-start | bytes 1327104 | tf_op jit(solution)/shard_map/all_gather | solution.py:24
  23.5 473.9 %reduce-scatter.2.cloned.1.call-start = ((), (), s32[]{:S(2)}) async-start(), calls=%async_computation.2 | async-start | bytes 2654208 | tf_op jit(solution)/shard_map/reduce_scatter | solution.py:90
  57.3 2.0 copy-start.24
  61.2 12.6 %copy-start.3 = (bf16[65,8192]{1,0:T(8,128)(2,1)S(1)}, bf16[65,8192]{1,0:T(8,128)(2,1)}, u32[]{:S(2)}) copy-start(bf16[65,8192]{1,0:T(8,128)(2,1)} %all-gather.2.cloned.1.call-done) | copy-start | bytes 3194884
  61.2 10.8 %collective-permute-start = (bf16[16,8192]{1,0:T(8,128)(2,1)}, bf16[16,8192]{1,0:T(8,128)(2,1)}, u32[]{:S(2)}, u32[]{:S(2)}) collective-permute-start(bf16[16,8192]{1,0:T(8,128)(2,1)} %add_convert_fusion.21), channel_id=1, source_target_pairs={{32,0},{64,32},{96,64},{128,96},{160,128},{192,160},{224,192},{256... | collective-permute-start | bytes 786440 | tf_op jit(solution)/shard_map/eval_jaxpr/ppermute | solution.py:14
  79.1 9.7 %collective-permute-start.1 = (bf16[16,8192]{1,0:T(8,128)(2,1)}, bf16[16,8192]{1,0:T(8,128)(2,1)S(1)}, u32[]{:S(2)}, u32[]{:S(2)}) collective-permute-start(bf16[16,8192]{1,0:T(8,128)(2,1)} %add_convert_fusion.20), channel_id=1, source_target_pairs={{32,0},{64,32},{96,64},{128,96},{160,128},{192,160},{224,192},{256... | collective-permute-start | bytes 786440 | tf_op jit(solution)/shard_map/eval_jaxpr/ppermute | solution.py:14
  88.8 0.7 copy-start.6
  95.5 8.8 %collective-permute-start.2 = (bf16[16,8192]{1,0:T(8,128)(2,1)}, bf16[16,8192]{1,0:T(8,128)(2,1)S(1)}, u32[]{:S(2)}, u32[]{:S(2)}) collective-permute-start(bf16[16,8192]{1,0:T(8,128)(2,1)} %add_convert_fusion.19), channel_id=1, source_target_pairs={{32,0},{64,32},{96,64},{128,96},{160,128},{192,160},{224,192},{256... | collective-permute-start | bytes 786440 | tf_op jit(solution)/shard_map/eval_jaxpr/ppermute | solution.py:14
  104.3 0.7 copy-start.7
  111.0 9.5 %collective-permute-start.3 = (bf16[16,8192]{1,0:T(8,128)(2,1)}, bf16[16,8192]{1,0:T(8,128)(2,1)S(1)}, u32[]{:S(2)}, u32[]{:S(2)}) collective-permute-start(bf16[16,8192]{1,0:T(8,128)(2,1)} %add_convert_fusion.18), channel_id=1, source_target_pairs={{32,0},{64,32},{96,64},{128,96},{160,128},{192,160},{224,192},{256... | collective-permute-start | bytes 786440 | tf_op jit(solution)/shard_map/eval_jaxpr/ppermute | solution.py:14
  120.5 0.7 copy-start.4
  128.4 8.8 %collective-permute-start.4 = (bf16[16,8192]{1,0:T(8,128)(2,1)}, bf16[16,8192]{1,0:T(8,128)(2,1)S(1)}, u32[]{:S(2)}, u32[]{:S(2)}) collective-permute-start(bf16[16,8192]{1,0:T(8,128)(2,1)} %add_convert_fusion.17), channel_id=1, source_target_pairs={{32,0},{64,32},{96,64},{128,96},{160,128},{192,160},{224,192},{256... | collective-permute-start | bytes 786440 | tf_op jit(solution)/shard_map/eval_jaxpr/ppermute | solution.py:14
  137.2 0.7 copy-start.8
  145.1 9.3 %collective-permute-start.5 = (bf16[16,8192]{1,0:T(8,128)(2,1)}, bf16[16,8192]{1,0:T(8,128)(2,1)S(1)}, u32[]{:S(2)}, u32[]{:S(2)}) collective-permute-start(bf16[16,8192]{1,0:T(8,128)(2,1)} %add_convert_fusion.16), channel_id=1, source_target_pairs={{32,0},{64,32},{96,64},{128,96},{160,128},{192,160},{224,192},{256... | collective-permute-start | bytes 786440 | tf_op jit(solution)/shard_map/eval_jaxpr/ppermute | solution.py:14
  154.5 0.7 copy-start.9
  162.4 9.7 %collective-permute-start.6 = (bf16[16,8192]{1,0:T(8,128)(2,1)}, bf16[16,8192]{1,0:T(8,128)(2,1)S(1)}, u32[]{:S(2)}, u32[]{:S(2)}) collective-permute-start(bf16[16,8192]{1,0:T(8,128)(2,1)} %add_convert_fusion.15), channel_id=1, source_target_pairs={{32,0},{64,32},{96,64},{128,96},{160,128},{192,160},{224,192},{256... | collective-permute-start | bytes 786440 | tf_op jit(solution)/shard_map/eval_jaxpr/ppermute | solution.py:14
  172.1 0.7 copy-start.10
  180.0 9.7 %collective-permute-start.7 = (bf16[16,8192]{1,0:T(8,128)(2,1)}, bf16[16,8192]{1,0:T(8,128)(2,1)S(1)}, u32[]{:S(2)}, u32[]{:S(2)}) collective-permute-start(bf16[16,8192]{1,0:T(8,128)(2,1)} %add_convert_fusion.14), channel_id=1, source_target_pairs={{32,0},{64,32},{96,64},{128,96},{160,128},{192,160},{224,192},{256... | collective-permute-start | bytes 786440 | tf_op jit(solution)/shard_map/eval_jaxpr/ppermute | solution.py:14
  189.7 0.7 copy-start.11
  197.6 9.7 %collective-permute-start.8 = (bf16[16,8192]{1,0:T(8,128)(2,1)}, bf16[16,8192]{1,0:T(8,128)(2,1)S(1)}, u32[]{:S(2)}, u32[]{:S(2)}) collective-permute-start(bf16[16,8192]{1,0:T(8,128)(2,1)} %add_convert_fusion.13), channel_id=1, source_target_pairs={{32,0},{64,32},{96,64},{128,96},{160,128},{192,160},{224,192},{256... | collective-permute-start | bytes 786440 | tf_op jit(solution)/shard_map/eval_jaxpr/ppermute | solution.py:14
  207.2 0.7 copy-start.12
  215.2 9.7 %collective-permute-start.9 = (bf16[16,8192]{1,0:T(8,128)(2,1)}, bf16[16,8192]{1,0:T(8,128)(2,1)S(1)}, u32[]{:S(2)}, u32[]{:S(2)}) collective-permute-start(bf16[16,8192]{1,0:T(8,128)(2,1)} %add_convert_fusion.12), channel_id=1, source_target_pairs={{32,0},{64,32},{96,64},{128,96},{160,128},{192,160},{224,192},{256... | collective-permute-start | bytes 786440 | tf_op jit(solution)/shard_map/eval_jaxpr/ppermute | solution.py:14
  224.8 0.7 copy-start.13
  232.7 9.7 %collective-permute-start.10 = (bf16[16,8192]{1,0:T(8,128)(2,1)}, bf16[16,8192]{1,0:T(8,128)(2,1)S(1)}, u32[]{:S(2)}, u32[]{:S(2)}) collective-permute-start(bf16[16,8192]{1,0:T(8,128)(2,1)} %add_convert_fusion.11), channel_id=1, source_target_pairs={{32,0},{64,32},{96,64},{128,96},{160,128},{192,160},{224,192},{256... | collective-permute-start | bytes 786440 | tf_op jit(solution)/shard_map/eval_jaxpr/ppermute | solution.py:14
  242.4 0.7 copy-start.14
  250.3 9.7 %collective-permute-start.11 = (bf16[16,8192]{1,0:T(8,128)(2,1)}, bf16[16,8192]{1,0:T(8,128)(2,1)S(1)}, u32[]{:S(2)}, u32[]{:S(2)}) collective-permute-start(bf16[16,8192]{1,0:T(8,128)(2,1)} %add_convert_fusion.10), channel_id=1, source_target_pairs={{32,0},{64,32},{96,64},{128,96},{160,128},{192,160},{224,192},{256... | collective-permute-start | bytes 786440 | tf_op jit(solution)/shard_map/eval_jaxpr/ppermute | solution.py:14
  260.0 0.7 copy-start.15
  267.9 9.9 %collective-permute-start.12 = (bf16[16,8192]{1,0:T(8,128)(2,1)}, bf16[16,8192]{1,0:T(8,128)(2,1)S(1)}, u32[]{:S(2)}, u32[]{:S(2)}) collective-permute-start(bf16[16,8192]{1,0:T(8,128)(2,1)} %add_convert_fusion.9), channel_id=1, source_target_pairs={{32,0},{64,32},{96,64},{128,96},{160,128},{192,160},{224,192},{256... | collective-permute-start | bytes 786440 | tf_op jit(solution)/shard_map/eval_jaxpr/ppermute | solution.py:14
  277.8 0.7 copy-start.16
  285.7 10.0 %collective-permute-start.13 = (bf16[16,8192]{1,0:T(8,128)(2,1)}, bf16[16,8192]{1,0:T(8,128)(2,1)S(1)}, u32[]{:S(2)}, u32[]{:S(2)}) collective-permute-start(bf16[16,8192]{1,0:T(8,128)(2,1)} %add_convert_fusion.8), channel_id=1, source_target_pairs={{32,0},{64,32},{96,64},{128,96},{160,128},{192,160},{224,192},{256... | collective-permute-start | bytes 786440 | tf_op jit(solution)/shard_map/eval_jaxpr/ppermute | solution.py:14
  295.7 0.7 copy-start.17
  303.6 11.4 %collective-permute-start.14 = (bf16[16,8192]{1,0:T(8,128)(2,1)}, bf16[16,8192]{1,0:T(8,128)(2,1)S(1)}, u32[]{:S(2)}, u32[]{:S(2)}) collective-permute-start(bf16[16,8192]{1,0:T(8,128)(2,1)} %add_convert_fusion.7), channel_id=1, source_target_pairs={{32,0},{64,32},{96,64},{128,96},{160,128},{192,160},{224,192},{256... | collective-permute-start | bytes 786440 | tf_op jit(solution)/shard_map/eval_jaxpr/ppermute | solution.py:14
  315.0 0.7 copy-start.18
  323.0 13.0 %collective-permute-start.15 = (bf16[16,8192]{1,0:T(8,128)(2,1)}, bf16[16,8192]{1,0:T(8,128)(2,1)S(1)}, u32[]{:S(2)}, u32[]{:S(2)}) collective-permute-start(bf16[16,8192]{1,0:T(8,128)(2,1)} %add_convert_fusion.6), channel_id=1, source_target_pairs={{32,0},{64,32},{96,64},{128,96},{160,128},{192,160},{224,192},{256... | collective-permute-start | bytes 786440 | tf_op jit(solution)/shard_map/eval_jaxpr/ppermute | solution.py:14
  335.9 0.7 copy-start.19
  343.9 12.4 %collective-permute-start.16 = (bf16[16,8192]{1,0:T(8,128)(2,1)}, bf16[16,8192]{1,0:T(8,128)(2,1)S(1)}, u32[]{:S(2)}, u32[]{:S(2)}) collective-permute-start(bf16[16,8192]{1,0:T(8,128)(2,1)} %add_convert_fusion.5), channel_id=1, source_target_pairs={{32,0},{64,32},{96,64},{128,96},{160,128},{192,160},{224,192},{256... | collective-permute-start | bytes 786440 | tf_op jit(solution)/shard_map/eval_jaxpr/ppermute | solution.py:14
  356.2 0.7 copy-start.20
  364.1 10.5 %collective-permute-start.17 = (bf16[16,8192]{1,0:T(8,128)(2,1)}, bf16[16,8192]{1,0:T(8,128)(2,1)S(1)}, u32[]{:S(2)}, u32[]{:S(2)}) collective-permute-start(bf16[16,8192]{1,0:T(8,128)(2,1)} %add_convert_fusion.4), channel_id=1, source_target_pairs={{32,0},{64,32},{96,64},{128,96},{160,128},{192,160},{224,192},{256... | collective-permute-start | bytes 786440 | tf_op jit(solution)/shard_map/eval_jaxpr/ppermute | solution.py:14
  374.7 0.7 copy-start.21
  382.5 9.2 %collective-permute-start.18 = (bf16[16,8192]{1,0:T(8,128)(2,1)}, bf16[16,8192]{1,0:T(8,128)(2,1)S(1)}, u32[]{:S(2)}, u32[]{:S(2)}) collective-permute-start(bf16[16,8192]{1,0:T(8,128)(2,1)} %add_convert_fusion.3), channel_id=1, source_target_pairs={{32,0},{64,32},{96,64},{128,96},{160,128},{192,160},{224,192},{256... | collective-permute-start | bytes 786440 | tf_op jit(solution)/shard_map/eval_jaxpr/ppermute | solution.py:14
  391.7 0.7 copy-start.22
  399.6 8.9 %collective-permute-start.19 = (bf16[16,8192]{1,0:T(8,128)(2,1)}, bf16[16,8192]{1,0:T(8,128)(2,1)S(1)}, u32[]{:S(2)}, u32[]{:S(2)}) collective-permute-start(bf16[16,8192]{1,0:T(8,128)(2,1)} %add_convert_fusion.2), channel_id=1, source_target_pairs={{32,0},{64,32},{96,64},{128,96},{160,128},{192,160},{224,192},{256... | collective-permute-start | bytes 786440 | tf_op jit(solution)/shard_map/eval_jaxpr/ppermute | solution.py:14
  408.4 0.7 copy-start.23
  415.1 9.3 %collective-permute-start.20 = (bf16[16,8192]{1,0:T(8,128)(2,1)}, bf16[16,8192]{1,0:T(8,128)(2,1)S(1)}, u32[]{:S(2)}, u32[]{:S(2)}) collective-permute-start(bf16[16,8192]{1,0:T(8,128)(2,1)} %add_convert_fusion.1), channel_id=1, source_target_pairs={{32,0},{64,32},{96,64},{128,96},{160,128},{192,160},{224,192},{256... | collective-permute-start | bytes 786440 | tf_op jit(solution)/shard_map/eval_jaxpr/ppermute | solution.py:14
  424.5 0.7 copy-start.5
  430.5 9.4 %collective-permute-start.21 = (bf16[16,8192]{1,0:T(8,128)(2,1)S(1)}, bf16[16,8192]{1,0:T(8,128)(2,1)S(1)}, u32[]{:S(2)}, u32[]{:S(2)}) collective-permute-start(bf16[16,8192]{1,0:T(8,128)(2,1)S(1)} %add_convert_fusion), channel_id=1, source_target_pairs={{32,0},{64,32},{96,64},{128,96},{160,128},{192,160},{224,192},{256... | collective-permute-start | bytes 786440 | tf_op jit(solution)/shard_map/eval_jaxpr/ppermute | solution.py:14
  433.1 11.1 %copy-start.1 = (bf16[128,8192]{1,0:T(8,128)(2,1)}, bf16[128,8192]{1,0:T(8,128)(2,1)S(1)}, u32[]{:S(2)}) copy-start(bf16[128,8192]{1,0:T(8,128)(2,1)S(1)} %multiply_convert_fusion) | copy-start | bytes 6291460
  443.4 1.3 copy-start.2
  530.9 4.3 collective-permute-start.22
  536.5 6.6 %collective-permute-start.23 = (f32[]{:T(128)}, f32[]{:T(128)}, u32[]{:S(2)}, u32[]{:S(2)}) collective-permute-start(f32[]{:T(128)} %add.383), channel_id=1, source_target_pairs={{0,8},{4,12},{8,16},{12,20},{16,24},{20,28},{24,0},{28,4},{1,9},{5... | collective-permute-start | bytes 20 | tf_op jit(solution)/shard_map/ppermute | solution.py:98
  543.8 6.9 %collective-permute-start.24 = (f32[]{:T(128)}, f32[]{:T(128)}, u32[]{:S(2)}, u32[]{:S(2)}) collective-permute-start(f32[]{:T(128)} %add.384), channel_id=1, source_target_pairs={{0,16},{4,20},{8,24},{12,28},{16,0},{20,4},{24,8},{28,12},{1,17},{... | collective-permute-start | bytes 20 | tf_op jit(solution)/shard_map/ppermute | solution.py:98
  552.6 9.8 %collective-permute-start.27 = (f32[65,256]{1,0:T(8,128)S(1)}, f32[65,256]{1,0:T(8,128)S(1)}, u32[]{:S(2)}, u32[]{:S(2)}) collective-permute-start(f32[65,256]{1,0:T(8,128)S(1)} %get-tuple-element.47), channel_id=1, source_target_pairs={{0,3},{1,0},{2,1},{3,2},{4,7},{5,4},{6,5},{7,6},{8,11},{9,8},{10,9... | collective-permute-start | bytes 199688 | tf_op jit(solution)/shard_map/ppermute | solution.py:110
  555.4 7.8 %collective-permute-start.26 = (f32[65,256]{1,0:T(8,128)S(1)}, f32[65,256]{1,0:T(8,128)S(1)}, u32[]{:S(2)}, u32[]{:S(2)}) collective-permute-start(f32[65,256]{1,0:T(8,128)S(1)} %get-tuple-element.48), channel_id=1, source_target_pairs={{0,2},{1,3},{2,0},{3,1},{4,6},{5,7},{6,4},{7,5},{8,10},{9,11},{10,... | collective-permute-start | bytes 199688 | tf_op jit(solution)/shard_map/ppermute | solution.py:110
  558.5 6.3 %collective-permute-start.25 = (f32[65,256]{1,0:T(8,128)S(1)}, f32[65,256]{1,0:T(8,128)S(1)}, u32[]{:S(2)}, u32[]{:S(2)}) collective-permute-start(f32[65,256]{1,0:T(8,128)S(1)} %get-tuple-element.46), channel_id=1, source_target_pairs={{0,1},{1,2},{2,3},{3,0},{4,5},{5,6},{6,7},{7,4},{8,9},{9,10},{10,1... | collective-permute-start | bytes 199688 | tf_op jit(solution)/shard_map/ppermute | solution.py:110
Sparse Core Ops, SparseCore 0:
  23.6 32.7 all-gather.1
  452.3 45.0 reduce-scatter.1

commit v3 on v2

--- a/solution.py
+++ b/solution.py
@@ -39,53 +39,51 @@
     contract_last = (((1,), (1,)), ((), ()))
     contract_first = (((0,), (0,)), ((), ()))
 
-    def back_block(upstream_gradient, block_offset):
+    def turn(turn_index, carry):
+        incoming, sum_a, sum_b, sum_g = carry
+        block_index = turn_index - (sections - 1 - section)
+        inside = jnp.logical_and(block_index >= 0, block_index < block_total)
+        block_offset = jnp.clip(block_index, 0, block_total - 1) * rows_per_block
+        top_block = lax.dynamic_slice_in_dim(top, block_offset, rows_per_block, 0)
+        source = jnp.where(section == sections - 1, top_block, incoming)
         hidden_part = lax.dynamic_slice_in_dim(hidden, block_offset, rows_per_block, 0)
         r_part = lax.dynamic_slice_in_dim(inverse_root_mean, block_offset, rows_per_block, 0)
         input_portion = hidden_part.astype(jnp.float32) / r_part
         d_low = lax.dot_general(
-            upstream_gradient, b_full, contract_last, preferred_element_type=jnp.float32
+            source, b_full, contract_last, preferred_element_type=jnp.float32
         ).astype(jnp.bfloat16)
         normalized_gradient = jnp.dot(d_low, a_full, preferred_element_type=jnp.float32)
         input_gradient = normalized_gradient * gain_float
         hidden_gradient = (
-            upstream_gradient.astype(jnp.float32)
+            source.astype(jnp.float32)
             + (
                 input_gradient
                 - input_portion * jnp.mean(input_gradient * input_portion, axis=-1, keepdims=True)
             )
             / r_part
         )
-        return hidden_gradient.astype(jnp.bfloat16)
-
-    def turn(turn_index, carry):
-        incoming, store = carry
-        block_index = turn_index - (sections - 1 - section)
-        inside = jnp.logical_and(block_index >= 0, block_index < block_total)
-        block_offset = jnp.clip(block_index, 0, block_total - 1) * rows_per_block
-        top_block = lax.dynamic_slice_in_dim(top, block_offset, rows_per_block, 0)
-        source = jnp.where(section == sections - 1, top_block, incoming)
-        slot = jnp.where(inside, block_index, block_total)
-        store = lax.dynamic_update_slice_in_dim(store, source[None], slot, 0)
-        result = back_block(source, block_offset)
-        incoming = from_behind(result, "pipe", -1)
-        return (incoming, store)
+        incoming = from_behind(hidden_gradient.astype(jnp.bfloat16), "pipe", -1)
+        normalized_part = (input_portion * gain_float).astype(jnp.bfloat16)
+        low_part = lax.dynamic_slice_in_dim(low, block_offset, rows_per_block, 0)
+        part_a = lax.dot_general(
+            d_low, normalized_part, contract_first, preferred_element_type=jnp.float32
+        )
+        part_b = lax.dot_general(low_part, source, contract_first, preferred_element_type=jnp.float32)
+        part_g = jnp.sum(normalized_gradient * input_portion, axis=0)[None, :]
+        sum_a = sum_a + jnp.where(inside, part_a, 0.0)
+        sum_b = sum_b + jnp.where(inside, part_b, 0.0)
+        sum_g = sum_g + jnp.where(inside, part_g, 0.0)
+        return (incoming, sum_a, sum_b, sum_g)
 
     begin = (
         jnp.zeros((rows_per_block, width), jnp.bfloat16),
-        jnp.zeros((block_total + 1, rows_per_block, width), jnp.bfloat16),
+        jnp.zeros((rank, width), jnp.float32),
+        jnp.zeros((rank, width), jnp.float32),
+        jnp.zeros((1, width), jnp.float32),
     )
-    store = lax.fori_loop(0, sections + block_total - 1, turn, begin, unroll=True)[1]
-    mine = store[:block_total].reshape(rows, width)
-    d_low = lax.dot_general(mine, b_full, contract_last, preferred_element_type=jnp.float32).astype(
-        jnp.bfloat16
+    _, grad_a, grad_b, gain_gradient = lax.fori_loop(
+        0, sections + block_total - 1, turn, begin
     )
-    normalized_gradient = jnp.dot(d_low, a_full, preferred_element_type=jnp.float32)
-    grad_a = lax.dot_general(
-        d_low, normalized_rows, contract_first, preferred_element_type=jnp.float32
-    )
-    grad_b = lax.dot_general(low, mine, contract_first, preferred_element_type=jnp.float32)
-    gain_gradient = jnp.sum(normalized_gradient * input_normalized, axis=0)[None, :]
     grads = jnp.concatenate([grad_a, grad_b, gain_gradient], axis=0)
     part = lax.psum_scatter(grads, "seq", scatter_dimension=1, tiled=True)
     examples = lax.axis_size("dp")

time: 579 us -> 508 us (0.88)
  other arithmetic: 104 us -> 60.2 us
  waiting for transfers between devices: 274 us -> 245 us
  matrix products: 65.5 us -> 82.7 us
  local copies, waits for them, and re-layouts: 19.7 us -> 5.16 us
    dynamic_update_slice x23 -> x0, other arithmetic: 41 us -> none  [turn(): store = lax.dynamic_update_slice_in_dim(store, source[None], slot, 0)]
    ppermute x22 -> x23, waiting for transfers between devices: 184 us -> 152 us  [from_behind(): lax.ppermute(value, axis, [(source, source + steps) for source in range(i...]
    select_n x0 -> x46, other arithmetic: none -> 23.4 us  [the longest x23 23.3 us: turn(): source = jnp.where(section == sections - 1, top_block, incoming)]
    dot_general x26 -> x93, matrix products: 65.5 us -> 82.7 us  [the longest x23 35.1 us: turn(): jnp.dot(d_low, a_full, preferred_element_type=jnp.float32)]
    convert_element_type x23 -> x24, other arithmetic: 43.5 us -> 27.7 us  [the longest x23 26.8 us: turn(): incoming = from_behind(hidden_gradient.astype(jnp.bfloat16), 'pipe', -1)]
    unnamed x50 -> x5, local copies, waits for them, and re-layouts: 14.2 us -> 0.14 us
    div x22 -> x23, other arithmetic: 11.2 us -> 0.15 us  [turn(): jnp.mean(input_gradient * input_portion, axis=-1, keepdims=True)]
    ppermute x22 -> x23, starting transfers between devices: 28.5 us -> 29.7 us  [from_behind(): lax.ppermute(value, axis, [(source, source + steps) for source in range(i...]
  transfers between devices with their start and end apart: 30 -> 31, of which waited for: 29 -> 30; matrix products, arithmetic and copies ran while one was open for 1% -> 9% of each run, Pallas kernels for 0% -> 0%
where the time goes in v3:
time: 508 us; the launch traced here: 504 us
  waiting for transfers between devices  245 us (48%)
  matrix products  82.7 us (16%)
  other arithmetic  60.2 us (12%)
  blocking collectives  47.2 us (9%)
  starting transfers between devices  44.9 us (9%)
  between operations  17.9 us (4%)
  local copies, waits for them, and re-layouts  5.16 us (1%)
    ppermute x23, waiting for transfers between devices, from_behind(): lax.ppermute(value, axis, [(source, source + steps) for source in range(i...  152 us
    reduce_scatter x1, waiting for transfers between devices, on_device(): part = lax.psum_scatter(grads, 'seq', scatter_dimension=1, tiled=True)  45.1 us
    dot_general x23, matrix products, turn(): jnp.dot(d_low, a_full, preferred_element_type=jnp.float32)  35.1 us
    psum x1, blocking collectives, on_device(): total = lax.psum(square, 'pipe')  31.9 us
    dot_general x23, matrix products, turn(): lax.dot_general(d_low, normalized_part, contract_first, preferred_element...  31.3 us
    all_gather x1, waiting for transfers between devices, on_device(): lax.all_gather(lax.all_gather(params, 'dp', axis=1, tiled=True), 'seq', a...  30.7 us
    ppermute x23, starting transfers between devices, from_behind(): lax.ppermute(value, axis, [(source, source + steps) for source in range(i...  29.7 us
    convert_element_type x23, other arithmetic, turn(): incoming = from_behind(hidden_gradient.astype(jnp.bfloat16), 'pipe', -1)  26.8 us
  transfers between devices with their start and end apart: 31, of which 30 were waited for; matrix products, arithmetic and copies ran while one was open for 9% of the time, Pallas kernels for 0%

profile of v3, /device:TPU:6, one launch (start us, length us, event | category | flops | bytes accessed | tf_op | source)
XLA Modules:
  0.0 504.1 jit_solution(4897689407077352204)
XLA Ops:
  8.1 15.4 %all_gather.6 = bf16[65,1024]{1,0:T(8,128)(2,1)} all-gather(bf16[65,256]{1,0:T(8,128)(2,1)S(1)} %pad_maximum_fusion.1), channel_id=1, replica_groups=mesh['pipe'=16,'seq'=8,'dp'=4] {'dp'}, dimensions={1}, use_global_device_ids=true | all-gather | bytes 166400 | tf_op jit(solution)/shard_map/all_gather | solution.py:24
  23.6 2.1 fusion.7
  25.7 30.7 %all-gather.2.cloned.1.call-done = bf16[65,8192]{1,0:T(8,128)(2,1)} async-done(((bf16[65,1024]{1,0:T(8,128)(2,1)}), bf16[65,8192]{1,0:T(8,128)(2,1)}) %all-gather.2.cloned.1.call-update) | async-done | bytes 1064976 | tf_op jit(solution)/shard_map/all_gather | solution.py:24
  57.3 1.9 fusion.12
  59.4 2.1 fusion.18
  61.6 317.4 %while.22 = (s32[]{:T(128)}, bf16[16,8192]{1,0:T(8,128)(2,1)S(1)}, f32[32,8192]{1,0:T(8,128)S(1)}, f32[32,8192]{1,0:T(8,128)S(1)}, f32[1,8192]{1,0:T(1,128)S(1)}...) while((s32[]{:T(128)}, bf16[16,8192]{1,0:T(8,128)(2,1)S(1)}, ...), condition=%wide.region_4.5_spmd.clone, body=%wide.region_1.4_spmd.clone.sunk | while | flops 37896712 | bytes 10264492 | solution.py:84
  63.0 1.5 multiply_reduce_fusion.4
  68.8 7.2 %collective-permute-done = bf16[16,8192]{1,0:T(8,128)(2,1)S(1)} collective-permute-done((bf16[16,8192]{1,0:T(8,128)(2,1)S(1)}, bf16[16,8192]{1,0:T(8,128)(2,1)S(1)}, u32[]{:S(2)}, u32[]{:S(2)}) %collective-permute-start) | collective-permute-done | bytes 262176 | tf_op jit(solution)/shard_map/while/body/eval_jaxpr/ppermute | solution.py:14
  77.3 1.5 multiply_reduce_fusion.4
  83.2 6.3 %collective-permute-done = bf16[16,8192]{1,0:T(8,128)(2,1)S(1)} collective-permute-done((bf16[16,8192]{1,0:T(8,128)(2,1)S(1)}, bf16[16,8192]{1,0:T(8,128)(2,1)S(1)}, u32[]{:S(2)}, u32[]{:S(2)}) %collective-permute-start) | collective-permute-done | bytes 262176 | tf_op jit(solution)/shard_map/while/body/eval_jaxpr/ppermute | solution.py:14
  90.8 1.5 multiply_reduce_fusion.4
  96.7 5.5 %collective-permute-done = bf16[16,8192]{1,0:T(8,128)(2,1)S(1)} collective-permute-done((bf16[16,8192]{1,0:T(8,128)(2,1)S(1)}, bf16[16,8192]{1,0:T(8,128)(2,1)S(1)}, u32[]{:S(2)}, u32[]{:S(2)}) %collective-permute-start) | collective-permute-done | bytes 262176 | tf_op jit(solution)/shard_map/while/body/eval_jaxpr/ppermute | solution.py:14
  103.5 1.5 multiply_reduce_fusion.4
  109.4 6.1 %collective-permute-done = bf16[16,8192]{1,0:T(8,128)(2,1)S(1)} collective-permute-done((bf16[16,8192]{1,0:T(8,128)(2,1)S(1)}, bf16[16,8192]{1,0:T(8,128)(2,1)S(1)}, u32[]{:S(2)}, u32[]{:S(2)}) %collective-permute-start) | collective-permute-done | bytes 262176 | tf_op jit(solution)/shard_map/while/body/eval_jaxpr/ppermute | solution.py:14
  116.8 1.5 multiply_reduce_fusion.4
  122.7 5.5 %collective-permute-done = bf16[16,8192]{1,0:T(8,128)(2,1)S(1)} collective-permute-done((bf16[16,8192]{1,0:T(8,128)(2,1)S(1)}, bf16[16,8192]{1,0:T(8,128)(2,1)S(1)}, u32[]{:S(2)}, u32[]{:S(2)}) %collective-permute-start) | collective-permute-done | bytes 262176 | tf_op jit(solution)/shard_map/while/body/eval_jaxpr/ppermute | solution.py:14
  129.5 1.5 multiply_reduce_fusion.4
  135.4 6.0 %collective-permute-done = bf16[16,8192]{1,0:T(8,128)(2,1)S(1)} collective-permute-done((bf16[16,8192]{1,0:T(8,128)(2,1)S(1)}, bf16[16,8192]{1,0:T(8,128)(2,1)S(1)}, u32[]{:S(2)}, u32[]{:S(2)}) %collective-permute-start) | collective-permute-done | bytes 262176 | tf_op jit(solution)/shard_map/while/body/eval_jaxpr/ppermute | solution.py:14
  142.7 1.5 multiply_reduce_fusion.4
  148.5 6.3 %collective-permute-done = bf16[16,8192]{1,0:T(8,128)(2,1)S(1)} collective-permute-done((bf16[16,8192]{1,0:T(8,128)(2,1)S(1)}, bf16[16,8192]{1,0:T(8,128)(2,1)S(1)}, u32[]{:S(2)}, u32[]{:S(2)}) %collective-permute-start) | collective-permute-done | bytes 262176 | tf_op jit(solution)/shard_map/while/body/eval_jaxpr/ppermute | solution.py:14
  156.2 1.5 multiply_reduce_fusion.4
  162.0 6.3 %collective-permute-done = bf16[16,8192]{1,0:T(8,128)(2,1)S(1)} collective-permute-done((bf16[16,8192]{1,0:T(8,128)(2,1)S(1)}, bf16[16,8192]{1,0:T(8,128)(2,1)S(1)}, u32[]{:S(2)}, u32[]{:S(2)}) %collective-permute-start) | collective-permute-done | bytes 262176 | tf_op jit(solution)/shard_map/while/body/eval_jaxpr/ppermute | solution.py:14
  169.7 1.5 multiply_reduce_fusion.4
  175.6 6.3 %collective-permute-done = bf16[16,8192]{1,0:T(8,128)(2,1)S(1)} collective-permute-done((bf16[16,8192]{1,0:T(8,128)(2,1)S(1)}, bf16[16,8192]{1,0:T(8,128)(2,1)S(1)}, u32[]{:S(2)}, u32[]{:S(2)}) %collective-permute-start) | collective-permute-done | bytes 262176 | tf_op jit(solution)/shard_map/while/body/eval_jaxpr/ppermute | solution.py:14
  183.2 1.5 multiply_reduce_fusion.4
  189.1 6.3 %collective-permute-done = bf16[16,8192]{1,0:T(8,128)(2,1)S(1)} collective-permute-done((bf16[16,8192]{1,0:T(8,128)(2,1)S(1)}, bf16[16,8192]{1,0:T(8,128)(2,1)S(1)}, u32[]{:S(2)}, u32[]{:S(2)}) %collective-permute-start) | collective-permute-done | bytes 262176 | tf_op jit(solution)/shard_map/while/body/eval_jaxpr/ppermute | solution.py:14
  202.6 7.4 %collective-permute-done = bf16[16,8192]{1,0:T(8,128)(2,1)S(1)} collective-permute-done((bf16[16,8192]{1,0:T(8,128)(2,1)S(1)}, bf16[16,8192]{1,0:T(8,128)(2,1)S(1)}, u32[]{:S(2)}, u32[]{:S(2)}) %collective-permute-start) | collective-permute-done | bytes 262176 | tf_op jit(solution)/shard_map/while/body/eval_jaxpr/ppermute | solution.py:14
  211.3 1.5 multiply_reduce_fusion.4
  217.2 9.0 %collective-permute-done = bf16[16,8192]{1,0:T(8,128)(2,1)S(1)} collective-permute-done((bf16[16,8192]{1,0:T(8,128)(2,1)S(1)}, bf16[16,8192]{1,0:T(8,128)(2,1)S(1)}, u32[]{:S(2)}, u32[]{:S(2)}) %collective-permute-start) | collective-permute-done | bytes 262176 | tf_op jit(solution)/shard_map/while/body/eval_jaxpr/ppermute | solution.py:14
  227.5 1.5 multiply_reduce_fusion.4
  233.4 9.5 %collective-permute-done = bf16[16,8192]{1,0:T(8,128)(2,1)S(1)} collective-permute-done((bf16[16,8192]{1,0:T(8,128)(2,1)S(1)}, bf16[16,8192]{1,0:T(8,128)(2,1)S(1)}, u32[]{:S(2)}, u32[]{:S(2)}) %collective-permute-start) | collective-permute-done | bytes 262176 | tf_op jit(solution)/shard_map/while/body/eval_jaxpr/ppermute | solution.py:14
  244.2 1.5 multiply_reduce_fusion.4
  250.1 8.4 %collective-permute-done = bf16[16,8192]{1,0:T(8,128)(2,1)S(1)} collective-permute-done((bf16[16,8192]{1,0:T(8,128)(2,1)S(1)}, bf16[16,8192]{1,0:T(8,128)(2,1)S(1)}, u32[]{:S(2)}, u32[]{:S(2)}) %collective-permute-start) | collective-permute-done | bytes 262176 | tf_op jit(solution)/shard_map/while/body/eval_jaxpr/ppermute | solution.py:14
  259.9 1.5 multiply_reduce_fusion.4
  265.7 6.9 %collective-permute-done = bf16[16,8192]{1,0:T(8,128)(2,1)S(1)} collective-permute-done((bf16[16,8192]{1,0:T(8,128)(2,1)S(1)}, bf16[16,8192]{1,0:T(8,128)(2,1)S(1)}, u32[]{:S(2)}, u32[]{:S(2)}) %collective-permute-start) | collective-permute-done | bytes 262176 | tf_op jit(solution)/shard_map/while/body/eval_jaxpr/ppermute | solution.py:14
  273.9 1.5 multiply_reduce_fusion.4
  279.8 5.5 %collective-permute-done = bf16[16,8192]{1,0:T(8,128)(2,1)S(1)} collective-permute-done((bf16[16,8192]{1,0:T(8,128)(2,1)S(1)}, bf16[16,8192]{1,0:T(8,128)(2,1)S(1)}, u32[]{:S(2)}, u32[]{:S(2)}) %collective-permute-start) | collective-permute-done | bytes 262176 | tf_op jit(solution)/shard_map/while/body/eval_jaxpr/ppermute | solution.py:14
  286.6 1.5 multiply_reduce_fusion.4
  292.5 5.7 %collective-permute-done = bf16[16,8192]{1,0:T(8,128)(2,1)S(1)} collective-permute-done((bf16[16,8192]{1,0:T(8,128)(2,1)S(1)}, bf16[16,8192]{1,0:T(8,128)(2,1)S(1)}, u32[]{:S(2)}, u32[]{:S(2)}) %collective-permute-start) | collective-permute-done | bytes 262176 | tf_op jit(solution)/shard_map/while/body/eval_jaxpr/ppermute | solution.py:14
  299.6 1.5 multiply_reduce_fusion.4
  305.4 6.0 %collective-permute-done = bf16[16,8192]{1,0:T(8,128)(2,1)S(1)} collective-permute-done((bf16[16,8192]{1,0:T(8,128)(2,1)S(1)}, bf16[16,8192]{1,0:T(8,128)(2,1)S(1)}, u32[]{:S(2)}, u32[]{:S(2)}) %collective-permute-start) | collective-permute-done | bytes 262176 | tf_op jit(solution)/shard_map/while/body/eval_jaxpr/ppermute | solution.py:14
  318.7 6.3 %collective-permute-done = bf16[16,8192]{1,0:T(8,128)(2,1)S(1)} collective-permute-done((bf16[16,8192]{1,0:T(8,128)(2,1)S(1)}, bf16[16,8192]{1,0:T(8,128)(2,1)S(1)}, u32[]{:S(2)}, u32[]{:S(2)}) %collective-permute-start) | collective-permute-done | bytes 262176 | tf_op jit(solution)/shard_map/while/body/eval_jaxpr/ppermute | solution.py:14
  326.3 1.5 multiply_reduce_fusion.4
  332.2 6.3 %collective-permute-done = bf16[16,8192]{1,0:T(8,128)(2,1)S(1)} collective-permute-done((bf16[16,8192]{1,0:T(8,128)(2,1)S(1)}, bf16[16,8192]{1,0:T(8,128)(2,1)S(1)}, u32[]{:S(2)}, u32[]{:S(2)}) %collective-permute-start) | collective-permute-done | bytes 262176 | tf_op jit(solution)/shard_map/while/body/eval_jaxpr/ppermute | solution.py:14
  339.8 1.5 multiply_reduce_fusion.4
  345.7 6.3 %collective-permute-done = bf16[16,8192]{1,0:T(8,128)(2,1)S(1)} collective-permute-done((bf16[16,8192]{1,0:T(8,128)(2,1)S(1)}, bf16[16,8192]{1,0:T(8,128)(2,1)S(1)}, u32[]{:S(2)}, u32[]{:S(2)}) %collective-permute-start) | collective-permute-done | bytes 262176 | tf_op jit(solution)/shard_map/while/body/eval_jaxpr/ppermute | solution.py:14
  353.3 1.5 multiply_reduce_fusion.4
  359.2 6.3 %collective-permute-done = bf16[16,8192]{1,0:T(8,128)(2,1)S(1)} collective-permute-done((bf16[16,8192]{1,0:T(8,128)(2,1)S(1)}, bf16[16,8192]{1,0:T(8,128)(2,1)S(1)}, u32[]{:S(2)}, u32[]{:S(2)}) %collective-permute-start) | collective-permute-done | bytes 262176 | tf_op jit(solution)/shard_map/while/body/eval_jaxpr/ppermute | solution.py:14
  366.8 1.5 multiply_reduce_fusion.4
  372.7 6.3 %collective-permute-done = bf16[16,8192]{1,0:T(8,128)(2,1)S(1)} collective-permute-done((bf16[16,8192]{1,0:T(8,128)(2,1)S(1)}, bf16[16,8192]{1,0:T(8,128)(2,1)S(1)}, u32[]{:S(2)}, u32[]{:S(2)}) %collective-permute-start) | collective-permute-done | bytes 262176 | tf_op jit(solution)/shard_map/while/body/eval_jaxpr/ppermute | solution.py:14
  379.0 1.6 pad_maximum_fusion
  380.7 45.1 %reduce-scatter.2.cloned.1.call-done = f32[65,1024]{1,0:T(8,128)} async-done(((f32[65,8192]{1,0:T(8,128)}), f32[65,1024]{1,0:T(8,128)}) %reduce-scatter.2.cloned.1.call-update) | async-done | bytes 266256 | tf_op jit(solution)/shard_map/reduce_scatter | solution.py:88
  425.8 1.6 multiply_reduce_fusion.2
  427.4 31.9 %psum.7 = f32[]{:T(128)} all-reduce(f32[]{:T(128)} %multiply_reduce_fusion.2), channel_id=1, replica_groups=mesh['pipe'=16,'seq'=8,'dp'=4] {'pipe'}, use_global_device_ids=true, to_apply=%region_7.8 | all-reduce | flops 1 | bytes 8 | tf_op jit(solution)/shard_map/psum | solution.py:92
  459.3 4.3 collective-permute-done.1
  464.9 3.2 collective-permute-start.2
  468.1 3.4 collective-permute-done.2
  472.1 3.2 collective-permute-start.3
  475.3 3.7 collective-permute-done.3
  480.7 2.5 collective-permute-start.4
  483.2 4.3 collective-permute-start.5
  487.5 1.9 collective-permute-start.6
  489.4 1.5 collective-permute-done.5
  491.0 4.0 collective-permute-done.6
  (255 shorter events, 136.5 us)
Async XLA Ops:
  7.2 50.2 %copy-start = (bf16[1,1,128,8192]{3,2,1,0:T(8,128)(2,1)S(1)}, bf16[1,1,128,8192]{3,2,1,0:T(8,128)(2,1)}, u32[]{:S(2)}) copy-start(bf16[1,1,128,8192]{3,2,1,0:T(8,128)(2,1)} %param.7) | copy-start | bytes 6291460
  7.2 49.2 %all-gather.2.cloned.1.call-start = ((), (), s32[]{:S(2)}) async-start(), calls=%async_computation.1 | async-start | bytes 1327104 | tf_op jit(solution)/shard_map/all_gather | solution.py:24
  23.5 402.3 %reduce-scatter.2.cloned.1.call-start = ((), (), s32[]{:S(2)}) async-start(), calls=%async_computation.2 | async-start | bytes 2654208 | tf_op jit(solution)/shard_map/reduce_scatter | solution.py:88
  59.3 2.3 copy-start.1
  65.7 10.3 %collective-permute-start = (bf16[16,8192]{1,0:T(8,128)(2,1)S(1)}, bf16[16,8192]{1,0:T(8,128)(2,1)S(1)}, u32[]{:S(2)}, u32[]{:S(2)}) collective-permute-start(bf16[16,8192]{1,0:T(8,128)(2,1)S(1)} %add_convert_fusion.2), channel_id=1, source_target_pairs={{32,0},{64,32},{96,64},{128,96},{160,128},{192,160},{224,192},{256... | collective-permute-start | bytes 786440 | tf_op jit(solution)/shard_map/while/body/eval_jaxpr/ppermute | solution.py:14
  80.0 9.5 %collective-permute-start = (bf16[16,8192]{1,0:T(8,128)(2,1)S(1)}, bf16[16,8192]{1,0:T(8,128)(2,1)S(1)}, u32[]{:S(2)}, u32[]{:S(2)}) collective-permute-start(bf16[16,8192]{1,0:T(8,128)(2,1)S(1)} %add_convert_fusion.2), channel_id=1, source_target_pairs={{32,0},{64,32},{96,64},{128,96},{160,128},{192,160},{224,192},{256... | collective-permute-start | bytes 786440 | tf_op jit(solution)/shard_map/while/body/eval_jaxpr/ppermute | solution.py:14
  93.5 8.6 %collective-permute-start = (bf16[16,8192]{1,0:T(8,128)(2,1)S(1)}, bf16[16,8192]{1,0:T(8,128)(2,1)S(1)}, u32[]{:S(2)}, u32[]{:S(2)}) collective-permute-start(bf16[16,8192]{1,0:T(8,128)(2,1)S(1)} %add_convert_fusion.2), channel_id=1, source_target_pairs={{32,0},{64,32},{96,64},{128,96},{160,128},{192,160},{224,192},{256... | collective-permute-start | bytes 786440 | tf_op jit(solution)/shard_map/while/body/eval_jaxpr/ppermute | solution.py:14
  106.2 9.3 %collective-permute-start = (bf16[16,8192]{1,0:T(8,128)(2,1)S(1)}, bf16[16,8192]{1,0:T(8,128)(2,1)S(1)}, u32[]{:S(2)}, u32[]{:S(2)}) collective-permute-start(bf16[16,8192]{1,0:T(8,128)(2,1)S(1)} %add_convert_fusion.2), channel_id=1, source_target_pairs={{32,0},{64,32},{96,64},{128,96},{160,128},{192,160},{224,192},{256... | collective-permute-start | bytes 786440 | tf_op jit(solution)/shard_map/while/body/eval_jaxpr/ppermute | solution.py:14
  119.5 8.6 %collective-permute-start = (bf16[16,8192]{1,0:T(8,128)(2,1)S(1)}, bf16[16,8192]{1,0:T(8,128)(2,1)S(1)}, u32[]{:S(2)}, u32[]{:S(2)}) collective-permute-start(bf16[16,8192]{1,0:T(8,128)(2,1)S(1)} %add_convert_fusion.2), channel_id=1, source_target_pairs={{32,0},{64,32},{96,64},{128,96},{160,128},{192,160},{224,192},{256... | collective-permute-start | bytes 786440 | tf_op jit(solution)/shard_map/while/body/eval_jaxpr/ppermute | solution.py:14
  132.2 9.1 %collective-permute-start = (bf16[16,8192]{1,0:T(8,128)(2,1)S(1)}, bf16[16,8192]{1,0:T(8,128)(2,1)S(1)}, u32[]{:S(2)}, u32[]{:S(2)}) collective-permute-start(bf16[16,8192]{1,0:T(8,128)(2,1)S(1)} %add_convert_fusion.2), channel_id=1, source_target_pairs={{32,0},{64,32},{96,64},{128,96},{160,128},{192,160},{224,192},{256... | collective-permute-start | bytes 786440 | tf_op jit(solution)/shard_map/while/body/eval_jaxpr/ppermute | solution.py:14
  145.4 9.5 %collective-permute-start = (bf16[16,8192]{1,0:T(8,128)(2,1)S(1)}, bf16[16,8192]{1,0:T(8,128)(2,1)S(1)}, u32[]{:S(2)}, u32[]{:S(2)}) collective-permute-start(bf16[16,8192]{1,0:T(8,128)(2,1)S(1)} %add_convert_fusion.2), channel_id=1, source_target_pairs={{32,0},{64,32},{96,64},{128,96},{160,128},{192,160},{224,192},{256... | collective-permute-start | bytes 786440 | tf_op jit(solution)/shard_map/while/body/eval_jaxpr/ppermute | solution.py:14
  158.9 9.5 %collective-permute-start = (bf16[16,8192]{1,0:T(8,128)(2,1)S(1)}, bf16[16,8192]{1,0:T(8,128)(2,1)S(1)}, u32[]{:S(2)}, u32[]{:S(2)}) collective-permute-start(bf16[16,8192]{1,0:T(8,128)(2,1)S(1)} %add_convert_fusion.2), channel_id=1, source_target_pairs={{32,0},{64,32},{96,64},{128,96},{160,128},{192,160},{224,192},{256... | collective-permute-start | bytes 786440 | tf_op jit(solution)/shard_map/while/body/eval_jaxpr/ppermute | solution.py:14
  172.4 9.5 %collective-permute-start = (bf16[16,8192]{1,0:T(8,128)(2,1)S(1)}, bf16[16,8192]{1,0:T(8,128)(2,1)S(1)}, u32[]{:S(2)}, u32[]{:S(2)}) collective-permute-start(bf16[16,8192]{1,0:T(8,128)(2,1)S(1)} %add_convert_fusion.2), channel_id=1, source_target_pairs={{32,0},{64,32},{96,64},{128,96},{160,128},{192,160},{224,192},{256... | collective-permute-start | bytes 786440 | tf_op jit(solution)/shard_map/while/body/eval_jaxpr/ppermute | solution.py:14
  185.9 9.5 %collective-permute-start = (bf16[16,8192]{1,0:T(8,128)(2,1)S(1)}, bf16[16,8192]{1,0:T(8,128)(2,1)S(1)}, u32[]{:S(2)}, u32[]{:S(2)}) collective-permute-start(bf16[16,8192]{1,0:T(8,128)(2,1)S(1)} %add_convert_fusion.2), channel_id=1, source_target_pairs={{32,0},{64,32},{96,64},{128,96},{160,128},{192,160},{224,192},{256... | collective-permute-start | bytes 786440 | tf_op jit(solution)/shard_map/while/body/eval_jaxpr/ppermute | solution.py:14
  199.4 10.6 %collective-permute-start = (bf16[16,8192]{1,0:T(8,128)(2,1)S(1)}, bf16[16,8192]{1,0:T(8,128)(2,1)S(1)}, u32[]{:S(2)}, u32[]{:S(2)}) collective-permute-start(bf16[16,8192]{1,0:T(8,128)(2,1)S(1)} %add_convert_fusion.2), channel_id=1, source_target_pairs={{32,0},{64,32},{96,64},{128,96},{160,128},{192,160},{224,192},{256... | collective-permute-start | bytes 786440 | tf_op jit(solution)/shard_map/while/body/eval_jaxpr/ppermute | solution.py:14
  214.0 12.2 %collective-permute-start = (bf16[16,8192]{1,0:T(8,128)(2,1)S(1)}, bf16[16,8192]{1,0:T(8,128)(2,1)S(1)}, u32[]{:S(2)}, u32[]{:S(2)}) collective-permute-start(bf16[16,8192]{1,0:T(8,128)(2,1)S(1)} %add_convert_fusion.2), channel_id=1, source_target_pairs={{32,0},{64,32},{96,64},{128,96},{160,128},{192,160},{224,192},{256... | collective-permute-start | bytes 786440 | tf_op jit(solution)/shard_map/while/body/eval_jaxpr/ppermute | solution.py:14
  230.2 12.7 %collective-permute-start = (bf16[16,8192]{1,0:T(8,128)(2,1)S(1)}, bf16[16,8192]{1,0:T(8,128)(2,1)S(1)}, u32[]{:S(2)}, u32[]{:S(2)}) collective-permute-start(bf16[16,8192]{1,0:T(8,128)(2,1)S(1)} %add_convert_fusion.2), channel_id=1, source_target_pairs={{32,0},{64,32},{96,64},{128,96},{160,128},{192,160},{224,192},{256... | collective-permute-start | bytes 786440 | tf_op jit(solution)/shard_map/while/body/eval_jaxpr/ppermute | solution.py:14
  246.9 11.6 %collective-permute-start = (bf16[16,8192]{1,0:T(8,128)(2,1)S(1)}, bf16[16,8192]{1,0:T(8,128)(2,1)S(1)}, u32[]{:S(2)}, u32[]{:S(2)}) collective-permute-start(bf16[16,8192]{1,0:T(8,128)(2,1)S(1)} %add_convert_fusion.2), channel_id=1, source_target_pairs={{32,0},{64,32},{96,64},{128,96},{160,128},{192,160},{224,192},{256... | collective-permute-start | bytes 786440 | tf_op jit(solution)/shard_map/while/body/eval_jaxpr/ppermute | solution.py:14
  262.6 10.0 %collective-permute-start = (bf16[16,8192]{1,0:T(8,128)(2,1)S(1)}, bf16[16,8192]{1,0:T(8,128)(2,1)S(1)}, u32[]{:S(2)}, u32[]{:S(2)}) collective-permute-start(bf16[16,8192]{1,0:T(8,128)(2,1)S(1)} %add_convert_fusion.2), channel_id=1, source_target_pairs={{32,0},{64,32},{96,64},{128,96},{160,128},{192,160},{224,192},{256... | collective-permute-start | bytes 786440 | tf_op jit(solution)/shard_map/while/body/eval_jaxpr/ppermute | solution.py:14
  276.6 8.7 %collective-permute-start = (bf16[16,8192]{1,0:T(8,128)(2,1)S(1)}, bf16[16,8192]{1,0:T(8,128)(2,1)S(1)}, u32[]{:S(2)}, u32[]{:S(2)}) collective-permute-start(bf16[16,8192]{1,0:T(8,128)(2,1)S(1)} %add_convert_fusion.2), channel_id=1, source_target_pairs={{32,0},{64,32},{96,64},{128,96},{160,128},{192,160},{224,192},{256... | collective-permute-start | bytes 786440 | tf_op jit(solution)/shard_map/while/body/eval_jaxpr/ppermute | solution.py:14
  289.3 8.9 %collective-permute-start = (bf16[16,8192]{1,0:T(8,128)(2,1)S(1)}, bf16[16,8192]{1,0:T(8,128)(2,1)S(1)}, u32[]{:S(2)}, u32[]{:S(2)}) collective-permute-start(bf16[16,8192]{1,0:T(8,128)(2,1)S(1)} %add_convert_fusion.2), channel_id=1, source_target_pairs={{32,0},{64,32},{96,64},{128,96},{160,128},{192,160},{224,192},{256... | collective-permute-start | bytes 786440 | tf_op jit(solution)/shard_map/while/body/eval_jaxpr/ppermute | solution.py:14
  302.3 9.2 %collective-permute-start = (bf16[16,8192]{1,0:T(8,128)(2,1)S(1)}, bf16[16,8192]{1,0:T(8,128)(2,1)S(1)}, u32[]{:S(2)}, u32[]{:S(2)}) collective-permute-start(bf16[16,8192]{1,0:T(8,128)(2,1)S(1)} %add_convert_fusion.2), channel_id=1, source_target_pairs={{32,0},{64,32},{96,64},{128,96},{160,128},{192,160},{224,192},{256... | collective-permute-start | bytes 786440 | tf_op jit(solution)/shard_map/while/body/eval_jaxpr/ppermute | solution.py:14
  315.5 9.5 %collective-permute-start = (bf16[16,8192]{1,0:T(8,128)(2,1)S(1)}, bf16[16,8192]{1,0:T(8,128)(2,1)S(1)}, u32[]{:S(2)}, u32[]{:S(2)}) collective-permute-start(bf16[16,8192]{1,0:T(8,128)(2,1)S(1)} %add_convert_fusion.2), channel_id=1, source_target_pairs={{32,0},{64,32},{96,64},{128,96},{160,128},{192,160},{224,192},{256... | collective-permute-start | bytes 786440 | tf_op jit(solution)/shard_map/while/body/eval_jaxpr/ppermute | solution.py:14
  329.0 9.5 %collective-permute-start = (bf16[16,8192]{1,0:T(8,128)(2,1)S(1)}, bf16[16,8192]{1,0:T(8,128)(2,1)S(1)}, u32[]{:S(2)}, u32[]{:S(2)}) collective-permute-start(bf16[16,8192]{1,0:T(8,128)(2,1)S(1)} %add_convert_fusion.2), channel_id=1, source_target_pairs={{32,0},{64,32},{96,64},{128,96},{160,128},{192,160},{224,192},{256... | collective-permute-start | bytes 786440 | tf_op jit(solution)/shard_map/while/body/eval_jaxpr/ppermute | solution.py:14
  342.5 9.5 %collective-permute-start = (bf16[16,8192]{1,0:T(8,128)(2,1)S(1)}, bf16[16,8192]{1,0:T(8,128)(2,1)S(1)}, u32[]{:S(2)}, u32[]{:S(2)}) collective-permute-start(bf16[16,8192]{1,0:T(8,128)(2,1)S(1)} %add_convert_fusion.2), channel_id=1, source_target_pairs={{32,0},{64,32},{96,64},{128,96},{160,128},{192,160},{224,192},{256... | collective-permute-start | bytes 786440 | tf_op jit(solution)/shard_map/while/body/eval_jaxpr/ppermute | solution.py:14
  356.0 9.5 %collective-permute-start = (bf16[16,8192]{1,0:T(8,128)(2,1)S(1)}, bf16[16,8192]{1,0:T(8,128)(2,1)S(1)}, u32[]{:S(2)}, u32[]{:S(2)}) collective-permute-start(bf16[16,8192]{1,0:T(8,128)(2,1)S(1)} %add_convert_fusion.2), channel_id=1, source_target_pairs={{32,0},{64,32},{96,64},{128,96},{160,128},{192,160},{224,192},{256... | collective-permute-start | bytes 786440 | tf_op jit(solution)/shard_map/while/body/eval_jaxpr/ppermute | solution.py:14
  369.5 9.5 %collective-permute-start = (bf16[16,8192]{1,0:T(8,128)(2,1)S(1)}, bf16[16,8192]{1,0:T(8,128)(2,1)S(1)}, u32[]{:S(2)}, u32[]{:S(2)}) collective-permute-start(bf16[16,8192]{1,0:T(8,128)(2,1)S(1)} %add_convert_fusion.2), channel_id=1, source_target_pairs={{32,0},{64,32},{96,64},{128,96},{160,128},{192,160},{224,192},{256... | collective-permute-start | bytes 786440 | tf_op jit(solution)/shard_map/while/body/eval_jaxpr/ppermute | solution.py:14
  459.3 4.3 collective-permute-start.1
  464.9 6.6 %collective-permute-start.2 = (f32[]{:T(128)}, f32[]{:T(128)}, u32[]{:S(2)}, u32[]{:S(2)}) collective-permute-start(f32[]{:T(128)} %add.131), channel_id=1, source_target_pairs={{0,8},{4,12},{8,16},{12,20},{16,24},{20,28},{24,0},{28,4},{1,9},{5... | collective-permute-start | bytes 20 | tf_op jit(solution)/shard_map/ppermute | solution.py:96
  472.1 6.9 %collective-permute-start.3 = (f32[]{:T(128)}, f32[]{:T(128)}, u32[]{:S(2)}, u32[]{:S(2)}) collective-permute-start(f32[]{:T(128)} %add.132), channel_id=1, source_target_pairs={{0,16},{4,20},{8,24},{12,28},{16,0},{20,4},{24,8},{28,12},{1,17},{... | collective-permute-start | bytes 20 | tf_op jit(solution)/shard_map/ppermute | solution.py:96
  480.7 8.7 %collective-permute-start.4 = (f32[65,256]{1,0:T(8,128)S(1)}, f32[65,256]{1,0:T(8,128)S(1)}, u32[]{:S(2)}, u32[]{:S(2)}) collective-permute-start(f32[65,256]{1,0:T(8,128)S(1)} %get-tuple-element.416), channel_id=1, source_target_pairs={{0,1},{1,2},{2,3},{3,0},{4,5},{5,6},{6,7},{7,4},{8,9},{9,10},{10,1... | collective-permute-start | bytes 199688 | tf_op jit(solution)/shard_map/ppermute | solution.py:108
  483.2 7.8 %collective-permute-start.5 = (f32[65,256]{1,0:T(8,128)S(1)}, f32[65,256]{1,0:T(8,128)S(1)}, u32[]{:S(2)}, u32[]{:S(2)}) collective-permute-start(f32[65,256]{1,0:T(8,128)S(1)} %get-tuple-element.418), channel_id=1, source_target_pairs={{0,2},{1,3},{2,0},{3,1},{4,6},{5,7},{6,4},{7,5},{8,10},{9,11},{10,... | collective-permute-start | bytes 199688 | tf_op jit(solution)/shard_map/ppermute | solution.py:108
  487.5 7.5 %collective-permute-start.6 = (f32[65,256]{1,0:T(8,128)S(1)}, f32[65,256]{1,0:T(8,128)S(1)}, u32[]{:S(2)}, u32[]{:S(2)}) collective-permute-start(f32[65,256]{1,0:T(8,128)S(1)} %get-tuple-element.417), channel_id=1, source_target_pairs={{0,3},{1,0},{2,1},{3,2},{4,7},{5,4},{6,5},{7,6},{8,11},{9,8},{10,9... | collective-permute-start | bytes 199688 | tf_op jit(solution)/shard_map/ppermute | solution.py:108
Sparse Core Ops, SparseCore 0:
  23.6 32.7 all-gather.1
  380.8 44.9 reduce-scatter.1

commit v4 on v3

v4 whole, which is shorter than its diff:
```python
import math

import jax
import jax.numpy as jnp
from jax import lax
from jax.sharding import PartitionSpec as P

rows_per_block = 16


def shifted(value, axis, steps):
    count = lax.axis_size(axis)
    initial, last = (max(0, -steps), min(count, count - steps))
    return lax.ppermute(value, axis, [(source, source + steps) for source in range(initial, last)])


def partner_swap(value, axis):
    count = lax.axis_size(axis)
    return lax.ppermute(value, axis, [(source, source ^ 1) for source in range(count)])


def on_device(acts, top_grad, a_rows, b_rows, gain):
    sections = lax.axis_size("pipe")
    section = lax.axis_index("pipe")
    pairs = sections // 2
    pair = section // 2
    upper_half = section % 2 == 1
    rank = a_rows.shape[1]
    own_hidden = acts[0, 0]
    rows, width = own_hidden.shape
    half_rows = rows // 2
    my_offset = jnp.where(upper_half, 0, half_rows)
    other_offset = half_rows - my_offset
    own_mine = lax.dynamic_slice_in_dim(own_hidden, my_offset, half_rows, 0)
    partner_rows = partner_swap(lax.dynamic_slice_in_dim(own_hidden, other_offset, half_rows, 0), "pipe")
    hidden_pair = (
        jnp.where(upper_half, own_mine, partner_rows),
        jnp.where(upper_half, partner_rows, own_mine),
    )
    top = lax.dynamic_slice_in_dim(top_grad[0], my_offset, half_rows, 0)
    params = jnp.concatenate([a_rows[0], b_rows[0], gain], axis=0)
    partner_params = partner_swap(params, "pipe")
    stacked = jnp.stack(
        [jnp.where(upper_half, params, partner_params), jnp.where(upper_half, partner_params, params)]
    )
    whole = lax.all_gather(lax.all_gather(stacked, "dp", axis=2, tiled=True), "seq", axis=2, tiled=True)
    contract_last = (((1,), (1,)), ((), ()))
    contract_first = (((0,), (0,)), ((), ()))
    layers = []
    for index in range(2):
        hidden = hidden_pair[index]
        a_full = whole[index, :rank]
        b_full = whole[index, rank : 2 * rank]
        gain_float = whole[index, 2 * rank].astype(jnp.float32)
        hidden_float = hidden.astype(jnp.float32)
        inverse_root_mean = jnp.sqrt(
            jnp.mean(hidden_float * hidden_float, axis=-1, keepdims=True) + 1e-05
        )
        normalized_rows = ((hidden_float / inverse_root_mean) * gain_float).astype(jnp.bfloat16)
        low = jnp.dot(normalized_rows, a_full.T, preferred_element_type=jnp.float32).astype(
            jnp.bfloat16
        )
        layers.append((hidden, inverse_root_mean, low, a_full, b_full, gain_float))
    block_total = half_rows // rows_per_block

    def layer_block(layer, source, block_offset, sums, inside):
        hidden, inverse_root_mean, low, a_full, b_full, gain_float = layer
        sum_a, sum_b, sum_g = sums
        hidden_part = lax.dynamic_slice_in_dim(hidden, block_offset, rows_per_block, 0)
        r_part = lax.dynamic_slice_in_dim(inverse_root_mean, block_offset, rows_per_block, 0)
        input_portion = hidden_part.astype(jnp.float32) / r_part
        d_low = lax.dot_general(
            source, b_full, contract_last, preferred_element_type=jnp.float32
        ).astype(jnp.bfloat16)
        normalized_gradient = jnp.dot(d_low, a_full, preferred_element_type=jnp.float32)
        input_gradient = normalized_gradient * gain_float
        hidden_gradient = (
            source.astype(jnp.float32)
            + (
                input_gradient
                - input_portion * jnp.mean(input_gradient * input_portion, axis=-1, keepdims=True)
            )
            / r_part
        ).astype(jnp.bfloat16)
        normalized_part = (input_portion * gain_float).astype(jnp.bfloat16)
        low_part = lax.dynamic_slice_in_dim(low, block_offset, rows_per_block, 0)
        part_a = lax.dot_general(
            d_low, normalized_part, contract_first, preferred_element_type=jnp.float32
        )
        part_b = lax.dot_general(low_part, source, contract_first, preferred_element_type=jnp.float32)
        part_g = jnp.sum(normalized_gradient * input_portion, axis=0)[None, :]
        sums = (
            sum_a + jnp.where(inside, part_a, 0.0),
            sum_b + jnp.where(inside, part_b, 0.0),
            sum_g + jnp.where(inside, part_g, 0.0),
        )
        return hidden_gradient, sums

    def turn(turn_index, carry):
        incoming, upper_sums, lower_sums = carry
        block_index = turn_index - (pairs - 1 - pair)
        inside = jnp.logical_and(block_index >= 0, block_index < block_total)
        block_offset = jnp.clip(block_index, 0, block_total - 1) * rows_per_block
        top_block = lax.dynamic_slice_in_dim(top, block_offset, rows_per_block, 0)
        source = jnp.where(pair == pairs - 1, top_block, incoming)
        middle, upper_sums = layer_block(layers[0], source, block_offset, upper_sums, inside)
        result, lower_sums = layer_block(layers[1], middle, block_offset, lower_sums, inside)
        incoming = shifted(result, "pipe", -2)
        return (incoming, upper_sums, lower_sums)

    def zero_sums():
        return (
            jnp.zeros((rank, width), jnp.float32),
            jnp.zeros((rank, width), jnp.float32),
            jnp.zeros((1, width), jnp.float32),
        )

    begin = (jnp.zeros((rows_per_block, width), jnp.bfloat16), zero_sums(), zero_sums())
    _, upper_sums, lower_sums = lax.fori_loop(0, pairs + block_total - 1, turn, begin)
    grads = jnp.stack(
        [jnp.concatenate(upper_sums, axis=0), jnp.concatenate(lower_sums, axis=0)]
    )
    reduced = lax.psum_scatter(grads, "seq", scatter_dimension=2, tiled=True)
    own_layer = jnp.where(upper_half, reduced[0], reduced[1])
    other_layer = jnp.where(upper_half, reduced[1], reduced[0])
    part = own_layer + partner_swap(other_layer, "pipe")
    examples = lax.axis_size("dp")
    example = lax.axis_index("dp")
    square = jnp.sum(part * part)
    total = lax.psum(square, "pipe")
    count = lax.axis_size("seq")
    step = 1
    while step < count:
        total = total + lax.ppermute(
            total, "seq", [(source, (source + step) % count) for source in range(count)]
        )
        step *= 2
    bound = math.sqrt(sections * (2 * rank + 1) * width)
    factor = bound / (jnp.sqrt(total) + 0.01 * bound)
    scaled = factor * part
    share = part.shape[1] // examples
    combined = lax.dynamic_slice_in_dim(scaled, example * share, share, 1)
    for step in range(1, examples):
        target = lax.rem(example + step, examples)
        piece = lax.dynamic_slice_in_dim(scaled, target * share, share, 1)
        combined = combined + lax.ppermute(
            piece, "dp", [(source, (source + step) % examples) for source in range(examples)]
        )
    out_a = combined[:rank]
    out_b = combined[rank : 2 * rank]
    out_g = combined[2 * rank :]
    factor = jnp.reshape(factor, (1,))
    return (out_a[None], out_b[None], out_g, factor)


def solution(mesh):
    in_specs = (
        P("pipe", "dp", "seq", None),
        P("dp", "seq", None),
        P("pipe", None, ("seq", "dp")),
        P("pipe", None, ("seq", "dp")),
        P("pipe", ("seq", "dp")),
    )
    out_specs = (
        P("pipe", None, ("seq", "dp")),
        P("pipe", None, ("seq", "dp")),
        P("pipe", ("seq", "dp")),
        P("dp"),
    )
    return jax.shard_map(
        on_device, mesh=mesh, in_specs=in_specs, out_specs=out_specs, check_vma=False
    )
```

time: 508 us -> 478 us (0.941)
  waiting for transfers between devices: 245 us -> 171 us
  matrix products: 82.7 us -> 120 us
  local copies, waits for them, and re-layouts: 5.16 us -> 17.9 us
  starting transfers between devices: 44.9 us -> 38.3 us
    ppermute x23 -> x14, waiting for transfers between devices: 152 us -> 71.2 us  [the longest x11 46.7 us: shifted(): lax.ppermute(value, axis, [(source, source + steps) for source in range(i...]
    dot_general x92 -> x88, matrix products: 80.8 us -> 117 us  [the longest x22 49.5 us: layer_block(): lax.dot_general(d_low, normalized_part, contract_first, preferred_element...]
    reduce_scatter x1, waiting for transfers between devices: 45.1 us -> 72.5 us  [on_device(): reduced = lax.psum_scatter(grads, 'seq', scatter_dimension=2, tiled=True)]
    all_gather x1, waiting for transfers between devices: 30.7 us -> 9.64 us  [on_device(): lax.all_gather(lax.all_gather(stacked, 'dp', axis=2, tiled=True), 'seq',...]
    select_n x46 -> x34, other arithmetic: 23.4 us -> 13.2 us  [the longest x11 12 us: turn(): source = jnp.where(pair == pairs - 1, top_block, incoming)]
    div x23 -> x22, local copies, waits for them, and re-layouts: 1.65 us -> 8.62 us  [layer_block(): input_portion = hidden_part.astype(jnp.float32) / r_part]
    ppermute x23 -> x14, starting transfers between devices: 29.7 us -> 23.2 us  [the longest x11 14.1 us: shifted(): lax.ppermute(value, axis, [(source, source + steps) for source in range(i...]
    another operation x0 -> x5, other arithmetic: none -> 5.39 us  [the longest x3 4.62 us: on_device(): jnp.stack([jnp.concatenate(upper_sums, axis=0), jnp.concatenate(lower_sum...]
  transfers between devices with their start and end apart: 31 -> 22, of which waited for: 30 -> 21; matrix products, arithmetic and copies ran while one was open for 9% -> 17% of each run, Pallas kernels for 0% -> 0%
where the time goes in v4:
time: 478 us; the launch traced here: 474 us
  waiting for transfers between devices  171 us (36%)
  matrix products  120 us (25%)
  other arithmetic  59.1 us (12%)
  blocking collectives  47.6 us (10%)
  starting transfers between devices  38.3 us (8%)
  local copies, waits for them, and re-layouts  17.9 us (4%)
  between operations  17.9 us (4%)
    reduce_scatter x1, waiting for transfers between devices, on_device(): reduced = lax.psum_scatter(grads, 'seq', scatter_dimension=2, tiled=True)  72.5 us
    dot_general x22, matrix products, layer_block(): lax.dot_general(d_low, normalized_part, contract_first, preferred_element...  49.5 us
    ppermute x11, waiting for transfers between devices, shifted(): lax.ppermute(value, axis, [(source, source + steps) for source in range(i...  46.7 us
    dot_general x22, matrix products, layer_block(): jnp.dot(d_low, a_full, preferred_element_type=jnp.float32)  36.5 us
    psum x1, blocking collectives, on_device(): total = lax.psum(square, 'pipe')  31.9 us
    convert_element_type x22, other arithmetic, layer_block(): hidden_gradient = (source.astype(jnp.float32) + (input_gradient - input_p...  31.4 us
    dot_general x22, matrix products, layer_block(): lax.dot_general(low_part, source, contract_first, preferred_element_type=...  25.3 us
    ppermute x3, waiting for transfers between devices, partner_swap(): lax.ppermute(value, axis, [(source, source ^ 1) for source in range(count)])  24.6 us
  transfers between devices with their start and end apart: 22, of which 21 were waited for; matrix products, arithmetic and copies ran while one was open for 17% of the time, Pallas kernels for 0%

profile of v4, /device:TPU:6, one launch (start us, length us, event | category | flops | bytes accessed | tf_op | source)
XLA Modules:
  0.0 474.0 jit_solution(12551226534759277676)
XLA Ops:
  8.1 3.8 collective-permute-start.1
  12.0 2.0 collective-permute-done.1
  14.8 15.7 %all_gather.6 = bf16[2,65,1024]{2,1,0:T(8,128)(2,1)} all-gather(bf16[2,65,256]{2,1,0:T(8,128)(2,1)S(1)} %pad_maximum_fusion.1), channel_id=1, replica_groups=mesh['pipe'=16,'seq'=8,'dp'=4] {'dp'}, dimensions={2}, use_global_device_ids=true | all-gather | bytes 332800 | tf_op jit(solution)/shard_map/all_gather | solution.py:46
  31.8 1.9 collective-permute-start.2
  34.9 17.3 %collective-permute-done.2 = bf16[64,8192]{1,0:T(8,128)(2,1)} collective-permute-done((bf16[64,8192]{1,0:T(8,128)(2,1)S(1)}, bf16[64,8192]{1,0:T(8,128)(2,1)}, u32[]{:S(2)}, u32[]{:S(2)}) %collective-permute-start.2) | collective-permute-done | bytes 1048608 | tf_op jit(solution)/shard_map/ppermute | solution.py:19
  52.2 3.0 fusion.17
  55.8 9.6 %all-gather.2.cloned.1.call-done = bf16[2,65,8192]{2,1,0:T(8,128)(2,1)} async-done(((bf16[2,65,1024]{2,1,0:T(8,128)(2,1)}), bf16[2,65,8192]{2,1,0:T(8,128)(2,1)}) %all-gather.2.cloned.1.call-update) | async-done | bytes 2129936 | tf_op jit(solution)/shard_map/all_gather | solution.py:46
  69.3 1.9 convolution_convert_fusion.3
  71.9 2.7 slice_bitcast_fusion
  75.3 233.8 %while.28 = (s32[]{:T(128)}, bf16[16,8192]{1,0:T(8,128)(2,1)}, f32[32,8192]{1,0:T(8,128)}, f32[32,8192]{1,0:T(8,128)}, f32[1,8192]{1,0:T(1,128)S(1)}, /*index=5*...) while((s32[]{:T(128)}, bf16[16,8192]{1,0:T(8,128)(2,1)}, ...), condition=%wide.region_7.8_spmd.clone, body=%wide.region_2.7_spmd.clone.sunk | while | flops 75662344 | bytes 54476668 | solution.py:119
  77.4 2.1 multiply_reduce_fusion.7
  82.2 1.7 add_convert_fusion.5
  85.3 2.6 fusion.76
  91.9 9.1 %collective-permute-done = bf16[16,8192]{1,0:T(8,128)(2,1)} collective-permute-done((bf16[16,8192]{1,0:T(8,128)(2,1)}, bf16[16,8192]{1,0:T(8,128)(2,1)}, u32[]{:S(2)}, u32[]{:S(2)}) %collective-permute-start) | collective-permute-done | bytes 262176 | tf_op jit(solution)/shard_map/while/body/eval_jaxpr/ppermute | solution.py:14
  103.2 2.2 multiply_reduce_fusion.7
  111.1 2.9 fusion.76
  118.1 6.7 %collective-permute-done = bf16[16,8192]{1,0:T(8,128)(2,1)} collective-permute-done((bf16[16,8192]{1,0:T(8,128)(2,1)}, bf16[16,8192]{1,0:T(8,128)(2,1)}, u32[]{:S(2)}, u32[]{:S(2)}) %collective-permute-start) | collective-permute-done | bytes 262176 | tf_op jit(solution)/shard_map/while/body/eval_jaxpr/ppermute | solution.py:14
  126.9 2.2 multiply_reduce_fusion.7
  131.7 1.7 add_convert_fusion.5
  134.8 2.9 fusion.76
  141.8 4.1 collective-permute-done
  148.1 2.2 multiply_reduce_fusion.7
  152.9 1.7 add_convert_fusion.5
  155.9 2.9 fusion.76
  163.0 3.3 collective-permute-done
  168.4 2.2 multiply_reduce_fusion.7
  176.3 2.9 fusion.76
  183.3 2.4 collective-permute-done
  187.9 2.2 multiply_reduce_fusion.7
  192.7 1.7 add_convert_fusion.5
  195.7 2.9 fusion.76
  202.8 5.1 %collective-permute-done = bf16[16,8192]{1,0:T(8,128)(2,1)} collective-permute-done((bf16[16,8192]{1,0:T(8,128)(2,1)}, bf16[16,8192]{1,0:T(8,128)(2,1)}, u32[]{:S(2)}, u32[]{:S(2)}) %collective-permute-start) | collective-permute-done | bytes 262176 | tf_op jit(solution)/shard_map/while/body/eval_jaxpr/ppermute | solution.py:14
  210.0 2.2 multiply_reduce_fusion.7
  214.8 1.7 add_convert_fusion.5
  217.8 2.9 fusion.76
  224.9 3.1 collective-permute-done
  230.1 2.2 multiply_reduce_fusion.7
  238.0 2.9 fusion.76
  245.1 6.1 %collective-permute-done = bf16[16,8192]{1,0:T(8,128)(2,1)} collective-permute-done((bf16[16,8192]{1,0:T(8,128)(2,1)}, bf16[16,8192]{1,0:T(8,128)(2,1)}, u32[]{:S(2)}, u32[]{:S(2)}) %collective-permute-start) | collective-permute-done | bytes 262176 | tf_op jit(solution)/shard_map/while/body/eval_jaxpr/ppermute | solution.py:14
  253.2 2.2 multiply_reduce_fusion.7
  261.1 2.9 fusion.76
  268.2 2.3 collective-permute-done
  272.5 2.2 multiply_reduce_fusion.7
  280.4 2.9 fusion.76
  287.5 2.3 collective-permute-done
  291.9 2.2 multiply_reduce_fusion.7
  299.8 2.9 fusion.76
  306.8 2.3 collective-permute-done
  309.1 1.9 maximum_bitcast_fusion
  311.5 2.6 pad_maximum_fusion
  314.1 72.5 %reduce-scatter.2.cloned.1.call-done = f32[2,65,1024]{2,1,0:T(8,128)} async-done(((f32[2,65,8192]{2,1,0:T(8,128)}), f32[2,65,1024]{2,1,0:T(8,128)}) %reduce-scatter.2.cloned.1.call-update) | async-done | bytes 532496 | tf_op jit(solution)/shard_map/reduce_scatter | solution.py:123
  387.7 3.4 collective-permute-start.3
  391.1 5.2 %collective-permute-done.3 = f32[65,1024]{1,0:T(8,128)S(1)} collective-permute-done((f32[65,1024]{1,0:T(8,128)S(1)}, f32[65,1024]{1,0:T(8,128)S(1)}, u32[]{:S(2)}, u32[]{:S(2)}) %collective-permute-start.3) | collective-permute-done | bytes 266272 | tf_op jit(solution)/shard_map/ppermute | solution.py:19
  396.3 1.7 multiply_reduce_fusion.4
  398.0 31.9 %psum.7 = f32[]{:T(128)} all-reduce(f32[]{:T(128)} %get-tuple-element.650), channel_id=1, replica_groups=mesh['pipe'=16,'seq'=8,'dp'=4] {'pipe'}, use_global_device_ids=true, to_apply=%region_10.11 | all-reduce | flops 1 | bytes 8 | tf_op jit(solution)/shard_map/psum | solution.py:130
  429.9 4.4 collective-permute-done.4
  435.6 3.2 collective-permute-start.5
  438.8 3.6 collective-permute-done.5
  442.9 3.2 collective-permute-start.6
  446.1 3.9 collective-permute-done.6
  450.7 2.4 collective-permute-start.7
  453.1 4.3 collective-permute-start.8
  457.4 1.9 collective-permute-start.9
  460.9 4.0 collective-permute-done.9
  (465 shorter events, 135.4 us)
Async XLA Ops:
  7.2 26.6 %copy-start = (bf16[1,128,8192]{2,1,0:T(8,128)(2,1)S(1)}, bf16[1,128,8192]{2,1,0:T(8,128)(2,1)}, u32[]{:S(2)}) copy-start(bf16[1,128,8192]{2,1,0:T(8,128)(2,1)} %param.8) | copy-start | bytes 6291460
  7.2 58.3 %all-gather.2.cloned.1.call-start = ((), (), s32[]{:S(2)}) async-start(), calls=%async_computation.1 | async-start | bytes 2654208 | tf_op jit(solution)/shard_map/all_gather | solution.py:46
  8.1 5.8 %collective-permute-start.1 = (bf16[65,256]{1,0:T(8,128)(2,1)S(1)}, bf16[65,256]{1,0:T(8,128)(2,1)S(1)}, u32[]{:S(2)}, u32[]{:S(2)}) collective-permute-start(bf16[65,256]{1,0:T(8,128)(2,1)S(1)} %pad_maximum_fusion.2), channel_id=1, source_target_pairs={{0,32},{32,0},{64,96},{96,64},{128,160},{160,128},{192,224},{224,1... | collective-permute-start | bytes 99848 | tf_op jit(solution)/shard_map/ppermute | solution.py:19
  30.4 356.1 %reduce-scatter.2.cloned.1.call-start = ((), (), s32[]{:S(2)}) async-start(), calls=%async_computation.2 | async-start | bytes 5308416 | tf_op jit(solution)/shard_map/reduce_scatter | solution.py:123
  31.8 20.4 %collective-permute-start.2 = (bf16[64,8192]{1,0:T(8,128)(2,1)S(1)}, bf16[64,8192]{1,0:T(8,128)(2,1)}, u32[]{:S(2)}, u32[]{:S(2)}) collective-permute-start(bf16[64,8192]{1,0:T(8,128)(2,1)S(1)} %dynamic-slice_bitcast_fusion), channel_id=1, source_target_pairs={{0,32},{32,0},{64,96},{96,64},{128,160},{160,128},{192,224},{224,1... | collective-permute-start | bytes 3145736 | tf_op jit(solution)/shard_map/ppermute | solution.py:19
  33.8 18.4 %copy-start.10 = (bf16[1,1,128,8192]{3,2,1,0:T(8,128)(2,1)S(1)}, bf16[1,1,128,8192]{3,2,1,0:T(8,128)(2,1)}, u32[]{:S(2)}) copy-start(bf16[1,1,128,8192]{3,2,1,0:T(8,128)(2,1)} %param.7) | copy-start | bytes 6291460
  55.2 13.4 %copy-start.8 = (bf16[64,8192]{1,0:T(8,128)(2,1)}, bf16[64,8192]{1,0:T(8,128)(2,1)S(1)}, u32[]{:S(2)}) copy-start(bf16[64,8192]{1,0:T(8,128)(2,1)S(1)} %get-tuple-element.855) | copy-start | bytes 3145732
  80.8 4.4 copy-start.14
  83.9 17.2 %collective-permute-start = (bf16[16,8192]{1,0:T(8,128)(2,1)}, bf16[16,8192]{1,0:T(8,128)(2,1)}, u32[]{:S(2)}, u32[]{:S(2)}) collective-permute-start(bf16[16,8192]{1,0:T(8,128)(2,1)} %add_convert_fusion.5), channel_id=1, source_target_pairs={{64,0},{96,32},{128,64},{160,96},{192,128},{224,160},{256,192},{28... | collective-permute-start | bytes 786440 | tf_op jit(solution)/shard_map/while/body/eval_jaxpr/ppermute | solution.py:14
  89.0 12.1 %copy-start.7 = (bf16[32,8192]{1,0:T(8,128)(2,1)S(1)}, bf16[32,8192]{1,0:T(8,128)(2,1)}, u32[]{:S(2)}) copy-start(bf16[32,8192]{1,0:T(8,128)(2,1)} %copy-done.6) | copy-start | bytes 1572868 | tf_op jit(solution)/shard_map/while
  90.2 10.9 %copy-start.2 = (f32[32,8192]{1,0:T(8,128)}, f32[32,8192]{1,0:T(8,128)S(1)}, u32[]{:S(2)}) copy-start(f32[32,8192]{1,0:T(8,128)S(1)} %fusion.74) | copy-start | bytes 3145732 | tf_op jit(solution)/shard_map/while
  91.9 9.1 %copy-start.12 = (f32[32,8192]{1,0:T(8,128)}, f32[32,8192]{1,0:T(8,128)S(1)}, u32[]{:S(2)}) copy-start(f32[32,8192]{1,0:T(8,128)S(1)} %fusion.73) | copy-start | bytes 3145732 | tf_op jit(solution)/shard_map/while
  106.6 4.4 copy-start.14
  109.7 15.1 %collective-permute-start = (bf16[16,8192]{1,0:T(8,128)(2,1)}, bf16[16,8192]{1,0:T(8,128)(2,1)}, u32[]{:S(2)}, u32[]{:S(2)}) collective-permute-start(bf16[16,8192]{1,0:T(8,128)(2,1)} %add_convert_fusion.5), channel_id=1, source_target_pairs={{64,0},{96,32},{128,64},{160,96},{192,128},{224,160},{256,192},{28... | collective-permute-start | bytes 786440 | tf_op jit(solution)/shard_map/while/body/eval_jaxpr/ppermute | solution.py:14
  115.1 9.6 %copy-start.7 = (bf16[32,8192]{1,0:T(8,128)(2,1)S(1)}, bf16[32,8192]{1,0:T(8,128)(2,1)}, u32[]{:S(2)}) copy-start(bf16[32,8192]{1,0:T(8,128)(2,1)} %copy-done.6) | copy-start | bytes 1572868 | tf_op jit(solution)/shard_map/while
  116.3 8.4 %copy-start.2 = (f32[32,8192]{1,0:T(8,128)}, f32[32,8192]{1,0:T(8,128)S(1)}, u32[]{:S(2)}) copy-start(f32[32,8192]{1,0:T(8,128)S(1)} %fusion.74) | copy-start | bytes 3145732 | tf_op jit(solution)/shard_map/while
  118.1 6.7 %copy-start.12 = (f32[32,8192]{1,0:T(8,128)}, f32[32,8192]{1,0:T(8,128)S(1)}, u32[]{:S(2)}) copy-start(f32[32,8192]{1,0:T(8,128)S(1)} %fusion.73) | copy-start | bytes 3145732 | tf_op jit(solution)/shard_map/while
  130.3 4.4 copy-start.14
  133.4 12.5 %collective-permute-start = (bf16[16,8192]{1,0:T(8,128)(2,1)}, bf16[16,8192]{1,0:T(8,128)(2,1)}, u32[]{:S(2)}, u32[]{:S(2)}) collective-permute-start(bf16[16,8192]{1,0:T(8,128)(2,1)} %add_convert_fusion.5), channel_id=1, source_target_pairs={{64,0},{96,32},{128,64},{160,96},{192,128},{224,160},{256,192},{28... | collective-permute-start | bytes 786440 | tf_op jit(solution)/shard_map/while/body/eval_jaxpr/ppermute | solution.py:14
  138.8 7.1 %copy-start.7 = (bf16[32,8192]{1,0:T(8,128)(2,1)S(1)}, bf16[32,8192]{1,0:T(8,128)(2,1)}, u32[]{:S(2)}) copy-start(bf16[32,8192]{1,0:T(8,128)(2,1)} %copy-done.6) | copy-start | bytes 1572868 | tf_op jit(solution)/shard_map/while
  140.0 5.9 %copy-start.2 = (f32[32,8192]{1,0:T(8,128)}, f32[32,8192]{1,0:T(8,128)S(1)}, u32[]{:S(2)}) copy-start(f32[32,8192]{1,0:T(8,128)S(1)} %fusion.74) | copy-start | bytes 3145732 | tf_op jit(solution)/shard_map/while
  146.0 4.3 copy-start.6
  151.5 4.4 copy-start.14
  154.6 11.7 %collective-permute-start = (bf16[16,8192]{1,0:T(8,128)(2,1)}, bf16[16,8192]{1,0:T(8,128)(2,1)}, u32[]{:S(2)}, u32[]{:S(2)}) collective-permute-start(bf16[16,8192]{1,0:T(8,128)(2,1)} %add_convert_fusion.5), channel_id=1, source_target_pairs={{64,0},{96,32},{128,64},{160,96},{192,128},{224,160},{256,192},{28... | collective-permute-start | bytes 786440 | tf_op jit(solution)/shard_map/while/body/eval_jaxpr/ppermute | solution.py:14
  160.0 6.3 %copy-start.7 = (bf16[32,8192]{1,0:T(8,128)(2,1)S(1)}, bf16[32,8192]{1,0:T(8,128)(2,1)}, u32[]{:S(2)}) copy-start(bf16[32,8192]{1,0:T(8,128)(2,1)} %copy-done.6) | copy-start | bytes 1572868 | tf_op jit(solution)/shard_map/while
  161.2 5.1 %copy-start.2 = (f32[32,8192]{1,0:T(8,128)}, f32[32,8192]{1,0:T(8,128)S(1)}, u32[]{:S(2)}) copy-start(f32[32,8192]{1,0:T(8,128)S(1)} %fusion.74) | copy-start | bytes 3145732 | tf_op jit(solution)/shard_map/while
  166.3 4.3 copy-start.6
  171.8 4.4 copy-start.14
  174.9 10.8 %collective-permute-start = (bf16[16,8192]{1,0:T(8,128)(2,1)}, bf16[16,8192]{1,0:T(8,128)(2,1)}, u32[]{:S(2)}, u32[]{:S(2)}) collective-permute-start(bf16[16,8192]{1,0:T(8,128)(2,1)} %add_convert_fusion.5), channel_id=1, source_target_pairs={{64,0},{96,32},{128,64},{160,96},{192,128},{224,160},{256,192},{28... | collective-permute-start | bytes 786440 | tf_op jit(solution)/shard_map/while/body/eval_jaxpr/ppermute | solution.py:14
  180.4 5.4 %copy-start.7 = (bf16[32,8192]{1,0:T(8,128)(2,1)S(1)}, bf16[32,8192]{1,0:T(8,128)(2,1)}, u32[]{:S(2)}) copy-start(bf16[32,8192]{1,0:T(8,128)(2,1)} %copy-done.6) | copy-start | bytes 1572868 | tf_op jit(solution)/shard_map/while
  191.3 4.4 copy-start.14
  194.4 13.5 %collective-permute-start = (bf16[16,8192]{1,0:T(8,128)(2,1)}, bf16[16,8192]{1,0:T(8,128)(2,1)}, u32[]{:S(2)}, u32[]{:S(2)}) collective-permute-start(bf16[16,8192]{1,0:T(8,128)(2,1)} %add_convert_fusion.5), channel_id=1, source_target_pairs={{64,0},{96,32},{128,64},{160,96},{192,128},{224,160},{256,192},{28... | collective-permute-start | bytes 786440 | tf_op jit(solution)/shard_map/while/body/eval_jaxpr/ppermute | solution.py:14
  199.8 8.0 %copy-start.7 = (bf16[32,8192]{1,0:T(8,128)(2,1)S(1)}, bf16[32,8192]{1,0:T(8,128)(2,1)}, u32[]{:S(2)}) copy-start(bf16[32,8192]{1,0:T(8,128)(2,1)} %copy-done.6) | copy-start | bytes 1572868 | tf_op jit(solution)/shard_map/while
  201.0 6.8 %copy-start.2 = (f32[32,8192]{1,0:T(8,128)}, f32[32,8192]{1,0:T(8,128)S(1)}, u32[]{:S(2)}) copy-start(f32[32,8192]{1,0:T(8,128)S(1)} %fusion.74) | copy-start | bytes 3145732 | tf_op jit(solution)/shard_map/while
  202.8 5.1 %copy-start.12 = (f32[32,8192]{1,0:T(8,128)}, f32[32,8192]{1,0:T(8,128)S(1)}, u32[]{:S(2)}) copy-start(f32[32,8192]{1,0:T(8,128)S(1)} %fusion.73) | copy-start | bytes 3145732 | tf_op jit(solution)/shard_map/while
  213.4 4.4 copy-start.14
  216.5 11.5 %collective-permute-start = (bf16[16,8192]{1,0:T(8,128)(2,1)}, bf16[16,8192]{1,0:T(8,128)(2,1)}, u32[]{:S(2)}, u32[]{:S(2)}) collective-permute-start(bf16[16,8192]{1,0:T(8,128)(2,1)} %add_convert_fusion.5), channel_id=1, source_target_pairs={{64,0},{96,32},{128,64},{160,96},{192,128},{224,160},{256,192},{28... | collective-permute-start | bytes 786440 | tf_op jit(solution)/shard_map/while/body/eval_jaxpr/ppermute | solution.py:14
  221.9 6.1 %copy-start.7 = (bf16[32,8192]{1,0:T(8,128)(2,1)S(1)}, bf16[32,8192]{1,0:T(8,128)(2,1)}, u32[]{:S(2)}) copy-start(bf16[32,8192]{1,0:T(8,128)(2,1)} %copy-done.6) | copy-start | bytes 1572868 | tf_op jit(solution)/shard_map/while
  223.1 4.9 %copy-start.2 = (f32[32,8192]{1,0:T(8,128)}, f32[32,8192]{1,0:T(8,128)S(1)}, u32[]{:S(2)}) copy-start(f32[32,8192]{1,0:T(8,128)S(1)} %fusion.74) | copy-start | bytes 3145732 | tf_op jit(solution)/shard_map/while
  228.0 4.3 copy-start.6
  233.5 4.4 copy-start.14
  236.7 14.5 %collective-permute-start = (bf16[16,8192]{1,0:T(8,128)(2,1)}, bf16[16,8192]{1,0:T(8,128)(2,1)}, u32[]{:S(2)}, u32[]{:S(2)}) collective-permute-start(bf16[16,8192]{1,0:T(8,128)(2,1)} %add_convert_fusion.5), channel_id=1, source_target_pairs={{64,0},{96,32},{128,64},{160,96},{192,128},{224,160},{256,192},{28... | collective-permute-start | bytes 786440 | tf_op jit(solution)/shard_map/while/body/eval_jaxpr/ppermute | solution.py:14
  242.1 9.0 %copy-start.7 = (bf16[32,8192]{1,0:T(8,128)(2,1)S(1)}, bf16[32,8192]{1,0:T(8,128)(2,1)}, u32[]{:S(2)}) copy-start(bf16[32,8192]{1,0:T(8,128)(2,1)} %copy-done.6) | copy-start | bytes 1572868 | tf_op jit(solution)/shard_map/while
  243.3 7.8 %copy-start.2 = (f32[32,8192]{1,0:T(8,128)}, f32[32,8192]{1,0:T(8,128)S(1)}, u32[]{:S(2)}) copy-start(f32[32,8192]{1,0:T(8,128)S(1)} %fusion.74) | copy-start | bytes 3145732 | tf_op jit(solution)/shard_map/while
  245.1 6.1 %copy-start.12 = (f32[32,8192]{1,0:T(8,128)}, f32[32,8192]{1,0:T(8,128)S(1)}, u32[]{:S(2)}) copy-start(f32[32,8192]{1,0:T(8,128)S(1)} %fusion.73) | copy-start | bytes 3145732 | tf_op jit(solution)/shard_map/while
  251.1 4.3 copy-start.6
  256.6 4.4 copy-start.14
  259.8 10.7 %collective-permute-start = (bf16[16,8192]{1,0:T(8,128)(2,1)}, bf16[16,8192]{1,0:T(8,128)(2,1)}, u32[]{:S(2)}, u32[]{:S(2)}) collective-permute-start(bf16[16,8192]{1,0:T(8,128)(2,1)} %add_convert_fusion.5), channel_id=1, source_target_pairs={{64,0},{96,32},{128,64},{160,96},{192,128},{224,160},{256,192},{28... | collective-permute-start | bytes 786440 | tf_op jit(solution)/shard_map/while/body/eval_jaxpr/ppermute | solution.py:14
  265.2 5.2 %copy-start.7 = (bf16[32,8192]{1,0:T(8,128)(2,1)S(1)}, bf16[32,8192]{1,0:T(8,128)(2,1)}, u32[]{:S(2)}) copy-start(bf16[32,8192]{1,0:T(8,128)(2,1)} %copy-done.6) | copy-start | bytes 1572868 | tf_op jit(solution)/shard_map/while
  270.4 4.3 copy-start.6
  275.9 4.4 copy-start.14
  279.1 10.7 %collective-permute-start = (bf16[16,8192]{1,0:T(8,128)(2,1)}, bf16[16,8192]{1,0:T(8,128)(2,1)}, u32[]{:S(2)}, u32[]{:S(2)}) collective-permute-start(bf16[16,8192]{1,0:T(8,128)(2,1)} %add_convert_fusion.5), channel_id=1, source_target_pairs={{64,0},{96,32},{128,64},{160,96},{192,128},{224,160},{256,192},{28... | collective-permute-start | bytes 786440 | tf_op jit(solution)/shard_map/while/body/eval_jaxpr/ppermute | solution.py:14
  284.5 5.3 %copy-start.7 = (bf16[32,8192]{1,0:T(8,128)(2,1)S(1)}, bf16[32,8192]{1,0:T(8,128)(2,1)}, u32[]{:S(2)}) copy-start(bf16[32,8192]{1,0:T(8,128)(2,1)} %copy-done.6) | copy-start | bytes 1572868 | tf_op jit(solution)/shard_map/while
  289.8 4.3 copy-start.6
  295.3 4.4 copy-start.14
  298.4 10.7 %collective-permute-start = (bf16[16,8192]{1,0:T(8,128)(2,1)}, bf16[16,8192]{1,0:T(8,128)(2,1)}, u32[]{:S(2)}, u32[]{:S(2)}) collective-permute-start(bf16[16,8192]{1,0:T(8,128)(2,1)} %add_convert_fusion.5), channel_id=1, source_target_pairs={{64,0},{96,32},{128,64},{160,96},{192,128},{224,160},{256,192},{28... | collective-permute-start | bytes 786440 | tf_op jit(solution)/shard_map/while/body/eval_jaxpr/ppermute | solution.py:14
  303.8 5.2 %copy-start.7 = (bf16[32,8192]{1,0:T(8,128)(2,1)S(1)}, bf16[32,8192]{1,0:T(8,128)(2,1)}, u32[]{:S(2)}) copy-start(bf16[32,8192]{1,0:T(8,128)(2,1)} %copy-done.6) | copy-start | bytes 1572868 | tf_op jit(solution)/shard_map/while
  387.7 8.6 %collective-permute-start.3 = (f32[65,1024]{1,0:T(8,128)S(1)}, f32[65,1024]{1,0:T(8,128)S(1)}, u32[]{:S(2)}, u32[]{:S(2)}) collective-permute-start(f32[65,1024]{1,0:T(8,128)S(1)} %select_bitcast_fusion), channel_id=1, source_target_pairs={{0,32},{32,0},{64,96},{96,64},{128,160},{160,128},{192,224},{224,1... | collective-permute-start | bytes 798728 | tf_op jit(solution)/shard_map/ppermute | solution.py:19
  429.9 4.4 collective-permute-start.4
  435.6 6.8 %collective-permute-start.5 = (f32[]{:T(128)}, f32[]{:T(128)}, u32[]{:S(2)}, u32[]{:S(2)}) collective-permute-start(f32[]{:T(128)} %add.197), channel_id=1, source_target_pairs={{0,8},{4,12},{8,16},{12,20},{16,24},{20,28},{24,0},{28,4},{1,9},{5... | collective-permute-start | bytes 20 | tf_op jit(solution)/shard_map/ppermute | solution.py:134
  442.9 7.1 %collective-permute-start.6 = (f32[]{:T(128)}, f32[]{:T(128)}, u32[]{:S(2)}, u32[]{:S(2)}) collective-permute-start(f32[]{:T(128)} %add.198), channel_id=1, source_target_pairs={{0,16},{4,20},{8,24},{12,28},{16,0},{20,4},{24,8},{28,12},{1,17},{... | collective-permute-start | bytes 20 | tf_op jit(solution)/shard_map/ppermute | solution.py:134
  450.7 8.7 %collective-permute-start.7 = (f32[65,256]{1,0:T(8,128)S(1)}, f32[65,256]{1,0:T(8,128)S(1)}, u32[]{:S(2)}, u32[]{:S(2)}) collective-permute-start(f32[65,256]{1,0:T(8,128)S(1)} %get-tuple-element.668), channel_id=1, source_target_pairs={{0,1},{1,2},{2,3},{3,0},{4,5},{5,6},{6,7},{7,4},{8,9},{9,10},{10,1... | collective-permute-start | bytes 199688 | tf_op jit(solution)/shard_map/ppermute | solution.py:146
  453.1 7.8 %collective-permute-start.8 = (f32[65,256]{1,0:T(8,128)S(1)}, f32[65,256]{1,0:T(8,128)S(1)}, u32[]{:S(2)}, u32[]{:S(2)}) collective-permute-start(f32[65,256]{1,0:T(8,128)S(1)} %get-tuple-element.670), channel_id=1, source_target_pairs={{0,2},{1,3},{2,0},{3,1},{4,6},{5,7},{6,4},{7,5},{8,10},{9,11},{10,... | collective-permute-start | bytes 199688 | tf_op jit(solution)/shard_map/ppermute | solution.py:146
  457.4 7.5 %collective-permute-start.9 = (f32[65,256]{1,0:T(8,128)S(1)}, f32[65,256]{1,0:T(8,128)S(1)}, u32[]{:S(2)}, u32[]{:S(2)}) collective-permute-start(f32[65,256]{1,0:T(8,128)S(1)} %get-tuple-element.669), channel_id=1, source_target_pairs={{0,3},{1,0},{2,1},{3,2},{4,7},{5,4},{6,5},{7,6},{8,11},{9,8},{10,9... | collective-permute-start | bytes 199688 | tf_op jit(solution)/shard_map/ppermute | solution.py:146
  (84 other events, 278.9 us)
Sparse Core Ops, SparseCore 0:
  30.6 34.8 all-gather.1
  314.2 72.3 reduce-scatter.1

commit v5 on v4

--- a/solution.py
+++ b/solution.py
@@ -63,9 +63,8 @@
         layers.append((hidden, inverse_root_mean, low, a_full, b_full, gain_float))
     block_total = half_rows // rows_per_block
 
-    def layer_block(layer, source, block_offset, sums, inside):
+    def layer_block(layer, source, block_offset):
         hidden, inverse_root_mean, low, a_full, b_full, gain_float = layer
-        sum_a, sum_b, sum_g = sums
         hidden_part = lax.dynamic_slice_in_dim(hidden, block_offset, rows_per_block, 0)
         r_part = lax.dynamic_slice_in_dim(inverse_root_mean, block_offset, rows_per_block, 0)
         input_portion = hidden_part.astype(jnp.float32) / r_part
@@ -82,45 +81,44 @@
             )
             / r_part
         ).astype(jnp.bfloat16)
-        normalized_part = (input_portion * gain_float).astype(jnp.bfloat16)
-        low_part = lax.dynamic_slice_in_dim(low, block_offset, rows_per_block, 0)
-        part_a = lax.dot_general(
-            d_low, normalized_part, contract_first, preferred_element_type=jnp.float32
-        )
-        part_b = lax.dot_general(low_part, source, contract_first, preferred_element_type=jnp.float32)
-        part_g = jnp.sum(normalized_gradient * input_portion, axis=0)[None, :]
-        sums = (
-            sum_a + jnp.where(inside, part_a, 0.0),
-            sum_b + jnp.where(inside, part_b, 0.0),
-            sum_g + jnp.where(inside, part_g, 0.0),
-        )
-        return hidden_gradient, sums
+        return hidden_gradient
 
     def turn(turn_index, carry):
-        incoming, upper_sums, lower_sums = carry
+        incoming, upper_store, lower_store = carry
         block_index = turn_index - (pairs - 1 - pair)
         inside = jnp.logical_and(block_index >= 0, block_index < block_total)
         block_offset = jnp.clip(block_index, 0, block_total - 1) * rows_per_block
         top_block = lax.dynamic_slice_in_dim(top, block_offset, rows_per_block, 0)
         source = jnp.where(pair == pairs - 1, top_block, incoming)
-        middle, upper_sums = layer_block(layers[0], source, block_offset, upper_sums, inside)
-        result, lower_sums = layer_block(layers[1], middle, block_offset, lower_sums, inside)
+        middle = layer_block(layers[0], source, block_offset)
+        result = layer_block(layers[1], middle, block_offset)
         incoming = shifted(result, "pipe", -2)
-        return (incoming, upper_sums, lower_sums)
+        slot = jnp.where(inside, block_index, block_total)
+        upper_store = lax.dynamic_update_slice_in_dim(upper_store, source[None], slot, 0)
+        lower_store = lax.dynamic_update_slice_in_dim(lower_store, middle[None], slot, 0)
+        return (incoming, upper_store, lower_store)
 
-    def zero_sums():
-        return (
-            jnp.zeros((rank, width), jnp.float32),
-            jnp.zeros((rank, width), jnp.float32),
-            jnp.zeros((1, width), jnp.float32),
+    store = jnp.zeros((block_total + 1, rows_per_block, width), jnp.bfloat16)
+    begin = (jnp.zeros((rows_per_block, width), jnp.bfloat16), store, store)
+    _, upper_store, lower_store = lax.fori_loop(0, pairs + block_total - 1, turn, begin)
+    per_layer = []
+    for layer, stored in zip(layers, (upper_store, lower_store)):
+        hidden, inverse_root_mean, low, a_full, b_full, gain_float = layer
+        mine = stored[:block_total].reshape(half_rows, width)
+        input_normalized = hidden.astype(jnp.float32) / inverse_root_mean
+        normalized_rows = (input_normalized * gain_float).astype(jnp.bfloat16)
+        d_low = lax.dot_general(
+            mine, b_full, contract_last, preferred_element_type=jnp.float32
+        ).astype(jnp.bfloat16)
+        normalized_gradient = jnp.dot(d_low, a_full, preferred_element_type=jnp.float32)
+        grad_a = lax.dot_general(
+            d_low, normalized_rows, contract_first, preferred_element_type=jnp.float32
         )
-
-    begin = (jnp.zeros((rows_per_block, width), jnp.bfloat16), zero_sums(), zero_sums())
-    _, upper_sums, lower_sums = lax.fori_loop(0, pairs + block_total - 1, turn, begin)
-    grads = jnp.stack(
-        [jnp.concatenate(upper_sums, axis=0), jnp.concatenate(lower_sums, axis=0)]
-    )
-    reduced = lax.psum_scatter(grads, "seq", scatter_dimension=2, tiled=True)
+        grad_b = lax.dot_general(low, mine, contract_first, preferred_element_type=jnp.float32)
+        gain_gradient = jnp.sum(normalized_gradient * input_normalized, axis=0)[None, :]
+        per_layer.append(jnp.concatenate([grad_a, grad_b, gain_gradient], axis=0))
+    grads = jnp.stack(per_layer).astype(jnp.bfloat16)
+    reduced = lax.psum_scatter(grads, "seq", scatter_dimension=2, tiled=True).astype(jnp.float32)
     own_layer = jnp.where(upper_half, reduced[0], reduced[1])
     other_layer = jnp.where(upper_half, reduced[1], reduced[0])
     part = own_layer + partner_swap(other_layer, "pipe")

time: 478 us -> 487 us (1.019)
  waiting for transfers between devices: 171 us -> 245 us
  matrix products: 120 us -> 55.4 us
  other arithmetic: 59.1 us -> 65.7 us
  local copies, waits for them, and re-layouts: 17.9 us -> 12.8 us
    ppermute x11, waiting for transfers between devices: 46.7 us -> 119 us  [shifted(): lax.ppermute(value, axis, [(source, source + steps) for source in range(i...]
    dot_general x68 -> x8, matrix products: 83.6 us -> 12.6 us  [the longest x2 6.87 us: on_device(): lax.dot_general(low, mine, contract_first, preferred_element_type=jnp.flo...]
    dynamic_update_slice x0 -> x22, other arithmetic: none -> 39.6 us  [the longest x11 20.6 us: turn(): lax.dynamic_update_slice_in_dim(lower_store, middle[None], slot, 0)]
    convert_element_type x22 -> x11, other arithmetic: 31.4 us -> 12.8 us  [layer_block(): hidden_gradient = (source.astype(jnp.float32) + (input_gradient - input_p...]
    select_n x33 -> x0, other arithmetic: 12.2 us -> none  [the longest x11 12 us: turn(): source = jnp.where(pair == pairs - 1, top_block, incoming)]
    div x22 -> x11, local copies, waits for them, and re-layouts: 8.62 us -> 0.8 us  [layer_block(): input_portion = hidden_part.astype(jnp.float32) / r_part]
    dot_general x22, matrix products: 36.5 us -> 42.8 us  [layer_block(): jnp.dot(d_low, a_full, preferred_element_type=jnp.float32)]
  transfers between devices with their start and end apart: 22 -> 22, of which waited for: 21 -> 21; matrix products, arithmetic and copies ran while one was open for 17% -> 1% of each run, Pallas kernels for 0% -> 0%
where the time goes in v5:
time: 487 us; the launch traced here: 484 us
  waiting for transfers between devices  245 us (50%)
  other arithmetic  65.7 us (13%)
  matrix products  55.4 us (11%)
  blocking collectives  47.6 us (10%)
  starting transfers between devices  38.6 us (8%)
  between operations  18.1 us (4%)
  local copies, waits for them, and re-layouts  12.8 us (3%)
    ppermute x11, waiting for transfers between devices, shifted(): lax.ppermute(value, axis, [(source, source + steps) for source in range(i...  119 us
    reduce_scatter x1, waiting for transfers between devices, on_device(): lax.psum_scatter(grads, 'seq', scatter_dimension=2, tiled=True)  74.6 us
    dot_general x22, matrix products, layer_block(): jnp.dot(d_low, a_full, preferred_element_type=jnp.float32)  42.8 us
    psum x1, blocking collectives, on_device(): total = lax.psum(square, 'pipe')  31.9 us
    ppermute x3, waiting for transfers between devices, partner_swap(): lax.ppermute(value, axis, [(source, source ^ 1) for source in range(count)])  24.5 us
    dynamic_update_slice x11, other arithmetic, turn(): lax.dynamic_update_slice_in_dim(lower_store, middle[None], slot, 0)  20.6 us
    dynamic_update_slice x11, other arithmetic, turn(): lax.dynamic_update_slice_in_dim(upper_store, source[None], slot, 0)  19 us
    all_gather x1, blocking collectives, on_device(): lax.all_gather(stacked, 'dp', axis=2, tiled=True)  15.7 us
  transfers between devices with their start and end apart: 22, of which 21 were waited for; matrix products, arithmetic and copies ran while one was open for 1% of the time, Pallas kernels for 0%

profile of v5, /device:TPU:6, one launch (start us, length us, event | category | flops | bytes accessed | tf_op | source)
XLA Modules:
  0.0 484.0 jit_solution(2107118704781500472)
XLA Ops:
  8.1 3.8 collective-permute-start.1
  12.0 2.0 collective-permute-done.1
  14.8 15.7 %all_gather.6 = bf16[2,65,1024]{2,1,0:T(8,128)(2,1)} all-gather(bf16[2,65,256]{2,1,0:T(8,128)(2,1)S(1)} %pad_maximum_fusion.1), channel_id=1, replica_groups=mesh['pipe'=16,'seq'=8,'dp'=4] {'dp'}, dimensions={2}, use_global_device_ids=true | all-gather | bytes 332800 | tf_op jit(solution)/shard_map/all_gather | solution.py:46
  31.8 1.9 collective-permute-start.2
  34.8 17.4 %collective-permute-done.2 = bf16[64,8192]{1,0:T(8,128)(2,1)} collective-permute-done((bf16[64,8192]{1,0:T(8,128)(2,1)S(1)}, bf16[64,8192]{1,0:T(8,128)(2,1)}, u32[]{:S(2)}, u32[]{:S(2)}) %collective-permute-start.2) | collective-permute-done | bytes 1048608 | tf_op jit(solution)/shard_map/ppermute | solution.py:19
  52.2 3.4 fusion.2
  55.6 9.8 %all-gather.2.cloned.1.call-done = bf16[2,65,8192]{2,1,0:T(8,128)(2,1)} async-done(((bf16[2,65,1024]{2,1,0:T(8,128)(2,1)}), bf16[2,65,8192]{2,1,0:T(8,128)(2,1)}) %all-gather.2.cloned.1.call-update) | async-done | bytes 2129936 | tf_op jit(solution)/shard_map/all_gather | solution.py:46
  65.4 2.9 slice_bitcast_fusion
  71.8 229.8 %while.19 = (s32[]{:T(128)}, bf16[16,8192]{1,0:T(8,128)(2,1)S(1)}, bf16[5,16,8192]{2,1,0:T(8,128)(2,1)}, bf16[5,16,8192]{2,1,0:T(8,128)(2,1)}, pred[]{:T(512)}, ...) while((s32[]{:T(128)}, bf16[16,8192]{1,0:T(8,128)(2,1)S(1)}, ...), condition=%wide.region_5.6_spmd, body=%wide.region_2.5_spmd.sunk | while | flops 37094416 | bytes 9242547 | solution.py:103
  73.6 1.9 multiply_reduce_fusion.5
  75.6 1.9 bitcast_dynamic-update-slice_fusion.5
  77.5 1.9 multiply_reduce_fusion.6
  81.9 15.5 %collective-permute-done = bf16[16,8192]{1,0:T(8,128)(2,1)S(1)} collective-permute-done((bf16[16,8192]{1,0:T(8,128)(2,1)S(1)}, bf16[16,8192]{1,0:T(8,128)(2,1)S(1)}, u32[]{:S(2)}, u32[]{:S(2)}) %collective-permute-start) | collective-permute-done | bytes 262176 | tf_op jit(solution)/shard_map/while/body/eval_jaxpr/ppermute | solution.py:14
  99.2 1.9 multiply_reduce_fusion.5
  101.2 1.9 bitcast_dynamic-update-slice_fusion.5
  103.1 1.9 multiply_reduce_fusion.6
  107.5 13.4 %collective-permute-done = bf16[16,8192]{1,0:T(8,128)(2,1)S(1)} collective-permute-done((bf16[16,8192]{1,0:T(8,128)(2,1)S(1)}, bf16[16,8192]{1,0:T(8,128)(2,1)S(1)}, u32[]{:S(2)}, u32[]{:S(2)}) %collective-permute-start) | collective-permute-done | bytes 262176 | tf_op jit(solution)/shard_map/while/body/eval_jaxpr/ppermute | solution.py:14
  122.7 1.9 multiply_reduce_fusion.5
  124.7 1.9 bitcast_dynamic-update-slice_fusion.5
  126.6 1.9 multiply_reduce_fusion.6
  131.0 10.9 %collective-permute-done = bf16[16,8192]{1,0:T(8,128)(2,1)S(1)} collective-permute-done((bf16[16,8192]{1,0:T(8,128)(2,1)S(1)}, bf16[16,8192]{1,0:T(8,128)(2,1)S(1)}, u32[]{:S(2)}, u32[]{:S(2)}) %collective-permute-start) | collective-permute-done | bytes 262176 | tf_op jit(solution)/shard_map/while/body/eval_jaxpr/ppermute | solution.py:14
  143.7 1.9 multiply_reduce_fusion.5
  145.7 1.9 bitcast_dynamic-update-slice_fusion.5
  147.5 1.9 multiply_reduce_fusion.6
  152.0 10.1 %collective-permute-done = bf16[16,8192]{1,0:T(8,128)(2,1)S(1)} collective-permute-done((bf16[16,8192]{1,0:T(8,128)(2,1)S(1)}, bf16[16,8192]{1,0:T(8,128)(2,1)S(1)}, u32[]{:S(2)}, u32[]{:S(2)}) %collective-permute-start) | collective-permute-done | bytes 262176 | tf_op jit(solution)/shard_map/while/body/eval_jaxpr/ppermute | solution.py:14
  163.8 1.9 multiply_reduce_fusion.5
  165.8 1.9 bitcast_dynamic-update-slice_fusion.5
  167.7 1.9 multiply_reduce_fusion.6
  172.1 9.2 %collective-permute-done = bf16[16,8192]{1,0:T(8,128)(2,1)S(1)} collective-permute-done((bf16[16,8192]{1,0:T(8,128)(2,1)S(1)}, bf16[16,8192]{1,0:T(8,128)(2,1)S(1)}, u32[]{:S(2)}, u32[]{:S(2)}) %collective-permute-start) | collective-permute-done | bytes 262176 | tf_op jit(solution)/shard_map/while/body/eval_jaxpr/ppermute | solution.py:14
  183.1 1.9 multiply_reduce_fusion.5
  186.9 1.9 multiply_reduce_fusion.6
  191.4 12.1 %collective-permute-done = bf16[16,8192]{1,0:T(8,128)(2,1)S(1)} collective-permute-done((bf16[16,8192]{1,0:T(8,128)(2,1)S(1)}, bf16[16,8192]{1,0:T(8,128)(2,1)S(1)}, u32[]{:S(2)}, u32[]{:S(2)}) %collective-permute-start) | collective-permute-done | bytes 262176 | tf_op jit(solution)/shard_map/while/body/eval_jaxpr/ppermute | solution.py:14
  205.2 1.9 multiply_reduce_fusion.5
  209.1 1.9 multiply_reduce_fusion.6
  213.5 9.6 %collective-permute-done = bf16[16,8192]{1,0:T(8,128)(2,1)S(1)} collective-permute-done((bf16[16,8192]{1,0:T(8,128)(2,1)S(1)}, bf16[16,8192]{1,0:T(8,128)(2,1)S(1)}, u32[]{:S(2)}, u32[]{:S(2)}) %collective-permute-start) | collective-permute-done | bytes 262176 | tf_op jit(solution)/shard_map/while/body/eval_jaxpr/ppermute | solution.py:14
  224.9 1.9 multiply_reduce_fusion.5
  226.9 1.9 bitcast_dynamic-update-slice_fusion.5
  228.7 1.9 multiply_reduce_fusion.6
  233.2 8.9 %collective-permute-done = bf16[16,8192]{1,0:T(8,128)(2,1)S(1)} collective-permute-done((bf16[16,8192]{1,0:T(8,128)(2,1)S(1)}, bf16[16,8192]{1,0:T(8,128)(2,1)S(1)}, u32[]{:S(2)}, u32[]{:S(2)}) %collective-permute-start) | collective-permute-done | bytes 262176 | tf_op jit(solution)/shard_map/while/body/eval_jaxpr/ppermute | solution.py:14
  243.9 1.9 multiply_reduce_fusion.5
  247.7 1.9 multiply_reduce_fusion.6
  252.1 9.1 %collective-permute-done = bf16[16,8192]{1,0:T(8,128)(2,1)S(1)} collective-permute-done((bf16[16,8192]{1,0:T(8,128)(2,1)S(1)}, bf16[16,8192]{1,0:T(8,128)(2,1)S(1)}, u32[]{:S(2)}, u32[]{:S(2)}) %collective-permute-start) | collective-permute-done | bytes 262176 | tf_op jit(solution)/shard_map/while/body/eval_jaxpr/ppermute | solution.py:14
  263.1 1.9 multiply_reduce_fusion.5
  266.9 1.9 multiply_reduce_fusion.6
  271.3 9.1 %collective-permute-done = bf16[16,8192]{1,0:T(8,128)(2,1)S(1)} collective-permute-done((bf16[16,8192]{1,0:T(8,128)(2,1)S(1)}, bf16[16,8192]{1,0:T(8,128)(2,1)S(1)}, u32[]{:S(2)}, u32[]{:S(2)}) %collective-permute-start) | collective-permute-done | bytes 262176 | tf_op jit(solution)/shard_map/while/body/eval_jaxpr/ppermute | solution.py:14
  282.2 1.9 multiply_reduce_fusion.5
  286.0 1.9 multiply_reduce_fusion.6
  290.4 11.2 %collective-permute-done = bf16[16,8192]{1,0:T(8,128)(2,1)S(1)} collective-permute-done((bf16[16,8192]{1,0:T(8,128)(2,1)S(1)}, bf16[16,8192]{1,0:T(8,128)(2,1)S(1)}, u32[]{:S(2)}, u32[]{:S(2)}) %collective-permute-start) | collective-permute-done | bytes 262176 | tf_op jit(solution)/shard_map/while/body/eval_jaxpr/ppermute | solution.py:14
  310.4 3.6 convolution_convert_fusion.4
  313.9 2.3 maximum_bitcast_fusion
  316.3 3.3 convolution_convert_fusion.2
  322.8 74.6 %reduce-scatter.2.cloned.1.call-done = bf16[2,65,1024]{2,1,0:T(8,128)(2,1)} async-done(((bf16[2,65,8192]{2,1,0:T(8,128)(2,1)}), bf16[2,65,1024]{2,1,0:T(8,128)(2,1)}) %reduce-scatter.2.cloned.1.call-update) | async-done | bytes 266256 | tf_op jit(solution)/shard_map/reduce_scatter | solution.py:121
  398.4 3.5 collective-permute-start.3
  402.0 5.1 %collective-permute-done.3 = f32[65,1024]{1,0:T(8,128)S(1)} collective-permute-done((f32[65,1024]{1,0:T(8,128)S(1)}, f32[65,1024]{1,0:T(8,128)S(1)}, u32[]{:S(2)}, u32[]{:S(2)}) %collective-permute-start.3) | collective-permute-done | bytes 266272 | tf_op jit(solution)/shard_map/ppermute | solution.py:19
  407.7 31.9 %psum.7 = f32[]{:T(128)} all-reduce(f32[]{:T(128)} %get-tuple-element.409), channel_id=1, replica_groups=mesh['pipe'=16,'seq'=8,'dp'=4] {'pipe'}, use_global_device_ids=true, to_apply=%region_10.11 | all-reduce | flops 1 | bytes 8 | tf_op jit(solution)/shard_map/psum | solution.py:128
  439.6 4.4 collective-permute-done.4
  445.4 3.2 collective-permute-start.5
  448.6 3.6 collective-permute-done.5
  452.8 3.2 collective-permute-start.6
  456.0 3.9 collective-permute-done.6
  460.6 2.5 collective-permute-start.7
  463.1 4.3 collective-permute-start.8
  467.4 1.9 collective-permute-start.9
  470.9 4.0 collective-permute-done.9
  (126 shorter events, 80.2 us)
Async XLA Ops:
  7.2 26.6 %copy-start = (bf16[1,128,8192]{2,1,0:T(8,128)(2,1)S(1)}, bf16[1,128,8192]{2,1,0:T(8,128)(2,1)}, u32[]{:S(2)}) copy-start(bf16[1,128,8192]{2,1,0:T(8,128)(2,1)} %param.8) | copy-start | bytes 6291460
  7.2 58.3 %all-gather.2.cloned.1.call-start = ((), (), s32[]{:S(2)}) async-start(), calls=%async_computation.1 | async-start | bytes 2654208 | tf_op jit(solution)/shard_map/all_gather | solution.py:46
  8.1 5.8 %collective-permute-start.1 = (bf16[65,256]{1,0:T(8,128)(2,1)S(1)}, bf16[65,256]{1,0:T(8,128)(2,1)S(1)}, u32[]{:S(2)}, u32[]{:S(2)}) collective-permute-start(bf16[65,256]{1,0:T(8,128)(2,1)S(1)} %pad_maximum_fusion.2), channel_id=1, source_target_pairs={{0,32},{32,0},{64,96},{96,64},{128,160},{160,128},{192,224},{224,1... | collective-permute-start | bytes 99848 | tf_op jit(solution)/shard_map/ppermute | solution.py:19
  30.4 366.9 %reduce-scatter.2.cloned.1.call-start = ((), (), s32[]{:S(2)}) async-start(), calls=%async_computation.2 | async-start | bytes 2654208 | tf_op jit(solution)/shard_map/reduce_scatter | solution.py:121
  31.8 20.4 %collective-permute-start.2 = (bf16[64,8192]{1,0:T(8,128)(2,1)S(1)}, bf16[64,8192]{1,0:T(8,128)(2,1)}, u32[]{:S(2)}, u32[]{:S(2)}) collective-permute-start(bf16[64,8192]{1,0:T(8,128)(2,1)S(1)} %dynamic-slice_bitcast_fusion), channel_id=1, source_target_pairs={{0,32},{32,0},{64,96},{96,64},{128,160},{160,128},{192,224},{224,1... | collective-permute-start | bytes 3145736 | tf_op jit(solution)/shard_map/ppermute | solution.py:19
  33.8 18.5 %copy-start.8 = (bf16[1,1,128,8192]{3,2,1,0:T(8,128)(2,1)S(1)}, bf16[1,1,128,8192]{3,2,1,0:T(8,128)(2,1)}, u32[]{:S(2)}) copy-start(bf16[1,1,128,8192]{3,2,1,0:T(8,128)(2,1)} %param.7) | copy-start | bytes 6291460
  80.6 16.9 %collective-permute-start = (bf16[16,8192]{1,0:T(8,128)(2,1)S(1)}, bf16[16,8192]{1,0:T(8,128)(2,1)S(1)}, u32[]{:S(2)}, u32[]{:S(2)}) collective-permute-start(bf16[16,8192]{1,0:T(8,128)(2,1)S(1)} %add_convert_fusion.4), channel_id=1, source_target_pairs={{64,0},{96,32},{128,64},{160,96},{192,128},{224,160},{256,192},{28... | collective-permute-start | bytes 786440 | tf_op jit(solution)/shard_map/while/body/eval_jaxpr/ppermute | solution.py:14
  106.2 14.7 %collective-permute-start = (bf16[16,8192]{1,0:T(8,128)(2,1)S(1)}, bf16[16,8192]{1,0:T(8,128)(2,1)S(1)}, u32[]{:S(2)}, u32[]{:S(2)}) collective-permute-start(bf16[16,8192]{1,0:T(8,128)(2,1)S(1)} %add_convert_fusion.4), channel_id=1, source_target_pairs={{64,0},{96,32},{128,64},{160,96},{192,128},{224,160},{256,192},{28... | collective-permute-start | bytes 786440 | tf_op jit(solution)/shard_map/while/body/eval_jaxpr/ppermute | solution.py:14
  129.7 12.2 %collective-permute-start = (bf16[16,8192]{1,0:T(8,128)(2,1)S(1)}, bf16[16,8192]{1,0:T(8,128)(2,1)S(1)}, u32[]{:S(2)}, u32[]{:S(2)}) collective-permute-start(bf16[16,8192]{1,0:T(8,128)(2,1)S(1)} %add_convert_fusion.4), channel_id=1, source_target_pairs={{64,0},{96,32},{128,64},{160,96},{192,128},{224,160},{256,192},{28... | collective-permute-start | bytes 786440 | tf_op jit(solution)/shard_map/while/body/eval_jaxpr/ppermute | solution.py:14
  150.7 11.4 %collective-permute-start = (bf16[16,8192]{1,0:T(8,128)(2,1)S(1)}, bf16[16,8192]{1,0:T(8,128)(2,1)S(1)}, u32[]{:S(2)}, u32[]{:S(2)}) collective-permute-start(bf16[16,8192]{1,0:T(8,128)(2,1)S(1)} %add_convert_fusion.4), channel_id=1, source_target_pairs={{64,0},{96,32},{128,64},{160,96},{192,128},{224,160},{256,192},{28... | collective-permute-start | bytes 786440 | tf_op jit(solution)/shard_map/while/body/eval_jaxpr/ppermute | solution.py:14
  170.8 10.5 %collective-permute-start = (bf16[16,8192]{1,0:T(8,128)(2,1)S(1)}, bf16[16,8192]{1,0:T(8,128)(2,1)S(1)}, u32[]{:S(2)}, u32[]{:S(2)}) collective-permute-start(bf16[16,8192]{1,0:T(8,128)(2,1)S(1)} %add_convert_fusion.4), channel_id=1, source_target_pairs={{64,0},{96,32},{128,64},{160,96},{192,128},{224,160},{256,192},{28... | collective-permute-start | bytes 786440 | tf_op jit(solution)/shard_map/while/body/eval_jaxpr/ppermute | solution.py:14
  190.1 13.4 %collective-permute-start = (bf16[16,8192]{1,0:T(8,128)(2,1)S(1)}, bf16[16,8192]{1,0:T(8,128)(2,1)S(1)}, u32[]{:S(2)}, u32[]{:S(2)}) collective-permute-start(bf16[16,8192]{1,0:T(8,128)(2,1)S(1)} %add_convert_fusion.4), channel_id=1, source_target_pairs={{64,0},{96,32},{128,64},{160,96},{192,128},{224,160},{256,192},{28... | collective-permute-start | bytes 786440 | tf_op jit(solution)/shard_map/while/body/eval_jaxpr/ppermute | solution.py:14
  212.2 10.9 %collective-permute-start = (bf16[16,8192]{1,0:T(8,128)(2,1)S(1)}, bf16[16,8192]{1,0:T(8,128)(2,1)S(1)}, u32[]{:S(2)}, u32[]{:S(2)}) collective-permute-start(bf16[16,8192]{1,0:T(8,128)(2,1)S(1)} %add_convert_fusion.4), channel_id=1, source_target_pairs={{64,0},{96,32},{128,64},{160,96},{192,128},{224,160},{256,192},{28... | collective-permute-start | bytes 786440 | tf_op jit(solution)/shard_map/while/body/eval_jaxpr/ppermute | solution.py:14
  231.9 10.2 %collective-permute-start = (bf16[16,8192]{1,0:T(8,128)(2,1)S(1)}, bf16[16,8192]{1,0:T(8,128)(2,1)S(1)}, u32[]{:S(2)}, u32[]{:S(2)}) collective-permute-start(bf16[16,8192]{1,0:T(8,128)(2,1)S(1)} %add_convert_fusion.4), channel_id=1, source_target_pairs={{64,0},{96,32},{128,64},{160,96},{192,128},{224,160},{256,192},{28... | collective-permute-start | bytes 786440 | tf_op jit(solution)/shard_map/while/body/eval_jaxpr/ppermute | solution.py:14
  250.8 10.4 %collective-permute-start = (bf16[16,8192]{1,0:T(8,128)(2,1)S(1)}, bf16[16,8192]{1,0:T(8,128)(2,1)S(1)}, u32[]{:S(2)}, u32[]{:S(2)}) collective-permute-start(bf16[16,8192]{1,0:T(8,128)(2,1)S(1)} %add_convert_fusion.4), channel_id=1, source_target_pairs={{64,0},{96,32},{128,64},{160,96},{192,128},{224,160},{256,192},{28... | collective-permute-start | bytes 786440 | tf_op jit(solution)/shard_map/while/body/eval_jaxpr/ppermute | solution.py:14
  270.0 10.4 %collective-permute-start = (bf16[16,8192]{1,0:T(8,128)(2,1)S(1)}, bf16[16,8192]{1,0:T(8,128)(2,1)S(1)}, u32[]{:S(2)}, u32[]{:S(2)}) collective-permute-start(bf16[16,8192]{1,0:T(8,128)(2,1)S(1)} %add_convert_fusion.4), channel_id=1, source_target_pairs={{64,0},{96,32},{128,64},{160,96},{192,128},{224,160},{256,192},{28... | collective-permute-start | bytes 786440 | tf_op jit(solution)/shard_map/while/body/eval_jaxpr/ppermute | solution.py:14
  289.1 12.5 %collective-permute-start = (bf16[16,8192]{1,0:T(8,128)(2,1)S(1)}, bf16[16,8192]{1,0:T(8,128)(2,1)S(1)}, u32[]{:S(2)}, u32[]{:S(2)}) collective-permute-start(bf16[16,8192]{1,0:T(8,128)(2,1)S(1)} %add_convert_fusion.4), channel_id=1, source_target_pairs={{64,0},{96,32},{128,64},{160,96},{192,128},{224,160},{256,192},{28... | collective-permute-start | bytes 786440 | tf_op jit(solution)/shard_map/while/body/eval_jaxpr/ppermute | solution.py:14
  301.6 3.2 copy-start.2
  303.0 1.8 copy-start.7
  304.8 1.9 copy-start.4
  306.7 1.3 copy-start.5
  307.2 1.3 copy-start.1
  308.1 1.7 copy-start.6
  319.5 1.6 copy-start.3
  398.4 8.6 %collective-permute-start.3 = (f32[65,1024]{1,0:T(8,128)S(1)}, f32[65,1024]{1,0:T(8,128)S(1)}, u32[]{:S(2)}, u32[]{:S(2)}) collective-permute-start(f32[65,1024]{1,0:T(8,128)S(1)} %select_bitcast_fusion), channel_id=1, source_target_pairs={{0,32},{32,0},{64,96},{96,64},{128,160},{160,128},{192,224},{224,1... | collective-permute-start | bytes 798728 | tf_op jit(solution)/shard_map/ppermute | solution.py:19
  439.6 4.4 collective-permute-start.4
  445.4 6.8 %collective-permute-start.5 = (f32[]{:T(128)}, f32[]{:T(128)}, u32[]{:S(2)}, u32[]{:S(2)}) collective-permute-start(f32[]{:T(128)} %add.151), channel_id=1, source_target_pairs={{0,8},{4,12},{8,16},{12,20},{16,24},{20,28},{24,0},{28,4},{1,9},{5... | collective-permute-start | bytes 20 | tf_op jit(solution)/shard_map/ppermute | solution.py:132
  452.8 7.1 %collective-permute-start.6 = (f32[]{:T(128)}, f32[]{:T(128)}, u32[]{:S(2)}, u32[]{:S(2)}) collective-permute-start(f32[]{:T(128)} %add.152), channel_id=1, source_target_pairs={{0,16},{4,20},{8,24},{12,28},{16,0},{20,4},{24,8},{28,12},{1,17},{... | collective-permute-start | bytes 20 | tf_op jit(solution)/shard_map/ppermute | solution.py:132
  460.6 8.7 %collective-permute-start.7 = (f32[65,256]{1,0:T(8,128)S(1)}, f32[65,256]{1,0:T(8,128)S(1)}, u32[]{:S(2)}, u32[]{:S(2)}) collective-permute-start(f32[65,256]{1,0:T(8,128)S(1)} %get-tuple-element.429), channel_id=1, source_target_pairs={{0,1},{1,2},{2,3},{3,0},{4,5},{5,6},{6,7},{7,4},{8,9},{9,10},{10,1... | collective-permute-start | bytes 199688 | tf_op jit(solution)/shard_map/ppermute | solution.py:144
  463.1 7.8 %collective-permute-start.8 = (f32[65,256]{1,0:T(8,128)S(1)}, f32[65,256]{1,0:T(8,128)S(1)}, u32[]{:S(2)}, u32[]{:S(2)}) collective-permute-start(f32[65,256]{1,0:T(8,128)S(1)} %get-tuple-element.431), channel_id=1, source_target_pairs={{0,2},{1,3},{2,0},{3,1},{4,6},{5,7},{6,4},{7,5},{8,10},{9,11},{10,... | collective-permute-start | bytes 199688 | tf_op jit(solution)/shard_map/ppermute | solution.py:144
  467.4 7.5 %collective-permute-start.9 = (f32[65,256]{1,0:T(8,128)S(1)}, f32[65,256]{1,0:T(8,128)S(1)}, u32[]{:S(2)}, u32[]{:S(2)}) collective-permute-start(f32[65,256]{1,0:T(8,128)S(1)} %get-tuple-element.430), channel_id=1, source_target_pairs={{0,3},{1,0},{2,1},{3,2},{4,7},{5,4},{6,5},{7,6},{8,11},{9,8},{10,9... | collective-permute-start | bytes 199688 | tf_op jit(solution)/shard_map/ppermute | solution.py:144
Sparse Core Ops, SparseCore 0:
  30.6 34.8 all-gather.1
  322.9 74.4 reduce-scatter.1

commit v6 on v4

--- a/solution.py
+++ b/solution.py
@@ -5,7 +5,7 @@
 from jax import lax
 from jax.sharding import PartitionSpec as P
 
-rows_per_block = 16
+rows_per_block = 8
 
 
 def shifted(value, axis, steps):

time: 478 us -> 538 us (1.13)
  waiting for transfers between devices: 171 us -> 114 us
  matrix products: 120 us -> 176 us
  local copies, waits for them, and re-layouts: 17.9 us -> 45.2 us
  other arithmetic: 59.1 us -> 84.4 us
    ppermute x11 -> x15, waiting for transfers between devices: 46.7 us -> 12.6 us  [shifted(): lax.ppermute(value, axis, [(source, source + steps) for source in range(i...]
    while x242 -> x450, local copies, waits for them, and re-layouts: 0.49 us -> 22.9 us
    reduce_scatter x1, waiting for transfers between devices: 72.5 us -> 51.1 us  [on_device(): reduced = lax.psum_scatter(grads, 'seq', scatter_dimension=2, tiled=True)]
    dot_general x22 -> x30, matrix products: 36.5 us -> 55.1 us  [layer_block(): jnp.dot(d_low, a_full, preferred_element_type=jnp.float32)]
    dot_general x22 -> x30, matrix products: 5.44 us -> 22.8 us  [layer_block(): lax.dot_general(source, b_full, contract_last, preferred_element_type=jnp...]
    select_n x22 -> x30, other arithmetic: 0.14 us -> 13.6 us  [layer_block(): jnp.where(inside, part_g, 0.0)]
    dot_general x22 -> x30, matrix products: 49.5 us -> 61 us  [layer_block(): lax.dot_general(d_low, normalized_part, contract_first, preferred_element...]
    convert_element_type x22 -> x30, other arithmetic: 31.4 us -> 41.3 us  [layer_block(): hidden_gradient = (source.astype(jnp.float32) + (input_gradient - input_p...]
  transfers between devices with their start and end apart: 22 -> 26, of which waited for: 21 -> 25; matrix products, arithmetic and copies ran while one was open for 17% -> 22% of each run, Pallas kernels for 0% -> 0%
where the time goes in v6:
time: 538 us; the launch traced here: 532 us
  matrix products  176 us (33%)
  waiting for transfers between devices  114 us (21%)
  other arithmetic  84.4 us (16%)
  blocking collectives  47.5 us (9%)
  local copies, waits for them, and re-layouts  45.2 us (8%)
  starting transfers between devices  43.5 us (8%)
  between operations  18.1 us (3%)
    dot_general x30, matrix products, layer_block(): lax.dot_general(d_low, normalized_part, contract_first, preferred_element...  61 us
    dot_general x30, matrix products, layer_block(): jnp.dot(d_low, a_full, preferred_element_type=jnp.float32)  55.1 us
    reduce_scatter x1, waiting for transfers between devices, on_device(): reduced = lax.psum_scatter(grads, 'seq', scatter_dimension=2, tiled=True)  51.1 us
    convert_element_type x30, other arithmetic, layer_block(): hidden_gradient = (source.astype(jnp.float32) + (input_gradient - input_p...  41.3 us
    dot_general x30, matrix products, layer_block(): lax.dot_general(low_part, source, contract_first, preferred_element_type=...  33.8 us
    psum x1, blocking collectives, on_device(): total = lax.psum(square, 'pipe')  31.9 us
    ppermute x3, waiting for transfers between devices, partner_swap(): lax.ppermute(value, axis, [(source, source ^ 1) for source in range(count)])  24.7 us
    while x450, local copies, waits for them, and re-layouts  22.9 us
  transfers between devices with their start and end apart: 26, of which 25 were waited for; matrix products, arithmetic and copies ran while one was open for 22% of the time, Pallas kernels for 0%

profile of v6, /device:TPU:6, one launch (start us, length us, event | category | flops | bytes accessed | tf_op | source)
XLA Modules:
  0.0 531.6 jit_solution(8745552704537866143)
XLA Ops:
  8.1 3.8 collective-permute-start.1
  12.0 2.0 collective-permute-done.1
  14.8 15.7 %all_gather.6 = bf16[2,65,1024]{2,1,0:T(8,128)(2,1)} all-gather(bf16[2,65,256]{2,1,0:T(8,128)(2,1)S(1)} %pad_maximum_fusion.1), channel_id=1, replica_groups=mesh['pipe'=16,'seq'=8,'dp'=4] {'dp'}, dimensions={2}, use_global_device_ids=true | all-gather | bytes 332800 | tf_op jit(solution)/shard_map/all_gather | solution.py:46
  30.5 2.3 dynamic-slice_bitcast_fusion
  32.8 1.9 collective-permute-start.2
  35.9 17.6 %collective-permute-done.2 = bf16[64,8192]{1,0:T(8,128)(2,1)} collective-permute-done((bf16[64,8192]{1,0:T(8,128)(2,1)}, bf16[64,8192]{1,0:T(8,128)(2,1)}, u32[]{:S(2)}, u32[]{:S(2)}) %collective-permute-start.2) | collective-permute-done | bytes 1048608 | tf_op jit(solution)/shard_map/ppermute | solution.py:19
  53.4 3.4 fusion.17
  57.3 8.1 %all-gather.2.cloned.1.call-done = bf16[2,65,8192]{2,1,0:T(8,128)(2,1)} async-done(((bf16[2,65,1024]{2,1,0:T(8,128)(2,1)}), bf16[2,65,8192]{2,1,0:T(8,128)(2,1)}) %all-gather.2.cloned.1.call-update) | async-done | bytes 2129936 | tf_op jit(solution)/shard_map/all_gather | solution.py:46
  67.1 1.8 convolution_convert_fusion.2
  69.6 1.8 convolution_convert_fusion.3
  72.1 2.9 slice_bitcast_fusion
  75.1 313.5 %while.28 = (s32[]{:T(128)}, bf16[8,8192]{1,0:T(8,128)(2,1)S(1)}, f32[32,8192]{1,0:T(8,128)S(1)}, f32[32,8192]{1,0:T(8,128)}, f32[1,8192]{1,0:T(1,128)}, /*index...) while((s32[]{:T(128)}, bf16[8,8192]{1,0:T(8,128)(2,1)S(1)}, ...), condition=%wide.region_7.8_spmd.clone, body=%wide.region_2.7_spmd.clone.sunk | while | flops 39420424 | bytes 36776356 | solution.py:119
  78.1 1.9 multiply_reduce_fusion.7
  81.5 1.8 multiply_reduce_fusion.8
  86.3 2.4 fusion.76
  94.0 2.3 collective-permute-done
  99.4 1.9 multiply_reduce_fusion.7
  107.5 2.8 fusion.76
  119.2 1.9 multiply_reduce_fusion.7
  122.5 1.8 multiply_reduce_fusion.8
  127.3 2.8 fusion.76
  140.1 1.9 multiply_reduce_fusion.7
  143.4 1.8 multiply_reduce_fusion.8
  148.2 2.8 fusion.76
  160.1 1.9 multiply_reduce_fusion.7
  163.4 1.8 multiply_reduce_fusion.8
  168.2 2.8 fusion.76
  180.0 1.9 multiply_reduce_fusion.7
  183.3 1.8 multiply_reduce_fusion.8
  188.1 2.8 fusion.76
  200.0 1.9 multiply_reduce_fusion.7
  203.3 1.8 multiply_reduce_fusion.8
  208.1 2.8 fusion.76
  219.9 1.9 multiply_reduce_fusion.7
  229.7 2.6 fusion.76
  241.4 1.9 multiply_reduce_fusion.7
  251.1 2.6 fusion.76
  262.8 1.9 multiply_reduce_fusion.7
  266.2 1.8 multiply_reduce_fusion.8
  272.6 2.7 fusion.76
  284.3 1.9 multiply_reduce_fusion.7
  294.1 2.6 fusion.76
  305.8 1.9 multiply_reduce_fusion.7
  315.5 2.6 fusion.76
  327.2 1.9 multiply_reduce_fusion.7
  337.0 2.6 fusion.76
  348.7 1.9 multiply_reduce_fusion.7
  358.5 2.6 fusion.76
  370.1 1.9 multiply_reduce_fusion.7
  379.9 2.6 fusion.76
  390.7 2.6 pad_maximum_fusion
  393.3 51.1 %reduce-scatter.2.cloned.1.call-done = f32[2,65,1024]{2,1,0:T(8,128)} async-done(((f32[2,65,8192]{2,1,0:T(8,128)}), f32[2,65,1024]{2,1,0:T(8,128)}) %reduce-scatter.2.cloned.1.call-update) | async-done | bytes 532496 | tf_op jit(solution)/shard_map/reduce_scatter | solution.py:123
  445.5 3.4 collective-permute-start.3
  448.9 5.2 collective-permute-done.3
  455.8 31.9 %psum.7 = f32[]{:T(128)} all-reduce(f32[]{:T(128)} %get-tuple-element.650), channel_id=1, replica_groups=mesh['pipe'=16,'seq'=8,'dp'=4] {'pipe'}, use_global_device_ids=true, to_apply=%region_10.11 | all-reduce | flops 1 | bytes 8 | tf_op jit(solution)/shard_map/psum | solution.py:130
  487.7 4.3 collective-permute-done.4
  493.2 3.2 collective-permute-start.5
  496.5 3.4 collective-permute-done.5
  500.5 3.2 collective-permute-start.6
  503.7 3.7 collective-permute-done.6
  508.2 2.4 collective-permute-start.7
  510.6 4.3 collective-permute-start.8
  515.0 1.9 collective-permute-start.9
  518.4 4.0 collective-permute-done.9
  (755 shorter events, 241.0 us)
Async XLA Ops:
  7.2 27.6 %copy-start = (bf16[1,128,8192]{2,1,0:T(8,128)(2,1)S(1)}, bf16[1,128,8192]{2,1,0:T(8,128)(2,1)}, u32[]{:S(2)}) copy-start(bf16[1,128,8192]{2,1,0:T(8,128)(2,1)} %param.8) | copy-start | bytes 6291460
  7.2 58.3 %all-gather.2.cloned.1.call-start = ((), (), s32[]{:S(2)}) async-start(), calls=%async_computation.1 | async-start | bytes 2654208 | tf_op jit(solution)/shard_map/all_gather | solution.py:46
  8.1 5.8 %collective-permute-start.1 = (bf16[65,256]{1,0:T(8,128)(2,1)S(1)}, bf16[65,256]{1,0:T(8,128)(2,1)S(1)}, u32[]{:S(2)}, u32[]{:S(2)}) collective-permute-start(bf16[65,256]{1,0:T(8,128)(2,1)S(1)} %pad_maximum_fusion.2), channel_id=1, source_target_pairs={{0,32},{32,0},{64,96},{96,64},{128,160},{160,128},{192,224},{224,1... | collective-permute-start | bytes 99848 | tf_op jit(solution)/shard_map/ppermute | solution.py:19
  30.4 413.9 %reduce-scatter.2.cloned.1.call-start = ((), (), s32[]{:S(2)}) async-start(), calls=%async_computation.2 | async-start | bytes 5308416 | tf_op jit(solution)/shard_map/reduce_scatter | solution.py:123
  32.8 20.6 %collective-permute-start.2 = (bf16[64,8192]{1,0:T(8,128)(2,1)}, bf16[64,8192]{1,0:T(8,128)(2,1)}, u32[]{:S(2)}, u32[]{:S(2)}) collective-permute-start(bf16[64,8192]{1,0:T(8,128)(2,1)} %dynamic-slice_bitcast_fusion), channel_id=1, source_target_pairs={{0,32},{32,0},{64,96},{96,64},{128,160},{160,128},{192,224},{224,1... | collective-permute-start | bytes 3145736 | tf_op jit(solution)/shard_map/ppermute | solution.py:19
  34.8 18.6 %copy-start.12 = (bf16[1,1,128,8192]{3,2,1,0:T(8,128)(2,1)S(1)}, bf16[1,1,128,8192]{3,2,1,0:T(8,128)(2,1)}, u32[]{:S(2)}) copy-start(bf16[1,1,128,8192]{3,2,1,0:T(8,128)(2,1)} %param.7) | copy-start | bytes 6291460
  75.1 6.3 %copy-start.9 = (f32[8192]{0:T(1024)S(1)}, f32[8192]{0:T(1024)}, u32[]{:S(2)}) copy-start(f32[8192]{0:T(1024)} %get-tuple-element.910) | copy-start | bytes 98308 | tf_op jit(solution)/shard_map/while
  75.2 6.3 %copy-start.18 = (bf16[32,8192]{1,0:T(8,128)(2,1)S(1)}, bf16[32,8192]{1,0:T(8,128)(2,1)}, u32[]{:S(2)}) copy-start(bf16[32,8192]{1,0:T(8,128)(2,1)} %get-tuple-element.909) | copy-start | bytes 1572868 | tf_op jit(solution)/shard_map/while
  84.9 11.4 %collective-permute-start = (bf16[8,8192]{1,0:T(8,128)(2,1)}, bf16[8,8192]{1,0:T(8,128)(2,1)S(1)}, u32[]{:S(2)}, u32[]{:S(2)}) collective-permute-start(bf16[8,8192]{1,0:T(8,128)(2,1)} %add_convert_fusion.5), channel_id=1, source_target_pairs={{64,0},{96,32},{128,64},{160,96},{192,128},{224,160},{256,192},{28... | collective-permute-start | bytes 393224 | tf_op jit(solution)/shard_map/while/body/eval_jaxpr/ppermute | solution.py:14
  89.8 6.6 %copy-start.11 = (f32[8192]{0:T(1024)S(1)}, f32[8192]{0:T(1024)}, u32[]{:S(2)}) copy-start(f32[8192]{0:T(1024)} %copy-done.10) | copy-start | bytes 98308 | tf_op jit(solution)/shard_map/while
  89.8 6.6 %copy-start.20 = (f32[64,1]{0,1:T(1,128)S(1)}, f32[64,1]{0,1:T(1,128)}, u32[]{:S(2)}) copy-start(f32[64,1]{0,1:T(1,128)} %copy-done.19) | copy-start | bytes 772 | tf_op jit(solution)/shard_map/while
  96.4 6.3 %copy-start.9 = (f32[8192]{0:T(1024)S(1)}, f32[8192]{0:T(1024)}, u32[]{:S(2)}) copy-start(f32[8192]{0:T(1024)} %get-tuple-element.910) | copy-start | bytes 98308 | tf_op jit(solution)/shard_map/while
  96.4 6.3 %copy-start.18 = (bf16[32,8192]{1,0:T(8,128)(2,1)S(1)}, bf16[32,8192]{1,0:T(8,128)(2,1)}, u32[]{:S(2)}) copy-start(bf16[32,8192]{1,0:T(8,128)(2,1)} %get-tuple-element.909) | copy-start | bytes 1572868 | tf_op jit(solution)/shard_map/while
  106.1 10.0 %collective-permute-start = (bf16[8,8192]{1,0:T(8,128)(2,1)}, bf16[8,8192]{1,0:T(8,128)(2,1)S(1)}, u32[]{:S(2)}, u32[]{:S(2)}) collective-permute-start(bf16[8,8192]{1,0:T(8,128)(2,1)} %add_convert_fusion.5), channel_id=1, source_target_pairs={{64,0},{96,32},{128,64},{160,96},{192,128},{224,160},{256,192},{28... | collective-permute-start | bytes 393224 | tf_op jit(solution)/shard_map/while/body/eval_jaxpr/ppermute | solution.py:14
  116.2 6.1 %copy-start.7 = (bf16[32,8192]{1,0:T(8,128)(2,1)S(1)}, bf16[32,8192]{1,0:T(8,128)(2,1)}, u32[]{:S(2)}) copy-start(bf16[32,8192]{1,0:T(8,128)(2,1)} %get-tuple-element.908) | copy-start | bytes 1572868 | tf_op jit(solution)/shard_map/while
  116.2 6.3 %copy-start.9 = (f32[8192]{0:T(1024)S(1)}, f32[8192]{0:T(1024)}, u32[]{:S(2)}) copy-start(f32[8192]{0:T(1024)} %get-tuple-element.910) | copy-start | bytes 98308 | tf_op jit(solution)/shard_map/while
  116.2 6.3 %copy-start.18 = (bf16[32,8192]{1,0:T(8,128)(2,1)S(1)}, bf16[32,8192]{1,0:T(8,128)(2,1)}, u32[]{:S(2)}) copy-start(bf16[32,8192]{1,0:T(8,128)(2,1)} %get-tuple-element.909) | copy-start | bytes 1572868 | tf_op jit(solution)/shard_map/while
  126.0 11.1 %collective-permute-start = (bf16[8,8192]{1,0:T(8,128)(2,1)}, bf16[8,8192]{1,0:T(8,128)(2,1)S(1)}, u32[]{:S(2)}, u32[]{:S(2)}) collective-permute-start(bf16[8,8192]{1,0:T(8,128)(2,1)} %add_convert_fusion.5), channel_id=1, source_target_pairs={{64,0},{96,32},{128,64},{160,96},{192,128},{224,160},{256,192},{28... | collective-permute-start | bytes 393224 | tf_op jit(solution)/shard_map/while/body/eval_jaxpr/ppermute | solution.py:14
  137.1 6.1 %copy-start.7 = (bf16[32,8192]{1,0:T(8,128)(2,1)S(1)}, bf16[32,8192]{1,0:T(8,128)(2,1)}, u32[]{:S(2)}) copy-start(bf16[32,8192]{1,0:T(8,128)(2,1)} %get-tuple-element.908) | copy-start | bytes 1572868 | tf_op jit(solution)/shard_map/while
  137.1 6.3 %copy-start.9 = (f32[8192]{0:T(1024)S(1)}, f32[8192]{0:T(1024)}, u32[]{:S(2)}) copy-start(f32[8192]{0:T(1024)} %get-tuple-element.910) | copy-start | bytes 98308 | tf_op jit(solution)/shard_map/while
  137.1 6.3 %copy-start.18 = (bf16[32,8192]{1,0:T(8,128)(2,1)S(1)}, bf16[32,8192]{1,0:T(8,128)(2,1)}, u32[]{:S(2)}) copy-start(bf16[32,8192]{1,0:T(8,128)(2,1)} %get-tuple-element.909) | copy-start | bytes 1572868 | tf_op jit(solution)/shard_map/while
  146.9 10.1 %collective-permute-start = (bf16[8,8192]{1,0:T(8,128)(2,1)}, bf16[8,8192]{1,0:T(8,128)(2,1)S(1)}, u32[]{:S(2)}, u32[]{:S(2)}) collective-permute-start(bf16[8,8192]{1,0:T(8,128)(2,1)} %add_convert_fusion.5), channel_id=1, source_target_pairs={{64,0},{96,32},{128,64},{160,96},{192,128},{224,160},{256,192},{28... | collective-permute-start | bytes 393224 | tf_op jit(solution)/shard_map/while/body/eval_jaxpr/ppermute | solution.py:14
  157.0 6.1 %copy-start.7 = (bf16[32,8192]{1,0:T(8,128)(2,1)S(1)}, bf16[32,8192]{1,0:T(8,128)(2,1)}, u32[]{:S(2)}) copy-start(bf16[32,8192]{1,0:T(8,128)(2,1)} %get-tuple-element.908) | copy-start | bytes 1572868 | tf_op jit(solution)/shard_map/while
  157.1 6.3 %copy-start.9 = (f32[8192]{0:T(1024)S(1)}, f32[8192]{0:T(1024)}, u32[]{:S(2)}) copy-start(f32[8192]{0:T(1024)} %get-tuple-element.910) | copy-start | bytes 98308 | tf_op jit(solution)/shard_map/while
  157.1 6.3 %copy-start.18 = (bf16[32,8192]{1,0:T(8,128)(2,1)S(1)}, bf16[32,8192]{1,0:T(8,128)(2,1)}, u32[]{:S(2)}) copy-start(bf16[32,8192]{1,0:T(8,128)(2,1)} %get-tuple-element.909) | copy-start | bytes 1572868 | tf_op jit(solution)/shard_map/while
  166.8 10.1 %collective-permute-start = (bf16[8,8192]{1,0:T(8,128)(2,1)}, bf16[8,8192]{1,0:T(8,128)(2,1)S(1)}, u32[]{:S(2)}, u32[]{:S(2)}) collective-permute-start(bf16[8,8192]{1,0:T(8,128)(2,1)} %add_convert_fusion.5), channel_id=1, source_target_pairs={{64,0},{96,32},{128,64},{160,96},{192,128},{224,160},{256,192},{28... | collective-permute-start | bytes 393224 | tf_op jit(solution)/shard_map/while/body/eval_jaxpr/ppermute | solution.py:14
  177.0 6.3 %copy-start.9 = (f32[8192]{0:T(1024)S(1)}, f32[8192]{0:T(1024)}, u32[]{:S(2)}) copy-start(f32[8192]{0:T(1024)} %get-tuple-element.910) | copy-start | bytes 98308 | tf_op jit(solution)/shard_map/while
  177.0 6.3 %copy-start.18 = (bf16[32,8192]{1,0:T(8,128)(2,1)S(1)}, bf16[32,8192]{1,0:T(8,128)(2,1)}, u32[]{:S(2)}) copy-start(bf16[32,8192]{1,0:T(8,128)(2,1)} %get-tuple-element.909) | copy-start | bytes 1572868 | tf_op jit(solution)/shard_map/while
  186.8 10.1 %collective-permute-start = (bf16[8,8192]{1,0:T(8,128)(2,1)}, bf16[8,8192]{1,0:T(8,128)(2,1)S(1)}, u32[]{:S(2)}, u32[]{:S(2)}) collective-permute-start(bf16[8,8192]{1,0:T(8,128)(2,1)} %add_convert_fusion.5), channel_id=1, source_target_pairs={{64,0},{96,32},{128,64},{160,96},{192,128},{224,160},{256,192},{28... | collective-permute-start | bytes 393224 | tf_op jit(solution)/shard_map/while/body/eval_jaxpr/ppermute | solution.py:14
  196.9 6.1 %copy-start.7 = (bf16[32,8192]{1,0:T(8,128)(2,1)S(1)}, bf16[32,8192]{1,0:T(8,128)(2,1)}, u32[]{:S(2)}) copy-start(bf16[32,8192]{1,0:T(8,128)(2,1)} %get-tuple-element.908) | copy-start | bytes 1572868 | tf_op jit(solution)/shard_map/while
  197.0 6.3 %copy-start.9 = (f32[8192]{0:T(1024)S(1)}, f32[8192]{0:T(1024)}, u32[]{:S(2)}) copy-start(f32[8192]{0:T(1024)} %get-tuple-element.910) | copy-start | bytes 98308 | tf_op jit(solution)/shard_map/while
  197.0 6.3 %copy-start.18 = (bf16[32,8192]{1,0:T(8,128)(2,1)S(1)}, bf16[32,8192]{1,0:T(8,128)(2,1)}, u32[]{:S(2)}) copy-start(bf16[32,8192]{1,0:T(8,128)(2,1)} %get-tuple-element.909) | copy-start | bytes 1572868 | tf_op jit(solution)/shard_map/while
  206.7 10.1 %collective-permute-start = (bf16[8,8192]{1,0:T(8,128)(2,1)}, bf16[8,8192]{1,0:T(8,128)(2,1)S(1)}, u32[]{:S(2)}, u32[]{:S(2)}) collective-permute-start(bf16[8,8192]{1,0:T(8,128)(2,1)} %add_convert_fusion.5), channel_id=1, source_target_pairs={{64,0},{96,32},{128,64},{160,96},{192,128},{224,160},{256,192},{28... | collective-permute-start | bytes 393224 | tf_op jit(solution)/shard_map/while/body/eval_jaxpr/ppermute | solution.py:14
  216.9 6.3 %copy-start.9 = (f32[8192]{0:T(1024)S(1)}, f32[8192]{0:T(1024)}, u32[]{:S(2)}) copy-start(f32[8192]{0:T(1024)} %get-tuple-element.910) | copy-start | bytes 98308 | tf_op jit(solution)/shard_map/while
  216.9 6.3 %copy-start.18 = (bf16[32,8192]{1,0:T(8,128)(2,1)S(1)}, bf16[32,8192]{1,0:T(8,128)(2,1)}, u32[]{:S(2)}) copy-start(bf16[32,8192]{1,0:T(8,128)(2,1)} %get-tuple-element.909) | copy-start | bytes 1572868 | tf_op jit(solution)/shard_map/while
  226.7 11.7 %collective-permute-start = (bf16[8,8192]{1,0:T(8,128)(2,1)}, bf16[8,8192]{1,0:T(8,128)(2,1)S(1)}, u32[]{:S(2)}, u32[]{:S(2)}) collective-permute-start(bf16[8,8192]{1,0:T(8,128)(2,1)} %add_convert_fusion.5), channel_id=1, source_target_pairs={{64,0},{96,32},{128,64},{160,96},{192,128},{224,160},{256,192},{28... | collective-permute-start | bytes 393224 | tf_op jit(solution)/shard_map/while/body/eval_jaxpr/ppermute | solution.py:14
  238.4 6.3 %copy-start.9 = (f32[8192]{0:T(1024)S(1)}, f32[8192]{0:T(1024)}, u32[]{:S(2)}) copy-start(f32[8192]{0:T(1024)} %get-tuple-element.910) | copy-start | bytes 98308 | tf_op jit(solution)/shard_map/while
  238.4 6.3 %copy-start.18 = (bf16[32,8192]{1,0:T(8,128)(2,1)S(1)}, bf16[32,8192]{1,0:T(8,128)(2,1)}, u32[]{:S(2)}) copy-start(bf16[32,8192]{1,0:T(8,128)(2,1)} %get-tuple-element.909) | copy-start | bytes 1572868 | tf_op jit(solution)/shard_map/while
  248.1 11.7 %collective-permute-start = (bf16[8,8192]{1,0:T(8,128)(2,1)}, bf16[8,8192]{1,0:T(8,128)(2,1)S(1)}, u32[]{:S(2)}, u32[]{:S(2)}) collective-permute-start(bf16[8,8192]{1,0:T(8,128)(2,1)} %add_convert_fusion.5), channel_id=1, source_target_pairs={{64,0},{96,32},{128,64},{160,96},{192,128},{224,160},{256,192},{28... | collective-permute-start | bytes 393224 | tf_op jit(solution)/shard_map/while/body/eval_jaxpr/ppermute | solution.py:14
  259.8 6.3 %copy-start.9 = (f32[8192]{0:T(1024)S(1)}, f32[8192]{0:T(1024)}, u32[]{:S(2)}) copy-start(f32[8192]{0:T(1024)} %get-tuple-element.910) | copy-start | bytes 98308 | tf_op jit(solution)/shard_map/while
  259.9 6.3 %copy-start.18 = (bf16[32,8192]{1,0:T(8,128)(2,1)S(1)}, bf16[32,8192]{1,0:T(8,128)(2,1)}, u32[]{:S(2)}) copy-start(bf16[32,8192]{1,0:T(8,128)(2,1)} %get-tuple-element.909) | copy-start | bytes 1572868 | tf_op jit(solution)/shard_map/while
  269.6 11.7 %collective-permute-start = (bf16[8,8192]{1,0:T(8,128)(2,1)}, bf16[8,8192]{1,0:T(8,128)(2,1)S(1)}, u32[]{:S(2)}, u32[]{:S(2)}) collective-permute-start(bf16[8,8192]{1,0:T(8,128)(2,1)} %add_convert_fusion.5), channel_id=1, source_target_pairs={{64,0},{96,32},{128,64},{160,96},{192,128},{224,160},{256,192},{28... | collective-permute-start | bytes 393224 | tf_op jit(solution)/shard_map/while/body/eval_jaxpr/ppermute | solution.py:14
  281.3 6.3 %copy-start.9 = (f32[8192]{0:T(1024)S(1)}, f32[8192]{0:T(1024)}, u32[]{:S(2)}) copy-start(f32[8192]{0:T(1024)} %get-tuple-element.910) | copy-start | bytes 98308 | tf_op jit(solution)/shard_map/while
  281.3 6.3 %copy-start.18 = (bf16[32,8192]{1,0:T(8,128)(2,1)S(1)}, bf16[32,8192]{1,0:T(8,128)(2,1)}, u32[]{:S(2)}) copy-start(bf16[32,8192]{1,0:T(8,128)(2,1)} %get-tuple-element.909) | copy-start | bytes 1572868 | tf_op jit(solution)/shard_map/while
  291.1 11.6 %collective-permute-start = (bf16[8,8192]{1,0:T(8,128)(2,1)}, bf16[8,8192]{1,0:T(8,128)(2,1)S(1)}, u32[]{:S(2)}, u32[]{:S(2)}) collective-permute-start(bf16[8,8192]{1,0:T(8,128)(2,1)} %add_convert_fusion.5), channel_id=1, source_target_pairs={{64,0},{96,32},{128,64},{160,96},{192,128},{224,160},{256,192},{28... | collective-permute-start | bytes 393224 | tf_op jit(solution)/shard_map/while/body/eval_jaxpr/ppermute | solution.py:14
  302.8 6.3 %copy-start.9 = (f32[8192]{0:T(1024)S(1)}, f32[8192]{0:T(1024)}, u32[]{:S(2)}) copy-start(f32[8192]{0:T(1024)} %get-tuple-element.910) | copy-start | bytes 98308 | tf_op jit(solution)/shard_map/while
  302.8 6.3 %copy-start.18 = (bf16[32,8192]{1,0:T(8,128)(2,1)S(1)}, bf16[32,8192]{1,0:T(8,128)(2,1)}, u32[]{:S(2)}) copy-start(bf16[32,8192]{1,0:T(8,128)(2,1)} %get-tuple-element.909) | copy-start | bytes 1572868 | tf_op jit(solution)/shard_map/while
  312.5 11.7 %collective-permute-start = (bf16[8,8192]{1,0:T(8,128)(2,1)}, bf16[8,8192]{1,0:T(8,128)(2,1)S(1)}, u32[]{:S(2)}, u32[]{:S(2)}) collective-permute-start(bf16[8,8192]{1,0:T(8,128)(2,1)} %add_convert_fusion.5), channel_id=1, source_target_pairs={{64,0},{96,32},{128,64},{160,96},{192,128},{224,160},{256,192},{28... | collective-permute-start | bytes 393224 | tf_op jit(solution)/shard_map/while/body/eval_jaxpr/ppermute | solution.py:14
  324.2 6.3 %copy-start.9 = (f32[8192]{0:T(1024)S(1)}, f32[8192]{0:T(1024)}, u32[]{:S(2)}) copy-start(f32[8192]{0:T(1024)} %get-tuple-element.910) | copy-start | bytes 98308 | tf_op jit(solution)/shard_map/while
  324.2 6.3 %copy-start.18 = (bf16[32,8192]{1,0:T(8,128)(2,1)S(1)}, bf16[32,8192]{1,0:T(8,128)(2,1)}, u32[]{:S(2)}) copy-start(bf16[32,8192]{1,0:T(8,128)(2,1)} %get-tuple-element.909) | copy-start | bytes 1572868 | tf_op jit(solution)/shard_map/while
  334.0 11.7 %collective-permute-start = (bf16[8,8192]{1,0:T(8,128)(2,1)}, bf16[8,8192]{1,0:T(8,128)(2,1)S(1)}, u32[]{:S(2)}, u32[]{:S(2)}) collective-permute-start(bf16[8,8192]{1,0:T(8,128)(2,1)} %add_convert_fusion.5), channel_id=1, source_target_pairs={{64,0},{96,32},{128,64},{160,96},{192,128},{224,160},{256,192},{28... | collective-permute-start | bytes 393224 | tf_op jit(solution)/shard_map/while/body/eval_jaxpr/ppermute | solution.py:14
  345.7 6.3 %copy-start.9 = (f32[8192]{0:T(1024)S(1)}, f32[8192]{0:T(1024)}, u32[]{:S(2)}) copy-start(f32[8192]{0:T(1024)} %get-tuple-element.910) | copy-start | bytes 98308 | tf_op jit(solution)/shard_map/while
  345.7 6.3 %copy-start.18 = (bf16[32,8192]{1,0:T(8,128)(2,1)S(1)}, bf16[32,8192]{1,0:T(8,128)(2,1)}, u32[]{:S(2)}) copy-start(bf16[32,8192]{1,0:T(8,128)(2,1)} %get-tuple-element.909) | copy-start | bytes 1572868 | tf_op jit(solution)/shard_map/while
  355.5 11.7 %collective-permute-start = (bf16[8,8192]{1,0:T(8,128)(2,1)}, bf16[8,8192]{1,0:T(8,128)(2,1)S(1)}, u32[]{:S(2)}, u32[]{:S(2)}) collective-permute-start(bf16[8,8192]{1,0:T(8,128)(2,1)} %add_convert_fusion.5), channel_id=1, source_target_pairs={{64,0},{96,32},{128,64},{160,96},{192,128},{224,160},{256,192},{28... | collective-permute-start | bytes 393224 | tf_op jit(solution)/shard_map/while/body/eval_jaxpr/ppermute | solution.py:14
  367.2 6.3 %copy-start.9 = (f32[8192]{0:T(1024)S(1)}, f32[8192]{0:T(1024)}, u32[]{:S(2)}) copy-start(f32[8192]{0:T(1024)} %get-tuple-element.910) | copy-start | bytes 98308 | tf_op jit(solution)/shard_map/while
  367.2 6.3 %copy-start.18 = (bf16[32,8192]{1,0:T(8,128)(2,1)S(1)}, bf16[32,8192]{1,0:T(8,128)(2,1)}, u32[]{:S(2)}) copy-start(bf16[32,8192]{1,0:T(8,128)(2,1)} %get-tuple-element.909) | copy-start | bytes 1572868 | tf_op jit(solution)/shard_map/while
  376.9 11.7 %collective-permute-start = (bf16[8,8192]{1,0:T(8,128)(2,1)}, bf16[8,8192]{1,0:T(8,128)(2,1)S(1)}, u32[]{:S(2)}, u32[]{:S(2)}) collective-permute-start(bf16[8,8192]{1,0:T(8,128)(2,1)} %add_convert_fusion.5), channel_id=1, source_target_pairs={{64,0},{96,32},{128,64},{160,96},{192,128},{224,160},{256,192},{28... | collective-permute-start | bytes 393224 | tf_op jit(solution)/shard_map/while/body/eval_jaxpr/ppermute | solution.py:14
  445.5 8.6 %collective-permute-start.3 = (f32[65,1024]{1,0:T(8,128)S(1)}, f32[65,1024]{1,0:T(8,128)S(1)}, u32[]{:S(2)}, u32[]{:S(2)}) collective-permute-start(f32[65,1024]{1,0:T(8,128)S(1)} %select_bitcast_fusion), channel_id=1, source_target_pairs={{0,32},{32,0},{64,96},{96,64},{128,160},{160,128},{192,224},{224,1... | collective-permute-start | bytes 798728 | tf_op jit(solution)/shard_map/ppermute | solution.py:19
  487.7 4.3 collective-permute-start.4
  493.2 6.6 %collective-permute-start.5 = (f32[]{:T(128)}, f32[]{:T(128)}, u32[]{:S(2)}, u32[]{:S(2)}) collective-permute-start(f32[]{:T(128)} %add.197), channel_id=1, source_target_pairs={{0,8},{4,12},{8,16},{12,20},{16,24},{20,28},{24,0},{28,4},{1,9},{5... | collective-permute-start | bytes 20 | tf_op jit(solution)/shard_map/ppermute | solution.py:134
  500.5 6.9 %collective-permute-start.6 = (f32[]{:T(128)}, f32[]{:T(128)}, u32[]{:S(2)}, u32[]{:S(2)}) collective-permute-start(f32[]{:T(128)} %add.198), channel_id=1, source_target_pairs={{0,16},{4,20},{8,24},{12,28},{16,0},{20,4},{24,8},{28,12},{1,17},{... | collective-permute-start | bytes 20 | tf_op jit(solution)/shard_map/ppermute | solution.py:134
  508.2 8.7 %collective-permute-start.7 = (f32[65,256]{1,0:T(8,128)S(1)}, f32[65,256]{1,0:T(8,128)S(1)}, u32[]{:S(2)}, u32[]{:S(2)}) collective-permute-start(f32[65,256]{1,0:T(8,128)S(1)} %get-tuple-element.668), channel_id=1, source_target_pairs={{0,1},{1,2},{2,3},{3,0},{4,5},{5,6},{6,7},{7,4},{8,9},{9,10},{10,1... | collective-permute-start | bytes 199688 | tf_op jit(solution)/shard_map/ppermute | solution.py:146
  510.6 7.8 %collective-permute-start.8 = (f32[65,256]{1,0:T(8,128)S(1)}, f32[65,256]{1,0:T(8,128)S(1)}, u32[]{:S(2)}, u32[]{:S(2)}) collective-permute-start(f32[65,256]{1,0:T(8,128)S(1)} %get-tuple-element.670), channel_id=1, source_target_pairs={{0,2},{1,3},{2,0},{3,1},{4,6},{5,7},{6,4},{7,5},{8,10},{9,11},{10,... | collective-permute-start | bytes 199688 | tf_op jit(solution)/shard_map/ppermute | solution.py:146
  515.0 7.5 %collective-permute-start.9 = (f32[65,256]{1,0:T(8,128)S(1)}, f32[65,256]{1,0:T(8,128)S(1)}, u32[]{:S(2)}, u32[]{:S(2)}) collective-permute-start(f32[65,256]{1,0:T(8,128)S(1)} %get-tuple-element.669), channel_id=1, source_target_pairs={{0,3},{1,0},{2,1},{3,2},{4,7},{5,4},{6,5},{7,6},{8,11},{9,8},{10,9... | collective-permute-start | bytes 199688 | tf_op jit(solution)/shard_map/ppermute | solution.py:146
  (193 other events, 623.6 us)
Sparse Core Ops, SparseCore 0:
  30.6 34.8 all-gather.1
  393.4 50.9 reduce-scatter.1

commit v7 on v4

--- a/solution.py
+++ b/solution.py
@@ -3,6 +3,8 @@
 import jax
 import jax.numpy as jnp
 from jax import lax
+from jax.experimental import pallas as pl
+from jax.experimental.pallas import tpu as pltpu
 from jax.sharding import PartitionSpec as P
 
 rows_per_block = 16
@@ -17,6 +19,63 @@
 def partner_swap(value, axis):
     count = lax.axis_size(axis)
     return lax.ppermute(value, axis, [(source, source ^ 1) for source in range(count)])
+
+
+def chain_kernel(flags, top_ref, incoming_ref, *refs):
+    (hidden_u, root_u, b_u, a_u, g_u, hidden_l, root_l, b_l, a_l, g_l,
+     source_ref, middle_ref, result_ref, low_u_ref, low_l_ref, pg_u_ref, pg_l_ref) = refs
+    source = jnp.where(flags[1] == 1, top_ref[...], incoming_ref[...])
+    source_ref[...] = source
+
+    def one_layer(upstream, hidden_ref, root_ref, b_ref, a_ref, g_ref, low_ref, pg_ref):
+        root = root_ref[...]
+        normalized = hidden_ref[...].astype(jnp.float32) / root
+        d_low = lax.dot_general(
+            upstream, b_ref[...], (((1,), (1,)), ((), ())), preferred_element_type=jnp.float32
+        ).astype(jnp.bfloat16)
+        normalized_gradient = jnp.dot(d_low, a_ref[...], preferred_element_type=jnp.float32)
+        input_gradient = normalized_gradient * g_ref[...]
+        mean = jnp.mean(input_gradient * normalized, axis=-1, keepdims=True)
+        low_ref[...] = d_low
+        pg_ref[...] = jnp.sum(normalized_gradient * normalized, axis=0, keepdims=True)
+        return (upstream.astype(jnp.float32) + (input_gradient - normalized * mean) / root).astype(
+            jnp.bfloat16
+        )
+
+    middle = one_layer(source, hidden_u, root_u, b_u, a_u, g_u, low_u_ref, pg_u_ref)
+    middle_ref[...] = middle
+    result_ref[...] = one_layer(middle, hidden_l, root_l, b_l, a_l, g_l, low_l_ref, pg_l_ref)
+
+
+def chain_step(flags, top, incoming, upper, lower, rows):
+    width = incoming.shape[1]
+    rank = upper[2].shape[0]
+    whole = lambda shape: pl.BlockSpec(shape, lambda i, f: (0, 0))
+    block = lambda last: pl.BlockSpec((rows, last), lambda i, f: (f[0], 0))
+    layer_specs = [block(width), block(1), whole((rank, width)), whole((rank, width)), whole((1, width))]
+    out_shape = [
+        jax.ShapeDtypeStruct((rows, width), jnp.bfloat16),
+        jax.ShapeDtypeStruct((rows, width), jnp.bfloat16),
+        jax.ShapeDtypeStruct((rows, width), jnp.bfloat16),
+        jax.ShapeDtypeStruct((rows, rank), jnp.bfloat16),
+        jax.ShapeDtypeStruct((rows, rank), jnp.bfloat16),
+        jax.ShapeDtypeStruct((1, width), jnp.float32),
+        jax.ShapeDtypeStruct((1, width), jnp.float32),
+    ]
+    out_specs = [whole((rows, width))] * 3 + [whole((rows, rank))] * 2 + [whole((1, width))] * 2
+    return pl.pallas_call(
+        chain_kernel,
+        out_shape=out_shape,
+        grid_spec=pltpu.PrefetchScalarGridSpec(
+            num_scalar_prefetch=1,
+            grid=(1,),
+            in_specs=[block(width), whole((rows, width))] + layer_specs + layer_specs,
+            out_specs=out_specs,
+        ),
+        cost_estimate=pl.CostEstimate(
+            flops=8 * rows * width * rank, transcendentals=0, bytes_accessed=4 * rank * width * 2 + 12 * rows * width
+        ),
+    )(flags, top, incoming, *upper, *lower)
 
 
 def on_device(acts, top_grad, a_rows, b_rows, gain):
@@ -47,6 +106,7 @@
     contract_last = (((1,), (1,)), ((), ()))
     contract_first = (((0,), (0,)), ((), ()))
     layers = []
+    operands = []
     for index in range(2):
         hidden = hidden_pair[index]
         a_full = whole[index, :rank]
@@ -61,51 +121,39 @@
             jnp.bfloat16
         )
         layers.append((hidden, inverse_root_mean, low, a_full, b_full, gain_float))
+        operands.append((hidden, inverse_root_mean, b_full, a_full, gain_float[None, :]))
     block_total = half_rows // rows_per_block
 
-    def layer_block(layer, source, block_offset, sums, inside):
+    def accumulate(layer, source, d_low, part_g, block_offset, sums, inside):
         hidden, inverse_root_mean, low, a_full, b_full, gain_float = layer
         sum_a, sum_b, sum_g = sums
         hidden_part = lax.dynamic_slice_in_dim(hidden, block_offset, rows_per_block, 0)
         r_part = lax.dynamic_slice_in_dim(inverse_root_mean, block_offset, rows_per_block, 0)
-        input_portion = hidden_part.astype(jnp.float32) / r_part
-        d_low = lax.dot_general(
-            source, b_full, contract_last, preferred_element_type=jnp.float32
-        ).astype(jnp.bfloat16)
-        normalized_gradient = jnp.dot(d_low, a_full, preferred_element_type=jnp.float32)
-        input_gradient = normalized_gradient * gain_float
-        hidden_gradient = (
-            source.astype(jnp.float32)
-            + (
-                input_gradient
-                - input_portion * jnp.mean(input_gradient * input_portion, axis=-1, keepdims=True)
-            )
-            / r_part
-        ).astype(jnp.bfloat16)
-        normalized_part = (input_portion * gain_float).astype(jnp.bfloat16)
+        normalized_part = ((hidden_part.astype(jnp.float32) / r_part) * gain_float).astype(jnp.bfloat16)
         low_part = lax.dynamic_slice_in_dim(low, block_offset, rows_per_block, 0)
         part_a = lax.dot_general(
             d_low, normalized_part, contract_first, preferred_element_type=jnp.float32
         )
         part_b = lax.dot_general(low_part, source, contract_first, preferred_element_type=jnp.float32)
-        part_g = jnp.sum(normalized_gradient * input_portion, axis=0)[None, :]
-        sums = (
+        return (
             sum_a + jnp.where(inside, part_a, 0.0),
             sum_b + jnp.where(inside, part_b, 0.0),
             sum_g + jnp.where(inside, part_g, 0.0),
         )
-        return hidden_gradient, sums
 
     def turn(turn_index, carry):
         incoming, upper_sums, lower_sums = carry
         block_index = turn_index - (pairs - 1 - pair)
         inside = jnp.logical_and(block_index >= 0, block_index < block_total)
-        block_offset = jnp.clip(block_index, 0, block_total - 1) * rows_per_block
-        top_block = lax.dynamic_slice_in_dim(top, block_offset, rows_per_block, 0)
-        source = jnp.where(pair == pairs - 1, top_block, incoming)
-        middle, upper_sums = layer_block(layers[0], source, block_offset, upper_sums, inside)
-        result, lower_sums = layer_block(layers[1], middle, block_offset, lower_sums, inside)
+        clipped = jnp.clip(block_index, 0, block_total - 1)
+        block_offset = clipped * rows_per_block
+        flags = jnp.stack([clipped, (pair == pairs - 1).astype(jnp.int32)]).astype(jnp.int32)
+        source, middle, result, low_u, low_l, pg_u, pg_l = chain_step(
+            flags, top, incoming, operands[0], operands[1], rows_per_block
+        )
         incoming = shifted(result, "pipe", -2)
+        upper_sums = accumulate(layers[0], source, low_u, pg_u, block_offset, upper_sums, inside)
+        lower_sums = accumulate(layers[1], middle, low_l, pg_l, block_offset, lower_sums, inside)
         return (incoming, upper_sums, lower_sums)
 
     def zero_sums():

time: 478 us -> 444 us (0.929)
  matrix products: 120 us -> 58.2 us
  Pallas kernels: 0 us -> 53.2 us
  other arithmetic: 59.1 us -> 21.7 us
  waiting for transfers between devices: 171 us -> 183 us
    dot_general x88 -> x44, matrix products: 117 us -> 54.5 us  [the longest x22 34.1 us: accumulate(): lax.dot_general(d_low, normalized_part, contract_first, preferred_element...]
    pallas_call x0 -> x11, Pallas kernels: none -> 53.2 us  [chain_step(): pl.pallas_call(chain_kernel, out_shape=out_shape, grid_spec=pltpu.Prefetc...]
    convert_element_type x22 -> x0, other arithmetic: 31.4 us -> none  [layer_block(): hidden_gradient = (source.astype(jnp.float32) + (input_gradient - input_p...]
    select_n x33 -> x0, other arithmetic: 12.2 us -> none  [the longest x11 12 us: turn(): source = jnp.where(pair == pairs - 1, top_block, incoming)]
    div x22 -> x0, local copies, waits for them, and re-layouts: 8.62 us -> none  [layer_block(): input_portion = hidden_part.astype(jnp.float32) / r_part]
    reduce_scatter x1, waiting for transfers between devices: 72.5 us -> 80.5 us  [on_device(): reduced = lax.psum_scatter(grads, 'seq', scatter_dimension=2, tiled=True)]
    dynamic_slice x0 -> x11, local copies, waits for them, and re-layouts: none -> 7.71 us  [accumulate(): lax.dynamic_slice_in_dim(inverse_root_mean, block_offset, rows_per_block, 0)]
    another operation x0 -> x11, other arithmetic: none -> 7.17 us  [turn(): jnp.stack([clipped, (pair == pairs - 1).astype(jnp.int32)])]
  transfers between devices with their start and end apart: 22 -> 22, of which waited for: 21 -> 21; matrix products, arithmetic and copies ran while one was open for 17% -> 16% of each run, Pallas kernels for 0% -> 0%
where the time goes in v7:
time: 444 us; the launch traced here: 441 us
  waiting for transfers between devices  183 us (41%)
  matrix products  58.2 us (13%)
  Pallas kernels  53.2 us (12%)
  blocking collectives  47.5 us (11%)
  starting transfers between devices  38.4 us (9%)
  other arithmetic  21.7 us (5%)
  between operations  18.2 us (4%)
  local copies, waits for them, and re-layouts  17.4 us (4%)
    reduce_scatter x1, waiting for transfers between devices, on_device(): reduced = lax.psum_scatter(grads, 'seq', scatter_dimension=2, tiled=True)  80.5 us
    pallas_call x11, Pallas kernels, chain_step(): pl.pallas_call(chain_kernel, out_shape=out_shape, grid_spec=pltpu.Prefetc...  53.2 us
    ppermute x11, waiting for transfers between devices, shifted(): lax.ppermute(value, axis, [(source, source + steps) for source in range(i...  52.2 us
    dot_general x22, matrix products, accumulate(): lax.dot_general(d_low, normalized_part, contract_first, preferred_element...  34.1 us
    psum x1, blocking collectives, on_device(): total = lax.psum(square, 'pipe')  31.9 us
    ppermute x3, waiting for transfers between devices, partner_swap(): lax.ppermute(value, axis, [(source, source ^ 1) for source in range(count)])  24.8 us
    dot_general x22, matrix products, accumulate(): lax.dot_general(low_part, source, contract_first, preferred_element_type=...  20.4 us
    all_gather x1, blocking collectives, on_device(): lax.all_gather(stacked, 'dp', axis=2, tiled=True)  15.7 us
  transfers between devices with their start and end apart: 22, of which 21 were waited for; matrix products, arithmetic and copies ran while one was open for 16% of the time, Pallas kernels for 0%

profile of v7, /device:TPU:6, one launch (start us, length us, event | category | flops | bytes accessed | tf_op | source)
XLA Modules:
  0.0 441.3 jit_solution(12099142261393415605)
XLA Ops:
  8.1 3.8 collective-permute-start.2
  12.0 2.0 collective-permute-done.2
  14.8 15.7 %all_gather.6 = bf16[2,65,1024]{2,1,0:T(8,128)(2,1)} all-gather(bf16[2,65,256]{2,1,0:T(8,128)(2,1)S(1)} %pad_maximum_fusion.1), channel_id=1, replica_groups=mesh['pipe'=16,'seq'=8,'dp'=4] {'dp'}, dimensions={2}, use_global_device_ids=true | all-gather | bytes 332800 | tf_op jit(solution)/shard_map/all_gather | solution.py:105
  30.5 2.3 dynamic-slice_bitcast_fusion
  32.8 1.9 collective-permute-start.1
  35.8 17.6 %collective-permute-done.1 = bf16[64,8192]{1,0:T(8,128)(2,1)} collective-permute-done((bf16[64,8192]{1,0:T(8,128)(2,1)}, bf16[64,8192]{1,0:T(8,128)(2,1)}, u32[]{:S(2)}, u32[]{:S(2)}) %collective-permute-start.1) | collective-permute-done | bytes 1048608 | tf_op jit(solution)/shard_map/ppermute | solution.py:21
  53.4 3.4 fusion.21
  57.0 8.5 %all-gather.2.cloned.1.call-done = bf16[2,65,8192]{2,1,0:T(8,128)(2,1)} async-done(((bf16[2,65,1024]{2,1,0:T(8,128)(2,1)}), bf16[2,65,8192]{2,1,0:T(8,128)(2,1)}) %all-gather.2.cloned.1.call-update) | async-done | bytes 2129936 | tf_op jit(solution)/shard_map/all_gather | solution.py:105
  66.5 1.9 convolution_convert_fusion
  68.5 1.8 convolution_convert_fusion.1
  71.0 2.9 slice_bitcast_fusion
  73.9 194.8 %while.28 = (s32[]{:T(128)}, bf16[16,8192]{1,0:T(8,128)(2,1)S(1)}, f32[32,8192]{1,0:T(8,128)}, f32[32,8192]{1,0:T(8,128)S(1)}, f32[1,8192]{1,0:T(1,128)}, /*inde...) while((s32[]{:T(128)}, bf16[16,8192]{1,0:T(8,128)(2,1)S(1)}, ...), condition=%wide.region_3.4_spmd.clone, body=%wide.region_2.3_spmd.clone.sunk | while | flops 71352328 | bytes 41701224 | solution.py:167
  74.6 4.8 %eval_jaxpr.7 = (bf16[16,8192]{1,0:T(8,128)(2,1)}, bf16[16,8192]{1,0:T(8,128)(2,1)}, bf16[16,8192]{1,0:T(8,128)(2,1)}, bf16[16,32]{1,0:T(8,128)(2,1)}, bf16[16,3...) custom-call(s32[2]{0:T(128)} %pad_add_fusion.2.flags, bf16[64,8192]{1,0:T(8,128)(2,1)} %get-tuple-element.992.top_ref, ...), custom_call_target="tpu_custom_call" | custom-call | flops 33554432 | bytes 3670016 | tf_op jit(solution)/shard_map/while/body/eval_jaxpr/pallas_call | solution.py:66
  83.5 1.6 fusion.51
  85.3 1.5 fusion.54
  86.9 9.6 %collective-permute-done = bf16[16,8192]{1,0:T(8,128)(2,1)S(1)} collective-permute-done((bf16[16,8192]{1,0:T(8,128)(2,1)}, bf16[16,8192]{1,0:T(8,128)(2,1)S(1)}, u32[]{:S(2)}, u32[]{:S(2)}) %collective-permute-start) | collective-permute-done | bytes 262176 | tf_op jit(solution)/shard_map/while/body/eval_jaxpr/ppermute | solution.py:16
  97.2 4.8 %eval_jaxpr.7 = (bf16[16,8192]{1,0:T(8,128)(2,1)}, bf16[16,8192]{1,0:T(8,128)(2,1)}, bf16[16,8192]{1,0:T(8,128)(2,1)}, bf16[16,32]{1,0:T(8,128)(2,1)}, bf16[16,3...) custom-call(s32[2]{0:T(128)} %pad_add_fusion.2.flags, bf16[64,8192]{1,0:T(8,128)(2,1)} %get-tuple-element.992.top_ref, ...), custom_call_target="tpu_custom_call" | custom-call | flops 33554432 | bytes 3670016 | tf_op jit(solution)/shard_map/while/body/eval_jaxpr/pallas_call | solution.py:66
  106.1 1.6 fusion.51
  107.9 1.5 fusion.54
  109.5 7.5 %collective-permute-done = bf16[16,8192]{1,0:T(8,128)(2,1)S(1)} collective-permute-done((bf16[16,8192]{1,0:T(8,128)(2,1)}, bf16[16,8192]{1,0:T(8,128)(2,1)S(1)}, u32[]{:S(2)}, u32[]{:S(2)}) %collective-permute-start) | collective-permute-done | bytes 262176 | tf_op jit(solution)/shard_map/while/body/eval_jaxpr/ppermute | solution.py:16
  117.7 4.8 %eval_jaxpr.7 = (bf16[16,8192]{1,0:T(8,128)(2,1)}, bf16[16,8192]{1,0:T(8,128)(2,1)}, bf16[16,8192]{1,0:T(8,128)(2,1)}, bf16[16,32]{1,0:T(8,128)(2,1)}, bf16[16,3...) custom-call(s32[2]{0:T(128)} %pad_add_fusion.2.flags, bf16[64,8192]{1,0:T(8,128)(2,1)} %get-tuple-element.992.top_ref, ...), custom_call_target="tpu_custom_call" | custom-call | flops 33554432 | bytes 3670016 | tf_op jit(solution)/shard_map/while/body/eval_jaxpr/pallas_call | solution.py:66
  126.6 1.6 fusion.51
  128.4 1.5 fusion.54
  130.0 5.0 %collective-permute-done = bf16[16,8192]{1,0:T(8,128)(2,1)S(1)} collective-permute-done((bf16[16,8192]{1,0:T(8,128)(2,1)}, bf16[16,8192]{1,0:T(8,128)(2,1)S(1)}, u32[]{:S(2)}, u32[]{:S(2)}) %collective-permute-start) | collective-permute-done | bytes 262176 | tf_op jit(solution)/shard_map/while/body/eval_jaxpr/ppermute | solution.py:16
  135.7 4.8 %eval_jaxpr.7 = (bf16[16,8192]{1,0:T(8,128)(2,1)}, bf16[16,8192]{1,0:T(8,128)(2,1)}, bf16[16,8192]{1,0:T(8,128)(2,1)}, bf16[16,32]{1,0:T(8,128)(2,1)}, bf16[16,3...) custom-call(s32[2]{0:T(128)} %pad_add_fusion.2.flags, bf16[64,8192]{1,0:T(8,128)(2,1)} %get-tuple-element.992.top_ref, ...), custom_call_target="tpu_custom_call" | custom-call | flops 33554432 | bytes 3670016 | tf_op jit(solution)/shard_map/while/body/eval_jaxpr/pallas_call | solution.py:66
  144.5 1.6 fusion.51
  147.9 4.1 collective-permute-done
  152.8 4.8 %eval_jaxpr.7 = (bf16[16,8192]{1,0:T(8,128)(2,1)}, bf16[16,8192]{1,0:T(8,128)(2,1)}, bf16[16,8192]{1,0:T(8,128)(2,1)}, bf16[16,32]{1,0:T(8,128)(2,1)}, bf16[16,3...) custom-call(s32[2]{0:T(128)} %pad_add_fusion.2.flags, bf16[64,8192]{1,0:T(8,128)(2,1)} %get-tuple-element.992.top_ref, ...), custom_call_target="tpu_custom_call" | custom-call | flops 33554432 | bytes 3670016 | tf_op jit(solution)/shard_map/while/body/eval_jaxpr/pallas_call | solution.py:66
  161.7 1.6 fusion.51
  165.0 3.2 collective-permute-done
  168.9 4.8 %eval_jaxpr.7 = (bf16[16,8192]{1,0:T(8,128)(2,1)}, bf16[16,8192]{1,0:T(8,128)(2,1)}, bf16[16,8192]{1,0:T(8,128)(2,1)}, bf16[16,32]{1,0:T(8,128)(2,1)}, bf16[16,3...) custom-call(s32[2]{0:T(128)} %pad_add_fusion.2.flags, bf16[64,8192]{1,0:T(8,128)(2,1)} %get-tuple-element.992.top_ref, ...), custom_call_target="tpu_custom_call" | custom-call | flops 33554432 | bytes 3670016 | tf_op jit(solution)/shard_map/while/body/eval_jaxpr/pallas_call | solution.py:66
  177.8 1.6 fusion.51
  181.2 6.4 %collective-permute-done = bf16[16,8192]{1,0:T(8,128)(2,1)S(1)} collective-permute-done((bf16[16,8192]{1,0:T(8,128)(2,1)}, bf16[16,8192]{1,0:T(8,128)(2,1)S(1)}, u32[]{:S(2)}, u32[]{:S(2)}) %collective-permute-start) | collective-permute-done | bytes 262176 | tf_op jit(solution)/shard_map/while/body/eval_jaxpr/ppermute | solution.py:16
  188.2 4.8 %eval_jaxpr.7 = (bf16[16,8192]{1,0:T(8,128)(2,1)}, bf16[16,8192]{1,0:T(8,128)(2,1)}, bf16[16,8192]{1,0:T(8,128)(2,1)}, bf16[16,32]{1,0:T(8,128)(2,1)}, bf16[16,3...) custom-call(s32[2]{0:T(128)} %pad_add_fusion.2.flags, bf16[64,8192]{1,0:T(8,128)(2,1)} %get-tuple-element.992.top_ref, ...), custom_call_target="tpu_custom_call" | custom-call | flops 33554432 | bytes 3670016 | tf_op jit(solution)/shard_map/while/body/eval_jaxpr/pallas_call | solution.py:66
  197.1 1.6 fusion.51
  200.5 2.9 collective-permute-done
  204.1 4.8 %eval_jaxpr.7 = (bf16[16,8192]{1,0:T(8,128)(2,1)}, bf16[16,8192]{1,0:T(8,128)(2,1)}, bf16[16,8192]{1,0:T(8,128)(2,1)}, bf16[16,32]{1,0:T(8,128)(2,1)}, bf16[16,3...) custom-call(s32[2]{0:T(128)} %pad_add_fusion.2.flags, bf16[64,8192]{1,0:T(8,128)(2,1)} %get-tuple-element.992.top_ref, ...), custom_call_target="tpu_custom_call" | custom-call | flops 33554432 | bytes 3670016 | tf_op jit(solution)/shard_map/while/body/eval_jaxpr/pallas_call | solution.py:66
  213.0 1.6 fusion.51
  216.4 3.2 collective-permute-done
  220.3 4.8 %eval_jaxpr.7 = (bf16[16,8192]{1,0:T(8,128)(2,1)}, bf16[16,8192]{1,0:T(8,128)(2,1)}, bf16[16,8192]{1,0:T(8,128)(2,1)}, bf16[16,32]{1,0:T(8,128)(2,1)}, bf16[16,3...) custom-call(s32[2]{0:T(128)} %pad_add_fusion.2.flags, bf16[64,8192]{1,0:T(8,128)(2,1)} %get-tuple-element.992.top_ref, ...), custom_call_target="tpu_custom_call" | custom-call | flops 33554432 | bytes 3670016 | tf_op jit(solution)/shard_map/while/body/eval_jaxpr/pallas_call | solution.py:66
  229.2 1.6 fusion.51
  232.6 4.1 collective-permute-done
  237.4 4.8 %eval_jaxpr.7 = (bf16[16,8192]{1,0:T(8,128)(2,1)}, bf16[16,8192]{1,0:T(8,128)(2,1)}, bf16[16,8192]{1,0:T(8,128)(2,1)}, bf16[16,32]{1,0:T(8,128)(2,1)}, bf16[16,3...) custom-call(s32[2]{0:T(128)} %pad_add_fusion.2.flags, bf16[64,8192]{1,0:T(8,128)(2,1)} %get-tuple-element.992.top_ref, ...), custom_call_target="tpu_custom_call" | custom-call | flops 33554432 | bytes 3670016 | tf_op jit(solution)/shard_map/while/body/eval_jaxpr/pallas_call | solution.py:66
  246.3 1.6 fusion.51
  249.6 3.0 collective-permute-done
  253.3 4.8 %eval_jaxpr.7 = (bf16[16,8192]{1,0:T(8,128)(2,1)}, bf16[16,8192]{1,0:T(8,128)(2,1)}, bf16[16,8192]{1,0:T(8,128)(2,1)}, bf16[16,32]{1,0:T(8,128)(2,1)}, bf16[16,3...) custom-call(s32[2]{0:T(128)} %pad_add_fusion.2.flags, bf16[64,8192]{1,0:T(8,128)(2,1)} %get-tuple-element.992.top_ref, ...), custom_call_target="tpu_custom_call" | custom-call | flops 33554432 | bytes 3670016 | tf_op jit(solution)/shard_map/while/body/eval_jaxpr/pallas_call | solution.py:66
  262.2 1.6 fusion.51
  265.6 3.2 collective-permute-done
  268.8 1.6 maximum_bitcast_fusion
  270.9 2.6 pad_maximum_fusion
  273.5 80.5 %reduce-scatter.2.cloned.1.call-done = f32[2,65,1024]{2,1,0:T(8,128)} async-done(((f32[2,65,8192]{2,1,0:T(8,128)}), f32[2,65,1024]{2,1,0:T(8,128)}) %reduce-scatter.2.cloned.1.call-update) | async-done | bytes 532496 | tf_op jit(solution)/shard_map/reduce_scatter | solution.py:171
  355.1 3.4 collective-permute-start.3
  358.5 5.2 %collective-permute-done.3 = f32[65,1024]{1,0:T(8,128)S(1)} collective-permute-done((f32[65,1024]{1,0:T(8,128)S(1)}, f32[65,1024]{1,0:T(8,128)S(1)}, u32[]{:S(2)}, u32[]{:S(2)}) %collective-permute-start.3) | collective-permute-done | bytes 266272 | tf_op jit(solution)/shard_map/ppermute | solution.py:21
  363.7 1.7 multiply_reduce_fusion
  365.5 31.9 %psum.7 = f32[]{:T(128)} all-reduce(f32[]{:T(128)} %get-tuple-element.714), channel_id=1, replica_groups=mesh['pipe'=16,'seq'=8,'dp'=4] {'pipe'}, use_global_device_ids=true, to_apply=%region_6.7 | all-reduce | flops 1 | bytes 8 | tf_op jit(solution)/shard_map/psum | solution.py:178
  397.3 4.3 collective-permute-done.4
  402.9 3.2 collective-permute-start.5
  406.1 3.4 collective-permute-done.5
  410.2 3.2 collective-permute-start.6
  413.4 3.7 collective-permute-done.6
  417.9 2.5 collective-permute-start.7
  420.4 4.3 collective-permute-start.8
  424.7 1.9 collective-permute-start.9
  428.1 4.0 collective-permute-done.9
  (537 shorter events, 73.1 us)
Async XLA Ops:
  7.2 27.6 %copy-start = (bf16[1,128,8192]{2,1,0:T(8,128)(2,1)S(1)}, bf16[1,128,8192]{2,1,0:T(8,128)(2,1)}, u32[]{:S(2)}) copy-start(bf16[1,128,8192]{2,1,0:T(8,128)(2,1)} %param.8) | copy-start | bytes 6291460
  7.2 58.3 %all-gather.2.cloned.1.call-start = ((), (), s32[]{:S(2)}) async-start(), calls=%async_computation.1 | async-start | bytes 2654208 | tf_op jit(solution)/shard_map/all_gather | solution.py:105
  8.1 5.8 %collective-permute-start.2 = (bf16[65,256]{1,0:T(8,128)(2,1)S(1)}, bf16[65,256]{1,0:T(8,128)(2,1)S(1)}, u32[]{:S(2)}, u32[]{:S(2)}) collective-permute-start(bf16[65,256]{1,0:T(8,128)(2,1)S(1)} %pad_maximum_fusion.2), channel_id=1, source_target_pairs={{0,32},{32,0},{64,96},{96,64},{128,160},{160,128},{192,224},{224,1... | collective-permute-start | bytes 99848 | tf_op jit(solution)/shard_map/ppermute | solution.py:21
  30.4 323.6 %reduce-scatter.2.cloned.1.call-start = ((), (), s32[]{:S(2)}) async-start(), calls=%async_computation.2 | async-start | bytes 5308416 | tf_op jit(solution)/shard_map/reduce_scatter | solution.py:171
  32.8 20.6 %collective-permute-start.1 = (bf16[64,8192]{1,0:T(8,128)(2,1)}, bf16[64,8192]{1,0:T(8,128)(2,1)}, u32[]{:S(2)}, u32[]{:S(2)}) collective-permute-start(bf16[64,8192]{1,0:T(8,128)(2,1)} %dynamic-slice_bitcast_fusion), channel_id=1, source_target_pairs={{0,32},{32,0},{64,96},{96,64},{128,160},{160,128},{192,224},{224,1... | collective-permute-start | bytes 3145736 | tf_op jit(solution)/shard_map/ppermute | solution.py:21
  34.8 18.6 %copy-start.5 = (bf16[1,1,128,8192]{3,2,1,0:T(8,128)(2,1)S(1)}, bf16[1,1,128,8192]{3,2,1,0:T(8,128)(2,1)}, u32[]{:S(2)}) copy-start(bf16[1,1,128,8192]{3,2,1,0:T(8,128)(2,1)} %param.7) | copy-start | bytes 6291460
  79.5 17.1 %collective-permute-start = (bf16[16,8192]{1,0:T(8,128)(2,1)}, bf16[16,8192]{1,0:T(8,128)(2,1)S(1)}, u32[]{:S(2)}, u32[]{:S(2)}) collective-permute-start(bf16[16,8192]{1,0:T(8,128)(2,1)} %get-tuple-element.909), channel_id=1, source_target_pairs={{64,0},{96,32},{128,64},{160,96},{192,128},{224,160},{256,192},{28... | collective-permute-start | bytes 786440 | tf_op jit(solution)/shard_map/while/body/eval_jaxpr/ppermute | solution.py:16
  83.5 3.4 copy-start.2
  85.1 11.4 %copy-start.12 = (f32[32,8192]{1,0:T(8,128)}, f32[32,8192]{1,0:T(8,128)S(1)}, u32[]{:S(2)}) copy-start(f32[32,8192]{1,0:T(8,128)S(1)} %fusion.51) | copy-start | bytes 3145732 | tf_op jit(solution)/shard_map/while
  85.3 11.3 %copy-start.7 = (f32[1,8192]{1,0:T(1,128)}, f32[1,8192]{1,0:T(1,128)S(1)}, u32[]{:S(2)}) copy-start(f32[1,8192]{1,0:T(1,128)S(1)} %get-tuple-element.986) | copy-start | bytes 98308 | tf_op jit(solution)/shard_map/while
  85.3 11.3 %copy-start.9 = (f32[1,8192]{1,0:T(1,128)}, f32[1,8192]{1,0:T(1,128)S(1)}, u32[]{:S(2)}) copy-start(f32[1,8192]{1,0:T(1,128)S(1)} %get-tuple-element.989) | copy-start | bytes 98308 | tf_op jit(solution)/shard_map/while
  86.9 9.6 %copy-start.14 = (f32[32,8192]{1,0:T(8,128)}, f32[32,8192]{1,0:T(8,128)S(1)}, u32[]{:S(2)}) copy-start(f32[32,8192]{1,0:T(8,128)S(1)} %fusion.54) | copy-start | bytes 3145732 | tf_op jit(solution)/shard_map/while
  102.0 14.9 %collective-permute-start = (bf16[16,8192]{1,0:T(8,128)(2,1)}, bf16[16,8192]{1,0:T(8,128)(2,1)S(1)}, u32[]{:S(2)}, u32[]{:S(2)}) collective-permute-start(bf16[16,8192]{1,0:T(8,128)(2,1)} %get-tuple-element.909), channel_id=1, source_target_pairs={{64,0},{96,32},{128,64},{160,96},{192,128},{224,160},{256,192},{28... | collective-permute-start | bytes 786440 | tf_op jit(solution)/shard_map/while/body/eval_jaxpr/ppermute | solution.py:16
  107.7 9.3 %copy-start.12 = (f32[32,8192]{1,0:T(8,128)}, f32[32,8192]{1,0:T(8,128)S(1)}, u32[]{:S(2)}) copy-start(f32[32,8192]{1,0:T(8,128)S(1)} %fusion.51) | copy-start | bytes 3145732 | tf_op jit(solution)/shard_map/while
  107.9 9.1 %copy-start.7 = (f32[1,8192]{1,0:T(1,128)}, f32[1,8192]{1,0:T(1,128)S(1)}, u32[]{:S(2)}) copy-start(f32[1,8192]{1,0:T(1,128)S(1)} %get-tuple-element.986) | copy-start | bytes 98308 | tf_op jit(solution)/shard_map/while
  107.9 9.1 %copy-start.9 = (f32[1,8192]{1,0:T(1,128)}, f32[1,8192]{1,0:T(1,128)S(1)}, u32[]{:S(2)}) copy-start(f32[1,8192]{1,0:T(1,128)S(1)} %get-tuple-element.989) | copy-start | bytes 98308 | tf_op jit(solution)/shard_map/while
  109.5 7.5 %copy-start.14 = (f32[32,8192]{1,0:T(8,128)}, f32[32,8192]{1,0:T(8,128)S(1)}, u32[]{:S(2)}) copy-start(f32[32,8192]{1,0:T(8,128)S(1)} %fusion.54) | copy-start | bytes 3145732 | tf_op jit(solution)/shard_map/while
  122.5 12.4 %collective-permute-start = (bf16[16,8192]{1,0:T(8,128)(2,1)}, bf16[16,8192]{1,0:T(8,128)(2,1)S(1)}, u32[]{:S(2)}, u32[]{:S(2)}) collective-permute-start(bf16[16,8192]{1,0:T(8,128)(2,1)} %get-tuple-element.909), channel_id=1, source_target_pairs={{64,0},{96,32},{128,64},{160,96},{192,128},{224,160},{256,192},{28... | collective-permute-start | bytes 786440 | tf_op jit(solution)/shard_map/while/body/eval_jaxpr/ppermute | solution.py:16
  128.2 6.8 %copy-start.12 = (f32[32,8192]{1,0:T(8,128)}, f32[32,8192]{1,0:T(8,128)S(1)}, u32[]{:S(2)}) copy-start(f32[32,8192]{1,0:T(8,128)S(1)} %fusion.51) | copy-start | bytes 3145732 | tf_op jit(solution)/shard_map/while
  128.3 6.6 %copy-start.7 = (f32[1,8192]{1,0:T(1,128)}, f32[1,8192]{1,0:T(1,128)S(1)}, u32[]{:S(2)}) copy-start(f32[1,8192]{1,0:T(1,128)S(1)} %get-tuple-element.986) | copy-start | bytes 98308 | tf_op jit(solution)/shard_map/while
  128.3 6.6 %copy-start.9 = (f32[1,8192]{1,0:T(1,128)}, f32[1,8192]{1,0:T(1,128)S(1)}, u32[]{:S(2)}) copy-start(f32[1,8192]{1,0:T(1,128)S(1)} %get-tuple-element.989) | copy-start | bytes 98308 | tf_op jit(solution)/shard_map/while
  129.9 5.0 %copy-start.14 = (f32[32,8192]{1,0:T(8,128)}, f32[32,8192]{1,0:T(8,128)S(1)}, u32[]{:S(2)}) copy-start(f32[32,8192]{1,0:T(8,128)S(1)} %fusion.54) | copy-start | bytes 3145732 | tf_op jit(solution)/shard_map/while
  140.5 11.6 %collective-permute-start = (bf16[16,8192]{1,0:T(8,128)(2,1)}, bf16[16,8192]{1,0:T(8,128)(2,1)S(1)}, u32[]{:S(2)}, u32[]{:S(2)}) collective-permute-start(bf16[16,8192]{1,0:T(8,128)(2,1)} %get-tuple-element.909), channel_id=1, source_target_pairs={{64,0},{96,32},{128,64},{160,96},{192,128},{224,160},{256,192},{28... | collective-permute-start | bytes 786440 | tf_op jit(solution)/shard_map/while/body/eval_jaxpr/ppermute | solution.py:16
  146.1 5.9 %copy-start.12 = (f32[32,8192]{1,0:T(8,128)}, f32[32,8192]{1,0:T(8,128)S(1)}, u32[]{:S(2)}) copy-start(f32[32,8192]{1,0:T(8,128)S(1)} %fusion.51) | copy-start | bytes 3145732 | tf_op jit(solution)/shard_map/while
  146.3 5.8 %copy-start.7 = (f32[1,8192]{1,0:T(1,128)}, f32[1,8192]{1,0:T(1,128)S(1)}, u32[]{:S(2)}) copy-start(f32[1,8192]{1,0:T(1,128)S(1)} %get-tuple-element.986) | copy-start | bytes 98308 | tf_op jit(solution)/shard_map/while
  146.3 5.8 %copy-start.9 = (f32[1,8192]{1,0:T(1,128)}, f32[1,8192]{1,0:T(1,128)S(1)}, u32[]{:S(2)}) copy-start(f32[1,8192]{1,0:T(1,128)S(1)} %get-tuple-element.989) | copy-start | bytes 98308 | tf_op jit(solution)/shard_map/while
  147.9 4.2 copy-start.14
  157.6 10.6 %collective-permute-start = (bf16[16,8192]{1,0:T(8,128)(2,1)}, bf16[16,8192]{1,0:T(8,128)(2,1)S(1)}, u32[]{:S(2)}, u32[]{:S(2)}) collective-permute-start(bf16[16,8192]{1,0:T(8,128)(2,1)} %get-tuple-element.909), channel_id=1, source_target_pairs={{64,0},{96,32},{128,64},{160,96},{192,128},{224,160},{256,192},{28... | collective-permute-start | bytes 786440 | tf_op jit(solution)/shard_map/while/body/eval_jaxpr/ppermute | solution.py:16
  163.2 5.0 %copy-start.12 = (f32[32,8192]{1,0:T(8,128)}, f32[32,8192]{1,0:T(8,128)S(1)}, u32[]{:S(2)}) copy-start(f32[32,8192]{1,0:T(8,128)S(1)} %fusion.51) | copy-start | bytes 3145732 | tf_op jit(solution)/shard_map/while
  163.4 4.8 %copy-start.7 = (f32[1,8192]{1,0:T(1,128)}, f32[1,8192]{1,0:T(1,128)S(1)}, u32[]{:S(2)}) copy-start(f32[1,8192]{1,0:T(1,128)S(1)} %get-tuple-element.986) | copy-start | bytes 98308 | tf_op jit(solution)/shard_map/while
  163.4 4.8 %copy-start.9 = (f32[1,8192]{1,0:T(1,128)}, f32[1,8192]{1,0:T(1,128)S(1)}, u32[]{:S(2)}) copy-start(f32[1,8192]{1,0:T(1,128)S(1)} %get-tuple-element.989) | copy-start | bytes 98308 | tf_op jit(solution)/shard_map/while
  173.8 13.8 %collective-permute-start = (bf16[16,8192]{1,0:T(8,128)(2,1)}, bf16[16,8192]{1,0:T(8,128)(2,1)S(1)}, u32[]{:S(2)}, u32[]{:S(2)}) collective-permute-start(bf16[16,8192]{1,0:T(8,128)(2,1)} %get-tuple-element.909), channel_id=1, source_target_pairs={{64,0},{96,32},{128,64},{160,96},{192,128},{224,160},{256,192},{28... | collective-permute-start | bytes 786440 | tf_op jit(solution)/shard_map/while/body/eval_jaxpr/ppermute | solution.py:16
  179.4 8.2 %copy-start.12 = (f32[32,8192]{1,0:T(8,128)}, f32[32,8192]{1,0:T(8,128)S(1)}, u32[]{:S(2)}) copy-start(f32[32,8192]{1,0:T(8,128)S(1)} %fusion.51) | copy-start | bytes 3145732 | tf_op jit(solution)/shard_map/while
  179.6 8.0 %copy-start.7 = (f32[1,8192]{1,0:T(1,128)}, f32[1,8192]{1,0:T(1,128)S(1)}, u32[]{:S(2)}) copy-start(f32[1,8192]{1,0:T(1,128)S(1)} %get-tuple-element.986) | copy-start | bytes 98308 | tf_op jit(solution)/shard_map/while
  179.6 8.0 %copy-start.9 = (f32[1,8192]{1,0:T(1,128)}, f32[1,8192]{1,0:T(1,128)S(1)}, u32[]{:S(2)}) copy-start(f32[1,8192]{1,0:T(1,128)S(1)} %get-tuple-element.989) | copy-start | bytes 98308 | tf_op jit(solution)/shard_map/while
  181.2 6.4 %copy-start.14 = (f32[32,8192]{1,0:T(8,128)}, f32[32,8192]{1,0:T(8,128)S(1)}, u32[]{:S(2)}) copy-start(f32[32,8192]{1,0:T(8,128)S(1)} %fusion.54) | copy-start | bytes 3145732 | tf_op jit(solution)/shard_map/while
  193.1 10.3 %collective-permute-start = (bf16[16,8192]{1,0:T(8,128)(2,1)}, bf16[16,8192]{1,0:T(8,128)(2,1)S(1)}, u32[]{:S(2)}, u32[]{:S(2)}) collective-permute-start(bf16[16,8192]{1,0:T(8,128)(2,1)} %get-tuple-element.909), channel_id=1, source_target_pairs={{64,0},{96,32},{128,64},{160,96},{192,128},{224,160},{256,192},{28... | collective-permute-start | bytes 786440 | tf_op jit(solution)/shard_map/while/body/eval_jaxpr/ppermute | solution.py:16
  198.7 4.7 %copy-start.12 = (f32[32,8192]{1,0:T(8,128)}, f32[32,8192]{1,0:T(8,128)S(1)}, u32[]{:S(2)}) copy-start(f32[32,8192]{1,0:T(8,128)S(1)} %fusion.51) | copy-start | bytes 3145732 | tf_op jit(solution)/shard_map/while
  198.9 4.5 %copy-start.7 = (f32[1,8192]{1,0:T(1,128)}, f32[1,8192]{1,0:T(1,128)S(1)}, u32[]{:S(2)}) copy-start(f32[1,8192]{1,0:T(1,128)S(1)} %get-tuple-element.986) | copy-start | bytes 98308 | tf_op jit(solution)/shard_map/while
  198.9 4.5 %copy-start.9 = (f32[1,8192]{1,0:T(1,128)}, f32[1,8192]{1,0:T(1,128)S(1)}, u32[]{:S(2)}) copy-start(f32[1,8192]{1,0:T(1,128)S(1)} %get-tuple-element.989) | copy-start | bytes 98308 | tf_op jit(solution)/shard_map/while
  208.9 10.7 %collective-permute-start = (bf16[16,8192]{1,0:T(8,128)(2,1)}, bf16[16,8192]{1,0:T(8,128)(2,1)S(1)}, u32[]{:S(2)}, u32[]{:S(2)}) collective-permute-start(bf16[16,8192]{1,0:T(8,128)(2,1)} %get-tuple-element.909), channel_id=1, source_target_pairs={{64,0},{96,32},{128,64},{160,96},{192,128},{224,160},{256,192},{28... | collective-permute-start | bytes 786440 | tf_op jit(solution)/shard_map/while/body/eval_jaxpr/ppermute | solution.py:16
  214.6 5.0 %copy-start.12 = (f32[32,8192]{1,0:T(8,128)}, f32[32,8192]{1,0:T(8,128)S(1)}, u32[]{:S(2)}) copy-start(f32[32,8192]{1,0:T(8,128)S(1)} %fusion.51) | copy-start | bytes 3145732 | tf_op jit(solution)/shard_map/while
  214.7 4.9 %copy-start.7 = (f32[1,8192]{1,0:T(1,128)}, f32[1,8192]{1,0:T(1,128)S(1)}, u32[]{:S(2)}) copy-start(f32[1,8192]{1,0:T(1,128)S(1)} %get-tuple-element.986) | copy-start | bytes 98308 | tf_op jit(solution)/shard_map/while
  214.7 4.9 %copy-start.9 = (f32[1,8192]{1,0:T(1,128)}, f32[1,8192]{1,0:T(1,128)S(1)}, u32[]{:S(2)}) copy-start(f32[1,8192]{1,0:T(1,128)S(1)} %get-tuple-element.989) | copy-start | bytes 98308 | tf_op jit(solution)/shard_map/while
  225.1 11.6 %collective-permute-start = (bf16[16,8192]{1,0:T(8,128)(2,1)}, bf16[16,8192]{1,0:T(8,128)(2,1)S(1)}, u32[]{:S(2)}, u32[]{:S(2)}) collective-permute-start(bf16[16,8192]{1,0:T(8,128)(2,1)} %get-tuple-element.909), channel_id=1, source_target_pairs={{64,0},{96,32},{128,64},{160,96},{192,128},{224,160},{256,192},{28... | collective-permute-start | bytes 786440 | tf_op jit(solution)/shard_map/while/body/eval_jaxpr/ppermute | solution.py:16
  230.8 5.9 %copy-start.12 = (f32[32,8192]{1,0:T(8,128)}, f32[32,8192]{1,0:T(8,128)S(1)}, u32[]{:S(2)}) copy-start(f32[32,8192]{1,0:T(8,128)S(1)} %fusion.51) | copy-start | bytes 3145732 | tf_op jit(solution)/shard_map/while
  230.9 5.7 %copy-start.7 = (f32[1,8192]{1,0:T(1,128)}, f32[1,8192]{1,0:T(1,128)S(1)}, u32[]{:S(2)}) copy-start(f32[1,8192]{1,0:T(1,128)S(1)} %get-tuple-element.986) | copy-start | bytes 98308 | tf_op jit(solution)/shard_map/while
  230.9 5.7 %copy-start.9 = (f32[1,8192]{1,0:T(1,128)}, f32[1,8192]{1,0:T(1,128)S(1)}, u32[]{:S(2)}) copy-start(f32[1,8192]{1,0:T(1,128)S(1)} %get-tuple-element.989) | copy-start | bytes 98308 | tf_op jit(solution)/shard_map/while
  232.6 4.1 copy-start.14
  242.2 10.4 %collective-permute-start = (bf16[16,8192]{1,0:T(8,128)(2,1)}, bf16[16,8192]{1,0:T(8,128)(2,1)S(1)}, u32[]{:S(2)}, u32[]{:S(2)}) collective-permute-start(bf16[16,8192]{1,0:T(8,128)(2,1)} %get-tuple-element.909), channel_id=1, source_target_pairs={{64,0},{96,32},{128,64},{160,96},{192,128},{224,160},{256,192},{28... | collective-permute-start | bytes 786440 | tf_op jit(solution)/shard_map/while/body/eval_jaxpr/ppermute | solution.py:16
  247.8 4.8 %copy-start.12 = (f32[32,8192]{1,0:T(8,128)}, f32[32,8192]{1,0:T(8,128)S(1)}, u32[]{:S(2)}) copy-start(f32[32,8192]{1,0:T(8,128)S(1)} %fusion.51) | copy-start | bytes 3145732 | tf_op jit(solution)/shard_map/while
  248.0 4.6 %copy-start.7 = (f32[1,8192]{1,0:T(1,128)}, f32[1,8192]{1,0:T(1,128)S(1)}, u32[]{:S(2)}) copy-start(f32[1,8192]{1,0:T(1,128)S(1)} %get-tuple-element.986) | copy-start | bytes 98308 | tf_op jit(solution)/shard_map/while
  248.0 4.6 %copy-start.9 = (f32[1,8192]{1,0:T(1,128)}, f32[1,8192]{1,0:T(1,128)S(1)}, u32[]{:S(2)}) copy-start(f32[1,8192]{1,0:T(1,128)S(1)} %get-tuple-element.989) | copy-start | bytes 98308 | tf_op jit(solution)/shard_map/while
  258.2 10.6 %collective-permute-start = (bf16[16,8192]{1,0:T(8,128)(2,1)}, bf16[16,8192]{1,0:T(8,128)(2,1)S(1)}, u32[]{:S(2)}, u32[]{:S(2)}) collective-permute-start(bf16[16,8192]{1,0:T(8,128)(2,1)} %get-tuple-element.909), channel_id=1, source_target_pairs={{64,0},{96,32},{128,64},{160,96},{192,128},{224,160},{256,192},{28... | collective-permute-start | bytes 786440 | tf_op jit(solution)/shard_map/while/body/eval_jaxpr/ppermute | solution.py:16
  263.8 4.9 %copy-start.12 = (f32[32,8192]{1,0:T(8,128)}, f32[32,8192]{1,0:T(8,128)S(1)}, u32[]{:S(2)}) copy-start(f32[32,8192]{1,0:T(8,128)S(1)} %fusion.51) | copy-start | bytes 3145732 | tf_op jit(solution)/shard_map/while
  264.0 4.8 %copy-start.7 = (f32[1,8192]{1,0:T(1,128)}, f32[1,8192]{1,0:T(1,128)S(1)}, u32[]{:S(2)}) copy-start(f32[1,8192]{1,0:T(1,128)S(1)} %get-tuple-element.986) | copy-start | bytes 98308 | tf_op jit(solution)/shard_map/while
  264.0 4.8 %copy-start.9 = (f32[1,8192]{1,0:T(1,128)}, f32[1,8192]{1,0:T(1,128)S(1)}, u32[]{:S(2)}) copy-start(f32[1,8192]{1,0:T(1,128)S(1)} %get-tuple-element.989) | copy-start | bytes 98308 | tf_op jit(solution)/shard_map/while
  355.1 8.6 %collective-permute-start.3 = (f32[65,1024]{1,0:T(8,128)S(1)}, f32[65,1024]{1,0:T(8,128)S(1)}, u32[]{:S(2)}, u32[]{:S(2)}) collective-permute-start(f32[65,1024]{1,0:T(8,128)S(1)} %select_bitcast_fusion), channel_id=1, source_target_pairs={{0,32},{32,0},{64,96},{96,64},{128,160},{160,128},{192,224},{224,1... | collective-permute-start | bytes 798728 | tf_op jit(solution)/shard_map/ppermute | solution.py:21
  397.3 4.3 collective-permute-start.4
  402.9 6.6 %collective-permute-start.5 = (f32[]{:T(128)}, f32[]{:T(128)}, u32[]{:S(2)}, u32[]{:S(2)}) collective-permute-start(f32[]{:T(128)} %add.178), channel_id=1, source_target_pairs={{0,8},{4,12},{8,16},{12,20},{16,24},{20,28},{24,0},{28,4},{1,9},{5... | collective-permute-start | bytes 20 | tf_op jit(solution)/shard_map/ppermute | solution.py:182
  410.2 6.9 %collective-permute-start.6 = (f32[]{:T(128)}, f32[]{:T(128)}, u32[]{:S(2)}, u32[]{:S(2)}) collective-permute-start(f32[]{:T(128)} %add.179), channel_id=1, source_target_pairs={{0,16},{4,20},{8,24},{12,28},{16,0},{20,4},{24,8},{28,12},{1,17},{... | collective-permute-start | bytes 20 | tf_op jit(solution)/shard_map/ppermute | solution.py:182
  417.9 8.7 %collective-permute-start.7 = (f32[65,256]{1,0:T(8,128)S(1)}, f32[65,256]{1,0:T(8,128)S(1)}, u32[]{:S(2)}, u32[]{:S(2)}) collective-permute-start(f32[65,256]{1,0:T(8,128)S(1)} %get-tuple-element.734), channel_id=1, source_target_pairs={{0,1},{1,2},{2,3},{3,0},{4,5},{5,6},{6,7},{7,4},{8,9},{9,10},{10,1... | collective-permute-start | bytes 199688 | tf_op jit(solution)/shard_map/ppermute | solution.py:194
  420.4 7.8 %collective-permute-start.8 = (f32[65,256]{1,0:T(8,128)S(1)}, f32[65,256]{1,0:T(8,128)S(1)}, u32[]{:S(2)}, u32[]{:S(2)}) collective-permute-start(f32[65,256]{1,0:T(8,128)S(1)} %get-tuple-element.736), channel_id=1, source_target_pairs={{0,2},{1,3},{2,0},{3,1},{4,6},{5,7},{6,4},{7,5},{8,10},{9,11},{10,... | collective-permute-start | bytes 199688 | tf_op jit(solution)/shard_map/ppermute | solution.py:194
  424.7 7.5 %collective-permute-start.9 = (f32[65,256]{1,0:T(8,128)S(1)}, f32[65,256]{1,0:T(8,128)S(1)}, u32[]{:S(2)}, u32[]{:S(2)}) collective-permute-start(f32[65,256]{1,0:T(8,128)S(1)} %get-tuple-element.735), channel_id=1, source_target_pairs={{0,3},{1,0},{2,1},{3,2},{4,7},{5,4},{6,5},{7,6},{8,11},{9,8},{10,9... | collective-permute-start | bytes 199688 | tf_op jit(solution)/shard_map/ppermute | solution.py:194
  (174 other events, 372.3 us)
Sparse Core Ops, SparseCore 0:
  30.6 34.8 all-gather.1
  273.6 80.3 reduce-scatter.1

commit v8 on v7

--- a/solution.py
+++ b/solution.py
@@ -24,12 +24,15 @@
 def chain_kernel(flags, top_ref, incoming_ref, *refs):
     (hidden_u, root_u, b_u, a_u, g_u, hidden_l, root_l, b_l, a_l, g_l,
      source_ref, middle_ref, result_ref, low_u_ref, low_l_ref, pg_u_ref, pg_l_ref) = refs
-    source = jnp.where(flags[1] == 1, top_ref[...], incoming_ref[...])
+    rows = incoming_ref.shape[0]
+    offset = pl.multiple_of(flags[0] * rows, rows)
+    window = pl.ds(offset, rows)
+    source = jnp.where(flags[1] == 1, top_ref[window, :], incoming_ref[...])
     source_ref[...] = source
 
     def one_layer(upstream, hidden_ref, root_ref, b_ref, a_ref, g_ref, low_ref, pg_ref):
-        root = root_ref[...]
-        normalized = hidden_ref[...].astype(jnp.float32) / root
+        root = root_ref[window, :]
+        normalized = hidden_ref[window, :].astype(jnp.float32) / root
         d_low = lax.dot_general(
             upstream, b_ref[...], (((1,), (1,)), ((), ())), preferred_element_type=jnp.float32
         ).astype(jnp.bfloat16)
@@ -50,9 +53,7 @@
 def chain_step(flags, top, incoming, upper, lower, rows):
     width = incoming.shape[1]
     rank = upper[2].shape[0]
-    whole = lambda shape: pl.BlockSpec(shape, lambda i, f: (0, 0))
-    block = lambda last: pl.BlockSpec((rows, last), lambda i, f: (f[0], 0))
-    layer_specs = [block(width), block(1), whole((rank, width)), whole((rank, width)), whole((1, width))]
+    resident = pl.BlockSpec(memory_space=pltpu.VMEM)
     out_shape = [
         jax.ShapeDtypeStruct((rows, width), jnp.bfloat16),
         jax.ShapeDtypeStruct((rows, width), jnp.bfloat16),
@@ -62,18 +63,13 @@
         jax.ShapeDtypeStruct((1, width), jnp.float32),
         jax.ShapeDtypeStruct((1, width), jnp.float32),
     ]
-    out_specs = [whole((rows, width))] * 3 + [whole((rows, rank))] * 2 + [whole((1, width))] * 2
     return pl.pallas_call(
         chain_kernel,
         out_shape=out_shape,
-        grid_spec=pltpu.PrefetchScalarGridSpec(
-            num_scalar_prefetch=1,
-            grid=(1,),
-            in_specs=[block(width), whole((rows, width))] + layer_specs + layer_specs,
-            out_specs=out_specs,
-        ),
+        in_specs=[pl.BlockSpec(memory_space=pltpu.SMEM)] + [resident] * 12,
+        out_specs=[resident] * 7,
         cost_estimate=pl.CostEstimate(
-            flops=8 * rows * width * rank, transcendentals=0, bytes_accessed=4 * rank * width * 2 + 12 * rows * width
+            flops=8 * rows * width * rank, transcendentals=0, bytes_accessed=16 * rows * width
         ),
     )(flags, top, incoming, *upper, *lower)
 

time: 444 us -> 443 us (level)
  no operation moved by 1% of the time
where the time goes in v8:
time: 443 us; the launch traced here: 441 us
  waiting for transfers between devices  182 us (41%)
  matrix products  58.3 us (13%)
  Pallas kernels  54 us (12%)
  blocking collectives  47.6 us (11%)
  starting transfers between devices  38.4 us (9%)
  other arithmetic  21.7 us (5%)
  between operations  18.2 us (4%)
  local copies, waits for them, and re-layouts  17.4 us (4%)
    reduce_scatter x1, waiting for transfers between devices, on_device(): reduced = lax.psum_scatter(grads, 'seq', scatter_dimension=2, tiled=True)  79.7 us
    pallas_call x11, Pallas kernels, chain_step(): pl.pallas_call(chain_kernel, out_shape=out_shape, in_specs=[pl.BlockSpec(...  54 us
    ppermute x11, waiting for transfers between devices, shifted(): lax.ppermute(value, axis, [(source, source + steps) for source in range(i...  52.1 us
    dot_general x22, matrix products, accumulate(): lax.dot_general(d_low, normalized_part, contract_first, preferred_element...  34.1 us
    psum x1, blocking collectives, on_device(): total = lax.psum(square, 'pipe')  31.9 us
    ppermute x3, waiting for transfers between devices, partner_swap(): lax.ppermute(value, axis, [(source, source ^ 1) for source in range(count)])  24.7 us
    dot_general x22, matrix products, accumulate(): lax.dot_general(low_part, source, contract_first, preferred_element_type=...  20.5 us
    all_gather x1, blocking collectives, on_device(): lax.all_gather(stacked, 'dp', axis=2, tiled=True)  15.7 us
  transfers between devices with their start and end apart: 22, of which 21 were waited for; matrix products, arithmetic and copies ran while one was open for 16% of the time, Pallas kernels for 0%

profile of v8, /device:TPU:6, one launch (start us, length us, event | category | flops | bytes accessed | tf_op | source)
XLA Modules:
  0.0 441.2 jit_solution(14196212468301525654)
XLA Ops:
  8.1 3.8 collective-permute-start.2
  12.0 2.0 collective-permute-done.2
  14.8 15.7 %all_gather.6 = bf16[2,65,1024]{2,1,0:T(8,128)(2,1)} all-gather(bf16[2,65,256]{2,1,0:T(8,128)(2,1)S(1)} %pad_maximum_fusion.1), channel_id=1, replica_groups=mesh['pipe'=16,'seq'=8,'dp'=4] {'dp'}, dimensions={2}, use_global_device_ids=true | all-gather | bytes 332800 | tf_op jit(solution)/shard_map/all_gather | solution.py:101
  30.5 2.3 dynamic-slice_bitcast_fusion
  32.8 1.9 collective-permute-start.1
  35.8 17.6 %collective-permute-done.1 = bf16[64,8192]{1,0:T(8,128)(2,1)} collective-permute-done((bf16[64,8192]{1,0:T(8,128)(2,1)}, bf16[64,8192]{1,0:T(8,128)(2,1)}, u32[]{:S(2)}, u32[]{:S(2)}) %collective-permute-start.1) | collective-permute-done | bytes 1048608 | tf_op jit(solution)/shard_map/ppermute | solution.py:21
  53.4 3.4 fusion.21
  57.0 8.5 %all-gather.2.cloned.1.call-done = bf16[2,65,8192]{2,1,0:T(8,128)(2,1)} async-done(((bf16[2,65,1024]{2,1,0:T(8,128)(2,1)}), bf16[2,65,8192]{2,1,0:T(8,128)(2,1)}) %all-gather.2.cloned.1.call-update) | async-done | bytes 2129936 | tf_op jit(solution)/shard_map/all_gather | solution.py:101
  66.5 1.9 convolution_convert_fusion
  68.5 1.8 convolution_convert_fusion.1
  71.0 2.9 slice_bitcast_fusion
  73.9 195.5 %while.28 = (s32[]{:T(128)}, bf16[16,8192]{1,0:T(8,128)(2,1)S(1)}, f32[32,8192]{1,0:T(8,128)}, f32[32,8192]{1,0:T(8,128)S(1)}, f32[1,8192]{1,0:T(1,128)}, /*inde...) while((s32[]{:T(128)}, bf16[16,8192]{1,0:T(8,128)(2,1)S(1)}, ...), condition=%wide.region_3.4_spmd.clone, body=%wide.region_2.3_spmd.clone.sunk | while | flops 71352328 | bytes 40128360 | solution.py:163
  74.6 4.9 %eval_jaxpr.7 = (bf16[16,8192]{1,0:T(8,128)(2,1)}, bf16[16,8192]{1,0:T(8,128)(2,1)}, bf16[16,8192]{1,0:T(8,128)(2,1)}, bf16[16,32]{1,0:T(8,128)(2,1)}, bf16[16,3...) custom-call(s32[2]{0:T(128)} %pad_add_fusion.2.flags, bf16[64,8192]{1,0:T(8,128)(2,1)} %get-tuple-element.992.top_ref, ...), custom_call_target="tpu_custom_call" | custom-call | flops 33554432 | bytes 2097152 | tf_op jit(solution)/shard_map/while/body/eval_jaxpr/pallas_call | solution.py:66
  83.6 1.6 fusion.51
  87.0 9.6 %collective-permute-done = bf16[16,8192]{1,0:T(8,128)(2,1)S(1)} collective-permute-done((bf16[16,8192]{1,0:T(8,128)(2,1)}, bf16[16,8192]{1,0:T(8,128)(2,1)S(1)}, u32[]{:S(2)}, u32[]{:S(2)}) %collective-permute-start) | collective-permute-done | bytes 262176 | tf_op jit(solution)/shard_map/while/body/eval_jaxpr/ppermute | solution.py:16
  97.3 4.9 %eval_jaxpr.7 = (bf16[16,8192]{1,0:T(8,128)(2,1)}, bf16[16,8192]{1,0:T(8,128)(2,1)}, bf16[16,8192]{1,0:T(8,128)(2,1)}, bf16[16,32]{1,0:T(8,128)(2,1)}, bf16[16,3...) custom-call(s32[2]{0:T(128)} %pad_add_fusion.2.flags, bf16[64,8192]{1,0:T(8,128)(2,1)} %get-tuple-element.992.top_ref, ...), custom_call_target="tpu_custom_call" | custom-call | flops 33554432 | bytes 2097152 | tf_op jit(solution)/shard_map/while/body/eval_jaxpr/pallas_call | solution.py:66
  106.3 1.6 fusion.51
  109.6 7.5 %collective-permute-done = bf16[16,8192]{1,0:T(8,128)(2,1)S(1)} collective-permute-done((bf16[16,8192]{1,0:T(8,128)(2,1)}, bf16[16,8192]{1,0:T(8,128)(2,1)S(1)}, u32[]{:S(2)}, u32[]{:S(2)}) %collective-permute-start) | collective-permute-done | bytes 262176 | tf_op jit(solution)/shard_map/while/body/eval_jaxpr/ppermute | solution.py:16
  117.8 4.9 %eval_jaxpr.7 = (bf16[16,8192]{1,0:T(8,128)(2,1)}, bf16[16,8192]{1,0:T(8,128)(2,1)}, bf16[16,8192]{1,0:T(8,128)(2,1)}, bf16[16,32]{1,0:T(8,128)(2,1)}, bf16[16,3...) custom-call(s32[2]{0:T(128)} %pad_add_fusion.2.flags, bf16[64,8192]{1,0:T(8,128)(2,1)} %get-tuple-element.992.top_ref, ...), custom_call_target="tpu_custom_call" | custom-call | flops 33554432 | bytes 2097152 | tf_op jit(solution)/shard_map/while/body/eval_jaxpr/pallas_call | solution.py:66
  126.8 1.6 fusion.51
  130.2 5.0 %collective-permute-done = bf16[16,8192]{1,0:T(8,128)(2,1)S(1)} collective-permute-done((bf16[16,8192]{1,0:T(8,128)(2,1)}, bf16[16,8192]{1,0:T(8,128)(2,1)S(1)}, u32[]{:S(2)}, u32[]{:S(2)}) %collective-permute-start) | collective-permute-done | bytes 262176 | tf_op jit(solution)/shard_map/while/body/eval_jaxpr/ppermute | solution.py:16
  135.9 4.9 %eval_jaxpr.7 = (bf16[16,8192]{1,0:T(8,128)(2,1)}, bf16[16,8192]{1,0:T(8,128)(2,1)}, bf16[16,8192]{1,0:T(8,128)(2,1)}, bf16[16,32]{1,0:T(8,128)(2,1)}, bf16[16,3...) custom-call(s32[2]{0:T(128)} %pad_add_fusion.2.flags, bf16[64,8192]{1,0:T(8,128)(2,1)} %get-tuple-element.992.top_ref, ...), custom_call_target="tpu_custom_call" | custom-call | flops 33554432 | bytes 2097152 | tf_op jit(solution)/shard_map/while/body/eval_jaxpr/pallas_call | solution.py:66
  144.9 1.6 fusion.51
  148.2 4.2 collective-permute-done
  153.1 4.9 %eval_jaxpr.7 = (bf16[16,8192]{1,0:T(8,128)(2,1)}, bf16[16,8192]{1,0:T(8,128)(2,1)}, bf16[16,8192]{1,0:T(8,128)(2,1)}, bf16[16,32]{1,0:T(8,128)(2,1)}, bf16[16,3...) custom-call(s32[2]{0:T(128)} %pad_add_fusion.2.flags, bf16[64,8192]{1,0:T(8,128)(2,1)} %get-tuple-element.992.top_ref, ...), custom_call_target="tpu_custom_call" | custom-call | flops 33554432 | bytes 2097152 | tf_op jit(solution)/shard_map/while/body/eval_jaxpr/pallas_call | solution.py:66
  162.0 1.6 fusion.51
  165.4 3.2 collective-permute-done
  169.3 4.9 %eval_jaxpr.7 = (bf16[16,8192]{1,0:T(8,128)(2,1)}, bf16[16,8192]{1,0:T(8,128)(2,1)}, bf16[16,8192]{1,0:T(8,128)(2,1)}, bf16[16,32]{1,0:T(8,128)(2,1)}, bf16[16,3...) custom-call(s32[2]{0:T(128)} %pad_add_fusion.2.flags, bf16[64,8192]{1,0:T(8,128)(2,1)} %get-tuple-element.992.top_ref, ...), custom_call_target="tpu_custom_call" | custom-call | flops 33554432 | bytes 2097152 | tf_op jit(solution)/shard_map/while/body/eval_jaxpr/pallas_call | solution.py:66
  178.3 1.6 fusion.51
  180.1 1.5 fusion.54
  181.7 6.3 %collective-permute-done = bf16[16,8192]{1,0:T(8,128)(2,1)S(1)} collective-permute-done((bf16[16,8192]{1,0:T(8,128)(2,1)}, bf16[16,8192]{1,0:T(8,128)(2,1)S(1)}, u32[]{:S(2)}, u32[]{:S(2)}) %collective-permute-start) | collective-permute-done | bytes 262176 | tf_op jit(solution)/shard_map/while/body/eval_jaxpr/ppermute | solution.py:16
  188.7 4.9 %eval_jaxpr.7 = (bf16[16,8192]{1,0:T(8,128)(2,1)}, bf16[16,8192]{1,0:T(8,128)(2,1)}, bf16[16,8192]{1,0:T(8,128)(2,1)}, bf16[16,32]{1,0:T(8,128)(2,1)}, bf16[16,3...) custom-call(s32[2]{0:T(128)} %pad_add_fusion.2.flags, bf16[64,8192]{1,0:T(8,128)(2,1)} %get-tuple-element.992.top_ref, ...), custom_call_target="tpu_custom_call" | custom-call | flops 33554432 | bytes 2097152 | tf_op jit(solution)/shard_map/while/body/eval_jaxpr/pallas_call | solution.py:66
  197.6 1.6 fusion.51
  201.0 2.9 collective-permute-done
  204.6 4.9 %eval_jaxpr.7 = (bf16[16,8192]{1,0:T(8,128)(2,1)}, bf16[16,8192]{1,0:T(8,128)(2,1)}, bf16[16,8192]{1,0:T(8,128)(2,1)}, bf16[16,32]{1,0:T(8,128)(2,1)}, bf16[16,3...) custom-call(s32[2]{0:T(128)} %pad_add_fusion.2.flags, bf16[64,8192]{1,0:T(8,128)(2,1)} %get-tuple-element.992.top_ref, ...), custom_call_target="tpu_custom_call" | custom-call | flops 33554432 | bytes 2097152 | tf_op jit(solution)/shard_map/while/body/eval_jaxpr/pallas_call | solution.py:66
  213.6 1.6 fusion.51
  216.9 3.2 collective-permute-done
  220.9 4.9 %eval_jaxpr.7 = (bf16[16,8192]{1,0:T(8,128)(2,1)}, bf16[16,8192]{1,0:T(8,128)(2,1)}, bf16[16,8192]{1,0:T(8,128)(2,1)}, bf16[16,32]{1,0:T(8,128)(2,1)}, bf16[16,3...) custom-call(s32[2]{0:T(128)} %pad_add_fusion.2.flags, bf16[64,8192]{1,0:T(8,128)(2,1)} %get-tuple-element.992.top_ref, ...), custom_call_target="tpu_custom_call" | custom-call | flops 33554432 | bytes 2097152 | tf_op jit(solution)/shard_map/while/body/eval_jaxpr/pallas_call | solution.py:66
  229.8 1.6 fusion.51
  231.6 1.5 fusion.54
  233.2 4.1 collective-permute-done
  238.0 4.9 %eval_jaxpr.7 = (bf16[16,8192]{1,0:T(8,128)(2,1)}, bf16[16,8192]{1,0:T(8,128)(2,1)}, bf16[16,8192]{1,0:T(8,128)(2,1)}, bf16[16,32]{1,0:T(8,128)(2,1)}, bf16[16,3...) custom-call(s32[2]{0:T(128)} %pad_add_fusion.2.flags, bf16[64,8192]{1,0:T(8,128)(2,1)} %get-tuple-element.992.top_ref, ...), custom_call_target="tpu_custom_call" | custom-call | flops 33554432 | bytes 2097152 | tf_op jit(solution)/shard_map/while/body/eval_jaxpr/pallas_call | solution.py:66
  246.9 1.6 fusion.51
  250.3 3.0 collective-permute-done
  254.0 4.9 %eval_jaxpr.7 = (bf16[16,8192]{1,0:T(8,128)(2,1)}, bf16[16,8192]{1,0:T(8,128)(2,1)}, bf16[16,8192]{1,0:T(8,128)(2,1)}, bf16[16,32]{1,0:T(8,128)(2,1)}, bf16[16,3...) custom-call(s32[2]{0:T(128)} %pad_add_fusion.2.flags, bf16[64,8192]{1,0:T(8,128)(2,1)} %get-tuple-element.992.top_ref, ...), custom_call_target="tpu_custom_call" | custom-call | flops 33554432 | bytes 2097152 | tf_op jit(solution)/shard_map/while/body/eval_jaxpr/pallas_call | solution.py:66
  263.0 1.6 fusion.51
  266.3 3.1 collective-permute-done
  269.5 1.6 maximum_bitcast_fusion
  271.6 2.6 pad_maximum_fusion
  274.2 79.7 %reduce-scatter.2.cloned.1.call-done = f32[2,65,1024]{2,1,0:T(8,128)} async-done(((f32[2,65,8192]{2,1,0:T(8,128)}), f32[2,65,1024]{2,1,0:T(8,128)}) %reduce-scatter.2.cloned.1.call-update) | async-done | bytes 532496 | tf_op jit(solution)/shard_map/reduce_scatter | solution.py:167
  355.0 3.5 collective-permute-start.3
  358.5 5.1 %collective-permute-done.3 = f32[65,1024]{1,0:T(8,128)S(1)} collective-permute-done((f32[65,1024]{1,0:T(8,128)S(1)}, f32[65,1024]{1,0:T(8,128)S(1)}, u32[]{:S(2)}, u32[]{:S(2)}) %collective-permute-start.3) | collective-permute-done | bytes 266272 | tf_op jit(solution)/shard_map/ppermute | solution.py:21
  363.6 1.7 multiply_reduce_fusion
  365.3 31.9 %psum.7 = f32[]{:T(128)} all-reduce(f32[]{:T(128)} %get-tuple-element.714), channel_id=1, replica_groups=mesh['pipe'=16,'seq'=8,'dp'=4] {'pipe'}, use_global_device_ids=true, to_apply=%region_6.7 | all-reduce | flops 1 | bytes 8 | tf_op jit(solution)/shard_map/psum | solution.py:174
  397.2 4.3 collective-permute-done.4
  402.8 3.2 collective-permute-start.5
  406.0 3.4 collective-permute-done.5
  410.1 3.2 collective-permute-start.6
  413.3 3.7 collective-permute-done.6
  417.8 2.5 collective-permute-start.7
  420.2 4.3 collective-permute-start.8
  424.5 1.9 collective-permute-start.9
  426.5 1.5 collective-permute-done.8
  428.0 4.0 collective-permute-done.9
  (537 shorter events, 73.2 us)
Async XLA Ops:
  7.2 27.6 %copy-start = (bf16[1,128,8192]{2,1,0:T(8,128)(2,1)S(1)}, bf16[1,128,8192]{2,1,0:T(8,128)(2,1)}, u32[]{:S(2)}) copy-start(bf16[1,128,8192]{2,1,0:T(8,128)(2,1)} %param.8) | copy-start | bytes 6291460
  7.2 58.3 %all-gather.2.cloned.1.call-start = ((), (), s32[]{:S(2)}) async-start(), calls=%async_computation.1 | async-start | bytes 2654208 | tf_op jit(solution)/shard_map/all_gather | solution.py:101
  8.1 5.8 %collective-permute-start.2 = (bf16[65,256]{1,0:T(8,128)(2,1)S(1)}, bf16[65,256]{1,0:T(8,128)(2,1)S(1)}, u32[]{:S(2)}, u32[]{:S(2)}) collective-permute-start(bf16[65,256]{1,0:T(8,128)(2,1)S(1)} %pad_maximum_fusion.2), channel_id=1, source_target_pairs={{0,32},{32,0},{64,96},{96,64},{128,160},{160,128},{192,224},{224,1... | collective-permute-start | bytes 99848 | tf_op jit(solution)/shard_map/ppermute | solution.py:21
  30.4 323.4 %reduce-scatter.2.cloned.1.call-start = ((), (), s32[]{:S(2)}) async-start(), calls=%async_computation.2 | async-start | bytes 5308416 | tf_op jit(solution)/shard_map/reduce_scatter | solution.py:167
  32.8 20.6 %collective-permute-start.1 = (bf16[64,8192]{1,0:T(8,128)(2,1)}, bf16[64,8192]{1,0:T(8,128)(2,1)}, u32[]{:S(2)}, u32[]{:S(2)}) collective-permute-start(bf16[64,8192]{1,0:T(8,128)(2,1)} %dynamic-slice_bitcast_fusion), channel_id=1, source_target_pairs={{0,32},{32,0},{64,96},{96,64},{128,160},{160,128},{192,224},{224,1... | collective-permute-start | bytes 3145736 | tf_op jit(solution)/shard_map/ppermute | solution.py:21
  34.8 18.6 %copy-start.5 = (bf16[1,1,128,8192]{3,2,1,0:T(8,128)(2,1)S(1)}, bf16[1,1,128,8192]{3,2,1,0:T(8,128)(2,1)}, u32[]{:S(2)}) copy-start(bf16[1,1,128,8192]{3,2,1,0:T(8,128)(2,1)} %param.7) | copy-start | bytes 6291460
  79.5 17.0 %collective-permute-start = (bf16[16,8192]{1,0:T(8,128)(2,1)}, bf16[16,8192]{1,0:T(8,128)(2,1)S(1)}, u32[]{:S(2)}, u32[]{:S(2)}) collective-permute-start(bf16[16,8192]{1,0:T(8,128)(2,1)} %get-tuple-element.909), channel_id=1, source_target_pairs={{64,0},{96,32},{128,64},{160,96},{192,128},{224,160},{256,192},{28... | collective-permute-start | bytes 786440 | tf_op jit(solution)/shard_map/while/body/eval_jaxpr/ppermute | solution.py:16
  85.2 11.4 %copy-start.12 = (f32[32,8192]{1,0:T(8,128)}, f32[32,8192]{1,0:T(8,128)S(1)}, u32[]{:S(2)}) copy-start(f32[32,8192]{1,0:T(8,128)S(1)} %fusion.51) | copy-start | bytes 3145732 | tf_op jit(solution)/shard_map/while
  85.3 11.3 %copy-start.7 = (f32[1,8192]{1,0:T(1,128)}, f32[1,8192]{1,0:T(1,128)S(1)}, u32[]{:S(2)}) copy-start(f32[1,8192]{1,0:T(1,128)S(1)} %get-tuple-element.986) | copy-start | bytes 98308 | tf_op jit(solution)/shard_map/while
  85.3 11.2 %copy-start.9 = (f32[1,8192]{1,0:T(1,128)}, f32[1,8192]{1,0:T(1,128)S(1)}, u32[]{:S(2)}) copy-start(f32[1,8192]{1,0:T(1,128)S(1)} %get-tuple-element.989) | copy-start | bytes 98308 | tf_op jit(solution)/shard_map/while
  86.9 9.7 %copy-start.14 = (f32[32,8192]{1,0:T(8,128)}, f32[32,8192]{1,0:T(8,128)S(1)}, u32[]{:S(2)}) copy-start(f32[32,8192]{1,0:T(8,128)S(1)} %fusion.54) | copy-start | bytes 3145732 | tf_op jit(solution)/shard_map/while
  102.2 15.0 %collective-permute-start = (bf16[16,8192]{1,0:T(8,128)(2,1)}, bf16[16,8192]{1,0:T(8,128)(2,1)S(1)}, u32[]{:S(2)}, u32[]{:S(2)}) collective-permute-start(bf16[16,8192]{1,0:T(8,128)(2,1)} %get-tuple-element.909), channel_id=1, source_target_pairs={{64,0},{96,32},{128,64},{160,96},{192,128},{224,160},{256,192},{28... | collective-permute-start | bytes 786440 | tf_op jit(solution)/shard_map/while/body/eval_jaxpr/ppermute | solution.py:16
  107.8 9.3 %copy-start.12 = (f32[32,8192]{1,0:T(8,128)}, f32[32,8192]{1,0:T(8,128)S(1)}, u32[]{:S(2)}) copy-start(f32[32,8192]{1,0:T(8,128)S(1)} %fusion.51) | copy-start | bytes 3145732 | tf_op jit(solution)/shard_map/while
  108.0 9.1 %copy-start.7 = (f32[1,8192]{1,0:T(1,128)}, f32[1,8192]{1,0:T(1,128)S(1)}, u32[]{:S(2)}) copy-start(f32[1,8192]{1,0:T(1,128)S(1)} %get-tuple-element.986) | copy-start | bytes 98308 | tf_op jit(solution)/shard_map/while
  108.0 9.1 %copy-start.9 = (f32[1,8192]{1,0:T(1,128)}, f32[1,8192]{1,0:T(1,128)S(1)}, u32[]{:S(2)}) copy-start(f32[1,8192]{1,0:T(1,128)S(1)} %get-tuple-element.989) | copy-start | bytes 98308 | tf_op jit(solution)/shard_map/while
  109.6 7.5 %copy-start.14 = (f32[32,8192]{1,0:T(8,128)}, f32[32,8192]{1,0:T(8,128)S(1)}, u32[]{:S(2)}) copy-start(f32[32,8192]{1,0:T(8,128)S(1)} %fusion.54) | copy-start | bytes 3145732 | tf_op jit(solution)/shard_map/while
  122.8 12.4 %collective-permute-start = (bf16[16,8192]{1,0:T(8,128)(2,1)}, bf16[16,8192]{1,0:T(8,128)(2,1)S(1)}, u32[]{:S(2)}, u32[]{:S(2)}) collective-permute-start(bf16[16,8192]{1,0:T(8,128)(2,1)} %get-tuple-element.909), channel_id=1, source_target_pairs={{64,0},{96,32},{128,64},{160,96},{192,128},{224,160},{256,192},{28... | collective-permute-start | bytes 786440 | tf_op jit(solution)/shard_map/while/body/eval_jaxpr/ppermute | solution.py:16
  128.4 6.8 %copy-start.12 = (f32[32,8192]{1,0:T(8,128)}, f32[32,8192]{1,0:T(8,128)S(1)}, u32[]{:S(2)}) copy-start(f32[32,8192]{1,0:T(8,128)S(1)} %fusion.51) | copy-start | bytes 3145732 | tf_op jit(solution)/shard_map/while
  128.6 6.6 %copy-start.7 = (f32[1,8192]{1,0:T(1,128)}, f32[1,8192]{1,0:T(1,128)S(1)}, u32[]{:S(2)}) copy-start(f32[1,8192]{1,0:T(1,128)S(1)} %get-tuple-element.986) | copy-start | bytes 98308 | tf_op jit(solution)/shard_map/while
  128.6 6.6 %copy-start.9 = (f32[1,8192]{1,0:T(1,128)}, f32[1,8192]{1,0:T(1,128)S(1)}, u32[]{:S(2)}) copy-start(f32[1,8192]{1,0:T(1,128)S(1)} %get-tuple-element.989) | copy-start | bytes 98308 | tf_op jit(solution)/shard_map/while
  130.2 5.0 %copy-start.14 = (f32[32,8192]{1,0:T(8,128)}, f32[32,8192]{1,0:T(8,128)S(1)}, u32[]{:S(2)}) copy-start(f32[32,8192]{1,0:T(8,128)S(1)} %fusion.54) | copy-start | bytes 3145732 | tf_op jit(solution)/shard_map/while
  140.8 11.6 %collective-permute-start = (bf16[16,8192]{1,0:T(8,128)(2,1)}, bf16[16,8192]{1,0:T(8,128)(2,1)S(1)}, u32[]{:S(2)}, u32[]{:S(2)}) collective-permute-start(bf16[16,8192]{1,0:T(8,128)(2,1)} %get-tuple-element.909), channel_id=1, source_target_pairs={{64,0},{96,32},{128,64},{160,96},{192,128},{224,160},{256,192},{28... | collective-permute-start | bytes 786440 | tf_op jit(solution)/shard_map/while/body/eval_jaxpr/ppermute | solution.py:16
  146.4 5.9 %copy-start.12 = (f32[32,8192]{1,0:T(8,128)}, f32[32,8192]{1,0:T(8,128)S(1)}, u32[]{:S(2)}) copy-start(f32[32,8192]{1,0:T(8,128)S(1)} %fusion.51) | copy-start | bytes 3145732 | tf_op jit(solution)/shard_map/while
  146.6 5.8 %copy-start.7 = (f32[1,8192]{1,0:T(1,128)}, f32[1,8192]{1,0:T(1,128)S(1)}, u32[]{:S(2)}) copy-start(f32[1,8192]{1,0:T(1,128)S(1)} %get-tuple-element.986) | copy-start | bytes 98308 | tf_op jit(solution)/shard_map/while
  146.6 5.8 %copy-start.9 = (f32[1,8192]{1,0:T(1,128)}, f32[1,8192]{1,0:T(1,128)S(1)}, u32[]{:S(2)}) copy-start(f32[1,8192]{1,0:T(1,128)S(1)} %get-tuple-element.989) | copy-start | bytes 98308 | tf_op jit(solution)/shard_map/while
  148.2 4.2 copy-start.14
  158.0 10.6 %collective-permute-start = (bf16[16,8192]{1,0:T(8,128)(2,1)}, bf16[16,8192]{1,0:T(8,128)(2,1)S(1)}, u32[]{:S(2)}, u32[]{:S(2)}) collective-permute-start(bf16[16,8192]{1,0:T(8,128)(2,1)} %get-tuple-element.909), channel_id=1, source_target_pairs={{64,0},{96,32},{128,64},{160,96},{192,128},{224,160},{256,192},{28... | collective-permute-start | bytes 786440 | tf_op jit(solution)/shard_map/while/body/eval_jaxpr/ppermute | solution.py:16
  163.6 5.0 %copy-start.12 = (f32[32,8192]{1,0:T(8,128)}, f32[32,8192]{1,0:T(8,128)S(1)}, u32[]{:S(2)}) copy-start(f32[32,8192]{1,0:T(8,128)S(1)} %fusion.51) | copy-start | bytes 3145732 | tf_op jit(solution)/shard_map/while
  163.8 4.8 %copy-start.7 = (f32[1,8192]{1,0:T(1,128)}, f32[1,8192]{1,0:T(1,128)S(1)}, u32[]{:S(2)}) copy-start(f32[1,8192]{1,0:T(1,128)S(1)} %get-tuple-element.986) | copy-start | bytes 98308 | tf_op jit(solution)/shard_map/while
  163.8 4.8 %copy-start.9 = (f32[1,8192]{1,0:T(1,128)}, f32[1,8192]{1,0:T(1,128)S(1)}, u32[]{:S(2)}) copy-start(f32[1,8192]{1,0:T(1,128)S(1)} %get-tuple-element.989) | copy-start | bytes 98308 | tf_op jit(solution)/shard_map/while
  174.2 13.8 %collective-permute-start = (bf16[16,8192]{1,0:T(8,128)(2,1)}, bf16[16,8192]{1,0:T(8,128)(2,1)S(1)}, u32[]{:S(2)}, u32[]{:S(2)}) collective-permute-start(bf16[16,8192]{1,0:T(8,128)(2,1)} %get-tuple-element.909), channel_id=1, source_target_pairs={{64,0},{96,32},{128,64},{160,96},{192,128},{224,160},{256,192},{28... | collective-permute-start | bytes 786440 | tf_op jit(solution)/shard_map/while/body/eval_jaxpr/ppermute | solution.py:16
  179.9 8.1 %copy-start.12 = (f32[32,8192]{1,0:T(8,128)}, f32[32,8192]{1,0:T(8,128)S(1)}, u32[]{:S(2)}) copy-start(f32[32,8192]{1,0:T(8,128)S(1)} %fusion.51) | copy-start | bytes 3145732 | tf_op jit(solution)/shard_map/while
  180.0 7.9 %copy-start.7 = (f32[1,8192]{1,0:T(1,128)}, f32[1,8192]{1,0:T(1,128)S(1)}, u32[]{:S(2)}) copy-start(f32[1,8192]{1,0:T(1,128)S(1)} %get-tuple-element.986) | copy-start | bytes 98308 | tf_op jit(solution)/shard_map/while
  180.1 7.9 %copy-start.9 = (f32[1,8192]{1,0:T(1,128)}, f32[1,8192]{1,0:T(1,128)S(1)}, u32[]{:S(2)}) copy-start(f32[1,8192]{1,0:T(1,128)S(1)} %get-tuple-element.989) | copy-start | bytes 98308 | tf_op jit(solution)/shard_map/while
  181.7 6.3 %copy-start.14 = (f32[32,8192]{1,0:T(8,128)}, f32[32,8192]{1,0:T(8,128)S(1)}, u32[]{:S(2)}) copy-start(f32[32,8192]{1,0:T(8,128)S(1)} %fusion.54) | copy-start | bytes 3145732 | tf_op jit(solution)/shard_map/while
  193.6 10.3 %collective-permute-start = (bf16[16,8192]{1,0:T(8,128)(2,1)}, bf16[16,8192]{1,0:T(8,128)(2,1)S(1)}, u32[]{:S(2)}, u32[]{:S(2)}) collective-permute-start(bf16[16,8192]{1,0:T(8,128)(2,1)} %get-tuple-element.909), channel_id=1, source_target_pairs={{64,0},{96,32},{128,64},{160,96},{192,128},{224,160},{256,192},{28... | collective-permute-start | bytes 786440 | tf_op jit(solution)/shard_map/while/body/eval_jaxpr/ppermute | solution.py:16
  199.2 4.7 %copy-start.12 = (f32[32,8192]{1,0:T(8,128)}, f32[32,8192]{1,0:T(8,128)S(1)}, u32[]{:S(2)}) copy-start(f32[32,8192]{1,0:T(8,128)S(1)} %fusion.51) | copy-start | bytes 3145732 | tf_op jit(solution)/shard_map/while
  199.4 4.5 %copy-start.7 = (f32[1,8192]{1,0:T(1,128)}, f32[1,8192]{1,0:T(1,128)S(1)}, u32[]{:S(2)}) copy-start(f32[1,8192]{1,0:T(1,128)S(1)} %get-tuple-element.986) | copy-start | bytes 98308 | tf_op jit(solution)/shard_map/while
  199.4 4.5 %copy-start.9 = (f32[1,8192]{1,0:T(1,128)}, f32[1,8192]{1,0:T(1,128)S(1)}, u32[]{:S(2)}) copy-start(f32[1,8192]{1,0:T(1,128)S(1)} %get-tuple-element.989) | copy-start | bytes 98308 | tf_op jit(solution)/shard_map/while
  209.5 10.7 %collective-permute-start = (bf16[16,8192]{1,0:T(8,128)(2,1)}, bf16[16,8192]{1,0:T(8,128)(2,1)S(1)}, u32[]{:S(2)}, u32[]{:S(2)}) collective-permute-start(bf16[16,8192]{1,0:T(8,128)(2,1)} %get-tuple-element.909), channel_id=1, source_target_pairs={{64,0},{96,32},{128,64},{160,96},{192,128},{224,160},{256,192},{28... | collective-permute-start | bytes 786440 | tf_op jit(solution)/shard_map/while/body/eval_jaxpr/ppermute | solution.py:16
  215.1 5.0 %copy-start.12 = (f32[32,8192]{1,0:T(8,128)}, f32[32,8192]{1,0:T(8,128)S(1)}, u32[]{:S(2)}) copy-start(f32[32,8192]{1,0:T(8,128)S(1)} %fusion.51) | copy-start | bytes 3145732 | tf_op jit(solution)/shard_map/while
  215.3 4.9 %copy-start.7 = (f32[1,8192]{1,0:T(1,128)}, f32[1,8192]{1,0:T(1,128)S(1)}, u32[]{:S(2)}) copy-start(f32[1,8192]{1,0:T(1,128)S(1)} %get-tuple-element.986) | copy-start | bytes 98308 | tf_op jit(solution)/shard_map/while
  215.3 4.9 %copy-start.9 = (f32[1,8192]{1,0:T(1,128)}, f32[1,8192]{1,0:T(1,128)S(1)}, u32[]{:S(2)}) copy-start(f32[1,8192]{1,0:T(1,128)S(1)} %get-tuple-element.989) | copy-start | bytes 98308 | tf_op jit(solution)/shard_map/while
  225.8 11.5 %collective-permute-start = (bf16[16,8192]{1,0:T(8,128)(2,1)}, bf16[16,8192]{1,0:T(8,128)(2,1)S(1)}, u32[]{:S(2)}, u32[]{:S(2)}) collective-permute-start(bf16[16,8192]{1,0:T(8,128)(2,1)} %get-tuple-element.909), channel_id=1, source_target_pairs={{64,0},{96,32},{128,64},{160,96},{192,128},{224,160},{256,192},{28... | collective-permute-start | bytes 786440 | tf_op jit(solution)/shard_map/while/body/eval_jaxpr/ppermute | solution.py:16
  229.8 3.4 copy-start.2
  231.4 5.9 %copy-start.12 = (f32[32,8192]{1,0:T(8,128)}, f32[32,8192]{1,0:T(8,128)S(1)}, u32[]{:S(2)}) copy-start(f32[32,8192]{1,0:T(8,128)S(1)} %fusion.51) | copy-start | bytes 3145732 | tf_op jit(solution)/shard_map/while
  231.6 5.7 %copy-start.7 = (f32[1,8192]{1,0:T(1,128)}, f32[1,8192]{1,0:T(1,128)S(1)}, u32[]{:S(2)}) copy-start(f32[1,8192]{1,0:T(1,128)S(1)} %get-tuple-element.986) | copy-start | bytes 98308 | tf_op jit(solution)/shard_map/while
  231.6 5.7 %copy-start.9 = (f32[1,8192]{1,0:T(1,128)}, f32[1,8192]{1,0:T(1,128)S(1)}, u32[]{:S(2)}) copy-start(f32[1,8192]{1,0:T(1,128)S(1)} %get-tuple-element.989) | copy-start | bytes 98308 | tf_op jit(solution)/shard_map/while
  233.2 4.1 copy-start.14
  242.9 10.4 %collective-permute-start = (bf16[16,8192]{1,0:T(8,128)(2,1)}, bf16[16,8192]{1,0:T(8,128)(2,1)S(1)}, u32[]{:S(2)}, u32[]{:S(2)}) collective-permute-start(bf16[16,8192]{1,0:T(8,128)(2,1)} %get-tuple-element.909), channel_id=1, source_target_pairs={{64,0},{96,32},{128,64},{160,96},{192,128},{224,160},{256,192},{28... | collective-permute-start | bytes 786440 | tf_op jit(solution)/shard_map/while/body/eval_jaxpr/ppermute | solution.py:16
  248.5 4.8 %copy-start.12 = (f32[32,8192]{1,0:T(8,128)}, f32[32,8192]{1,0:T(8,128)S(1)}, u32[]{:S(2)}) copy-start(f32[32,8192]{1,0:T(8,128)S(1)} %fusion.51) | copy-start | bytes 3145732 | tf_op jit(solution)/shard_map/while
  248.7 4.6 %copy-start.7 = (f32[1,8192]{1,0:T(1,128)}, f32[1,8192]{1,0:T(1,128)S(1)}, u32[]{:S(2)}) copy-start(f32[1,8192]{1,0:T(1,128)S(1)} %get-tuple-element.986) | copy-start | bytes 98308 | tf_op jit(solution)/shard_map/while
  248.7 4.6 %copy-start.9 = (f32[1,8192]{1,0:T(1,128)}, f32[1,8192]{1,0:T(1,128)S(1)}, u32[]{:S(2)}) copy-start(f32[1,8192]{1,0:T(1,128)S(1)} %get-tuple-element.989) | copy-start | bytes 98308 | tf_op jit(solution)/shard_map/while
  258.9 10.6 %collective-permute-start = (bf16[16,8192]{1,0:T(8,128)(2,1)}, bf16[16,8192]{1,0:T(8,128)(2,1)S(1)}, u32[]{:S(2)}, u32[]{:S(2)}) collective-permute-start(bf16[16,8192]{1,0:T(8,128)(2,1)} %get-tuple-element.909), channel_id=1, source_target_pairs={{64,0},{96,32},{128,64},{160,96},{192,128},{224,160},{256,192},{28... | collective-permute-start | bytes 786440 | tf_op jit(solution)/shard_map/while/body/eval_jaxpr/ppermute | solution.py:16
  264.5 4.9 %copy-start.12 = (f32[32,8192]{1,0:T(8,128)}, f32[32,8192]{1,0:T(8,128)S(1)}, u32[]{:S(2)}) copy-start(f32[32,8192]{1,0:T(8,128)S(1)} %fusion.51) | copy-start | bytes 3145732 | tf_op jit(solution)/shard_map/while
  264.7 4.8 %copy-start.7 = (f32[1,8192]{1,0:T(1,128)}, f32[1,8192]{1,0:T(1,128)S(1)}, u32[]{:S(2)}) copy-start(f32[1,8192]{1,0:T(1,128)S(1)} %get-tuple-element.986) | copy-start | bytes 98308 | tf_op jit(solution)/shard_map/while
  264.7 4.8 %copy-start.9 = (f32[1,8192]{1,0:T(1,128)}, f32[1,8192]{1,0:T(1,128)S(1)}, u32[]{:S(2)}) copy-start(f32[1,8192]{1,0:T(1,128)S(1)} %get-tuple-element.989) | copy-start | bytes 98308 | tf_op jit(solution)/shard_map/while
  355.0 8.6 %collective-permute-start.3 = (f32[65,1024]{1,0:T(8,128)S(1)}, f32[65,1024]{1,0:T(8,128)S(1)}, u32[]{:S(2)}, u32[]{:S(2)}) collective-permute-start(f32[65,1024]{1,0:T(8,128)S(1)} %select_bitcast_fusion), channel_id=1, source_target_pairs={{0,32},{32,0},{64,96},{96,64},{128,160},{160,128},{192,224},{224,1... | collective-permute-start | bytes 798728 | tf_op jit(solution)/shard_map/ppermute | solution.py:21
  397.2 4.3 collective-permute-start.4
  402.8 6.6 %collective-permute-start.5 = (f32[]{:T(128)}, f32[]{:T(128)}, u32[]{:S(2)}, u32[]{:S(2)}) collective-permute-start(f32[]{:T(128)} %add.178), channel_id=1, source_target_pairs={{0,8},{4,12},{8,16},{12,20},{16,24},{20,28},{24,0},{28,4},{1,9},{5... | collective-permute-start | bytes 20 | tf_op jit(solution)/shard_map/ppermute | solution.py:178
  410.1 6.9 %collective-permute-start.6 = (f32[]{:T(128)}, f32[]{:T(128)}, u32[]{:S(2)}, u32[]{:S(2)}) collective-permute-start(f32[]{:T(128)} %add.179), channel_id=1, source_target_pairs={{0,16},{4,20},{8,24},{12,28},{16,0},{20,4},{24,8},{28,12},{1,17},{... | collective-permute-start | bytes 20 | tf_op jit(solution)/shard_map/ppermute | solution.py:178
  417.8 8.7 %collective-permute-start.7 = (f32[65,256]{1,0:T(8,128)S(1)}, f32[65,256]{1,0:T(8,128)S(1)}, u32[]{:S(2)}, u32[]{:S(2)}) collective-permute-start(f32[65,256]{1,0:T(8,128)S(1)} %get-tuple-element.734), channel_id=1, source_target_pairs={{0,1},{1,2},{2,3},{3,0},{4,5},{5,6},{6,7},{7,4},{8,9},{9,10},{10,1... | collective-permute-start | bytes 199688 | tf_op jit(solution)/shard_map/ppermute | solution.py:190
  420.2 7.8 %collective-permute-start.8 = (f32[65,256]{1,0:T(8,128)S(1)}, f32[65,256]{1,0:T(8,128)S(1)}, u32[]{:S(2)}, u32[]{:S(2)}) collective-permute-start(f32[65,256]{1,0:T(8,128)S(1)} %get-tuple-element.736), channel_id=1, source_target_pairs={{0,2},{1,3},{2,0},{3,1},{4,6},{5,7},{6,4},{7,5},{8,10},{9,11},{10,... | collective-permute-start | bytes 199688 | tf_op jit(solution)/shard_map/ppermute | solution.py:190
  424.5 7.5 %collective-permute-start.9 = (f32[65,256]{1,0:T(8,128)S(1)}, f32[65,256]{1,0:T(8,128)S(1)}, u32[]{:S(2)}, u32[]{:S(2)}) collective-permute-start(f32[65,256]{1,0:T(8,128)S(1)} %get-tuple-element.735), channel_id=1, source_target_pairs={{0,3},{1,0},{2,1},{3,2},{4,7},{5,4},{6,5},{7,6},{8,11},{9,8},{10,9... | collective-permute-start | bytes 199688 | tf_op jit(solution)/shard_map/ppermute | solution.py:190
  (174 other events, 372.5 us)
Sparse Core Ops, SparseCore 0:
  30.6 34.8 all-gather.1
  274.3 79.5 reduce-scatter.1

commit v9 on v8

--- a/solution.py
+++ b/solution.py
@@ -33,9 +33,7 @@
     def one_layer(upstream, hidden_ref, root_ref, b_ref, a_ref, g_ref, low_ref, pg_ref):
         root = root_ref[window, :]
         normalized = hidden_ref[window, :].astype(jnp.float32) / root
-        d_low = lax.dot_general(
-            upstream, b_ref[...], (((1,), (1,)), ((), ())), preferred_element_type=jnp.float32
-        ).astype(jnp.bfloat16)
+        d_low = jnp.dot(upstream, b_ref[...], preferred_element_type=jnp.float32).astype(jnp.bfloat16)
         normalized_gradient = jnp.dot(d_low, a_ref[...], preferred_element_type=jnp.float32)
         input_gradient = normalized_gradient * g_ref[...]
         mean = jnp.mean(input_gradient * normalized, axis=-1, keepdims=True)
@@ -52,7 +50,7 @@
 
 def chain_step(flags, top, incoming, upper, lower, rows):
     width = incoming.shape[1]
-    rank = upper[2].shape[0]
+    rank = upper[2].shape[1]
     resident = pl.BlockSpec(memory_space=pltpu.VMEM)
     out_shape = [
         jax.ShapeDtypeStruct((rows, width), jnp.bfloat16),
@@ -117,7 +115,7 @@
             jnp.bfloat16
         )
         layers.append((hidden, inverse_root_mean, low, a_full, b_full, gain_float))
-        operands.append((hidden, inverse_root_mean, b_full, a_full, gain_float[None, :]))
+        operands.append((hidden, inverse_root_mean, b_full.T, a_full, gain_float[None, :]))
     block_total = half_rows // rows_per_block
 
     def accumulate(layer, source, d_low, part_g, block_offset, sums, inside):

time: 443 us -> 442 us (level)
  waiting for transfers between devices: 182 us -> 147 us
  matrix products: 58.3 us -> 81.5 us
  Pallas kernels: 54 us -> 60.8 us
    dot_general x22, matrix products: 20.5 us -> 43.7 us  [accumulate(): lax.dot_general(low_part, source, contract_first, preferred_element_type=...]
    ppermute x11, waiting for transfers between devices: 52.1 us -> 31.5 us  [shifted(): lax.ppermute(value, axis, [(source, source + steps) for source in range(i...]
    reduce_scatter x1, waiting for transfers between devices: 79.7 us -> 64.2 us  [on_device(): reduced = lax.psum_scatter(grads, 'seq', scatter_dimension=2, tiled=True)]
    pallas_call x11, Pallas kernels: 54 us -> 60.8 us  [chain_step(): pl.pallas_call(chain_kernel, out_shape=out_shape, in_specs=[pl.BlockSpec(...]
    unnamed x18 -> x20, local copies, waits for them, and re-layouts: 1.32 us -> 6.59 us
  transfers between devices with their start and end apart: 22 -> 22, of which waited for: 21 -> 21; matrix products, arithmetic and copies ran while one was open for 16% -> 21% of each run, Pallas kernels for 0% -> 0%
where the time goes in v9:
time: 442 us; the launch traced here: 440 us
  waiting for transfers between devices  147 us (33%)
  matrix products  81.5 us (18%)
  Pallas kernels  60.8 us (14%)
  blocking collectives  47.6 us (11%)
  starting transfers between devices  38.5 us (9%)
  other arithmetic  21.9 us (5%)
  local copies, waits for them, and re-layouts  21.5 us (5%)
  between operations  18.2 us (4%)
    reduce_scatter x1, waiting for transfers between devices, on_device(): reduced = lax.psum_scatter(grads, 'seq', scatter_dimension=2, tiled=True)  64.2 us
    pallas_call x11, Pallas kernels, chain_step(): pl.pallas_call(chain_kernel, out_shape=out_shape, in_specs=[pl.BlockSpec(...  60.8 us
    dot_general x22, matrix products, accumulate(): lax.dot_general(low_part, source, contract_first, preferred_element_type=...  43.7 us
    dot_general x22, matrix products, accumulate(): lax.dot_general(d_low, normalized_part, contract_first, preferred_element...  34.1 us
    psum x1, blocking collectives, on_device(): total = lax.psum(square, 'pipe')  31.9 us
    ppermute x11, waiting for transfers between devices, shifted(): lax.ppermute(value, axis, [(source, source + steps) for source in range(i...  31.5 us
    ppermute x3, waiting for transfers between devices, partner_swap(): lax.ppermute(value, axis, [(source, source ^ 1) for source in range(count)])  25.6 us
    all_gather x1, blocking collectives, on_device(): lax.all_gather(stacked, 'dp', axis=2, tiled=True)  15.7 us
  transfers between devices with their start and end apart: 22, of which 21 were waited for; matrix products, arithmetic and copies ran while one was open for 21% of the time, Pallas kernels for 0%

profile of v9, /device:TPU:6, one launch (start us, length us, event | category | flops | bytes accessed | tf_op | source)
XLA Modules:
  0.0 440.2 jit_solution(3974170604173068473)
XLA Ops:
  8.1 3.8 collective-permute-start.2
  12.0 2.0 collective-permute-done.2
  14.8 15.7 %all_gather.6 = bf16[2,65,1024]{2,1,0:T(8,128)(2,1)} all-gather(bf16[2,65,256]{2,1,0:T(8,128)(2,1)S(1)} %pad_maximum_fusion.1), channel_id=1, replica_groups=mesh['pipe'=16,'seq'=8,'dp'=4] {'dp'}, dimensions={2}, use_global_device_ids=true | all-gather | bytes 332800 | tf_op jit(solution)/shard_map/all_gather | solution.py:99
  30.5 2.3 dynamic-slice_bitcast_fusion
  32.8 1.9 collective-permute-start.1
  34.9 18.5 %collective-permute-done.1 = bf16[64,8192]{1,0:T(8,128)(2,1)} collective-permute-done((bf16[64,8192]{1,0:T(8,128)(2,1)}, bf16[64,8192]{1,0:T(8,128)(2,1)}, u32[]{:S(2)}, u32[]{:S(2)}) %collective-permute-start.1) | collective-permute-done | bytes 1048608 | tf_op jit(solution)/shard_map/ppermute | solution.py:21
  53.4 3.4 fusion.21
  57.0 8.4 %all-gather.2.cloned.1.call-done = bf16[2,65,8192]{2,1,0:T(8,128)(2,1)} async-done(((bf16[2,65,1024]{2,1,0:T(8,128)(2,1)}), bf16[2,65,8192]{2,1,0:T(8,128)(2,1)}) %all-gather.2.cloned.1.call-update) | async-done | bytes 2129936 | tf_op jit(solution)/shard_map/all_gather | solution.py:99
  66.5 1.9 convolution_convert_fusion.1
  68.5 1.8 convolution_convert_fusion
  71.0 2.9 slice_bitcast_fusion
  73.9 2.7 copy.16
  76.5 2.6 copy.18
  79.2 204.5 %while.28 = (s32[]{:T(128)}, bf16[16,8192]{1,0:T(8,128)(2,1)S(1)}, f32[32,8192]{1,0:T(8,128)}, f32[32,8192]{1,0:T(8,128)}, f32[1,8192]{1,0:T(1,128)}, /*index=5*...) while((s32[]{:T(128)}, bf16[16,8192]{1,0:T(8,128)(2,1)S(1)}, ...), condition=%wide.region_3.4_spmd.clone, body=%wide.region_2.3_spmd.clone.sunk | while | flops 71352328 | bytes 40128360 | solution.py:161
  79.9 5.5 %eval_jaxpr.7 = (bf16[16,8192]{1,0:T(8,128)(2,1)}, bf16[16,8192]{1,0:T(8,128)(2,1)}, bf16[16,8192]{1,0:T(8,128)(2,1)}, bf16[16,32]{1,0:T(8,128)(2,1)}, bf16[16,3...) custom-call(s32[2]{0:T(128)} %pad_add_fusion.2.flags, bf16[64,8192]{1,0:T(8,128)(2,1)S(1)} %get-tuple-element.992.top_ref, ...), custom_call_target="tpu_custom_call" | custom-call | flops 33554432 | bytes 2097152 | tf_op jit(solution)/shard_map/while/body/eval_jaxpr/pallas_call | solution.py:64
  87.4 2.5 fusion.52
  94.6 7.9 %collective-permute-done = bf16[16,8192]{1,0:T(8,128)(2,1)S(1)} collective-permute-done((bf16[16,8192]{1,0:T(8,128)(2,1)}, bf16[16,8192]{1,0:T(8,128)(2,1)S(1)}, u32[]{:S(2)}, u32[]{:S(2)}) %collective-permute-start) | collective-permute-done | bytes 262176 | tf_op jit(solution)/shard_map/while/body/eval_jaxpr/ppermute | solution.py:16
  103.1 5.5 %eval_jaxpr.7 = (bf16[16,8192]{1,0:T(8,128)(2,1)}, bf16[16,8192]{1,0:T(8,128)(2,1)}, bf16[16,8192]{1,0:T(8,128)(2,1)}, bf16[16,32]{1,0:T(8,128)(2,1)}, bf16[16,3...) custom-call(s32[2]{0:T(128)} %pad_add_fusion.2.flags, bf16[64,8192]{1,0:T(8,128)(2,1)S(1)} %get-tuple-element.992.top_ref, ...), custom_call_target="tpu_custom_call" | custom-call | flops 33554432 | bytes 2097152 | tf_op jit(solution)/shard_map/while/body/eval_jaxpr/pallas_call | solution.py:64
  110.7 2.9 fusion.52
  118.2 5.4 %collective-permute-done = bf16[16,8192]{1,0:T(8,128)(2,1)S(1)} collective-permute-done((bf16[16,8192]{1,0:T(8,128)(2,1)}, bf16[16,8192]{1,0:T(8,128)(2,1)S(1)}, u32[]{:S(2)}, u32[]{:S(2)}) %collective-permute-start) | collective-permute-done | bytes 262176 | tf_op jit(solution)/shard_map/while/body/eval_jaxpr/ppermute | solution.py:16
  124.3 5.5 %eval_jaxpr.7 = (bf16[16,8192]{1,0:T(8,128)(2,1)}, bf16[16,8192]{1,0:T(8,128)(2,1)}, bf16[16,8192]{1,0:T(8,128)(2,1)}, bf16[16,32]{1,0:T(8,128)(2,1)}, bf16[16,3...) custom-call(s32[2]{0:T(128)} %pad_add_fusion.2.flags, bf16[64,8192]{1,0:T(8,128)(2,1)S(1)} %get-tuple-element.992.top_ref, ...), custom_call_target="tpu_custom_call" | custom-call | flops 33554432 | bytes 2097152 | tf_op jit(solution)/shard_map/while/body/eval_jaxpr/pallas_call | solution.py:64
  131.8 2.9 fusion.52
  139.4 2.9 collective-permute-done
  142.9 5.5 %eval_jaxpr.7 = (bf16[16,8192]{1,0:T(8,128)(2,1)}, bf16[16,8192]{1,0:T(8,128)(2,1)}, bf16[16,8192]{1,0:T(8,128)(2,1)}, bf16[16,32]{1,0:T(8,128)(2,1)}, bf16[16,3...) custom-call(s32[2]{0:T(128)} %pad_add_fusion.2.flags, bf16[64,8192]{1,0:T(8,128)(2,1)S(1)} %get-tuple-element.992.top_ref, ...), custom_call_target="tpu_custom_call" | custom-call | flops 33554432 | bytes 2097152 | tf_op jit(solution)/shard_map/while/body/eval_jaxpr/pallas_call | solution.py:64
  150.5 2.9 fusion.52
  158.0 2.0 collective-permute-done
  160.7 5.5 %eval_jaxpr.7 = (bf16[16,8192]{1,0:T(8,128)(2,1)}, bf16[16,8192]{1,0:T(8,128)(2,1)}, bf16[16,8192]{1,0:T(8,128)(2,1)}, bf16[16,32]{1,0:T(8,128)(2,1)}, bf16[16,3...) custom-call(s32[2]{0:T(128)} %pad_add_fusion.2.flags, bf16[64,8192]{1,0:T(8,128)(2,1)S(1)} %get-tuple-element.992.top_ref, ...), custom_call_target="tpu_custom_call" | custom-call | flops 33554432 | bytes 2097152 | tf_op jit(solution)/shard_map/while/body/eval_jaxpr/pallas_call | solution.py:64
  168.3 2.9 fusion.52
  172.4 1.6 fusion.51
  178.1 5.5 %eval_jaxpr.7 = (bf16[16,8192]{1,0:T(8,128)(2,1)}, bf16[16,8192]{1,0:T(8,128)(2,1)}, bf16[16,8192]{1,0:T(8,128)(2,1)}, bf16[16,32]{1,0:T(8,128)(2,1)}, bf16[16,3...) custom-call(s32[2]{0:T(128)} %pad_add_fusion.2.flags, bf16[64,8192]{1,0:T(8,128)(2,1)S(1)} %get-tuple-element.992.top_ref, ...), custom_call_target="tpu_custom_call" | custom-call | flops 33554432 | bytes 2097152 | tf_op jit(solution)/shard_map/while/body/eval_jaxpr/pallas_call | solution.py:64
  185.6 2.9 fusion.52
  193.2 3.7 collective-permute-done
  197.6 5.5 %eval_jaxpr.7 = (bf16[16,8192]{1,0:T(8,128)(2,1)}, bf16[16,8192]{1,0:T(8,128)(2,1)}, bf16[16,8192]{1,0:T(8,128)(2,1)}, bf16[16,32]{1,0:T(8,128)(2,1)}, bf16[16,3...) custom-call(s32[2]{0:T(128)} %pad_add_fusion.2.flags, bf16[64,8192]{1,0:T(8,128)(2,1)S(1)} %get-tuple-element.992.top_ref, ...), custom_call_target="tpu_custom_call" | custom-call | flops 33554432 | bytes 2097152 | tf_op jit(solution)/shard_map/while/body/eval_jaxpr/pallas_call | solution.py:64
  205.1 2.9 fusion.52
  209.3 1.6 fusion.51
  212.7 1.6 collective-permute-done
  214.9 5.5 %eval_jaxpr.7 = (bf16[16,8192]{1,0:T(8,128)(2,1)}, bf16[16,8192]{1,0:T(8,128)(2,1)}, bf16[16,8192]{1,0:T(8,128)(2,1)}, bf16[16,32]{1,0:T(8,128)(2,1)}, bf16[16,3...) custom-call(s32[2]{0:T(128)} %pad_add_fusion.2.flags, bf16[64,8192]{1,0:T(8,128)(2,1)S(1)} %get-tuple-element.992.top_ref, ...), custom_call_target="tpu_custom_call" | custom-call | flops 33554432 | bytes 2097152 | tf_op jit(solution)/shard_map/while/body/eval_jaxpr/pallas_call | solution.py:64
  222.5 2.9 fusion.52
  226.6 1.6 fusion.51
  232.3 5.5 %eval_jaxpr.7 = (bf16[16,8192]{1,0:T(8,128)(2,1)}, bf16[16,8192]{1,0:T(8,128)(2,1)}, bf16[16,8192]{1,0:T(8,128)(2,1)}, bf16[16,32]{1,0:T(8,128)(2,1)}, bf16[16,3...) custom-call(s32[2]{0:T(128)} %pad_add_fusion.2.flags, bf16[64,8192]{1,0:T(8,128)(2,1)S(1)} %get-tuple-element.992.top_ref, ...), custom_call_target="tpu_custom_call" | custom-call | flops 33554432 | bytes 2097152 | tf_op jit(solution)/shard_map/while/body/eval_jaxpr/pallas_call | solution.py:64
  239.8 2.9 fusion.52
  247.3 1.6 collective-permute-done
  249.6 5.5 %eval_jaxpr.7 = (bf16[16,8192]{1,0:T(8,128)(2,1)}, bf16[16,8192]{1,0:T(8,128)(2,1)}, bf16[16,8192]{1,0:T(8,128)(2,1)}, bf16[16,32]{1,0:T(8,128)(2,1)}, bf16[16,3...) custom-call(s32[2]{0:T(128)} %pad_add_fusion.2.flags, bf16[64,8192]{1,0:T(8,128)(2,1)S(1)} %get-tuple-element.992.top_ref, ...), custom_call_target="tpu_custom_call" | custom-call | flops 33554432 | bytes 2097152 | tf_op jit(solution)/shard_map/while/body/eval_jaxpr/pallas_call | solution.py:64
  257.2 2.9 fusion.52
  264.7 1.6 collective-permute-done
  267.0 5.5 %eval_jaxpr.7 = (bf16[16,8192]{1,0:T(8,128)(2,1)}, bf16[16,8192]{1,0:T(8,128)(2,1)}, bf16[16,8192]{1,0:T(8,128)(2,1)}, bf16[16,32]{1,0:T(8,128)(2,1)}, bf16[16,3...) custom-call(s32[2]{0:T(128)} %pad_add_fusion.2.flags, bf16[64,8192]{1,0:T(8,128)(2,1)S(1)} %get-tuple-element.992.top_ref, ...), custom_call_target="tpu_custom_call" | custom-call | flops 33554432 | bytes 2097152 | tf_op jit(solution)/shard_map/while/body/eval_jaxpr/pallas_call | solution.py:64
  274.5 2.9 fusion.52
  282.0 1.6 collective-permute-done
  283.7 1.9 maximum_bitcast_fusion
  286.1 2.6 pad_maximum_fusion
  288.7 64.2 %reduce-scatter.2.cloned.1.call-done = f32[2,65,1024]{2,1,0:T(8,128)} async-done(((f32[2,65,8192]{2,1,0:T(8,128)}), f32[2,65,1024]{2,1,0:T(8,128)}) %reduce-scatter.2.cloned.1.call-update) | async-done | bytes 532496 | tf_op jit(solution)/shard_map/reduce_scatter | solution.py:165
  354.0 3.5 collective-permute-start.3
  357.5 5.1 %collective-permute-done.3 = f32[65,1024]{1,0:T(8,128)S(1)} collective-permute-done((f32[65,1024]{1,0:T(8,128)S(1)}, f32[65,1024]{1,0:T(8,128)S(1)}, u32[]{:S(2)}, u32[]{:S(2)}) %collective-permute-start.3) | collective-permute-done | bytes 266272 | tf_op jit(solution)/shard_map/ppermute | solution.py:21
  362.6 1.7 multiply_reduce_fusion
  364.3 31.9 %psum.7 = f32[]{:T(128)} all-reduce(f32[]{:T(128)} %get-tuple-element.714), channel_id=1, replica_groups=mesh['pipe'=16,'seq'=8,'dp'=4] {'pipe'}, use_global_device_ids=true, to_apply=%region_6.7 | all-reduce | flops 1 | bytes 8 | tf_op jit(solution)/shard_map/psum | solution.py:172
  396.3 4.3 collective-permute-done.4
  401.9 3.2 collective-permute-start.5
  405.1 3.4 collective-permute-done.5
  409.1 3.2 collective-permute-start.6
  412.3 3.7 collective-permute-done.6
  416.8 2.4 collective-permute-start.7
  419.3 4.3 collective-permute-start.8
  423.6 1.9 collective-permute-start.9
  427.0 4.0 collective-permute-done.9
  (539 shorter events, 84.3 us)
Async XLA Ops:
  7.2 27.6 %copy-start = (bf16[1,128,8192]{2,1,0:T(8,128)(2,1)S(1)}, bf16[1,128,8192]{2,1,0:T(8,128)(2,1)}, u32[]{:S(2)}) copy-start(bf16[1,128,8192]{2,1,0:T(8,128)(2,1)} %param.8) | copy-start | bytes 6291460
  7.2 58.3 %all-gather.2.cloned.1.call-start = ((), (), s32[]{:S(2)}) async-start(), calls=%async_computation.1 | async-start | bytes 2654208 | tf_op jit(solution)/shard_map/all_gather | solution.py:99
  8.1 5.8 %collective-permute-start.2 = (bf16[65,256]{1,0:T(8,128)(2,1)S(1)}, bf16[65,256]{1,0:T(8,128)(2,1)S(1)}, u32[]{:S(2)}, u32[]{:S(2)}) collective-permute-start(bf16[65,256]{1,0:T(8,128)(2,1)S(1)} %pad_maximum_fusion.2), channel_id=1, source_target_pairs={{0,32},{32,0},{64,96},{96,64},{128,160},{160,128},{192,224},{224,1... | collective-permute-start | bytes 99848 | tf_op jit(solution)/shard_map/ppermute | solution.py:21
  30.4 322.5 %reduce-scatter.2.cloned.1.call-start = ((), (), s32[]{:S(2)}) async-start(), calls=%async_computation.2 | async-start | bytes 5308416 | tf_op jit(solution)/shard_map/reduce_scatter | solution.py:165
  32.8 20.6 %collective-permute-start.1 = (bf16[64,8192]{1,0:T(8,128)(2,1)}, bf16[64,8192]{1,0:T(8,128)(2,1)}, u32[]{:S(2)}, u32[]{:S(2)}) collective-permute-start(bf16[64,8192]{1,0:T(8,128)(2,1)} %dynamic-slice_bitcast_fusion), channel_id=1, source_target_pairs={{0,32},{32,0},{64,96},{96,64},{128,160},{160,128},{192,224},{224,1... | collective-permute-start | bytes 3145736 | tf_op jit(solution)/shard_map/ppermute | solution.py:21
  34.8 18.6 %copy-start.5 = (bf16[1,1,128,8192]{3,2,1,0:T(8,128)(2,1)S(1)}, bf16[1,1,128,8192]{3,2,1,0:T(8,128)(2,1)}, u32[]{:S(2)}) copy-start(bf16[1,1,128,8192]{3,2,1,0:T(8,128)(2,1)} %param.7) | copy-start | bytes 6291460
  85.4 17.1 %collective-permute-start = (bf16[16,8192]{1,0:T(8,128)(2,1)}, bf16[16,8192]{1,0:T(8,128)(2,1)S(1)}, u32[]{:S(2)}, u32[]{:S(2)}) collective-permute-start(bf16[16,8192]{1,0:T(8,128)(2,1)} %get-tuple-element.909), channel_id=1, source_target_pairs={{64,0},{96,32},{128,64},{160,96},{192,128},{224,160},{256,192},{28... | collective-permute-start | bytes 786440 | tf_op jit(solution)/shard_map/while/body/eval_jaxpr/ppermute | solution.py:16
  92.8 9.7 %copy-start.12 = (f32[32,8192]{1,0:T(8,128)}, f32[32,8192]{1,0:T(8,128)S(1)}, u32[]{:S(2)}) copy-start(f32[32,8192]{1,0:T(8,128)S(1)} %fusion.51) | copy-start | bytes 3145732 | tf_op jit(solution)/shard_map/while
  92.9 9.5 %copy-start.7 = (f32[1,8192]{1,0:T(1,128)}, f32[1,8192]{1,0:T(1,128)S(1)}, u32[]{:S(2)}) copy-start(f32[1,8192]{1,0:T(1,128)S(1)} %get-tuple-element.986) | copy-start | bytes 98308 | tf_op jit(solution)/shard_map/while
  93.0 9.5 %copy-start.9 = (f32[1,8192]{1,0:T(1,128)}, f32[1,8192]{1,0:T(1,128)S(1)}, u32[]{:S(2)}) copy-start(f32[1,8192]{1,0:T(1,128)S(1)} %get-tuple-element.989) | copy-start | bytes 98308 | tf_op jit(solution)/shard_map/while
  94.6 7.9 %copy-start.14 = (f32[32,8192]{1,0:T(8,128)}, f32[32,8192]{1,0:T(8,128)S(1)}, u32[]{:S(2)}) copy-start(f32[32,8192]{1,0:T(8,128)S(1)} %fusion.54) | copy-start | bytes 3145732 | tf_op jit(solution)/shard_map/while
  108.7 15.0 %collective-permute-start = (bf16[16,8192]{1,0:T(8,128)(2,1)}, bf16[16,8192]{1,0:T(8,128)(2,1)S(1)}, u32[]{:S(2)}, u32[]{:S(2)}) collective-permute-start(bf16[16,8192]{1,0:T(8,128)(2,1)} %get-tuple-element.909), channel_id=1, source_target_pairs={{64,0},{96,32},{128,64},{160,96},{192,128},{224,160},{256,192},{28... | collective-permute-start | bytes 786440 | tf_op jit(solution)/shard_map/while/body/eval_jaxpr/ppermute | solution.py:16
  110.7 4.1 copy-start.21
  110.7 4.2 copy-start.23
  110.7 4.2 copy-start.25
  116.4 7.2 %copy-start.12 = (f32[32,8192]{1,0:T(8,128)}, f32[32,8192]{1,0:T(8,128)S(1)}, u32[]{:S(2)}) copy-start(f32[32,8192]{1,0:T(8,128)S(1)} %fusion.51) | copy-start | bytes 3145732 | tf_op jit(solution)/shard_map/while
  116.6 7.0 %copy-start.7 = (f32[1,8192]{1,0:T(1,128)}, f32[1,8192]{1,0:T(1,128)S(1)}, u32[]{:S(2)}) copy-start(f32[1,8192]{1,0:T(1,128)S(1)} %get-tuple-element.986) | copy-start | bytes 98308 | tf_op jit(solution)/shard_map/while
  116.6 7.0 %copy-start.9 = (f32[1,8192]{1,0:T(1,128)}, f32[1,8192]{1,0:T(1,128)S(1)}, u32[]{:S(2)}) copy-start(f32[1,8192]{1,0:T(1,128)S(1)} %get-tuple-element.989) | copy-start | bytes 98308 | tf_op jit(solution)/shard_map/while
  118.2 5.4 %copy-start.14 = (f32[32,8192]{1,0:T(8,128)}, f32[32,8192]{1,0:T(8,128)S(1)}, u32[]{:S(2)}) copy-start(f32[32,8192]{1,0:T(8,128)S(1)} %fusion.54) | copy-start | bytes 3145732 | tf_op jit(solution)/shard_map/while
  129.8 12.4 %collective-permute-start = (bf16[16,8192]{1,0:T(8,128)(2,1)}, bf16[16,8192]{1,0:T(8,128)(2,1)S(1)}, u32[]{:S(2)}, u32[]{:S(2)}) collective-permute-start(bf16[16,8192]{1,0:T(8,128)(2,1)} %get-tuple-element.909), channel_id=1, source_target_pairs={{64,0},{96,32},{128,64},{160,96},{192,128},{224,160},{256,192},{28... | collective-permute-start | bytes 786440 | tf_op jit(solution)/shard_map/while/body/eval_jaxpr/ppermute | solution.py:16
  131.8 4.1 copy-start.21
  131.8 4.2 copy-start.23
  131.8 4.2 copy-start.25
  137.6 4.7 %copy-start.12 = (f32[32,8192]{1,0:T(8,128)}, f32[32,8192]{1,0:T(8,128)S(1)}, u32[]{:S(2)}) copy-start(f32[32,8192]{1,0:T(8,128)S(1)} %fusion.51) | copy-start | bytes 3145732 | tf_op jit(solution)/shard_map/while
  137.7 4.5 %copy-start.7 = (f32[1,8192]{1,0:T(1,128)}, f32[1,8192]{1,0:T(1,128)S(1)}, u32[]{:S(2)}) copy-start(f32[1,8192]{1,0:T(1,128)S(1)} %get-tuple-element.986) | copy-start | bytes 98308 | tf_op jit(solution)/shard_map/while
  137.8 4.5 %copy-start.9 = (f32[1,8192]{1,0:T(1,128)}, f32[1,8192]{1,0:T(1,128)S(1)}, u32[]{:S(2)}) copy-start(f32[1,8192]{1,0:T(1,128)S(1)} %get-tuple-element.989) | copy-start | bytes 98308 | tf_op jit(solution)/shard_map/while
  148.5 11.6 %collective-permute-start = (bf16[16,8192]{1,0:T(8,128)(2,1)}, bf16[16,8192]{1,0:T(8,128)(2,1)S(1)}, u32[]{:S(2)}, u32[]{:S(2)}) collective-permute-start(bf16[16,8192]{1,0:T(8,128)(2,1)} %get-tuple-element.909), channel_id=1, source_target_pairs={{64,0},{96,32},{128,64},{160,96},{192,128},{224,160},{256,192},{28... | collective-permute-start | bytes 786440 | tf_op jit(solution)/shard_map/while/body/eval_jaxpr/ppermute | solution.py:16
  150.5 4.1 copy-start.21
  150.5 4.1 copy-start.23
  150.5 4.2 copy-start.25
  166.3 11.1 %collective-permute-start = (bf16[16,8192]{1,0:T(8,128)(2,1)}, bf16[16,8192]{1,0:T(8,128)(2,1)S(1)}, u32[]{:S(2)}, u32[]{:S(2)}) collective-permute-start(bf16[16,8192]{1,0:T(8,128)(2,1)} %get-tuple-element.909), channel_id=1, source_target_pairs={{64,0},{96,32},{128,64},{160,96},{192,128},{224,160},{256,192},{28... | collective-permute-start | bytes 786440 | tf_op jit(solution)/shard_map/while/body/eval_jaxpr/ppermute | solution.py:16
  168.3 4.1 copy-start.23
  168.3 4.1 copy-start.25
  183.6 13.3 %collective-permute-start = (bf16[16,8192]{1,0:T(8,128)(2,1)}, bf16[16,8192]{1,0:T(8,128)(2,1)S(1)}, u32[]{:S(2)}, u32[]{:S(2)}) collective-permute-start(bf16[16,8192]{1,0:T(8,128)(2,1)} %get-tuple-element.909), channel_id=1, source_target_pairs={{64,0},{96,32},{128,64},{160,96},{192,128},{224,160},{256,192},{28... | collective-permute-start | bytes 786440 | tf_op jit(solution)/shard_map/while/body/eval_jaxpr/ppermute | solution.py:16
  185.6 4.1 copy-start.21
  185.6 4.1 copy-start.23
  185.6 4.2 copy-start.25
  191.4 5.5 %copy-start.12 = (f32[32,8192]{1,0:T(8,128)}, f32[32,8192]{1,0:T(8,128)S(1)}, u32[]{:S(2)}) copy-start(f32[32,8192]{1,0:T(8,128)S(1)} %fusion.51) | copy-start | bytes 3145732 | tf_op jit(solution)/shard_map/while
  191.5 5.4 %copy-start.7 = (f32[1,8192]{1,0:T(1,128)}, f32[1,8192]{1,0:T(1,128)S(1)}, u32[]{:S(2)}) copy-start(f32[1,8192]{1,0:T(1,128)S(1)} %get-tuple-element.986) | copy-start | bytes 98308 | tf_op jit(solution)/shard_map/while
  191.5 5.4 %copy-start.9 = (f32[1,8192]{1,0:T(1,128)}, f32[1,8192]{1,0:T(1,128)S(1)}, u32[]{:S(2)}) copy-start(f32[1,8192]{1,0:T(1,128)S(1)} %get-tuple-element.989) | copy-start | bytes 98308 | tf_op jit(solution)/shard_map/while
  203.1 11.1 %collective-permute-start = (bf16[16,8192]{1,0:T(8,128)(2,1)}, bf16[16,8192]{1,0:T(8,128)(2,1)S(1)}, u32[]{:S(2)}, u32[]{:S(2)}) collective-permute-start(bf16[16,8192]{1,0:T(8,128)(2,1)} %get-tuple-element.909), channel_id=1, source_target_pairs={{64,0},{96,32},{128,64},{160,96},{192,128},{224,160},{256,192},{28... | collective-permute-start | bytes 786440 | tf_op jit(solution)/shard_map/while/body/eval_jaxpr/ppermute | solution.py:16
  205.1 4.1 copy-start.11
  205.1 4.1 copy-start.21
  205.1 4.2 copy-start.23
  205.1 4.2 copy-start.25
  220.5 11.1 %collective-permute-start = (bf16[16,8192]{1,0:T(8,128)(2,1)}, bf16[16,8192]{1,0:T(8,128)(2,1)S(1)}, u32[]{:S(2)}, u32[]{:S(2)}) collective-permute-start(bf16[16,8192]{1,0:T(8,128)(2,1)} %get-tuple-element.909), channel_id=1, source_target_pairs={{64,0},{96,32},{128,64},{160,96},{192,128},{224,160},{256,192},{28... | collective-permute-start | bytes 786440 | tf_op jit(solution)/shard_map/while/body/eval_jaxpr/ppermute | solution.py:16
  222.5 4.1 copy-start.23
  222.5 4.1 copy-start.25
  237.8 11.1 %collective-permute-start = (bf16[16,8192]{1,0:T(8,128)(2,1)}, bf16[16,8192]{1,0:T(8,128)(2,1)S(1)}, u32[]{:S(2)}, u32[]{:S(2)}) collective-permute-start(bf16[16,8192]{1,0:T(8,128)(2,1)} %get-tuple-element.909), channel_id=1, source_target_pairs={{64,0},{96,32},{128,64},{160,96},{192,128},{224,160},{256,192},{28... | collective-permute-start | bytes 786440 | tf_op jit(solution)/shard_map/while/body/eval_jaxpr/ppermute | solution.py:16
  239.8 4.1 copy-start.23
  239.8 4.1 copy-start.25
  255.2 11.1 %collective-permute-start = (bf16[16,8192]{1,0:T(8,128)(2,1)}, bf16[16,8192]{1,0:T(8,128)(2,1)S(1)}, u32[]{:S(2)}, u32[]{:S(2)}) collective-permute-start(bf16[16,8192]{1,0:T(8,128)(2,1)} %get-tuple-element.909), channel_id=1, source_target_pairs={{64,0},{96,32},{128,64},{160,96},{192,128},{224,160},{256,192},{28... | collective-permute-start | bytes 786440 | tf_op jit(solution)/shard_map/while/body/eval_jaxpr/ppermute | solution.py:16
  257.2 4.1 copy-start.21
  257.2 4.1 copy-start.23
  257.2 4.2 copy-start.25
  272.5 11.1 %collective-permute-start = (bf16[16,8192]{1,0:T(8,128)(2,1)}, bf16[16,8192]{1,0:T(8,128)(2,1)S(1)}, u32[]{:S(2)}, u32[]{:S(2)}) collective-permute-start(bf16[16,8192]{1,0:T(8,128)(2,1)} %get-tuple-element.909), channel_id=1, source_target_pairs={{64,0},{96,32},{128,64},{160,96},{192,128},{224,160},{256,192},{28... | collective-permute-start | bytes 786440 | tf_op jit(solution)/shard_map/while/body/eval_jaxpr/ppermute | solution.py:16
  274.5 4.1 copy-start.25
  354.0 8.6 %collective-permute-start.3 = (f32[65,1024]{1,0:T(8,128)S(1)}, f32[65,1024]{1,0:T(8,128)S(1)}, u32[]{:S(2)}, u32[]{:S(2)}) collective-permute-start(f32[65,1024]{1,0:T(8,128)S(1)} %select_bitcast_fusion), channel_id=1, source_target_pairs={{0,32},{32,0},{64,96},{96,64},{128,160},{160,128},{192,224},{224,1... | collective-permute-start | bytes 798728 | tf_op jit(solution)/shard_map/ppermute | solution.py:21
  396.3 4.3 collective-permute-start.4
  401.9 6.6 %collective-permute-start.5 = (f32[]{:T(128)}, f32[]{:T(128)}, u32[]{:S(2)}, u32[]{:S(2)}) collective-permute-start(f32[]{:T(128)} %add.178), channel_id=1, source_target_pairs={{0,8},{4,12},{8,16},{12,20},{16,24},{20,28},{24,0},{28,4},{1,9},{5... | collective-permute-start | bytes 20 | tf_op jit(solution)/shard_map/ppermute | solution.py:176
  409.1 6.9 %collective-permute-start.6 = (f32[]{:T(128)}, f32[]{:T(128)}, u32[]{:S(2)}, u32[]{:S(2)}) collective-permute-start(f32[]{:T(128)} %add.179), channel_id=1, source_target_pairs={{0,16},{4,20},{8,24},{12,28},{16,0},{20,4},{24,8},{28,12},{1,17},{... | collective-permute-start | bytes 20 | tf_op jit(solution)/shard_map/ppermute | solution.py:176
  416.8 8.7 %collective-permute-start.7 = (f32[65,256]{1,0:T(8,128)S(1)}, f32[65,256]{1,0:T(8,128)S(1)}, u32[]{:S(2)}, u32[]{:S(2)}) collective-permute-start(f32[65,256]{1,0:T(8,128)S(1)} %get-tuple-element.734), channel_id=1, source_target_pairs={{0,1},{1,2},{2,3},{3,0},{4,5},{5,6},{6,7},{7,4},{8,9},{9,10},{10,1... | collective-permute-start | bytes 199688 | tf_op jit(solution)/shard_map/ppermute | solution.py:188
  419.3 7.8 %collective-permute-start.8 = (f32[65,256]{1,0:T(8,128)S(1)}, f32[65,256]{1,0:T(8,128)S(1)}, u32[]{:S(2)}, u32[]{:S(2)}) collective-permute-start(f32[65,256]{1,0:T(8,128)S(1)} %get-tuple-element.736), channel_id=1, source_target_pairs={{0,2},{1,3},{2,0},{3,1},{4,6},{5,7},{6,4},{7,5},{8,10},{9,11},{10,... | collective-permute-start | bytes 199688 | tf_op jit(solution)/shard_map/ppermute | solution.py:188
  423.6 7.5 %collective-permute-start.9 = (f32[65,256]{1,0:T(8,128)S(1)}, f32[65,256]{1,0:T(8,128)S(1)}, u32[]{:S(2)}, u32[]{:S(2)}) collective-permute-start(f32[65,256]{1,0:T(8,128)S(1)} %get-tuple-element.735), channel_id=1, source_target_pairs={{0,3},{1,0},{2,1},{3,2},{4,7},{5,4},{6,5},{7,6},{8,11},{9,8},{10,9... | collective-permute-start | bytes 199688 | tf_op jit(solution)/shard_map/ppermute | solution.py:188
  (174 other events, 530.8 us)
Sparse Core Ops, SparseCore 0:
  30.6 34.8 all-gather.1
  288.8 64.0 reduce-scatter.1

commit v10 on v8

--- a/solution.py
+++ b/solution.py
@@ -1,3 +1,4 @@
+import functools
 import math
 
 import jax
@@ -21,16 +22,17 @@
     return lax.ppermute(value, axis, [(source, source ^ 1) for source in range(count)])
 
 
-def chain_kernel(flags, top_ref, incoming_ref, *refs):
-    (hidden_u, root_u, b_u, a_u, g_u, hidden_l, root_l, b_l, a_l, g_l,
+def chain_kernel(pairs, block_total, turn_ref, top_ref, incoming_ref, *refs):
+    (hidden_u, root_u, proj_u, b_u, a_u, g_u, hidden_l, root_l, proj_l, b_l, a_l, g_l,
      source_ref, middle_ref, result_ref, low_u_ref, low_l_ref, pg_u_ref, pg_l_ref) = refs
-    rows = incoming_ref.shape[0]
-    offset = pl.multiple_of(flags[0] * rows, rows)
-    window = pl.ds(offset, rows)
-    source = jnp.where(flags[1] == 1, top_ref[window, :], incoming_ref[...])
+    rows, width = incoming_ref.shape
+    pair = lax.axis_index("pipe") // 2
+    block = jnp.clip(turn_ref[0] - (pairs - 1 - pair), 0, block_total - 1)
+    window = pl.ds(pl.multiple_of(block * rows, rows), rows)
+    source = jnp.where(pair == pairs - 1, top_ref[window, :], incoming_ref[...])
     source_ref[...] = source
 
-    def one_layer(upstream, hidden_ref, root_ref, b_ref, a_ref, g_ref, low_ref, pg_ref):
+    def one_layer(upstream, hidden_ref, root_ref, proj_ref, b_ref, a_ref, g_ref, low_ref, pg_ref):
         root = root_ref[window, :]
         normalized = hidden_ref[window, :].astype(jnp.float32) / root
         d_low = lax.dot_general(
@@ -38,21 +40,21 @@
         ).astype(jnp.bfloat16)
         normalized_gradient = jnp.dot(d_low, a_ref[...], preferred_element_type=jnp.float32)
         input_gradient = normalized_gradient * g_ref[...]
-        mean = jnp.mean(input_gradient * normalized, axis=-1, keepdims=True)
+        mean = jnp.sum(d_low.astype(jnp.float32) * proj_ref[window, :], axis=-1, keepdims=True) / width
         low_ref[...] = d_low
         pg_ref[...] = jnp.sum(normalized_gradient * normalized, axis=0, keepdims=True)
         return (upstream.astype(jnp.float32) + (input_gradient - normalized * mean) / root).astype(
             jnp.bfloat16
         )
 
-    middle = one_layer(source, hidden_u, root_u, b_u, a_u, g_u, low_u_ref, pg_u_ref)
+    middle = one_layer(source, hidden_u, root_u, proj_u, b_u, a_u, g_u, low_u_ref, pg_u_ref)
     middle_ref[...] = middle
-    result_ref[...] = one_layer(middle, hidden_l, root_l, b_l, a_l, g_l, low_l_ref, pg_l_ref)
-
-
-def chain_step(flags, top, incoming, upper, lower, rows):
-    width = incoming.shape[1]
-    rank = upper[2].shape[0]
+    result_ref[...] = one_layer(middle, hidden_l, root_l, proj_l, b_l, a_l, g_l, low_l_ref, pg_l_ref)
+
+
+def chain_step(turn, top, incoming, upper, lower, pairs, block_total):
+    rows, width = incoming.shape
+    rank = upper[3].shape[0]
     resident = pl.BlockSpec(memory_space=pltpu.VMEM)
     out_shape = [
         jax.ShapeDtypeStruct((rows, width), jnp.bfloat16),
@@ -64,14 +66,14 @@
         jax.ShapeDtypeStruct((1, width), jnp.float32),
     ]
     return pl.pallas_call(
-        chain_kernel,
+        functools.partial(chain_kernel, pairs, block_total),
         out_shape=out_shape,
-        in_specs=[pl.BlockSpec(memory_space=pltpu.SMEM)] + [resident] * 12,
+        in_specs=[pl.BlockSpec(memory_space=pltpu.SMEM)] + [resident] * 14,
         out_specs=[resident] * 7,
         cost_estimate=pl.CostEstimate(
             flops=8 * rows * width * rank, transcendentals=0, bytes_accessed=16 * rows * width
         ),
-    )(flags, top, incoming, *upper, *lower)
+    )(turn, top, incoming, *upper, *lower)
 
 
 def on_device(acts, top_grad, a_rows, b_rows, gain):
@@ -117,7 +119,12 @@
             jnp.bfloat16
         )
         layers.append((hidden, inverse_root_mean, low, a_full, b_full, gain_float))
-        operands.append((hidden, inverse_root_mean, b_full, a_full, gain_float[None, :]))
+        projection = jnp.dot(
+            (hidden_float / inverse_root_mean) * gain_float,
+            a_full.astype(jnp.float32).T,
+            precision=lax.Precision.HIGHEST,
+        )
+        operands.append((hidden, inverse_root_mean, projection, b_full, a_full, gain_float[None, :]))
     block_total = half_rows // rows_per_block
 
     def accumulate(layer, source, d_low, part_g, block_offset, sums, inside):
@@ -143,9 +150,9 @@
         inside = jnp.logical_and(block_index >= 0, block_index < block_total)
         clipped = jnp.clip(block_index, 0, block_total - 1)
         block_offset = clipped * rows_per_block
-        flags = jnp.stack([clipped, (pair == pairs - 1).astype(jnp.int32)]).astype(jnp.int32)
         source, middle, result, low_u, low_l, pg_u, pg_l = chain_step(
-            flags, top, incoming, operands[0], operands[1], rows_per_block
+            jnp.reshape(turn_index, (1,)).astype(jnp.int32), top, incoming, operands[0], operands[1],
+            pairs, block_total,
         )
         incoming = shifted(result, "pipe", -2)
         upper_sums = accumulate(layers[0], source, low_u, pg_u, block_offset, upper_sums, inside)

time: 443 us -> 440 us (level)
  matrix products: 58.3 us -> 66.4 us
  other arithmetic: 21.7 us -> 14.5 us
    another operation x11 -> x0, other arithmetic: 7.17 us -> none  [turn(): jnp.stack([clipped, (pair == pairs - 1).astype(jnp.int32)])]
    dot_general x0 -> x2, matrix products: none -> 5.36 us  [on_device(): jnp.dot(hidden_float / inverse_root_mean * gain_float, a_full.astype(jnp....]
  transfers between devices with their start and end apart: 22 -> 22, of which waited for: 21 -> 21; matrix products, arithmetic and copies ran while one was open for 16% -> 17% of each run, Pallas kernels for 0% -> 0%
where the time goes in v10:
time: 440 us; the launch traced here: 439 us
  waiting for transfers between devices  184 us (42%)
  matrix products  66.4 us (15%)
  Pallas kernels  50.1 us (11%)
  blocking collectives  47.6 us (11%)
  starting transfers between devices  38.4 us (9%)
  between operations  17.9 us (4%)
  local copies, waits for them, and re-layouts  15.8 us (4%)
  other arithmetic  14.5 us (3%)
    reduce_scatter x1, waiting for transfers between devices, on_device(): reduced = lax.psum_scatter(grads, 'seq', scatter_dimension=2, tiled=True)  80.7 us
    ppermute x11, waiting for transfers between devices, shifted(): lax.ppermute(value, axis, [(source, source + steps) for source in range(i...  53 us
    pallas_call x11, Pallas kernels, chain_step(): pl.pallas_call(functools.partial(chain_kernel, pairs, block_total), out_s...  50.1 us
    dot_general x22, matrix products, accumulate(): lax.dot_general(d_low, normalized_part, contract_first, preferred_element...  36.9 us
    psum x1, blocking collectives, on_device(): total = lax.psum(square, 'pipe')  31.9 us
    ppermute x3, waiting for transfers between devices, partner_swap(): lax.ppermute(value, axis, [(source, source ^ 1) for source in range(count)])  24.7 us
    dot_general x22, matrix products, accumulate(): lax.dot_general(low_part, source, contract_first, preferred_element_type=...  20.4 us
    all_gather x1, blocking collectives, on_device(): lax.all_gather(stacked, 'dp', axis=2, tiled=True)  15.7 us
  transfers between devices with their start and end apart: 22, of which 21 were waited for; matrix products, arithmetic and copies ran while one was open for 17% of the time, Pallas kernels for 0%

profile of v10, /device:TPU:6, one launch (start us, length us, event | category | flops | bytes accessed | tf_op | source)
XLA Modules:
  0.0 438.5 jit_solution(215620436073305801)
XLA Ops:
  8.1 3.8 collective-permute-start.2
  12.0 2.0 collective-permute-done.2
  14.8 15.7 %all_gather.6 = bf16[2,65,1024]{2,1,0:T(8,128)(2,1)} all-gather(bf16[2,65,256]{2,1,0:T(8,128)(2,1)S(1)} %pad_maximum_fusion.1), channel_id=1, replica_groups=mesh['pipe'=16,'seq'=8,'dp'=4] {'dp'}, dimensions={2}, use_global_device_ids=true | all-gather | bytes 332800 | tf_op jit(solution)/shard_map/all_gather | solution.py:103
  30.5 2.3 dynamic-slice_bitcast_fusion
  32.8 1.9 collective-permute-start.1
  35.8 17.6 %collective-permute-done.1 = bf16[64,8192]{1,0:T(8,128)(2,1)} collective-permute-done((bf16[64,8192]{1,0:T(8,128)(2,1)}, bf16[64,8192]{1,0:T(8,128)(2,1)}, u32[]{:S(2)}, u32[]{:S(2)}) %collective-permute-start.1) | collective-permute-done | bytes 1048608 | tf_op jit(solution)/shard_map/ppermute | solution.py:22
  53.4 3.4 fusion.20
  57.0 8.4 %all-gather.2.cloned.1.call-done = bf16[2,65,8192]{2,1,0:T(8,128)(2,1)} async-done(((bf16[2,65,1024]{2,1,0:T(8,128)(2,1)}), bf16[2,65,8192]{2,1,0:T(8,128)(2,1)}) %all-gather.2.cloned.1.call-update) | async-done | bytes 2129936 | tf_op jit(solution)/shard_map/all_gather | solution.py:103
  66.5 1.9 convolution_convert_fusion
  68.5 1.8 convolution_convert_fusion.1
  71.0 3.4 fusion.23
  74.4 2.0 fusion.26
  77.8 187.9 %while.28 = (s32[]{:T(128)}, bf16[16,8192]{1,0:T(8,128)(2,1)S(1)}, f32[32,8192]{1,0:T(8,128)}, f32[32,8192]{1,0:T(8,128)S(1)}, f32[1,8192]{1,0:T(1,128)}, /*inde...) while((s32[]{:T(128)}, bf16[16,8192]{1,0:T(8,128)(2,1)S(1)}, ...), condition=%wide.region_3.4_spmd.clone, body=%wide.region_2.3_spmd.clone.sunk | while | flops 71352320 | bytes 40128352 | solution.py:170
  77.8 4.6 %eval_jaxpr.7 = (bf16[16,8192]{1,0:T(8,128)(2,1)}, bf16[16,8192]{1,0:T(8,128)(2,1)}, bf16[16,8192]{1,0:T(8,128)(2,1)}, bf16[16,32]{1,0:T(8,128)(2,1)}, bf16[16,3...) custom-call(s32[1]{0:T(128)} %bitcast.65.turn_ref, bf16[64,8192]{1,0:T(8,128)(2,1)} %get-tuple-element.1038.top_ref, ...), custom_call_target="tpu_custom_call" | custom-call | flops 33554432 | bytes 2097152 | tf_op jit(solution)/shard_map/while/body/eval_jaxpr/pallas_call | solution.py:68
  86.4 1.8 fusion.59
  90.0 9.4 %collective-permute-done = bf16[16,8192]{1,0:T(8,128)(2,1)S(1)} collective-permute-done((bf16[16,8192]{1,0:T(8,128)(2,1)}, bf16[16,8192]{1,0:T(8,128)(2,1)S(1)}, u32[]{:S(2)}, u32[]{:S(2)}) %collective-permute-start) | collective-permute-done | bytes 262176 | tf_op jit(solution)/shard_map/while/body/eval_jaxpr/ppermute | solution.py:17
  99.4 4.6 %eval_jaxpr.7 = (bf16[16,8192]{1,0:T(8,128)(2,1)}, bf16[16,8192]{1,0:T(8,128)(2,1)}, bf16[16,8192]{1,0:T(8,128)(2,1)}, bf16[16,32]{1,0:T(8,128)(2,1)}, bf16[16,3...) custom-call(s32[1]{0:T(128)} %bitcast.65.turn_ref, bf16[64,8192]{1,0:T(8,128)(2,1)} %get-tuple-element.1038.top_ref, ...), custom_call_target="tpu_custom_call" | custom-call | flops 33554432 | bytes 2097152 | tf_op jit(solution)/shard_map/while/body/eval_jaxpr/pallas_call | solution.py:68
  108.0 1.8 fusion.59
  111.6 7.3 %collective-permute-done = bf16[16,8192]{1,0:T(8,128)(2,1)S(1)} collective-permute-done((bf16[16,8192]{1,0:T(8,128)(2,1)}, bf16[16,8192]{1,0:T(8,128)(2,1)S(1)}, u32[]{:S(2)}, u32[]{:S(2)}) %collective-permute-start) | collective-permute-done | bytes 262176 | tf_op jit(solution)/shard_map/while/body/eval_jaxpr/ppermute | solution.py:17
  118.9 4.6 %eval_jaxpr.7 = (bf16[16,8192]{1,0:T(8,128)(2,1)}, bf16[16,8192]{1,0:T(8,128)(2,1)}, bf16[16,8192]{1,0:T(8,128)(2,1)}, bf16[16,32]{1,0:T(8,128)(2,1)}, bf16[16,3...) custom-call(s32[1]{0:T(128)} %bitcast.65.turn_ref, bf16[64,8192]{1,0:T(8,128)(2,1)} %get-tuple-element.1038.top_ref, ...), custom_call_target="tpu_custom_call" | custom-call | flops 33554432 | bytes 2097152 | tf_op jit(solution)/shard_map/while/body/eval_jaxpr/pallas_call | solution.py:68
  127.5 1.8 fusion.59
  129.6 1.5 fusion.62
  131.2 4.8 %collective-permute-done = bf16[16,8192]{1,0:T(8,128)(2,1)S(1)} collective-permute-done((bf16[16,8192]{1,0:T(8,128)(2,1)}, bf16[16,8192]{1,0:T(8,128)(2,1)S(1)}, u32[]{:S(2)}, u32[]{:S(2)}) %collective-permute-start) | collective-permute-done | bytes 262176 | tf_op jit(solution)/shard_map/while/body/eval_jaxpr/ppermute | solution.py:17
  136.0 4.6 %eval_jaxpr.7 = (bf16[16,8192]{1,0:T(8,128)(2,1)}, bf16[16,8192]{1,0:T(8,128)(2,1)}, bf16[16,8192]{1,0:T(8,128)(2,1)}, bf16[16,32]{1,0:T(8,128)(2,1)}, bf16[16,3...) custom-call(s32[1]{0:T(128)} %bitcast.65.turn_ref, bf16[64,8192]{1,0:T(8,128)(2,1)} %get-tuple-element.1038.top_ref, ...), custom_call_target="tpu_custom_call" | custom-call | flops 33554432 | bytes 2097152 | tf_op jit(solution)/shard_map/while/body/eval_jaxpr/pallas_call | solution.py:68
  144.6 1.8 fusion.59
  146.6 1.5 fusion.62
  148.2 3.9 collective-permute-done
  152.1 4.6 %eval_jaxpr.7 = (bf16[16,8192]{1,0:T(8,128)(2,1)}, bf16[16,8192]{1,0:T(8,128)(2,1)}, bf16[16,8192]{1,0:T(8,128)(2,1)}, bf16[16,32]{1,0:T(8,128)(2,1)}, bf16[16,3...) custom-call(s32[1]{0:T(128)} %bitcast.65.turn_ref, bf16[64,8192]{1,0:T(8,128)(2,1)} %get-tuple-element.1038.top_ref, ...), custom_call_target="tpu_custom_call" | custom-call | flops 33554432 | bytes 2097152 | tf_op jit(solution)/shard_map/while/body/eval_jaxpr/pallas_call | solution.py:68
  160.7 1.8 fusion.59
  164.3 3.0 collective-permute-done
  167.3 4.6 %eval_jaxpr.7 = (bf16[16,8192]{1,0:T(8,128)(2,1)}, bf16[16,8192]{1,0:T(8,128)(2,1)}, bf16[16,8192]{1,0:T(8,128)(2,1)}, bf16[16,32]{1,0:T(8,128)(2,1)}, bf16[16,3...) custom-call(s32[1]{0:T(128)} %bitcast.65.turn_ref, bf16[64,8192]{1,0:T(8,128)(2,1)} %get-tuple-element.1038.top_ref, ...), custom_call_target="tpu_custom_call" | custom-call | flops 33554432 | bytes 2097152 | tf_op jit(solution)/shard_map/while/body/eval_jaxpr/pallas_call | solution.py:68
  175.9 1.8 fusion.59
  179.5 6.1 %collective-permute-done = bf16[16,8192]{1,0:T(8,128)(2,1)S(1)} collective-permute-done((bf16[16,8192]{1,0:T(8,128)(2,1)}, bf16[16,8192]{1,0:T(8,128)(2,1)S(1)}, u32[]{:S(2)}, u32[]{:S(2)}) %collective-permute-start) | collective-permute-done | bytes 262176 | tf_op jit(solution)/shard_map/while/body/eval_jaxpr/ppermute | solution.py:17
  185.7 4.6 %eval_jaxpr.7 = (bf16[16,8192]{1,0:T(8,128)(2,1)}, bf16[16,8192]{1,0:T(8,128)(2,1)}, bf16[16,8192]{1,0:T(8,128)(2,1)}, bf16[16,32]{1,0:T(8,128)(2,1)}, bf16[16,3...) custom-call(s32[1]{0:T(128)} %bitcast.65.turn_ref, bf16[64,8192]{1,0:T(8,128)(2,1)} %get-tuple-element.1038.top_ref, ...), custom_call_target="tpu_custom_call" | custom-call | flops 33554432 | bytes 2097152 | tf_op jit(solution)/shard_map/while/body/eval_jaxpr/pallas_call | solution.py:68
  194.3 1.8 fusion.59
  197.9 2.6 collective-permute-done
  200.6 4.6 %eval_jaxpr.7 = (bf16[16,8192]{1,0:T(8,128)(2,1)}, bf16[16,8192]{1,0:T(8,128)(2,1)}, bf16[16,8192]{1,0:T(8,128)(2,1)}, bf16[16,32]{1,0:T(8,128)(2,1)}, bf16[16,3...) custom-call(s32[1]{0:T(128)} %bitcast.65.turn_ref, bf16[64,8192]{1,0:T(8,128)(2,1)} %get-tuple-element.1038.top_ref, ...), custom_call_target="tpu_custom_call" | custom-call | flops 33554432 | bytes 2097152 | tf_op jit(solution)/shard_map/while/body/eval_jaxpr/pallas_call | solution.py:68
  209.2 1.8 fusion.59
  212.8 3.0 collective-permute-done
  215.9 4.6 %eval_jaxpr.7 = (bf16[16,8192]{1,0:T(8,128)(2,1)}, bf16[16,8192]{1,0:T(8,128)(2,1)}, bf16[16,8192]{1,0:T(8,128)(2,1)}, bf16[16,32]{1,0:T(8,128)(2,1)}, bf16[16,3...) custom-call(s32[1]{0:T(128)} %bitcast.65.turn_ref, bf16[64,8192]{1,0:T(8,128)(2,1)} %get-tuple-element.1038.top_ref, ...), custom_call_target="tpu_custom_call" | custom-call | flops 33554432 | bytes 2097152 | tf_op jit(solution)/shard_map/while/body/eval_jaxpr/pallas_call | solution.py:68
  224.5 1.8 fusion.59
  228.1 4.7 %collective-permute-done = bf16[16,8192]{1,0:T(8,128)(2,1)S(1)} collective-permute-done((bf16[16,8192]{1,0:T(8,128)(2,1)}, bf16[16,8192]{1,0:T(8,128)(2,1)S(1)}, u32[]{:S(2)}, u32[]{:S(2)}) %collective-permute-start) | collective-permute-done | bytes 262176 | tf_op jit(solution)/shard_map/while/body/eval_jaxpr/ppermute | solution.py:17
  232.8 4.6 %eval_jaxpr.7 = (bf16[16,8192]{1,0:T(8,128)(2,1)}, bf16[16,8192]{1,0:T(8,128)(2,1)}, bf16[16,8192]{1,0:T(8,128)(2,1)}, bf16[16,32]{1,0:T(8,128)(2,1)}, bf16[16,3...) custom-call(s32[1]{0:T(128)} %bitcast.65.turn_ref, bf16[64,8192]{1,0:T(8,128)(2,1)} %get-tuple-element.1038.top_ref, ...), custom_call_target="tpu_custom_call" | custom-call | flops 33554432 | bytes 2097152 | tf_op jit(solution)/shard_map/while/body/eval_jaxpr/pallas_call | solution.py:68
  241.4 1.8 fusion.59
  245.0 2.8 collective-permute-done
  247.8 4.6 %eval_jaxpr.7 = (bf16[16,8192]{1,0:T(8,128)(2,1)}, bf16[16,8192]{1,0:T(8,128)(2,1)}, bf16[16,8192]{1,0:T(8,128)(2,1)}, bf16[16,32]{1,0:T(8,128)(2,1)}, bf16[16,3...) custom-call(s32[1]{0:T(128)} %bitcast.65.turn_ref, bf16[64,8192]{1,0:T(8,128)(2,1)} %get-tuple-element.1038.top_ref, ...), custom_call_target="tpu_custom_call" | custom-call | flops 33554432 | bytes 2097152 | tf_op jit(solution)/shard_map/while/body/eval_jaxpr/pallas_call | solution.py:68
  256.4 1.8 fusion.59
  260.1 5.6 %collective-permute-done = bf16[16,8192]{1,0:T(8,128)(2,1)S(1)} collective-permute-done((bf16[16,8192]{1,0:T(8,128)(2,1)}, bf16[16,8192]{1,0:T(8,128)(2,1)S(1)}, u32[]{:S(2)}, u32[]{:S(2)}) %collective-permute-start) | collective-permute-done | bytes 262176 | tf_op jit(solution)/shard_map/while/body/eval_jaxpr/ppermute | solution.py:17
  265.7 1.6 maximum_bitcast_fusion
  267.8 2.6 pad_maximum_fusion
  270.4 80.7 %reduce-scatter.2.cloned.1.call-done = f32[2,65,1024]{2,1,0:T(8,128)} async-done(((f32[2,65,8192]{2,1,0:T(8,128)}), f32[2,65,1024]{2,1,0:T(8,128)}) %reduce-scatter.2.cloned.1.call-update) | async-done | bytes 532496 | tf_op jit(solution)/shard_map/reduce_scatter | solution.py:174
  352.1 3.5 collective-permute-start.3
  355.6 5.1 %collective-permute-done.3 = f32[65,1024]{1,0:T(8,128)S(1)} collective-permute-done((f32[65,1024]{1,0:T(8,128)S(1)}, f32[65,1024]{1,0:T(8,128)S(1)}, u32[]{:S(2)}, u32[]{:S(2)}) %collective-permute-start.3) | collective-permute-done | bytes 266272 | tf_op jit(solution)/shard_map/ppermute | solution.py:22
  360.7 1.7 multiply_reduce_fusion
  362.5 31.9 %psum.7 = f32[]{:T(128)} all-reduce(f32[]{:T(128)} %get-tuple-element.754), channel_id=1, replica_groups=mesh['pipe'=16,'seq'=8,'dp'=4] {'pipe'}, use_global_device_ids=true, to_apply=%region_6.7 | all-reduce | flops 1 | bytes 8 | tf_op jit(solution)/shard_map/psum | solution.py:181
  394.4 4.4 %collective-permute-done.4 = f32[]{:T(128)} collective-permute-done((f32[]{:T(128)}, f32[]{:T(128)}, u32[]{:S(2)}, u32[]{:S(2)}) %collective-permute-start.4) | collective-permute-done | bytes 36 | tf_op jit(solution)/shard_map/ppermute | solution.py:185
  400.0 3.2 collective-permute-start.5
  403.2 3.6 collective-permute-done.5
  407.4 3.2 collective-permute-start.6
  410.6 3.9 collective-permute-done.6
  415.1 2.5 collective-permute-start.7
  417.6 4.3 collective-permute-start.8
  421.9 1.9 collective-permute-start.9
  425.4 4.0 collective-permute-done.9
  (532 shorter events, 68.8 us)
Async XLA Ops:
  7.2 27.6 %copy-start = (bf16[1,128,8192]{2,1,0:T(8,128)(2,1)S(1)}, bf16[1,128,8192]{2,1,0:T(8,128)(2,1)}, u32[]{:S(2)}) copy-start(bf16[1,128,8192]{2,1,0:T(8,128)(2,1)} %param.8) | copy-start | bytes 6291460
  7.2 58.3 %all-gather.2.cloned.1.call-start = ((), (), s32[]{:S(2)}) async-start(), calls=%async_computation.1 | async-start | bytes 2654208 | tf_op jit(solution)/shard_map/all_gather | solution.py:103
  8.1 5.8 %collective-permute-start.2 = (bf16[65,256]{1,0:T(8,128)(2,1)S(1)}, bf16[65,256]{1,0:T(8,128)(2,1)S(1)}, u32[]{:S(2)}, u32[]{:S(2)}) collective-permute-start(bf16[65,256]{1,0:T(8,128)(2,1)S(1)} %pad_maximum_fusion.2), channel_id=1, source_target_pairs={{0,32},{32,0},{64,96},{96,64},{128,160},{160,128},{192,224},{224,1... | collective-permute-start | bytes 99848 | tf_op jit(solution)/shard_map/ppermute | solution.py:22
  30.4 320.6 %reduce-scatter.2.cloned.1.call-start = ((), (), s32[]{:S(2)}) async-start(), calls=%async_computation.2 | async-start | bytes 5308416 | tf_op jit(solution)/shard_map/reduce_scatter | solution.py:174
  32.8 20.6 %collective-permute-start.1 = (bf16[64,8192]{1,0:T(8,128)(2,1)}, bf16[64,8192]{1,0:T(8,128)(2,1)}, u32[]{:S(2)}, u32[]{:S(2)}) collective-permute-start(bf16[64,8192]{1,0:T(8,128)(2,1)} %dynamic-slice_bitcast_fusion), channel_id=1, source_target_pairs={{0,32},{32,0},{64,96},{96,64},{128,160},{160,128},{192,224},{224,1... | collective-permute-start | bytes 3145736 | tf_op jit(solution)/shard_map/ppermute | solution.py:22
  34.8 18.6 %copy-start.6 = (bf16[1,1,128,8192]{3,2,1,0:T(8,128)(2,1)S(1)}, bf16[1,1,128,8192]{3,2,1,0:T(8,128)(2,1)}, u32[]{:S(2)}) copy-start(bf16[1,1,128,8192]{3,2,1,0:T(8,128)(2,1)} %param.7) | copy-start | bytes 6291460
  66.5 4.5 %copy-start.20 = (f32[1,1,8192]{2,1,0:T(1,128)}, f32[1,1,8192]{2,1,0:T(1,128)S(1)}, u32[]{:S(2)}) copy-start(f32[1,1,8192]{2,1,0:T(1,128)S(1)} %get-tuple-element.768) | copy-start | bytes 98308
  66.5 7.9 %copy-start.22 = (f32[1,1,8192]{2,1,0:T(1,128)}, f32[1,1,8192]{2,1,0:T(1,128)S(1)}, u32[]{:S(2)}) copy-start(f32[1,1,8192]{2,1,0:T(1,128)S(1)} %get-tuple-element.769) | copy-start | bytes 98308
  82.3 17.1 %collective-permute-start = (bf16[16,8192]{1,0:T(8,128)(2,1)}, bf16[16,8192]{1,0:T(8,128)(2,1)S(1)}, u32[]{:S(2)}, u32[]{:S(2)}) collective-permute-start(bf16[16,8192]{1,0:T(8,128)(2,1)} %get-tuple-element.955), channel_id=1, source_target_pairs={{64,0},{96,32},{128,64},{160,96},{192,128},{224,160},{256,192},{28... | collective-permute-start | bytes 786440 | tf_op jit(solution)/shard_map/while/body/eval_jaxpr/ppermute | solution.py:17
  88.2 11.2 %copy-start.14 = (f32[32,8192]{1,0:T(8,128)}, f32[32,8192]{1,0:T(8,128)S(1)}, u32[]{:S(2)}) copy-start(f32[32,8192]{1,0:T(8,128)S(1)} %fusion.59) | copy-start | bytes 3145732 | tf_op jit(solution)/shard_map/while
  88.4 11.0 %copy-start.9 = (f32[1,8192]{1,0:T(1,128)}, f32[1,8192]{1,0:T(1,128)S(1)}, u32[]{:S(2)}) copy-start(f32[1,8192]{1,0:T(1,128)S(1)} %get-tuple-element.1034) | copy-start | bytes 98308 | tf_op jit(solution)/shard_map/while
  88.4 11.0 %copy-start.11 = (f32[1,8192]{1,0:T(1,128)}, f32[1,8192]{1,0:T(1,128)S(1)}, u32[]{:S(2)}) copy-start(f32[1,8192]{1,0:T(1,128)S(1)} %get-tuple-element.1037) | copy-start | bytes 98308 | tf_op jit(solution)/shard_map/while
  90.0 9.4 %copy-start.16 = (f32[32,8192]{1,0:T(8,128)}, f32[32,8192]{1,0:T(8,128)S(1)}, u32[]{:S(2)}) copy-start(f32[32,8192]{1,0:T(8,128)S(1)} %fusion.62) | copy-start | bytes 3145732 | tf_op jit(solution)/shard_map/while
  104.0 14.9 %collective-permute-start = (bf16[16,8192]{1,0:T(8,128)(2,1)}, bf16[16,8192]{1,0:T(8,128)(2,1)S(1)}, u32[]{:S(2)}, u32[]{:S(2)}) collective-permute-start(bf16[16,8192]{1,0:T(8,128)(2,1)} %get-tuple-element.955), channel_id=1, source_target_pairs={{64,0},{96,32},{128,64},{160,96},{192,128},{224,160},{256,192},{28... | collective-permute-start | bytes 786440 | tf_op jit(solution)/shard_map/while/body/eval_jaxpr/ppermute | solution.py:17
  109.8 9.1 %copy-start.14 = (f32[32,8192]{1,0:T(8,128)}, f32[32,8192]{1,0:T(8,128)S(1)}, u32[]{:S(2)}) copy-start(f32[32,8192]{1,0:T(8,128)S(1)} %fusion.59) | copy-start | bytes 3145732 | tf_op jit(solution)/shard_map/while
  110.0 8.9 %copy-start.9 = (f32[1,8192]{1,0:T(1,128)}, f32[1,8192]{1,0:T(1,128)S(1)}, u32[]{:S(2)}) copy-start(f32[1,8192]{1,0:T(1,128)S(1)} %get-tuple-element.1034) | copy-start | bytes 98308 | tf_op jit(solution)/shard_map/while
  110.0 8.9 %copy-start.11 = (f32[1,8192]{1,0:T(1,128)}, f32[1,8192]{1,0:T(1,128)S(1)}, u32[]{:S(2)}) copy-start(f32[1,8192]{1,0:T(1,128)S(1)} %get-tuple-element.1037) | copy-start | bytes 98308 | tf_op jit(solution)/shard_map/while
  111.6 7.3 %copy-start.16 = (f32[32,8192]{1,0:T(8,128)}, f32[32,8192]{1,0:T(8,128)S(1)}, u32[]{:S(2)}) copy-start(f32[32,8192]{1,0:T(8,128)S(1)} %fusion.62) | copy-start | bytes 3145732 | tf_op jit(solution)/shard_map/while
  123.5 12.4 %collective-permute-start = (bf16[16,8192]{1,0:T(8,128)(2,1)}, bf16[16,8192]{1,0:T(8,128)(2,1)S(1)}, u32[]{:S(2)}, u32[]{:S(2)}) collective-permute-start(bf16[16,8192]{1,0:T(8,128)(2,1)} %get-tuple-element.955), channel_id=1, source_target_pairs={{64,0},{96,32},{128,64},{160,96},{192,128},{224,160},{256,192},{28... | collective-permute-start | bytes 786440 | tf_op jit(solution)/shard_map/while/body/eval_jaxpr/ppermute | solution.py:17
  129.4 6.6 %copy-start.14 = (f32[32,8192]{1,0:T(8,128)}, f32[32,8192]{1,0:T(8,128)S(1)}, u32[]{:S(2)}) copy-start(f32[32,8192]{1,0:T(8,128)S(1)} %fusion.59) | copy-start | bytes 3145732 | tf_op jit(solution)/shard_map/while
  129.5 6.4 %copy-start.9 = (f32[1,8192]{1,0:T(1,128)}, f32[1,8192]{1,0:T(1,128)S(1)}, u32[]{:S(2)}) copy-start(f32[1,8192]{1,0:T(1,128)S(1)} %get-tuple-element.1034) | copy-start | bytes 98308 | tf_op jit(solution)/shard_map/while
  129.5 6.4 %copy-start.11 = (f32[1,8192]{1,0:T(1,128)}, f32[1,8192]{1,0:T(1,128)S(1)}, u32[]{:S(2)}) copy-start(f32[1,8192]{1,0:T(1,128)S(1)} %get-tuple-element.1037) | copy-start | bytes 98308 | tf_op jit(solution)/shard_map/while
  131.1 4.8 %copy-start.16 = (f32[32,8192]{1,0:T(8,128)}, f32[32,8192]{1,0:T(8,128)S(1)}, u32[]{:S(2)}) copy-start(f32[32,8192]{1,0:T(8,128)S(1)} %fusion.62) | copy-start | bytes 3145732 | tf_op jit(solution)/shard_map/while
  140.5 11.6 %collective-permute-start = (bf16[16,8192]{1,0:T(8,128)(2,1)}, bf16[16,8192]{1,0:T(8,128)(2,1)S(1)}, u32[]{:S(2)}, u32[]{:S(2)}) collective-permute-start(bf16[16,8192]{1,0:T(8,128)(2,1)} %get-tuple-element.955), channel_id=1, source_target_pairs={{64,0},{96,32},{128,64},{160,96},{192,128},{224,160},{256,192},{28... | collective-permute-start | bytes 786440 | tf_op jit(solution)/shard_map/while/body/eval_jaxpr/ppermute | solution.py:17
  146.4 5.7 %copy-start.14 = (f32[32,8192]{1,0:T(8,128)}, f32[32,8192]{1,0:T(8,128)S(1)}, u32[]{:S(2)}) copy-start(f32[32,8192]{1,0:T(8,128)S(1)} %fusion.59) | copy-start | bytes 3145732 | tf_op jit(solution)/shard_map/while
  146.6 5.5 %copy-start.9 = (f32[1,8192]{1,0:T(1,128)}, f32[1,8192]{1,0:T(1,128)S(1)}, u32[]{:S(2)}) copy-start(f32[1,8192]{1,0:T(1,128)S(1)} %get-tuple-element.1034) | copy-start | bytes 98308 | tf_op jit(solution)/shard_map/while
  146.6 5.5 %copy-start.11 = (f32[1,8192]{1,0:T(1,128)}, f32[1,8192]{1,0:T(1,128)S(1)}, u32[]{:S(2)}) copy-start(f32[1,8192]{1,0:T(1,128)S(1)} %get-tuple-element.1037) | copy-start | bytes 98308 | tf_op jit(solution)/shard_map/while
  156.7 10.6 %collective-permute-start = (bf16[16,8192]{1,0:T(8,128)(2,1)}, bf16[16,8192]{1,0:T(8,128)(2,1)S(1)}, u32[]{:S(2)}, u32[]{:S(2)}) collective-permute-start(bf16[16,8192]{1,0:T(8,128)(2,1)} %get-tuple-element.955), channel_id=1, source_target_pairs={{64,0},{96,32},{128,64},{160,96},{192,128},{224,160},{256,192},{28... | collective-permute-start | bytes 786440 | tf_op jit(solution)/shard_map/while/body/eval_jaxpr/ppermute | solution.py:17
  162.5 4.8 %copy-start.14 = (f32[32,8192]{1,0:T(8,128)}, f32[32,8192]{1,0:T(8,128)S(1)}, u32[]{:S(2)}) copy-start(f32[32,8192]{1,0:T(8,128)S(1)} %fusion.59) | copy-start | bytes 3145732 | tf_op jit(solution)/shard_map/while
  162.7 4.6 %copy-start.9 = (f32[1,8192]{1,0:T(1,128)}, f32[1,8192]{1,0:T(1,128)S(1)}, u32[]{:S(2)}) copy-start(f32[1,8192]{1,0:T(1,128)S(1)} %get-tuple-element.1034) | copy-start | bytes 98308 | tf_op jit(solution)/shard_map/while
  162.7 4.6 %copy-start.11 = (f32[1,8192]{1,0:T(1,128)}, f32[1,8192]{1,0:T(1,128)S(1)}, u32[]{:S(2)}) copy-start(f32[1,8192]{1,0:T(1,128)S(1)} %get-tuple-element.1037) | copy-start | bytes 98308 | tf_op jit(solution)/shard_map/while
  171.9 13.8 %collective-permute-start = (bf16[16,8192]{1,0:T(8,128)(2,1)}, bf16[16,8192]{1,0:T(8,128)(2,1)S(1)}, u32[]{:S(2)}, u32[]{:S(2)}) collective-permute-start(bf16[16,8192]{1,0:T(8,128)(2,1)} %get-tuple-element.955), channel_id=1, source_target_pairs={{64,0},{96,32},{128,64},{160,96},{192,128},{224,160},{256,192},{28... | collective-permute-start | bytes 786440 | tf_op jit(solution)/shard_map/while/body/eval_jaxpr/ppermute | solution.py:17
  177.8 7.9 %copy-start.14 = (f32[32,8192]{1,0:T(8,128)}, f32[32,8192]{1,0:T(8,128)S(1)}, u32[]{:S(2)}) copy-start(f32[32,8192]{1,0:T(8,128)S(1)} %fusion.59) | copy-start | bytes 3145732 | tf_op jit(solution)/shard_map/while
  177.9 7.8 %copy-start.9 = (f32[1,8192]{1,0:T(1,128)}, f32[1,8192]{1,0:T(1,128)S(1)}, u32[]{:S(2)}) copy-start(f32[1,8192]{1,0:T(1,128)S(1)} %get-tuple-element.1034) | copy-start | bytes 98308 | tf_op jit(solution)/shard_map/while
  177.9 7.8 %copy-start.11 = (f32[1,8192]{1,0:T(1,128)}, f32[1,8192]{1,0:T(1,128)S(1)}, u32[]{:S(2)}) copy-start(f32[1,8192]{1,0:T(1,128)S(1)} %get-tuple-element.1037) | copy-start | bytes 98308 | tf_op jit(solution)/shard_map/while
  179.5 6.2 %copy-start.16 = (f32[32,8192]{1,0:T(8,128)}, f32[32,8192]{1,0:T(8,128)S(1)}, u32[]{:S(2)}) copy-start(f32[32,8192]{1,0:T(8,128)S(1)} %fusion.62) | copy-start | bytes 3145732 | tf_op jit(solution)/shard_map/while
  190.3 10.3 %collective-permute-start = (bf16[16,8192]{1,0:T(8,128)(2,1)}, bf16[16,8192]{1,0:T(8,128)(2,1)S(1)}, u32[]{:S(2)}, u32[]{:S(2)}) collective-permute-start(bf16[16,8192]{1,0:T(8,128)(2,1)} %get-tuple-element.955), channel_id=1, source_target_pairs={{64,0},{96,32},{128,64},{160,96},{192,128},{224,160},{256,192},{28... | collective-permute-start | bytes 786440 | tf_op jit(solution)/shard_map/while/body/eval_jaxpr/ppermute | solution.py:17
  196.1 4.4 %copy-start.14 = (f32[32,8192]{1,0:T(8,128)}, f32[32,8192]{1,0:T(8,128)S(1)}, u32[]{:S(2)}) copy-start(f32[32,8192]{1,0:T(8,128)S(1)} %fusion.59) | copy-start | bytes 3145732 | tf_op jit(solution)/shard_map/while
  196.3 4.3 copy-start.9
  205.1 10.7 %collective-permute-start = (bf16[16,8192]{1,0:T(8,128)(2,1)}, bf16[16,8192]{1,0:T(8,128)(2,1)S(1)}, u32[]{:S(2)}, u32[]{:S(2)}) collective-permute-start(bf16[16,8192]{1,0:T(8,128)(2,1)} %get-tuple-element.955), channel_id=1, source_target_pairs={{64,0},{96,32},{128,64},{160,96},{192,128},{224,160},{256,192},{28... | collective-permute-start | bytes 786440 | tf_op jit(solution)/shard_map/while/body/eval_jaxpr/ppermute | solution.py:17
  211.0 4.8 %copy-start.14 = (f32[32,8192]{1,0:T(8,128)}, f32[32,8192]{1,0:T(8,128)S(1)}, u32[]{:S(2)}) copy-start(f32[32,8192]{1,0:T(8,128)S(1)} %fusion.59) | copy-start | bytes 3145732 | tf_op jit(solution)/shard_map/while
  211.2 4.6 %copy-start.9 = (f32[1,8192]{1,0:T(1,128)}, f32[1,8192]{1,0:T(1,128)S(1)}, u32[]{:S(2)}) copy-start(f32[1,8192]{1,0:T(1,128)S(1)} %get-tuple-element.1034) | copy-start | bytes 98308 | tf_op jit(solution)/shard_map/while
  211.2 4.6 %copy-start.11 = (f32[1,8192]{1,0:T(1,128)}, f32[1,8192]{1,0:T(1,128)S(1)}, u32[]{:S(2)}) copy-start(f32[1,8192]{1,0:T(1,128)S(1)} %get-tuple-element.1037) | copy-start | bytes 98308 | tf_op jit(solution)/shard_map/while
  220.4 12.4 %collective-permute-start = (bf16[16,8192]{1,0:T(8,128)(2,1)}, bf16[16,8192]{1,0:T(8,128)(2,1)S(1)}, u32[]{:S(2)}, u32[]{:S(2)}) collective-permute-start(bf16[16,8192]{1,0:T(8,128)(2,1)} %get-tuple-element.955), channel_id=1, source_target_pairs={{64,0},{96,32},{128,64},{160,96},{192,128},{224,160},{256,192},{28... | collective-permute-start | bytes 786440 | tf_op jit(solution)/shard_map/while/body/eval_jaxpr/ppermute | solution.py:17
  226.3 6.5 %copy-start.14 = (f32[32,8192]{1,0:T(8,128)}, f32[32,8192]{1,0:T(8,128)S(1)}, u32[]{:S(2)}) copy-start(f32[32,8192]{1,0:T(8,128)S(1)} %fusion.59) | copy-start | bytes 3145732 | tf_op jit(solution)/shard_map/while
  226.5 6.3 %copy-start.9 = (f32[1,8192]{1,0:T(1,128)}, f32[1,8192]{1,0:T(1,128)S(1)}, u32[]{:S(2)}) copy-start(f32[1,8192]{1,0:T(1,128)S(1)} %get-tuple-element.1034) | copy-start | bytes 98308 | tf_op jit(solution)/shard_map/while
  226.5 6.3 %copy-start.11 = (f32[1,8192]{1,0:T(1,128)}, f32[1,8192]{1,0:T(1,128)S(1)}, u32[]{:S(2)}) copy-start(f32[1,8192]{1,0:T(1,128)S(1)} %get-tuple-element.1037) | copy-start | bytes 98308 | tf_op jit(solution)/shard_map/while
  228.1 4.7 %copy-start.16 = (f32[32,8192]{1,0:T(8,128)}, f32[32,8192]{1,0:T(8,128)S(1)}, u32[]{:S(2)}) copy-start(f32[32,8192]{1,0:T(8,128)S(1)} %fusion.62) | copy-start | bytes 3145732 | tf_op jit(solution)/shard_map/while
  237.4 10.4 %collective-permute-start = (bf16[16,8192]{1,0:T(8,128)(2,1)}, bf16[16,8192]{1,0:T(8,128)(2,1)S(1)}, u32[]{:S(2)}, u32[]{:S(2)}) collective-permute-start(bf16[16,8192]{1,0:T(8,128)(2,1)} %get-tuple-element.955), channel_id=1, source_target_pairs={{64,0},{96,32},{128,64},{160,96},{192,128},{224,160},{256,192},{28... | collective-permute-start | bytes 786440 | tf_op jit(solution)/shard_map/while/body/eval_jaxpr/ppermute | solution.py:17
  243.2 4.5 %copy-start.14 = (f32[32,8192]{1,0:T(8,128)}, f32[32,8192]{1,0:T(8,128)S(1)}, u32[]{:S(2)}) copy-start(f32[32,8192]{1,0:T(8,128)S(1)} %fusion.59) | copy-start | bytes 3145732 | tf_op jit(solution)/shard_map/while
  243.4 4.4 copy-start.9
  243.4 4.4 copy-start.11
  252.4 13.3 %collective-permute-start = (bf16[16,8192]{1,0:T(8,128)(2,1)}, bf16[16,8192]{1,0:T(8,128)(2,1)S(1)}, u32[]{:S(2)}, u32[]{:S(2)}) collective-permute-start(bf16[16,8192]{1,0:T(8,128)(2,1)} %get-tuple-element.955), channel_id=1, source_target_pairs={{64,0},{96,32},{128,64},{160,96},{192,128},{224,160},{256,192},{28... | collective-permute-start | bytes 786440 | tf_op jit(solution)/shard_map/while/body/eval_jaxpr/ppermute | solution.py:17
  258.3 7.4 %copy-start.14 = (f32[32,8192]{1,0:T(8,128)}, f32[32,8192]{1,0:T(8,128)S(1)}, u32[]{:S(2)}) copy-start(f32[32,8192]{1,0:T(8,128)S(1)} %fusion.59) | copy-start | bytes 3145732 | tf_op jit(solution)/shard_map/while
  258.4 7.2 %copy-start.9 = (f32[1,8192]{1,0:T(1,128)}, f32[1,8192]{1,0:T(1,128)S(1)}, u32[]{:S(2)}) copy-start(f32[1,8192]{1,0:T(1,128)S(1)} %get-tuple-element.1034) | copy-start | bytes 98308 | tf_op jit(solution)/shard_map/while
  258.5 7.2 %copy-start.11 = (f32[1,8192]{1,0:T(1,128)}, f32[1,8192]{1,0:T(1,128)S(1)}, u32[]{:S(2)}) copy-start(f32[1,8192]{1,0:T(1,128)S(1)} %get-tuple-element.1037) | copy-start | bytes 98308 | tf_op jit(solution)/shard_map/while
  260.1 5.6 %copy-start.16 = (f32[32,8192]{1,0:T(8,128)}, f32[32,8192]{1,0:T(8,128)S(1)}, u32[]{:S(2)}) copy-start(f32[32,8192]{1,0:T(8,128)S(1)} %fusion.62) | copy-start | bytes 3145732 | tf_op jit(solution)/shard_map/while
  352.1 8.6 %collective-permute-start.3 = (f32[65,1024]{1,0:T(8,128)S(1)}, f32[65,1024]{1,0:T(8,128)S(1)}, u32[]{:S(2)}, u32[]{:S(2)}) collective-permute-start(f32[65,1024]{1,0:T(8,128)S(1)} %select_bitcast_fusion), channel_id=1, source_target_pairs={{0,32},{32,0},{64,96},{96,64},{128,160},{160,128},{192,224},{224,1... | collective-permute-start | bytes 798728 | tf_op jit(solution)/shard_map/ppermute | solution.py:22
  394.4 4.4 %collective-permute-start.4 = (f32[]{:T(128)}, f32[]{:T(128)}, u32[]{:S(2)}, u32[]{:S(2)}) collective-permute-start(f32[]{:T(128)} %psum.7), channel_id=1, source_target_pairs={{0,4},{4,8},{8,12},{12,16},{16,20},{20,24},{24,28},{28,0},{1,5},{5... | collective-permute-start | bytes 20 | tf_op jit(solution)/shard_map/ppermute | solution.py:185
  400.0 6.8 %collective-permute-start.5 = (f32[]{:T(128)}, f32[]{:T(128)}, u32[]{:S(2)}, u32[]{:S(2)}) collective-permute-start(f32[]{:T(128)} %add.178), channel_id=1, source_target_pairs={{0,8},{4,12},{8,16},{12,20},{16,24},{20,28},{24,0},{28,4},{1,9},{5... | collective-permute-start | bytes 20 | tf_op jit(solution)/shard_map/ppermute | solution.py:185
  407.4 7.1 %collective-permute-start.6 = (f32[]{:T(128)}, f32[]{:T(128)}, u32[]{:S(2)}, u32[]{:S(2)}) collective-permute-start(f32[]{:T(128)} %add.179), channel_id=1, source_target_pairs={{0,16},{4,20},{8,24},{12,28},{16,0},{20,4},{24,8},{28,12},{1,17},{... | collective-permute-start | bytes 20 | tf_op jit(solution)/shard_map/ppermute | solution.py:185
  415.1 8.7 %collective-permute-start.7 = (f32[65,256]{1,0:T(8,128)S(1)}, f32[65,256]{1,0:T(8,128)S(1)}, u32[]{:S(2)}, u32[]{:S(2)}) collective-permute-start(f32[65,256]{1,0:T(8,128)S(1)} %get-tuple-element.774), channel_id=1, source_target_pairs={{0,1},{1,2},{2,3},{3,0},{4,5},{5,6},{6,7},{7,4},{8,9},{9,10},{10,1... | collective-permute-start | bytes 199688 | tf_op jit(solution)/shard_map/ppermute | solution.py:197
  417.6 7.8 %collective-permute-start.8 = (f32[65,256]{1,0:T(8,128)S(1)}, f32[65,256]{1,0:T(8,128)S(1)}, u32[]{:S(2)}, u32[]{:S(2)}) collective-permute-start(f32[65,256]{1,0:T(8,128)S(1)} %get-tuple-element.776), channel_id=1, source_target_pairs={{0,2},{1,3},{2,0},{3,1},{4,6},{5,7},{6,4},{7,5},{8,10},{9,11},{10,... | collective-permute-start | bytes 199688 | tf_op jit(solution)/shard_map/ppermute | solution.py:197
  421.9 7.5 %collective-permute-start.9 = (f32[65,256]{1,0:T(8,128)S(1)}, f32[65,256]{1,0:T(8,128)S(1)}, u32[]{:S(2)}, u32[]{:S(2)}) collective-permute-start(f32[65,256]{1,0:T(8,128)S(1)} %get-tuple-element.775), channel_id=1, source_target_pairs={{0,3},{1,0},{2,1},{3,2},{4,7},{5,4},{6,5},{7,6},{8,11},{9,8},{10,9... | collective-permute-start | bytes 199688 | tf_op jit(solution)/shard_map/ppermute | solution.py:197
  (176 other events, 373.6 us)
Sparse Core Ops, SparseCore 0:
  30.6 34.8 all-gather.1
  270.5 80.4 reduce-scatter.1

commit v11 on v10

--- a/solution.py
+++ b/solution.py
@@ -8,7 +8,7 @@
 from jax.experimental.pallas import tpu as pltpu
 from jax.sharding import PartitionSpec as P
 
-rows_per_block = 16
+rows_per_block = 8
 
 
 def shifted(value, axis, steps):

time: 440 us -> 509 us (1.16)
  matrix products: 66.4 us -> 163 us
  waiting for transfers between devices: 184 us -> 114 us
  other arithmetic: 14.5 us -> 36.4 us
  Pallas kernels: 50.1 us -> 60.2 us
  starting transfers between devices: 38.4 us -> 45.5 us
    dot_general x22 -> x30, matrix products: 20.4 us -> 78.9 us  [accumulate(): lax.dot_general(low_part, source, contract_first, preferred_element_type=...]
    ppermute x11 -> x15, waiting for transfers between devices: 53 us -> 6.91 us  [shifted(): lax.ppermute(value, axis, [(source, source + steps) for source in range(i...]
    dot_general x22 -> x30, matrix products: 36.9 us -> 77 us  [accumulate(): lax.dot_general(d_low, normalized_part, contract_first, preferred_element...]
    reduce_scatter x1, waiting for transfers between devices: 80.7 us -> 54.7 us  [on_device(): reduced = lax.psum_scatter(grads, 'seq', scatter_dimension=2, tiled=True)]
    add x11 -> x15, other arithmetic: 1.26 us -> 21.8 us  [accumulate(): sum_g + jnp.where(inside, part_g, 0.0)]
    pallas_call x11 -> x15, Pallas kernels: 50.1 us -> 60.2 us  [chain_step(): pl.pallas_call(functools.partial(chain_kernel, pairs, block_total), out_s...]
    while x418 -> x330, local copies, waits for them, and re-layouts: 0.94 us -> 9.88 us
    ppermute x11 -> x15, starting transfers between devices: 14.1 us -> 21.2 us  [shifted(): lax.ppermute(value, axis, [(source, source + steps) for source in range(i...]
  transfers between devices with their start and end apart: 22 -> 26, of which waited for: 21 -> 20; matrix products, arithmetic and copies ran while one was open for 17% -> 37% of each run, Pallas kernels for 0% -> 0%
where the time goes in v11:
time: 509 us; the launch traced here: 505 us
  matrix products  163 us (32%)
  waiting for transfers between devices  114 us (22%)
  Pallas kernels  60.2 us (12%)
  blocking collectives  47.6 us (9%)
  starting transfers between devices  45.5 us (9%)
  other arithmetic  36.4 us (7%)
  local copies, waits for them, and re-layouts  18.7 us (4%)
  between operations  18.1 us (4%)
    dot_general x30, matrix products, accumulate(): lax.dot_general(low_part, source, contract_first, preferred_element_type=...  78.9 us
    dot_general x30, matrix products, accumulate(): lax.dot_general(d_low, normalized_part, contract_first, preferred_element...  77 us
    pallas_call x15, Pallas kernels, chain_step(): pl.pallas_call(functools.partial(chain_kernel, pairs, block_total), out_s...  60.2 us
    reduce_scatter x1, waiting for transfers between devices, on_device(): reduced = lax.psum_scatter(grads, 'seq', scatter_dimension=2, tiled=True)  54.7 us
    psum x1, blocking collectives, on_device(): total = lax.psum(square, 'pipe')  31.9 us
    ppermute x3, waiting for transfers between devices, partner_swap(): lax.ppermute(value, axis, [(source, source ^ 1) for source in range(count)])  24.5 us
    add x15, other arithmetic, accumulate(): sum_g + jnp.where(inside, part_g, 0.0)  21.8 us
    ppermute x15, starting transfers between devices, shifted(): lax.ppermute(value, axis, [(source, source + steps) for source in range(i...  21.2 us
  transfers between devices with their start and end apart: 26, of which 20 were waited for; matrix products, arithmetic and copies ran while one was open for 37% of the time, Pallas kernels for 0%

profile of v11, /device:TPU:6, one launch (start us, length us, event | category | flops | bytes accessed | tf_op | source)
XLA Modules:
  0.0 504.6 jit_solution(15527495978394564248)
XLA Ops:
  8.1 3.8 collective-permute-start.2
  14.8 15.7 %all_gather.6 = bf16[2,65,1024]{2,1,0:T(8,128)(2,1)} all-gather(bf16[2,65,256]{2,1,0:T(8,128)(2,1)S(1)} %pad_maximum_fusion.1), channel_id=1, replica_groups=mesh['pipe'=16,'seq'=8,'dp'=4] {'dp'}, dimensions={2}, use_global_device_ids=true | all-gather | bytes 332800 | tf_op jit(solution)/shard_map/all_gather | solution.py:103
  34.9 17.4 %collective-permute-done.1 = bf16[64,8192]{1,0:T(8,128)(2,1)} collective-permute-done((bf16[64,8192]{1,0:T(8,128)(2,1)S(1)}, bf16[64,8192]{1,0:T(8,128)(2,1)}, u32[]{:S(2)}, u32[]{:S(2)}) %collective-permute-start.1) | collective-permute-done | bytes 1048608 | tf_op jit(solution)/shard_map/ppermute | solution.py:22
  52.2 3.0 fusion.20
  55.5 10.0 %all-gather.2.cloned.1.call-done = bf16[2,65,8192]{2,1,0:T(8,128)(2,1)} async-done(((bf16[2,65,1024]{2,1,0:T(8,128)(2,1)}), bf16[2,65,8192]{2,1,0:T(8,128)(2,1)}) %all-gather.2.cloned.1.call-update) | async-done | bytes 2129936 | tf_op jit(solution)/shard_map/all_gather | solution.py:103
  76.6 279.5 %while.28 = (s32[]{:T(128)}, bf16[8,8192]{1,0:T(8,128)(2,1)S(1)}, f32[32,8192]{1,0:T(8,128)}, f32[32,8192]{1,0:T(8,128)}, f32[1,8192]{1,0:T(1,128)}, /*index=5*/...) while((s32[]{:T(128)}, bf16[8,8192]{1,0:T(8,128)(2,1)S(1)}, ...), condition=%wide.region_3.4_spmd.clone, body=%wide.region_2.3_spmd.clone.sunk | while | flops 37273600 | bytes 11939735 | solution.py:170
  77.2 4.0 eval_jaxpr.7
  93.4 4.0 eval_jaxpr.7
  101.7 2.7 fusion.63
  104.4 2.7 fusion.59
  111.8 4.0 eval_jaxpr.7
  120.1 2.7 fusion.63
  122.8 2.7 fusion.59
  130.2 4.0 eval_jaxpr.7
  138.5 2.7 fusion.63
  141.2 2.7 fusion.59
  148.6 4.0 eval_jaxpr.7
  156.9 2.7 fusion.63
  159.6 2.7 fusion.59
  167.0 4.0 eval_jaxpr.7
  175.3 2.7 fusion.63
  178.0 2.7 fusion.59
  185.4 4.0 eval_jaxpr.7
  193.7 2.7 fusion.63
  196.4 2.7 fusion.59
  204.3 4.0 eval_jaxpr.7
  210.0 2.7 fusion.60
  212.6 2.7 fusion.63
  215.3 2.7 fusion.59
  223.4 4.0 eval_jaxpr.7
  231.7 2.7 fusion.63
  234.4 2.7 fusion.59
  242.4 4.0 eval_jaxpr.7
  248.1 2.7 fusion.60
  250.7 2.7 fusion.63
  253.4 2.7 fusion.59
  261.5 4.0 eval_jaxpr.7
  269.8 2.7 fusion.63
  272.5 2.7 fusion.59
  280.5 4.0 eval_jaxpr.7
  286.1 2.7 fusion.60
  288.8 2.7 fusion.63
  291.5 2.7 fusion.59
  299.6 4.0 eval_jaxpr.7
  307.9 2.7 fusion.63
  310.6 2.7 fusion.59
  318.6 4.0 eval_jaxpr.7
  324.2 2.7 fusion.60
  326.9 2.7 fusion.63
  329.6 2.7 fusion.59
  337.7 4.0 eval_jaxpr.7
  346.0 2.7 fusion.63
  348.6 2.7 fusion.59
  362.1 54.7 %reduce-scatter.2.cloned.1.call-done = f32[2,65,1024]{2,1,0:T(8,128)} async-done(((f32[2,65,8192]{2,1,0:T(8,128)}), f32[2,65,1024]{2,1,0:T(8,128)}) %reduce-scatter.2.cloned.1.call-update) | async-done | bytes 532496 | tf_op jit(solution)/shard_map/reduce_scatter | solution.py:174
  418.0 3.4 collective-permute-start.3
  421.4 5.2 %collective-permute-done.3 = f32[65,1024]{1,0:T(8,128)S(1)} collective-permute-done((f32[65,1024]{1,0:T(8,128)S(1)}, f32[65,1024]{1,0:T(8,128)S(1)}, u32[]{:S(2)}, u32[]{:S(2)}) %collective-permute-start.3) | collective-permute-done | bytes 266272 | tf_op jit(solution)/shard_map/ppermute | solution.py:22
  428.3 31.9 %psum.7 = f32[]{:T(128)} all-reduce(f32[]{:T(128)} %get-tuple-element.754), channel_id=1, replica_groups=mesh['pipe'=16,'seq'=8,'dp'=4] {'pipe'}, use_global_device_ids=true, to_apply=%region_6.7 | all-reduce | flops 1 | bytes 8 | tf_op jit(solution)/shard_map/psum | solution.py:181
  460.2 4.4 collective-permute-done.4
  465.9 3.2 collective-permute-start.5
  469.1 3.6 collective-permute-done.5
  473.3 3.2 collective-permute-start.6
  476.6 3.9 collective-permute-done.6
  483.7 4.3 collective-permute-start.8
  491.4 4.0 collective-permute-done.9
  (474 shorter events, 167.7 us)
Async XLA Ops:
  7.2 26.7 %copy-start = (bf16[1,128,8192]{2,1,0:T(8,128)(2,1)S(1)}, bf16[1,128,8192]{2,1,0:T(8,128)(2,1)}, u32[]{:S(2)}) copy-start(bf16[1,128,8192]{2,1,0:T(8,128)(2,1)} %param.8) | copy-start | bytes 6291460
  7.2 58.3 %all-gather.2.cloned.1.call-start = ((), (), s32[]{:S(2)}) async-start(), calls=%async_computation.1 | async-start | bytes 2654208 | tf_op jit(solution)/shard_map/all_gather | solution.py:103
  8.1 5.8 %collective-permute-start.2 = (bf16[65,256]{1,0:T(8,128)(2,1)S(1)}, bf16[65,256]{1,0:T(8,128)(2,1)S(1)}, u32[]{:S(2)}, u32[]{:S(2)}) collective-permute-start(bf16[65,256]{1,0:T(8,128)(2,1)S(1)} %pad_maximum_fusion.2), channel_id=1, source_target_pairs={{0,32},{32,0},{64,96},{96,64},{128,160},{160,128},{192,224},{224,1... | collective-permute-start | bytes 99848 | tf_op jit(solution)/shard_map/ppermute | solution.py:22
  30.4 386.4 %reduce-scatter.2.cloned.1.call-start = ((), (), s32[]{:S(2)}) async-start(), calls=%async_computation.2 | async-start | bytes 5308416 | tf_op jit(solution)/shard_map/reduce_scatter | solution.py:174
  31.8 20.4 %collective-permute-start.1 = (bf16[64,8192]{1,0:T(8,128)(2,1)S(1)}, bf16[64,8192]{1,0:T(8,128)(2,1)}, u32[]{:S(2)}, u32[]{:S(2)}) collective-permute-start(bf16[64,8192]{1,0:T(8,128)(2,1)S(1)} %dynamic-slice_bitcast_fusion), channel_id=1, source_target_pairs={{0,32},{32,0},{64,96},{96,64},{128,160},{160,128},{192,224},{224,1... | collective-permute-start | bytes 3145736 | tf_op jit(solution)/shard_map/ppermute | solution.py:22
  33.8 18.4 %copy-start.3 = (bf16[1,1,128,8192]{3,2,1,0:T(8,128)(2,1)S(1)}, bf16[1,1,128,8192]{3,2,1,0:T(8,128)(2,1)}, u32[]{:S(2)}) copy-start(bf16[1,1,128,8192]{3,2,1,0:T(8,128)(2,1)} %param.7) | copy-start | bytes 6291460
  66.5 7.3 %copy-start.7 = (f32[1,1,8192]{2,1,0:T(1,128)}, f32[1,1,8192]{2,1,0:T(1,128)S(1)}, u32[]{:S(2)}) copy-start(f32[1,1,8192]{2,1,0:T(1,128)S(1)} %get-tuple-element.769) | copy-start | bytes 98308
  81.2 11.6 %collective-permute-start = (bf16[8,8192]{1,0:T(8,128)(2,1)}, bf16[8,8192]{1,0:T(8,128)(2,1)S(1)}, u32[]{:S(2)}, u32[]{:S(2)}) collective-permute-start(bf16[8,8192]{1,0:T(8,128)(2,1)} %get-tuple-element.955), channel_id=1, source_target_pairs={{64,0},{96,32},{128,64},{160,96},{192,128},{224,160},{256,192},{28... | collective-permute-start | bytes 393224 | tf_op jit(solution)/shard_map/while/body/eval_jaxpr/ppermute | solution.py:17
  97.4 13.7 %collective-permute-start = (bf16[8,8192]{1,0:T(8,128)(2,1)}, bf16[8,8192]{1,0:T(8,128)(2,1)S(1)}, u32[]{:S(2)}, u32[]{:S(2)}) collective-permute-start(bf16[8,8192]{1,0:T(8,128)(2,1)} %get-tuple-element.955), channel_id=1, source_target_pairs={{64,0},{96,32},{128,64},{160,96},{192,128},{224,160},{256,192},{28... | collective-permute-start | bytes 393224 | tf_op jit(solution)/shard_map/while/body/eval_jaxpr/ppermute | solution.py:17
  101.7 6.9 %copy-start.6 = (f32[8192]{0:T(1024)S(1)}, f32[8192]{0:T(1024)}, u32[]{:S(2)}) copy-start(f32[8192]{0:T(1024)} %get-tuple-element.1052) | copy-start | bytes 98308 | tf_op jit(solution)/shard_map/while
  101.7 6.9 %copy-start.15 = (bf16[8,32]{1,0:T(8,128)(2,1)S(1)}, bf16[8,32]{1,0:T(8,128)(2,1)}, u32[]{:S(2)}) copy-start(bf16[8,32]{1,0:T(8,128)(2,1)} %get-tuple-element.962) | copy-start | bytes 1540 | tf_op jit(solution)/shard_map/while
  115.8 13.7 %collective-permute-start = (bf16[8,8192]{1,0:T(8,128)(2,1)}, bf16[8,8192]{1,0:T(8,128)(2,1)S(1)}, u32[]{:S(2)}, u32[]{:S(2)}) collective-permute-start(bf16[8,8192]{1,0:T(8,128)(2,1)} %get-tuple-element.955), channel_id=1, source_target_pairs={{64,0},{96,32},{128,64},{160,96},{192,128},{224,160},{256,192},{28... | collective-permute-start | bytes 393224 | tf_op jit(solution)/shard_map/while/body/eval_jaxpr/ppermute | solution.py:17
  120.1 6.9 %copy-start.6 = (f32[8192]{0:T(1024)S(1)}, f32[8192]{0:T(1024)}, u32[]{:S(2)}) copy-start(f32[8192]{0:T(1024)} %get-tuple-element.1052) | copy-start | bytes 98308 | tf_op jit(solution)/shard_map/while
  134.2 13.7 %collective-permute-start = (bf16[8,8192]{1,0:T(8,128)(2,1)}, bf16[8,8192]{1,0:T(8,128)(2,1)S(1)}, u32[]{:S(2)}, u32[]{:S(2)}) collective-permute-start(bf16[8,8192]{1,0:T(8,128)(2,1)} %get-tuple-element.955), channel_id=1, source_target_pairs={{64,0},{96,32},{128,64},{160,96},{192,128},{224,160},{256,192},{28... | collective-permute-start | bytes 393224 | tf_op jit(solution)/shard_map/while/body/eval_jaxpr/ppermute | solution.py:17
  138.5 6.9 %copy-start.6 = (f32[8192]{0:T(1024)S(1)}, f32[8192]{0:T(1024)}, u32[]{:S(2)}) copy-start(f32[8192]{0:T(1024)} %get-tuple-element.1052) | copy-start | bytes 98308 | tf_op jit(solution)/shard_map/while
  152.6 13.7 %collective-permute-start = (bf16[8,8192]{1,0:T(8,128)(2,1)}, bf16[8,8192]{1,0:T(8,128)(2,1)S(1)}, u32[]{:S(2)}, u32[]{:S(2)}) collective-permute-start(bf16[8,8192]{1,0:T(8,128)(2,1)} %get-tuple-element.955), channel_id=1, source_target_pairs={{64,0},{96,32},{128,64},{160,96},{192,128},{224,160},{256,192},{28... | collective-permute-start | bytes 393224 | tf_op jit(solution)/shard_map/while/body/eval_jaxpr/ppermute | solution.py:17
  156.9 6.9 %copy-start.6 = (f32[8192]{0:T(1024)S(1)}, f32[8192]{0:T(1024)}, u32[]{:S(2)}) copy-start(f32[8192]{0:T(1024)} %get-tuple-element.1052) | copy-start | bytes 98308 | tf_op jit(solution)/shard_map/while
  171.0 13.7 %collective-permute-start = (bf16[8,8192]{1,0:T(8,128)(2,1)}, bf16[8,8192]{1,0:T(8,128)(2,1)S(1)}, u32[]{:S(2)}, u32[]{:S(2)}) collective-permute-start(bf16[8,8192]{1,0:T(8,128)(2,1)} %get-tuple-element.955), channel_id=1, source_target_pairs={{64,0},{96,32},{128,64},{160,96},{192,128},{224,160},{256,192},{28... | collective-permute-start | bytes 393224 | tf_op jit(solution)/shard_map/while/body/eval_jaxpr/ppermute | solution.py:17
  175.3 6.9 %copy-start.6 = (f32[8192]{0:T(1024)S(1)}, f32[8192]{0:T(1024)}, u32[]{:S(2)}) copy-start(f32[8192]{0:T(1024)} %get-tuple-element.1052) | copy-start | bytes 98308 | tf_op jit(solution)/shard_map/while
  189.4 14.3 %collective-permute-start = (bf16[8,8192]{1,0:T(8,128)(2,1)}, bf16[8,8192]{1,0:T(8,128)(2,1)S(1)}, u32[]{:S(2)}, u32[]{:S(2)}) collective-permute-start(bf16[8,8192]{1,0:T(8,128)(2,1)} %get-tuple-element.955), channel_id=1, source_target_pairs={{64,0},{96,32},{128,64},{160,96},{192,128},{224,160},{256,192},{28... | collective-permute-start | bytes 393224 | tf_op jit(solution)/shard_map/while/body/eval_jaxpr/ppermute | solution.py:17
  193.7 6.9 %copy-start.6 = (f32[8192]{0:T(1024)S(1)}, f32[8192]{0:T(1024)}, u32[]{:S(2)}) copy-start(f32[8192]{0:T(1024)} %get-tuple-element.1052) | copy-start | bytes 98308 | tf_op jit(solution)/shard_map/while
  196.4 7.3 %copy-start.10 = (f32[64,32]{1,0:T(8,128)S(1)}, f32[64,32]{1,0:T(8,128)}, u32[]{:S(2)}) copy-start(f32[64,32]{1,0:T(8,128)} %copy-done.9) | copy-start | bytes 24580 | tf_op jit(solution)/shard_map/while
  196.4 7.3 %copy-start.12 = (f32[64,32]{1,0:T(8,128)S(1)}, f32[64,32]{1,0:T(8,128)}, u32[]{:S(2)}) copy-start(f32[64,32]{1,0:T(8,128)} %copy-done.11) | copy-start | bytes 24580 | tf_op jit(solution)/shard_map/while
  208.4 14.4 %collective-permute-start = (bf16[8,8192]{1,0:T(8,128)(2,1)}, bf16[8,8192]{1,0:T(8,128)(2,1)S(1)}, u32[]{:S(2)}, u32[]{:S(2)}) collective-permute-start(bf16[8,8192]{1,0:T(8,128)(2,1)} %get-tuple-element.955), channel_id=1, source_target_pairs={{64,0},{96,32},{128,64},{160,96},{192,128},{224,160},{256,192},{28... | collective-permute-start | bytes 393224 | tf_op jit(solution)/shard_map/while/body/eval_jaxpr/ppermute | solution.py:17
  212.6 6.9 %copy-start.6 = (f32[8192]{0:T(1024)S(1)}, f32[8192]{0:T(1024)}, u32[]{:S(2)}) copy-start(f32[8192]{0:T(1024)} %get-tuple-element.1052) | copy-start | bytes 98308 | tf_op jit(solution)/shard_map/while
  212.6 6.9 %copy-start.15 = (bf16[8,32]{1,0:T(8,128)(2,1)S(1)}, bf16[8,32]{1,0:T(8,128)(2,1)}, u32[]{:S(2)}) copy-start(bf16[8,32]{1,0:T(8,128)(2,1)} %get-tuple-element.962) | copy-start | bytes 1540 | tf_op jit(solution)/shard_map/while
  215.3 7.4 %copy-start.10 = (f32[64,32]{1,0:T(8,128)S(1)}, f32[64,32]{1,0:T(8,128)}, u32[]{:S(2)}) copy-start(f32[64,32]{1,0:T(8,128)} %copy-done.9) | copy-start | bytes 24580 | tf_op jit(solution)/shard_map/while
  215.3 7.4 %copy-start.12 = (f32[64,32]{1,0:T(8,128)S(1)}, f32[64,32]{1,0:T(8,128)}, u32[]{:S(2)}) copy-start(f32[64,32]{1,0:T(8,128)} %copy-done.11) | copy-start | bytes 24580 | tf_op jit(solution)/shard_map/while
  227.4 14.4 %collective-permute-start = (bf16[8,8192]{1,0:T(8,128)(2,1)}, bf16[8,8192]{1,0:T(8,128)(2,1)S(1)}, u32[]{:S(2)}, u32[]{:S(2)}) collective-permute-start(bf16[8,8192]{1,0:T(8,128)(2,1)} %get-tuple-element.955), channel_id=1, source_target_pairs={{64,0},{96,32},{128,64},{160,96},{192,128},{224,160},{256,192},{28... | collective-permute-start | bytes 393224 | tf_op jit(solution)/shard_map/while/body/eval_jaxpr/ppermute | solution.py:17
  231.7 6.9 %copy-start.6 = (f32[8192]{0:T(1024)S(1)}, f32[8192]{0:T(1024)}, u32[]{:S(2)}) copy-start(f32[8192]{0:T(1024)} %get-tuple-element.1052) | copy-start | bytes 98308 | tf_op jit(solution)/shard_map/while
  234.4 7.4 %copy-start.10 = (f32[64,32]{1,0:T(8,128)S(1)}, f32[64,32]{1,0:T(8,128)}, u32[]{:S(2)}) copy-start(f32[64,32]{1,0:T(8,128)} %copy-done.9) | copy-start | bytes 24580 | tf_op jit(solution)/shard_map/while
  234.4 7.4 %copy-start.12 = (f32[64,32]{1,0:T(8,128)S(1)}, f32[64,32]{1,0:T(8,128)}, u32[]{:S(2)}) copy-start(f32[64,32]{1,0:T(8,128)} %copy-done.11) | copy-start | bytes 24580 | tf_op jit(solution)/shard_map/while
  246.4 14.4 %collective-permute-start = (bf16[8,8192]{1,0:T(8,128)(2,1)}, bf16[8,8192]{1,0:T(8,128)(2,1)S(1)}, u32[]{:S(2)}, u32[]{:S(2)}) collective-permute-start(bf16[8,8192]{1,0:T(8,128)(2,1)} %get-tuple-element.955), channel_id=1, source_target_pairs={{64,0},{96,32},{128,64},{160,96},{192,128},{224,160},{256,192},{28... | collective-permute-start | bytes 393224 | tf_op jit(solution)/shard_map/while/body/eval_jaxpr/ppermute | solution.py:17
  250.7 6.9 %copy-start.6 = (f32[8192]{0:T(1024)S(1)}, f32[8192]{0:T(1024)}, u32[]{:S(2)}) copy-start(f32[8192]{0:T(1024)} %get-tuple-element.1052) | copy-start | bytes 98308 | tf_op jit(solution)/shard_map/while
  250.7 6.9 %copy-start.15 = (bf16[8,32]{1,0:T(8,128)(2,1)S(1)}, bf16[8,32]{1,0:T(8,128)(2,1)}, u32[]{:S(2)}) copy-start(bf16[8,32]{1,0:T(8,128)(2,1)} %get-tuple-element.962) | copy-start | bytes 1540 | tf_op jit(solution)/shard_map/while
  253.4 7.4 %copy-start.10 = (f32[64,32]{1,0:T(8,128)S(1)}, f32[64,32]{1,0:T(8,128)}, u32[]{:S(2)}) copy-start(f32[64,32]{1,0:T(8,128)} %copy-done.9) | copy-start | bytes 24580 | tf_op jit(solution)/shard_map/while
  253.4 7.4 %copy-start.12 = (f32[64,32]{1,0:T(8,128)S(1)}, f32[64,32]{1,0:T(8,128)}, u32[]{:S(2)}) copy-start(f32[64,32]{1,0:T(8,128)} %copy-done.11) | copy-start | bytes 24580 | tf_op jit(solution)/shard_map/while
  265.5 14.4 %collective-permute-start = (bf16[8,8192]{1,0:T(8,128)(2,1)}, bf16[8,8192]{1,0:T(8,128)(2,1)S(1)}, u32[]{:S(2)}, u32[]{:S(2)}) collective-permute-start(bf16[8,8192]{1,0:T(8,128)(2,1)} %get-tuple-element.955), channel_id=1, source_target_pairs={{64,0},{96,32},{128,64},{160,96},{192,128},{224,160},{256,192},{28... | collective-permute-start | bytes 393224 | tf_op jit(solution)/shard_map/while/body/eval_jaxpr/ppermute | solution.py:17
  269.8 6.9 %copy-start.6 = (f32[8192]{0:T(1024)S(1)}, f32[8192]{0:T(1024)}, u32[]{:S(2)}) copy-start(f32[8192]{0:T(1024)} %get-tuple-element.1052) | copy-start | bytes 98308 | tf_op jit(solution)/shard_map/while
  272.5 7.4 %copy-start.10 = (f32[64,32]{1,0:T(8,128)S(1)}, f32[64,32]{1,0:T(8,128)}, u32[]{:S(2)}) copy-start(f32[64,32]{1,0:T(8,128)} %copy-done.9) | copy-start | bytes 24580 | tf_op jit(solution)/shard_map/while
  272.5 7.4 %copy-start.12 = (f32[64,32]{1,0:T(8,128)S(1)}, f32[64,32]{1,0:T(8,128)}, u32[]{:S(2)}) copy-start(f32[64,32]{1,0:T(8,128)} %copy-done.11) | copy-start | bytes 24580 | tf_op jit(solution)/shard_map/while
  284.5 14.4 %collective-permute-start = (bf16[8,8192]{1,0:T(8,128)(2,1)}, bf16[8,8192]{1,0:T(8,128)(2,1)S(1)}, u32[]{:S(2)}, u32[]{:S(2)}) collective-permute-start(bf16[8,8192]{1,0:T(8,128)(2,1)} %get-tuple-element.955), channel_id=1, source_target_pairs={{64,0},{96,32},{128,64},{160,96},{192,128},{224,160},{256,192},{28... | collective-permute-start | bytes 393224 | tf_op jit(solution)/shard_map/while/body/eval_jaxpr/ppermute | solution.py:17
  288.8 6.9 %copy-start.6 = (f32[8192]{0:T(1024)S(1)}, f32[8192]{0:T(1024)}, u32[]{:S(2)}) copy-start(f32[8192]{0:T(1024)} %get-tuple-element.1052) | copy-start | bytes 98308 | tf_op jit(solution)/shard_map/while
  288.8 6.9 %copy-start.15 = (bf16[8,32]{1,0:T(8,128)(2,1)S(1)}, bf16[8,32]{1,0:T(8,128)(2,1)}, u32[]{:S(2)}) copy-start(bf16[8,32]{1,0:T(8,128)(2,1)} %get-tuple-element.962) | copy-start | bytes 1540 | tf_op jit(solution)/shard_map/while
  291.5 7.4 %copy-start.10 = (f32[64,32]{1,0:T(8,128)S(1)}, f32[64,32]{1,0:T(8,128)}, u32[]{:S(2)}) copy-start(f32[64,32]{1,0:T(8,128)} %copy-done.9) | copy-start | bytes 24580 | tf_op jit(solution)/shard_map/while
  291.5 7.4 %copy-start.12 = (f32[64,32]{1,0:T(8,128)S(1)}, f32[64,32]{1,0:T(8,128)}, u32[]{:S(2)}) copy-start(f32[64,32]{1,0:T(8,128)} %copy-done.11) | copy-start | bytes 24580 | tf_op jit(solution)/shard_map/while
  303.6 14.4 %collective-permute-start = (bf16[8,8192]{1,0:T(8,128)(2,1)}, bf16[8,8192]{1,0:T(8,128)(2,1)S(1)}, u32[]{:S(2)}, u32[]{:S(2)}) collective-permute-start(bf16[8,8192]{1,0:T(8,128)(2,1)} %get-tuple-element.955), channel_id=1, source_target_pairs={{64,0},{96,32},{128,64},{160,96},{192,128},{224,160},{256,192},{28... | collective-permute-start | bytes 393224 | tf_op jit(solution)/shard_map/while/body/eval_jaxpr/ppermute | solution.py:17
  310.5 7.4 %copy-start.10 = (f32[64,32]{1,0:T(8,128)S(1)}, f32[64,32]{1,0:T(8,128)}, u32[]{:S(2)}) copy-start(f32[64,32]{1,0:T(8,128)} %copy-done.9) | copy-start | bytes 24580 | tf_op jit(solution)/shard_map/while
  310.5 7.4 %copy-start.12 = (f32[64,32]{1,0:T(8,128)S(1)}, f32[64,32]{1,0:T(8,128)}, u32[]{:S(2)}) copy-start(f32[64,32]{1,0:T(8,128)} %copy-done.11) | copy-start | bytes 24580 | tf_op jit(solution)/shard_map/while
  322.6 14.4 %collective-permute-start = (bf16[8,8192]{1,0:T(8,128)(2,1)}, bf16[8,8192]{1,0:T(8,128)(2,1)S(1)}, u32[]{:S(2)}, u32[]{:S(2)}) collective-permute-start(bf16[8,8192]{1,0:T(8,128)(2,1)} %get-tuple-element.955), channel_id=1, source_target_pairs={{64,0},{96,32},{128,64},{160,96},{192,128},{224,160},{256,192},{28... | collective-permute-start | bytes 393224 | tf_op jit(solution)/shard_map/while/body/eval_jaxpr/ppermute | solution.py:17
  326.9 6.9 %copy-start.6 = (f32[8192]{0:T(1024)S(1)}, f32[8192]{0:T(1024)}, u32[]{:S(2)}) copy-start(f32[8192]{0:T(1024)} %get-tuple-element.1052) | copy-start | bytes 98308 | tf_op jit(solution)/shard_map/while
  326.9 6.9 %copy-start.15 = (bf16[8,32]{1,0:T(8,128)(2,1)S(1)}, bf16[8,32]{1,0:T(8,128)(2,1)}, u32[]{:S(2)}) copy-start(bf16[8,32]{1,0:T(8,128)(2,1)} %get-tuple-element.962) | copy-start | bytes 1540 | tf_op jit(solution)/shard_map/while
  329.6 7.4 %copy-start.10 = (f32[64,32]{1,0:T(8,128)S(1)}, f32[64,32]{1,0:T(8,128)}, u32[]{:S(2)}) copy-start(f32[64,32]{1,0:T(8,128)} %copy-done.9) | copy-start | bytes 24580 | tf_op jit(solution)/shard_map/while
  329.6 7.4 %copy-start.12 = (f32[64,32]{1,0:T(8,128)S(1)}, f32[64,32]{1,0:T(8,128)}, u32[]{:S(2)}) copy-start(f32[64,32]{1,0:T(8,128)} %copy-done.11) | copy-start | bytes 24580 | tf_op jit(solution)/shard_map/while
  341.7 14.4 %collective-permute-start = (bf16[8,8192]{1,0:T(8,128)(2,1)}, bf16[8,8192]{1,0:T(8,128)(2,1)S(1)}, u32[]{:S(2)}, u32[]{:S(2)}) collective-permute-start(bf16[8,8192]{1,0:T(8,128)(2,1)} %get-tuple-element.955), channel_id=1, source_target_pairs={{64,0},{96,32},{128,64},{160,96},{192,128},{224,160},{256,192},{28... | collective-permute-start | bytes 393224 | tf_op jit(solution)/shard_map/while/body/eval_jaxpr/ppermute | solution.py:17
  348.6 7.4 %copy-start.10 = (f32[64,32]{1,0:T(8,128)S(1)}, f32[64,32]{1,0:T(8,128)}, u32[]{:S(2)}) copy-start(f32[64,32]{1,0:T(8,128)} %copy-done.9) | copy-start | bytes 24580 | tf_op jit(solution)/shard_map/while
  348.6 7.4 %copy-start.12 = (f32[64,32]{1,0:T(8,128)S(1)}, f32[64,32]{1,0:T(8,128)}, u32[]{:S(2)}) copy-start(f32[64,32]{1,0:T(8,128)} %copy-done.11) | copy-start | bytes 24580 | tf_op jit(solution)/shard_map/while
  418.0 8.6 %collective-permute-start.3 = (f32[65,1024]{1,0:T(8,128)S(1)}, f32[65,1024]{1,0:T(8,128)S(1)}, u32[]{:S(2)}, u32[]{:S(2)}) collective-permute-start(f32[65,1024]{1,0:T(8,128)S(1)} %select_bitcast_fusion), channel_id=1, source_target_pairs={{0,32},{32,0},{64,96},{96,64},{128,160},{160,128},{192,224},{224,1... | collective-permute-start | bytes 798728 | tf_op jit(solution)/shard_map/ppermute | solution.py:22
  460.2 4.4 collective-permute-start.4
  465.9 6.8 %collective-permute-start.5 = (f32[]{:T(128)}, f32[]{:T(128)}, u32[]{:S(2)}, u32[]{:S(2)}) collective-permute-start(f32[]{:T(128)} %add.178), channel_id=1, source_target_pairs={{0,8},{4,12},{8,16},{12,20},{16,24},{20,28},{24,0},{28,4},{1,9},{5... | collective-permute-start | bytes 20 | tf_op jit(solution)/shard_map/ppermute | solution.py:185
  473.3 7.1 %collective-permute-start.6 = (f32[]{:T(128)}, f32[]{:T(128)}, u32[]{:S(2)}, u32[]{:S(2)}) collective-permute-start(f32[]{:T(128)} %add.179), channel_id=1, source_target_pairs={{0,16},{4,20},{8,24},{12,28},{16,0},{20,4},{24,8},{28,12},{1,17},{... | collective-permute-start | bytes 20 | tf_op jit(solution)/shard_map/ppermute | solution.py:185
  481.2 8.7 %collective-permute-start.7 = (f32[65,256]{1,0:T(8,128)S(1)}, f32[65,256]{1,0:T(8,128)S(1)}, u32[]{:S(2)}, u32[]{:S(2)}) collective-permute-start(f32[65,256]{1,0:T(8,128)S(1)} %get-tuple-element.774), channel_id=1, source_target_pairs={{0,1},{1,2},{2,3},{3,0},{4,5},{5,6},{6,7},{7,4},{8,9},{9,10},{10,1... | collective-permute-start | bytes 199688 | tf_op jit(solution)/shard_map/ppermute | solution.py:197
  483.7 7.8 %collective-permute-start.8 = (f32[65,256]{1,0:T(8,128)S(1)}, f32[65,256]{1,0:T(8,128)S(1)}, u32[]{:S(2)}, u32[]{:S(2)}) collective-permute-start(f32[65,256]{1,0:T(8,128)S(1)} %get-tuple-element.776), channel_id=1, source_target_pairs={{0,2},{1,3},{2,0},{3,1},{4,6},{5,7},{6,4},{7,5},{8,10},{9,11},{10,... | collective-permute-start | bytes 199688 | tf_op jit(solution)/shard_map/ppermute | solution.py:197
  487.9 7.5 %collective-permute-start.9 = (f32[65,256]{1,0:T(8,128)S(1)}, f32[65,256]{1,0:T(8,128)S(1)}, u32[]{:S(2)}, u32[]{:S(2)}) collective-permute-start(f32[65,256]{1,0:T(8,128)S(1)} %get-tuple-element.775), channel_id=1, source_target_pairs={{0,3},{1,0},{2,1},{3,2},{4,7},{5,4},{6,5},{7,6},{8,11},{9,8},{10,9... | collective-permute-start | bytes 199688 | tf_op jit(solution)/shard_map/ppermute | solution.py:197
  (133 other events, 576.4 us)
Sparse Core Ops, SparseCore 0:
  30.6 34.8 all-gather.1
  362.3 54.5 reduce-scatter.1

commit v12 on v10

--- a/solution.py
+++ b/solution.py
@@ -177,6 +177,14 @@
     part = own_layer + partner_swap(other_layer, "pipe")
     examples = lax.axis_size("dp")
     example = lax.axis_index("dp")
+    share = part.shape[1] // examples
+    arrived = []
+    for step in range(1, examples):
+        target = lax.rem(example + step, examples)
+        piece = lax.dynamic_slice_in_dim(part, target * share, share, 1)
+        arrived.append(
+            lax.ppermute(piece, "dp", [(source, (source + step) % examples) for source in range(examples)])
+        )
     square = jnp.sum(part * part)
     total = lax.psum(square, "pipe")
     count = lax.axis_size("seq")
@@ -188,15 +196,12 @@
         step *= 2
     bound = math.sqrt(sections * (2 * rank + 1) * width)
     factor = bound / (jnp.sqrt(total) + 0.01 * bound)
-    scaled = factor * part
-    share = part.shape[1] // examples
-    combined = lax.dynamic_slice_in_dim(scaled, example * share, share, 1)
-    for step in range(1, examples):
-        target = lax.rem(example + step, examples)
-        piece = lax.dynamic_slice_in_dim(scaled, target * share, share, 1)
-        combined = combined + lax.ppermute(
-            piece, "dp", [(source, (source + step) % examples) for source in range(examples)]
-        )
+    combined = factor * lax.dynamic_slice_in_dim(part, example * share, share, 1)
+    for step, piece in enumerate(arrived, start=1):
+        other = lax.ppermute(
+            total, "dp", [(source, (source + step) % examples) for source in range(examples)]
+        )
+        combined = combined + (bound / (jnp.sqrt(other) + 0.01 * bound)) * piece
     out_a = combined[:rank]
     out_b = combined[rank : 2 * rank]
     out_g = combined[2 * rank :]

time: 440 us -> 452 us (1.027)
  starting transfers between devices: 38.4 us -> 51.9 us
  waiting for transfers between devices: 184 us -> 179 us
    ppermute x0 -> x3, starting transfers between devices: none -> 11.8 us  [on_device(): lax.ppermute(total, 'dp', [(source, (source + step) % examples) for sourc...]
    ppermute x3, waiting for transfers between devices: 5.52 us -> 0.01 us  [on_device(): lax.ppermute(piece, 'dp', [(source, (source + step) % examples) for sourc...]
  transfers between devices with their start and end apart: 22 -> 25, of which waited for: 21 -> 20; matrix products, arithmetic and copies ran while one was open for 17% -> 16% of each run, Pallas kernels for 0% -> 0%
where the time goes in v12:
time: 452 us; the launch traced here: 449 us
  waiting for transfers between devices  179 us (40%)
  matrix products  66.4 us (15%)
  starting transfers between devices  51.9 us (11%)
  Pallas kernels  50.2 us (11%)
  blocking collectives  47.6 us (11%)
  between operations  20.1 us (4%)
  local copies, waits for them, and re-layouts  15.4 us (3%)
  other arithmetic  14.5 us (3%)
    reduce_scatter x1, waiting for transfers between devices, on_device(): reduced = lax.psum_scatter(grads, 'seq', scatter_dimension=2, tiled=True)  78.9 us
    ppermute x11, waiting for transfers between devices, shifted(): lax.ppermute(value, axis, [(source, source + steps) for source in range(i...  53.5 us
    pallas_call x11, Pallas kernels, chain_step(): pl.pallas_call(functools.partial(chain_kernel, pairs, block_total), out_s...  50.2 us
    dot_general x22, matrix products, accumulate(): lax.dot_general(d_low, normalized_part, contract_first, preferred_element...  36.9 us
    psum x1, blocking collectives, on_device(): total = lax.psum(square, 'pipe')  31.9 us
    ppermute x3, waiting for transfers between devices, partner_swap(): lax.ppermute(value, axis, [(source, source ^ 1) for source in range(count)])  24.8 us
    dot_general x22, matrix products, accumulate(): lax.dot_general(low_part, source, contract_first, preferred_element_type=...  20.4 us
    all_gather x1, blocking collectives, on_device(): lax.all_gather(stacked, 'dp', axis=2, tiled=True)  15.7 us
  transfers between devices with their start and end apart: 25, of which 20 were waited for; matrix products, arithmetic and copies ran while one was open for 16% of the time, Pallas kernels for 0%

profile of v12, /device:TPU:6, one launch (start us, length us, event | category | flops | bytes accessed | tf_op | source)
XLA Modules:
  0.0 448.5 jit_solution(2382266823802896192)
XLA Ops:
  8.1 3.8 collective-permute-start.2
  12.0 2.0 collective-permute-done.2
  14.8 15.7 %all_gather.6 = bf16[2,65,1024]{2,1,0:T(8,128)(2,1)} all-gather(bf16[2,65,256]{2,1,0:T(8,128)(2,1)S(1)} %pad_maximum_fusion.1), channel_id=1, replica_groups=mesh['pipe'=16,'seq'=8,'dp'=4] {'dp'}, dimensions={2}, use_global_device_ids=true | all-gather | bytes 332800 | tf_op jit(solution)/shard_map/all_gather | solution.py:103
  30.5 2.3 dynamic-slice_bitcast_fusion
  32.8 1.9 collective-permute-start.1
  35.8 17.6 %collective-permute-done.1 = bf16[64,8192]{1,0:T(8,128)(2,1)} collective-permute-done((bf16[64,8192]{1,0:T(8,128)(2,1)}, bf16[64,8192]{1,0:T(8,128)(2,1)}, u32[]{:S(2)}, u32[]{:S(2)}) %collective-permute-start.1) | collective-permute-done | bytes 1048608 | tf_op jit(solution)/shard_map/ppermute | solution.py:22
  53.4 3.3 fusion.20
  57.0 8.5 %all-gather.2.cloned.1.call-done = bf16[2,65,8192]{2,1,0:T(8,128)(2,1)} async-done(((bf16[2,65,1024]{2,1,0:T(8,128)(2,1)}), bf16[2,65,8192]{2,1,0:T(8,128)(2,1)}) %all-gather.2.cloned.1.call-update) | async-done | bytes 2129936 | tf_op jit(solution)/shard_map/all_gather | solution.py:103
  66.5 1.9 convolution_convert_fusion
  68.5 1.8 convolution_convert_fusion.1
  71.0 3.4 fusion.23
  74.5 2.0 fusion.26
  77.8 188.2 %while.28 = (s32[]{:T(128)}, bf16[16,8192]{1,0:T(8,128)(2,1)S(1)}, f32[32,8192]{1,0:T(8,128)}, f32[32,8192]{1,0:T(8,128)S(1)}, f32[1,8192]{1,0:T(1,128)}, /*inde...) while((s32[]{:T(128)}, bf16[16,8192]{1,0:T(8,128)(2,1)S(1)}, ...), condition=%wide.region_3.4_spmd.clone, body=%wide.region_2.3_spmd.clone.sunk | while | flops 71352320 | bytes 40128352 | solution.py:170
  77.8 4.6 %eval_jaxpr.7 = (bf16[16,8192]{1,0:T(8,128)(2,1)}, bf16[16,8192]{1,0:T(8,128)(2,1)}, bf16[16,8192]{1,0:T(8,128)(2,1)}, bf16[16,32]{1,0:T(8,128)(2,1)}, bf16[16,3...) custom-call(s32[1]{0:T(128)} %bitcast.65.turn_ref, bf16[64,8192]{1,0:T(8,128)(2,1)} %get-tuple-element.1038.top_ref, ...), custom_call_target="tpu_custom_call" | custom-call | flops 33554432 | bytes 2097152 | tf_op jit(solution)/shard_map/while/body/eval_jaxpr/pallas_call | solution.py:68
  86.4 1.8 fusion.59
  90.0 9.4 %collective-permute-done = bf16[16,8192]{1,0:T(8,128)(2,1)S(1)} collective-permute-done((bf16[16,8192]{1,0:T(8,128)(2,1)}, bf16[16,8192]{1,0:T(8,128)(2,1)S(1)}, u32[]{:S(2)}, u32[]{:S(2)}) %collective-permute-start) | collective-permute-done | bytes 262176 | tf_op jit(solution)/shard_map/while/body/eval_jaxpr/ppermute | solution.py:17
  99.5 4.6 %eval_jaxpr.7 = (bf16[16,8192]{1,0:T(8,128)(2,1)}, bf16[16,8192]{1,0:T(8,128)(2,1)}, bf16[16,8192]{1,0:T(8,128)(2,1)}, bf16[16,32]{1,0:T(8,128)(2,1)}, bf16[16,3...) custom-call(s32[1]{0:T(128)} %bitcast.65.turn_ref, bf16[64,8192]{1,0:T(8,128)(2,1)} %get-tuple-element.1038.top_ref, ...), custom_call_target="tpu_custom_call" | custom-call | flops 33554432 | bytes 2097152 | tf_op jit(solution)/shard_map/while/body/eval_jaxpr/pallas_call | solution.py:68
  108.1 1.8 fusion.59
  111.7 7.3 %collective-permute-done = bf16[16,8192]{1,0:T(8,128)(2,1)S(1)} collective-permute-done((bf16[16,8192]{1,0:T(8,128)(2,1)}, bf16[16,8192]{1,0:T(8,128)(2,1)S(1)}, u32[]{:S(2)}, u32[]{:S(2)}) %collective-permute-start) | collective-permute-done | bytes 262176 | tf_op jit(solution)/shard_map/while/body/eval_jaxpr/ppermute | solution.py:17
  119.0 4.6 %eval_jaxpr.7 = (bf16[16,8192]{1,0:T(8,128)(2,1)}, bf16[16,8192]{1,0:T(8,128)(2,1)}, bf16[16,8192]{1,0:T(8,128)(2,1)}, bf16[16,32]{1,0:T(8,128)(2,1)}, bf16[16,3...) custom-call(s32[1]{0:T(128)} %bitcast.65.turn_ref, bf16[64,8192]{1,0:T(8,128)(2,1)} %get-tuple-element.1038.top_ref, ...), custom_call_target="tpu_custom_call" | custom-call | flops 33554432 | bytes 2097152 | tf_op jit(solution)/shard_map/while/body/eval_jaxpr/pallas_call | solution.py:68
  127.6 1.8 fusion.59
  131.2 4.8 %collective-permute-done = bf16[16,8192]{1,0:T(8,128)(2,1)S(1)} collective-permute-done((bf16[16,8192]{1,0:T(8,128)(2,1)}, bf16[16,8192]{1,0:T(8,128)(2,1)S(1)}, u32[]{:S(2)}, u32[]{:S(2)}) %collective-permute-start) | collective-permute-done | bytes 262176 | tf_op jit(solution)/shard_map/while/body/eval_jaxpr/ppermute | solution.py:17
  136.0 4.6 %eval_jaxpr.7 = (bf16[16,8192]{1,0:T(8,128)(2,1)}, bf16[16,8192]{1,0:T(8,128)(2,1)}, bf16[16,8192]{1,0:T(8,128)(2,1)}, bf16[16,32]{1,0:T(8,128)(2,1)}, bf16[16,3...) custom-call(s32[1]{0:T(128)} %bitcast.65.turn_ref, bf16[64,8192]{1,0:T(8,128)(2,1)} %get-tuple-element.1038.top_ref, ...), custom_call_target="tpu_custom_call" | custom-call | flops 33554432 | bytes 2097152 | tf_op jit(solution)/shard_map/while/body/eval_jaxpr/pallas_call | solution.py:68
  144.6 1.8 fusion.59
  148.3 3.9 collective-permute-done
  152.2 4.6 %eval_jaxpr.7 = (bf16[16,8192]{1,0:T(8,128)(2,1)}, bf16[16,8192]{1,0:T(8,128)(2,1)}, bf16[16,8192]{1,0:T(8,128)(2,1)}, bf16[16,32]{1,0:T(8,128)(2,1)}, bf16[16,3...) custom-call(s32[1]{0:T(128)} %bitcast.65.turn_ref, bf16[64,8192]{1,0:T(8,128)(2,1)} %get-tuple-element.1038.top_ref, ...), custom_call_target="tpu_custom_call" | custom-call | flops 33554432 | bytes 2097152 | tf_op jit(solution)/shard_map/while/body/eval_jaxpr/pallas_call | solution.py:68
  160.8 1.8 fusion.59
  164.4 3.0 collective-permute-done
  167.4 4.6 %eval_jaxpr.7 = (bf16[16,8192]{1,0:T(8,128)(2,1)}, bf16[16,8192]{1,0:T(8,128)(2,1)}, bf16[16,8192]{1,0:T(8,128)(2,1)}, bf16[16,32]{1,0:T(8,128)(2,1)}, bf16[16,3...) custom-call(s32[1]{0:T(128)} %bitcast.65.turn_ref, bf16[64,8192]{1,0:T(8,128)(2,1)} %get-tuple-element.1038.top_ref, ...), custom_call_target="tpu_custom_call" | custom-call | flops 33554432 | bytes 2097152 | tf_op jit(solution)/shard_map/while/body/eval_jaxpr/pallas_call | solution.py:68
  176.0 1.8 fusion.59
  179.6 6.1 %collective-permute-done = bf16[16,8192]{1,0:T(8,128)(2,1)S(1)} collective-permute-done((bf16[16,8192]{1,0:T(8,128)(2,1)}, bf16[16,8192]{1,0:T(8,128)(2,1)S(1)}, u32[]{:S(2)}, u32[]{:S(2)}) %collective-permute-start) | collective-permute-done | bytes 262176 | tf_op jit(solution)/shard_map/while/body/eval_jaxpr/ppermute | solution.py:17
  185.8 4.6 %eval_jaxpr.7 = (bf16[16,8192]{1,0:T(8,128)(2,1)}, bf16[16,8192]{1,0:T(8,128)(2,1)}, bf16[16,8192]{1,0:T(8,128)(2,1)}, bf16[16,32]{1,0:T(8,128)(2,1)}, bf16[16,3...) custom-call(s32[1]{0:T(128)} %bitcast.65.turn_ref, bf16[64,8192]{1,0:T(8,128)(2,1)} %get-tuple-element.1038.top_ref, ...), custom_call_target="tpu_custom_call" | custom-call | flops 33554432 | bytes 2097152 | tf_op jit(solution)/shard_map/while/body/eval_jaxpr/pallas_call | solution.py:68
  194.4 1.8 fusion.59
  198.0 2.7 collective-permute-done
  200.7 4.6 %eval_jaxpr.7 = (bf16[16,8192]{1,0:T(8,128)(2,1)}, bf16[16,8192]{1,0:T(8,128)(2,1)}, bf16[16,8192]{1,0:T(8,128)(2,1)}, bf16[16,32]{1,0:T(8,128)(2,1)}, bf16[16,3...) custom-call(s32[1]{0:T(128)} %bitcast.65.turn_ref, bf16[64,8192]{1,0:T(8,128)(2,1)} %get-tuple-element.1038.top_ref, ...), custom_call_target="tpu_custom_call" | custom-call | flops 33554432 | bytes 2097152 | tf_op jit(solution)/shard_map/while/body/eval_jaxpr/pallas_call | solution.py:68
  209.3 1.8 fusion.59
  212.9 3.0 collective-permute-done
  216.0 4.6 %eval_jaxpr.7 = (bf16[16,8192]{1,0:T(8,128)(2,1)}, bf16[16,8192]{1,0:T(8,128)(2,1)}, bf16[16,8192]{1,0:T(8,128)(2,1)}, bf16[16,32]{1,0:T(8,128)(2,1)}, bf16[16,3...) custom-call(s32[1]{0:T(128)} %bitcast.65.turn_ref, bf16[64,8192]{1,0:T(8,128)(2,1)} %get-tuple-element.1038.top_ref, ...), custom_call_target="tpu_custom_call" | custom-call | flops 33554432 | bytes 2097152 | tf_op jit(solution)/shard_map/while/body/eval_jaxpr/pallas_call | solution.py:68
  224.6 1.8 fusion.59
  228.2 4.7 %collective-permute-done = bf16[16,8192]{1,0:T(8,128)(2,1)S(1)} collective-permute-done((bf16[16,8192]{1,0:T(8,128)(2,1)}, bf16[16,8192]{1,0:T(8,128)(2,1)S(1)}, u32[]{:S(2)}, u32[]{:S(2)}) %collective-permute-start) | collective-permute-done | bytes 262176 | tf_op jit(solution)/shard_map/while/body/eval_jaxpr/ppermute | solution.py:17
  233.0 4.6 %eval_jaxpr.7 = (bf16[16,8192]{1,0:T(8,128)(2,1)}, bf16[16,8192]{1,0:T(8,128)(2,1)}, bf16[16,8192]{1,0:T(8,128)(2,1)}, bf16[16,32]{1,0:T(8,128)(2,1)}, bf16[16,3...) custom-call(s32[1]{0:T(128)} %bitcast.65.turn_ref, bf16[64,8192]{1,0:T(8,128)(2,1)} %get-tuple-element.1038.top_ref, ...), custom_call_target="tpu_custom_call" | custom-call | flops 33554432 | bytes 2097152 | tf_op jit(solution)/shard_map/while/body/eval_jaxpr/pallas_call | solution.py:68
  241.6 1.8 fusion.59
  245.2 2.8 collective-permute-done
  248.0 4.6 %eval_jaxpr.7 = (bf16[16,8192]{1,0:T(8,128)(2,1)}, bf16[16,8192]{1,0:T(8,128)(2,1)}, bf16[16,8192]{1,0:T(8,128)(2,1)}, bf16[16,32]{1,0:T(8,128)(2,1)}, bf16[16,3...) custom-call(s32[1]{0:T(128)} %bitcast.65.turn_ref, bf16[64,8192]{1,0:T(8,128)(2,1)} %get-tuple-element.1038.top_ref, ...), custom_call_target="tpu_custom_call" | custom-call | flops 33554432 | bytes 2097152 | tf_op jit(solution)/shard_map/while/body/eval_jaxpr/pallas_call | solution.py:68
  256.6 1.8 fusion.59
  260.2 5.7 %collective-permute-done = bf16[16,8192]{1,0:T(8,128)(2,1)S(1)} collective-permute-done((bf16[16,8192]{1,0:T(8,128)(2,1)}, bf16[16,8192]{1,0:T(8,128)(2,1)S(1)}, u32[]{:S(2)}, u32[]{:S(2)}) %collective-permute-start) | collective-permute-done | bytes 262176 | tf_op jit(solution)/shard_map/while/body/eval_jaxpr/ppermute | solution.py:17
  266.0 1.6 maximum_bitcast_fusion
  268.1 2.6 pad_maximum_fusion
  270.7 78.9 %reduce-scatter.2.cloned.1.call-done = f32[2,65,1024]{2,1,0:T(8,128)} async-done(((f32[2,65,8192]{2,1,0:T(8,128)}), f32[2,65,1024]{2,1,0:T(8,128)}) %reduce-scatter.2.cloned.1.call-update) | async-done | bytes 532496 | tf_op jit(solution)/shard_map/reduce_scatter | solution.py:174
  350.6 3.4 collective-permute-start.3
  354.1 5.2 %collective-permute-done.3 = f32[65,1024]{1,0:T(8,128)S(1)} collective-permute-done((f32[65,1024]{1,0:T(8,128)S(1)}, f32[65,1024]{1,0:T(8,128)S(1)}, u32[]{:S(2)}, u32[]{:S(2)}) %collective-permute-start.3) | collective-permute-done | bytes 266272 | tf_op jit(solution)/shard_map/ppermute | solution.py:22
  359.2 1.7 multiply_reduce_fusion
  361.0 3.3 collective-permute-start.10
  364.3 1.9 collective-permute-start.12
  366.2 5.1 %collective-permute-start.8 = (f32[65,256]{1,0:T(8,128)S(1)}, f32[65,256]{1,0:T(8,128)S(1)}, u32[]{:S(2)}, u32[]{:S(2)}) collective-permute-start(f32[65,256]{1,0:T(8,128)S(1)} %get-tuple-element.774), channel_id=1, source_target_pairs={{0,1},{1,2},{2,3},{3,0},{4,5},{5,6},{6,7},{7,4},{8,9},{9,10},{10,1... | collective-permute-start | bytes 199688 | tf_op jit(solution)/shard_map/ppermute | solution.py:186
  371.4 31.9 %psum.7 = f32[]{:T(128)} all-reduce(f32[]{:T(128)} %get-tuple-element.754), channel_id=1, replica_groups=mesh['pipe'=16,'seq'=8,'dp'=4] {'pipe'}, use_global_device_ids=true, to_apply=%region_6.7 | all-reduce | flops 1 | bytes 8 | tf_op jit(solution)/shard_map/psum | solution.py:189
  403.3 4.4 collective-permute-done.4
  408.9 3.2 collective-permute-start.5
  412.1 3.6 collective-permute-done.5
  416.3 3.2 collective-permute-start.6
  419.5 3.9 collective-permute-done.6
  423.9 4.2 collective-permute-start.7
  428.1 3.2 collective-permute-start.9
  431.4 4.5 %collective-permute-start.11 = (f32[]{:T(128)}, f32[]{:T(128)}, u32[]{:S(2)}, u32[]{:S(2)}) collective-permute-start(f32[]{:T(128)} %add.189), channel_id=1, source_target_pairs={{0,3},{1,0},{2,1},{3,2},{4,7},{5,4},{6,5},{7,6},{8,11},{9,8},{10,9... | collective-permute-start | bytes 20 | tf_op jit(solution)/shard_map/ppermute | solution.py:201
  (537 shorter events, 71.3 us)
Async XLA Ops:
  7.2 27.6 %copy-start = (bf16[1,128,8192]{2,1,0:T(8,128)(2,1)S(1)}, bf16[1,128,8192]{2,1,0:T(8,128)(2,1)}, u32[]{:S(2)}) copy-start(bf16[1,128,8192]{2,1,0:T(8,128)(2,1)} %param.8) | copy-start | bytes 6291460
  7.2 58.3 %all-gather.2.cloned.1.call-start = ((), (), s32[]{:S(2)}) async-start(), calls=%async_computation.1 | async-start | bytes 2654208 | tf_op jit(solution)/shard_map/all_gather | solution.py:103
  8.1 5.8 %collective-permute-start.2 = (bf16[65,256]{1,0:T(8,128)(2,1)S(1)}, bf16[65,256]{1,0:T(8,128)(2,1)S(1)}, u32[]{:S(2)}, u32[]{:S(2)}) collective-permute-start(bf16[65,256]{1,0:T(8,128)(2,1)S(1)} %pad_maximum_fusion.2), channel_id=1, source_target_pairs={{0,32},{32,0},{64,96},{96,64},{128,160},{160,128},{192,224},{224,1... | collective-permute-start | bytes 99848 | tf_op jit(solution)/shard_map/ppermute | solution.py:22
  30.4 319.1 %reduce-scatter.2.cloned.1.call-start = ((), (), s32[]{:S(2)}) async-start(), calls=%async_computation.2 | async-start | bytes 5308416 | tf_op jit(solution)/shard_map/reduce_scatter | solution.py:174
  32.8 20.6 %collective-permute-start.1 = (bf16[64,8192]{1,0:T(8,128)(2,1)}, bf16[64,8192]{1,0:T(8,128)(2,1)}, u32[]{:S(2)}, u32[]{:S(2)}) collective-permute-start(bf16[64,8192]{1,0:T(8,128)(2,1)} %dynamic-slice_bitcast_fusion), channel_id=1, source_target_pairs={{0,32},{32,0},{64,96},{96,64},{128,160},{160,128},{192,224},{224,1... | collective-permute-start | bytes 3145736 | tf_op jit(solution)/shard_map/ppermute | solution.py:22
  34.8 18.6 %copy-start.6 = (bf16[1,1,128,8192]{3,2,1,0:T(8,128)(2,1)S(1)}, bf16[1,1,128,8192]{3,2,1,0:T(8,128)(2,1)}, u32[]{:S(2)}) copy-start(bf16[1,1,128,8192]{3,2,1,0:T(8,128)(2,1)} %param.7) | copy-start | bytes 6291460
  66.5 4.5 %copy-start.20 = (f32[1,1,8192]{2,1,0:T(1,128)}, f32[1,1,8192]{2,1,0:T(1,128)S(1)}, u32[]{:S(2)}) copy-start(f32[1,1,8192]{2,1,0:T(1,128)S(1)} %get-tuple-element.768) | copy-start | bytes 98308
  66.5 8.0 %copy-start.22 = (f32[1,1,8192]{2,1,0:T(1,128)}, f32[1,1,8192]{2,1,0:T(1,128)S(1)}, u32[]{:S(2)}) copy-start(f32[1,1,8192]{2,1,0:T(1,128)S(1)} %get-tuple-element.769) | copy-start | bytes 98308
  82.4 17.0 %collective-permute-start = (bf16[16,8192]{1,0:T(8,128)(2,1)}, bf16[16,8192]{1,0:T(8,128)(2,1)S(1)}, u32[]{:S(2)}, u32[]{:S(2)}) collective-permute-start(bf16[16,8192]{1,0:T(8,128)(2,1)} %get-tuple-element.955), channel_id=1, source_target_pairs={{64,0},{96,32},{128,64},{160,96},{192,128},{224,160},{256,192},{28... | collective-permute-start | bytes 786440 | tf_op jit(solution)/shard_map/while/body/eval_jaxpr/ppermute | solution.py:17
  88.2 11.2 %copy-start.14 = (f32[32,8192]{1,0:T(8,128)}, f32[32,8192]{1,0:T(8,128)S(1)}, u32[]{:S(2)}) copy-start(f32[32,8192]{1,0:T(8,128)S(1)} %fusion.59) | copy-start | bytes 3145732 | tf_op jit(solution)/shard_map/while
  88.4 11.0 %copy-start.9 = (f32[1,8192]{1,0:T(1,128)}, f32[1,8192]{1,0:T(1,128)S(1)}, u32[]{:S(2)}) copy-start(f32[1,8192]{1,0:T(1,128)S(1)} %get-tuple-element.1034) | copy-start | bytes 98308 | tf_op jit(solution)/shard_map/while
  88.4 11.0 %copy-start.11 = (f32[1,8192]{1,0:T(1,128)}, f32[1,8192]{1,0:T(1,128)S(1)}, u32[]{:S(2)}) copy-start(f32[1,8192]{1,0:T(1,128)S(1)} %get-tuple-element.1037) | copy-start | bytes 98308 | tf_op jit(solution)/shard_map/while
  90.0 9.4 %copy-start.16 = (f32[32,8192]{1,0:T(8,128)}, f32[32,8192]{1,0:T(8,128)S(1)}, u32[]{:S(2)}) copy-start(f32[32,8192]{1,0:T(8,128)S(1)} %fusion.62) | copy-start | bytes 3145732 | tf_op jit(solution)/shard_map/while
  104.0 14.9 %collective-permute-start = (bf16[16,8192]{1,0:T(8,128)(2,1)}, bf16[16,8192]{1,0:T(8,128)(2,1)S(1)}, u32[]{:S(2)}, u32[]{:S(2)}) collective-permute-start(bf16[16,8192]{1,0:T(8,128)(2,1)} %get-tuple-element.955), channel_id=1, source_target_pairs={{64,0},{96,32},{128,64},{160,96},{192,128},{224,160},{256,192},{28... | collective-permute-start | bytes 786440 | tf_op jit(solution)/shard_map/while/body/eval_jaxpr/ppermute | solution.py:17
  109.9 9.1 %copy-start.14 = (f32[32,8192]{1,0:T(8,128)}, f32[32,8192]{1,0:T(8,128)S(1)}, u32[]{:S(2)}) copy-start(f32[32,8192]{1,0:T(8,128)S(1)} %fusion.59) | copy-start | bytes 3145732 | tf_op jit(solution)/shard_map/while
  110.1 8.9 %copy-start.9 = (f32[1,8192]{1,0:T(1,128)}, f32[1,8192]{1,0:T(1,128)S(1)}, u32[]{:S(2)}) copy-start(f32[1,8192]{1,0:T(1,128)S(1)} %get-tuple-element.1034) | copy-start | bytes 98308 | tf_op jit(solution)/shard_map/while
  110.1 8.9 %copy-start.11 = (f32[1,8192]{1,0:T(1,128)}, f32[1,8192]{1,0:T(1,128)S(1)}, u32[]{:S(2)}) copy-start(f32[1,8192]{1,0:T(1,128)S(1)} %get-tuple-element.1037) | copy-start | bytes 98308 | tf_op jit(solution)/shard_map/while
  111.7 7.3 %copy-start.16 = (f32[32,8192]{1,0:T(8,128)}, f32[32,8192]{1,0:T(8,128)S(1)}, u32[]{:S(2)}) copy-start(f32[32,8192]{1,0:T(8,128)S(1)} %fusion.62) | copy-start | bytes 3145732 | tf_op jit(solution)/shard_map/while
  123.6 12.4 %collective-permute-start = (bf16[16,8192]{1,0:T(8,128)(2,1)}, bf16[16,8192]{1,0:T(8,128)(2,1)S(1)}, u32[]{:S(2)}, u32[]{:S(2)}) collective-permute-start(bf16[16,8192]{1,0:T(8,128)(2,1)} %get-tuple-element.955), channel_id=1, source_target_pairs={{64,0},{96,32},{128,64},{160,96},{192,128},{224,160},{256,192},{28... | collective-permute-start | bytes 786440 | tf_op jit(solution)/shard_map/while/body/eval_jaxpr/ppermute | solution.py:17
  129.4 6.6 %copy-start.14 = (f32[32,8192]{1,0:T(8,128)}, f32[32,8192]{1,0:T(8,128)S(1)}, u32[]{:S(2)}) copy-start(f32[32,8192]{1,0:T(8,128)S(1)} %fusion.59) | copy-start | bytes 3145732 | tf_op jit(solution)/shard_map/while
  129.6 6.4 %copy-start.9 = (f32[1,8192]{1,0:T(1,128)}, f32[1,8192]{1,0:T(1,128)S(1)}, u32[]{:S(2)}) copy-start(f32[1,8192]{1,0:T(1,128)S(1)} %get-tuple-element.1034) | copy-start | bytes 98308 | tf_op jit(solution)/shard_map/while
  129.6 6.4 %copy-start.11 = (f32[1,8192]{1,0:T(1,128)}, f32[1,8192]{1,0:T(1,128)S(1)}, u32[]{:S(2)}) copy-start(f32[1,8192]{1,0:T(1,128)S(1)} %get-tuple-element.1037) | copy-start | bytes 98308 | tf_op jit(solution)/shard_map/while
  131.2 4.8 %copy-start.16 = (f32[32,8192]{1,0:T(8,128)}, f32[32,8192]{1,0:T(8,128)S(1)}, u32[]{:S(2)}) copy-start(f32[32,8192]{1,0:T(8,128)S(1)} %fusion.62) | copy-start | bytes 3145732 | tf_op jit(solution)/shard_map/while
  140.6 11.6 %collective-permute-start = (bf16[16,8192]{1,0:T(8,128)(2,1)}, bf16[16,8192]{1,0:T(8,128)(2,1)S(1)}, u32[]{:S(2)}, u32[]{:S(2)}) collective-permute-start(bf16[16,8192]{1,0:T(8,128)(2,1)} %get-tuple-element.955), channel_id=1, source_target_pairs={{64,0},{96,32},{128,64},{160,96},{192,128},{224,160},{256,192},{28... | collective-permute-start | bytes 786440 | tf_op jit(solution)/shard_map/while/body/eval_jaxpr/ppermute | solution.py:17
  146.5 5.7 %copy-start.14 = (f32[32,8192]{1,0:T(8,128)}, f32[32,8192]{1,0:T(8,128)S(1)}, u32[]{:S(2)}) copy-start(f32[32,8192]{1,0:T(8,128)S(1)} %fusion.59) | copy-start | bytes 3145732 | tf_op jit(solution)/shard_map/while
  146.6 5.5 %copy-start.9 = (f32[1,8192]{1,0:T(1,128)}, f32[1,8192]{1,0:T(1,128)S(1)}, u32[]{:S(2)}) copy-start(f32[1,8192]{1,0:T(1,128)S(1)} %get-tuple-element.1034) | copy-start | bytes 98308 | tf_op jit(solution)/shard_map/while
  146.6 5.5 %copy-start.11 = (f32[1,8192]{1,0:T(1,128)}, f32[1,8192]{1,0:T(1,128)S(1)}, u32[]{:S(2)}) copy-start(f32[1,8192]{1,0:T(1,128)S(1)} %get-tuple-element.1037) | copy-start | bytes 98308 | tf_op jit(solution)/shard_map/while
  156.8 10.6 %collective-permute-start = (bf16[16,8192]{1,0:T(8,128)(2,1)}, bf16[16,8192]{1,0:T(8,128)(2,1)S(1)}, u32[]{:S(2)}, u32[]{:S(2)}) collective-permute-start(bf16[16,8192]{1,0:T(8,128)(2,1)} %get-tuple-element.955), channel_id=1, source_target_pairs={{64,0},{96,32},{128,64},{160,96},{192,128},{224,160},{256,192},{28... | collective-permute-start | bytes 786440 | tf_op jit(solution)/shard_map/while/body/eval_jaxpr/ppermute | solution.py:17
  162.6 4.8 %copy-start.14 = (f32[32,8192]{1,0:T(8,128)}, f32[32,8192]{1,0:T(8,128)S(1)}, u32[]{:S(2)}) copy-start(f32[32,8192]{1,0:T(8,128)S(1)} %fusion.59) | copy-start | bytes 3145732 | tf_op jit(solution)/shard_map/while
  162.8 4.6 %copy-start.9 = (f32[1,8192]{1,0:T(1,128)}, f32[1,8192]{1,0:T(1,128)S(1)}, u32[]{:S(2)}) copy-start(f32[1,8192]{1,0:T(1,128)S(1)} %get-tuple-element.1034) | copy-start | bytes 98308 | tf_op jit(solution)/shard_map/while
  162.8 4.6 %copy-start.11 = (f32[1,8192]{1,0:T(1,128)}, f32[1,8192]{1,0:T(1,128)S(1)}, u32[]{:S(2)}) copy-start(f32[1,8192]{1,0:T(1,128)S(1)} %get-tuple-element.1037) | copy-start | bytes 98308 | tf_op jit(solution)/shard_map/while
  172.0 13.8 %collective-permute-start = (bf16[16,8192]{1,0:T(8,128)(2,1)}, bf16[16,8192]{1,0:T(8,128)(2,1)S(1)}, u32[]{:S(2)}, u32[]{:S(2)}) collective-permute-start(bf16[16,8192]{1,0:T(8,128)(2,1)} %get-tuple-element.955), channel_id=1, source_target_pairs={{64,0},{96,32},{128,64},{160,96},{192,128},{224,160},{256,192},{28... | collective-permute-start | bytes 786440 | tf_op jit(solution)/shard_map/while/body/eval_jaxpr/ppermute | solution.py:17
  177.8 7.9 %copy-start.14 = (f32[32,8192]{1,0:T(8,128)}, f32[32,8192]{1,0:T(8,128)S(1)}, u32[]{:S(2)}) copy-start(f32[32,8192]{1,0:T(8,128)S(1)} %fusion.59) | copy-start | bytes 3145732 | tf_op jit(solution)/shard_map/while
  178.0 7.8 %copy-start.9 = (f32[1,8192]{1,0:T(1,128)}, f32[1,8192]{1,0:T(1,128)S(1)}, u32[]{:S(2)}) copy-start(f32[1,8192]{1,0:T(1,128)S(1)} %get-tuple-element.1034) | copy-start | bytes 98308 | tf_op jit(solution)/shard_map/while
  178.0 7.8 %copy-start.11 = (f32[1,8192]{1,0:T(1,128)}, f32[1,8192]{1,0:T(1,128)S(1)}, u32[]{:S(2)}) copy-start(f32[1,8192]{1,0:T(1,128)S(1)} %get-tuple-element.1037) | copy-start | bytes 98308 | tf_op jit(solution)/shard_map/while
  179.6 6.2 %copy-start.16 = (f32[32,8192]{1,0:T(8,128)}, f32[32,8192]{1,0:T(8,128)S(1)}, u32[]{:S(2)}) copy-start(f32[32,8192]{1,0:T(8,128)S(1)} %fusion.62) | copy-start | bytes 3145732 | tf_op jit(solution)/shard_map/while
  190.4 10.3 %collective-permute-start = (bf16[16,8192]{1,0:T(8,128)(2,1)}, bf16[16,8192]{1,0:T(8,128)(2,1)S(1)}, u32[]{:S(2)}, u32[]{:S(2)}) collective-permute-start(bf16[16,8192]{1,0:T(8,128)(2,1)} %get-tuple-element.955), channel_id=1, source_target_pairs={{64,0},{96,32},{128,64},{160,96},{192,128},{224,160},{256,192},{28... | collective-permute-start | bytes 786440 | tf_op jit(solution)/shard_map/while/body/eval_jaxpr/ppermute | solution.py:17
  196.2 4.5 %copy-start.14 = (f32[32,8192]{1,0:T(8,128)}, f32[32,8192]{1,0:T(8,128)S(1)}, u32[]{:S(2)}) copy-start(f32[32,8192]{1,0:T(8,128)S(1)} %fusion.59) | copy-start | bytes 3145732 | tf_op jit(solution)/shard_map/while
  205.3 10.7 %collective-permute-start = (bf16[16,8192]{1,0:T(8,128)(2,1)}, bf16[16,8192]{1,0:T(8,128)(2,1)S(1)}, u32[]{:S(2)}, u32[]{:S(2)}) collective-permute-start(bf16[16,8192]{1,0:T(8,128)(2,1)} %get-tuple-element.955), channel_id=1, source_target_pairs={{64,0},{96,32},{128,64},{160,96},{192,128},{224,160},{256,192},{28... | collective-permute-start | bytes 786440 | tf_op jit(solution)/shard_map/while/body/eval_jaxpr/ppermute | solution.py:17
  211.1 4.8 %copy-start.14 = (f32[32,8192]{1,0:T(8,128)}, f32[32,8192]{1,0:T(8,128)S(1)}, u32[]{:S(2)}) copy-start(f32[32,8192]{1,0:T(8,128)S(1)} %fusion.59) | copy-start | bytes 3145732 | tf_op jit(solution)/shard_map/while
  211.3 4.7 %copy-start.9 = (f32[1,8192]{1,0:T(1,128)}, f32[1,8192]{1,0:T(1,128)S(1)}, u32[]{:S(2)}) copy-start(f32[1,8192]{1,0:T(1,128)S(1)} %get-tuple-element.1034) | copy-start | bytes 98308 | tf_op jit(solution)/shard_map/while
  211.3 4.7 %copy-start.11 = (f32[1,8192]{1,0:T(1,128)}, f32[1,8192]{1,0:T(1,128)S(1)}, u32[]{:S(2)}) copy-start(f32[1,8192]{1,0:T(1,128)S(1)} %get-tuple-element.1037) | copy-start | bytes 98308 | tf_op jit(solution)/shard_map/while
  220.6 12.4 %collective-permute-start = (bf16[16,8192]{1,0:T(8,128)(2,1)}, bf16[16,8192]{1,0:T(8,128)(2,1)S(1)}, u32[]{:S(2)}, u32[]{:S(2)}) collective-permute-start(bf16[16,8192]{1,0:T(8,128)(2,1)} %get-tuple-element.955), channel_id=1, source_target_pairs={{64,0},{96,32},{128,64},{160,96},{192,128},{224,160},{256,192},{28... | collective-permute-start | bytes 786440 | tf_op jit(solution)/shard_map/while/body/eval_jaxpr/ppermute | solution.py:17
  226.4 6.5 %copy-start.14 = (f32[32,8192]{1,0:T(8,128)}, f32[32,8192]{1,0:T(8,128)S(1)}, u32[]{:S(2)}) copy-start(f32[32,8192]{1,0:T(8,128)S(1)} %fusion.59) | copy-start | bytes 3145732 | tf_op jit(solution)/shard_map/while
  226.6 6.4 %copy-start.9 = (f32[1,8192]{1,0:T(1,128)}, f32[1,8192]{1,0:T(1,128)S(1)}, u32[]{:S(2)}) copy-start(f32[1,8192]{1,0:T(1,128)S(1)} %get-tuple-element.1034) | copy-start | bytes 98308 | tf_op jit(solution)/shard_map/while
  226.6 6.4 %copy-start.11 = (f32[1,8192]{1,0:T(1,128)}, f32[1,8192]{1,0:T(1,128)S(1)}, u32[]{:S(2)}) copy-start(f32[1,8192]{1,0:T(1,128)S(1)} %get-tuple-element.1037) | copy-start | bytes 98308 | tf_op jit(solution)/shard_map/while
  228.2 4.8 %copy-start.16 = (f32[32,8192]{1,0:T(8,128)}, f32[32,8192]{1,0:T(8,128)S(1)}, u32[]{:S(2)}) copy-start(f32[32,8192]{1,0:T(8,128)S(1)} %fusion.62) | copy-start | bytes 3145732 | tf_op jit(solution)/shard_map/while
  237.6 10.4 %collective-permute-start = (bf16[16,8192]{1,0:T(8,128)(2,1)}, bf16[16,8192]{1,0:T(8,128)(2,1)S(1)}, u32[]{:S(2)}, u32[]{:S(2)}) collective-permute-start(bf16[16,8192]{1,0:T(8,128)(2,1)} %get-tuple-element.955), channel_id=1, source_target_pairs={{64,0},{96,32},{128,64},{160,96},{192,128},{224,160},{256,192},{28... | collective-permute-start | bytes 786440 | tf_op jit(solution)/shard_map/while/body/eval_jaxpr/ppermute | solution.py:17
  243.4 4.6 %copy-start.14 = (f32[32,8192]{1,0:T(8,128)}, f32[32,8192]{1,0:T(8,128)S(1)}, u32[]{:S(2)}) copy-start(f32[32,8192]{1,0:T(8,128)S(1)} %fusion.59) | copy-start | bytes 3145732 | tf_op jit(solution)/shard_map/while
  252.6 13.3 %collective-permute-start = (bf16[16,8192]{1,0:T(8,128)(2,1)}, bf16[16,8192]{1,0:T(8,128)(2,1)S(1)}, u32[]{:S(2)}, u32[]{:S(2)}) collective-permute-start(bf16[16,8192]{1,0:T(8,128)(2,1)} %get-tuple-element.955), channel_id=1, source_target_pairs={{64,0},{96,32},{128,64},{160,96},{192,128},{224,160},{256,192},{28... | collective-permute-start | bytes 786440 | tf_op jit(solution)/shard_map/while/body/eval_jaxpr/ppermute | solution.py:17
  258.4 7.5 %copy-start.14 = (f32[32,8192]{1,0:T(8,128)}, f32[32,8192]{1,0:T(8,128)S(1)}, u32[]{:S(2)}) copy-start(f32[32,8192]{1,0:T(8,128)S(1)} %fusion.59) | copy-start | bytes 3145732 | tf_op jit(solution)/shard_map/while
  258.6 7.3 %copy-start.9 = (f32[1,8192]{1,0:T(1,128)}, f32[1,8192]{1,0:T(1,128)S(1)}, u32[]{:S(2)}) copy-start(f32[1,8192]{1,0:T(1,128)S(1)} %get-tuple-element.1034) | copy-start | bytes 98308 | tf_op jit(solution)/shard_map/while
  258.6 7.3 %copy-start.11 = (f32[1,8192]{1,0:T(1,128)}, f32[1,8192]{1,0:T(1,128)S(1)}, u32[]{:S(2)}) copy-start(f32[1,8192]{1,0:T(1,128)S(1)} %get-tuple-element.1037) | copy-start | bytes 98308 | tf_op jit(solution)/shard_map/while
  260.2 5.7 %copy-start.16 = (f32[32,8192]{1,0:T(8,128)}, f32[32,8192]{1,0:T(8,128)S(1)}, u32[]{:S(2)}) copy-start(f32[32,8192]{1,0:T(8,128)S(1)} %fusion.62) | copy-start | bytes 3145732 | tf_op jit(solution)/shard_map/while
  350.6 8.6 %collective-permute-start.3 = (f32[65,1024]{1,0:T(8,128)S(1)}, f32[65,1024]{1,0:T(8,128)S(1)}, u32[]{:S(2)}, u32[]{:S(2)}) collective-permute-start(f32[65,1024]{1,0:T(8,128)S(1)} %select_bitcast_fusion), channel_id=1, source_target_pairs={{0,32},{32,0},{64,96},{96,64},{128,160},{160,128},{192,224},{224,1... | collective-permute-start | bytes 798728 | tf_op jit(solution)/shard_map/ppermute | solution.py:22
  361.0 78.3 %collective-permute-start.10 = (f32[65,256]{1,0:T(8,128)S(1)}, f32[65,256]{1,0:T(8,128)S(1)}, u32[]{:S(2)}, u32[]{:S(2)}) collective-permute-start(f32[65,256]{1,0:T(8,128)S(1)} %get-tuple-element.775), channel_id=1, source_target_pairs={{0,2},{1,3},{2,0},{3,1},{4,6},{5,7},{6,4},{7,5},{8,10},{9,11},{10,... | collective-permute-start | bytes 199688 | tf_op jit(solution)/shard_map/ppermute | solution.py:186
  364.3 75.0 %collective-permute-start.12 = (f32[65,256]{1,0:T(8,128)S(1)}, f32[65,256]{1,0:T(8,128)S(1)}, u32[]{:S(2)}, u32[]{:S(2)}) collective-permute-start(f32[65,256]{1,0:T(8,128)S(1)} %get-tuple-element.776), channel_id=1, source_target_pairs={{0,3},{1,0},{2,1},{3,2},{4,7},{5,4},{6,5},{7,6},{8,11},{9,8},{10,9... | collective-permute-start | bytes 199688 | tf_op jit(solution)/shard_map/ppermute | solution.py:186
  366.2 73.1 %collective-permute-start.8 = (f32[65,256]{1,0:T(8,128)S(1)}, f32[65,256]{1,0:T(8,128)S(1)}, u32[]{:S(2)}, u32[]{:S(2)}) collective-permute-start(f32[65,256]{1,0:T(8,128)S(1)} %get-tuple-element.774), channel_id=1, source_target_pairs={{0,1},{1,2},{2,3},{3,0},{4,5},{5,6},{6,7},{7,4},{8,9},{9,10},{10,1... | collective-permute-start | bytes 199688 | tf_op jit(solution)/shard_map/ppermute | solution.py:186
  403.3 4.4 collective-permute-start.4
  408.9 6.8 %collective-permute-start.5 = (f32[]{:T(128)}, f32[]{:T(128)}, u32[]{:S(2)}, u32[]{:S(2)}) collective-permute-start(f32[]{:T(128)} %add.187), channel_id=1, source_target_pairs={{0,8},{4,12},{8,16},{12,20},{16,24},{20,28},{24,0},{28,4},{1,9},{5... | collective-permute-start | bytes 20 | tf_op jit(solution)/shard_map/ppermute | solution.py:193
  416.3 7.1 %collective-permute-start.6 = (f32[]{:T(128)}, f32[]{:T(128)}, u32[]{:S(2)}, u32[]{:S(2)}) collective-permute-start(f32[]{:T(128)} %add.188), channel_id=1, source_target_pairs={{0,16},{4,20},{8,24},{12,28},{16,0},{20,4},{24,8},{28,12},{1,17},{... | collective-permute-start | bytes 20 | tf_op jit(solution)/shard_map/ppermute | solution.py:193
  423.9 7.4 %collective-permute-start.7 = (f32[]{:T(128)}, f32[]{:T(128)}, u32[]{:S(2)}, u32[]{:S(2)}) collective-permute-start(f32[]{:T(128)} %add.189), channel_id=1, source_target_pairs={{0,1},{1,2},{2,3},{3,0},{4,5},{5,6},{6,7},{7,4},{8,9},{9,10},{10,1... | collective-permute-start | bytes 20 | tf_op jit(solution)/shard_map/ppermute | solution.py:201
  428.1 8.5 %collective-permute-start.9 = (f32[]{:T(128)}, f32[]{:T(128)}, u32[]{:S(2)}, u32[]{:S(2)}) collective-permute-start(f32[]{:T(128)} %add.189), channel_id=1, source_target_pairs={{0,2},{1,3},{2,0},{3,1},{4,6},{5,7},{6,4},{7,5},{8,10},{9,11},{10,... | collective-permute-start | bytes 20 | tf_op jit(solution)/shard_map/ppermute | solution.py:201
  431.4 7.3 %collective-permute-start.11 = (f32[]{:T(128)}, f32[]{:T(128)}, u32[]{:S(2)}, u32[]{:S(2)}) collective-permute-start(f32[]{:T(128)} %add.189), channel_id=1, source_target_pairs={{0,3},{1,0},{2,1},{3,2},{4,7},{5,4},{6,5},{7,6},{8,11},{9,8},{10,9... | collective-permute-start | bytes 20 | tf_op jit(solution)/shard_map/ppermute | solution.py:201
  (179 other events, 387.6 us)
Sparse Core Ops, SparseCore 0:
  30.6 34.8 all-gather.1
  270.8 78.7 reduce-scatter.1
